TPU v7x, 32 devices: a whole 2x2x4 slice. The times are simulated.
32 devices in a mesh: dp: 8 (over y, x, core), mp: 4 (over z).
Axes of the slice: x: 2, y: 2, z: 4, core: 2. Of those that a mesh axis runs over, the one named last changes fastest.
Arguments:
- inputs: bfloat16 [120, 128, 768], P('dp'), may hold values from -6 to 6
- timesteps: int32 [120], P('dp'), may hold values from 0 to 999
- segments: int32 [120, 128], P('dp'), may hold values from 0 to 5, never falling along the last dimension, each value on 1 to 48 neighbouring positions
- valid_mask: int32 [120, 128], P('dp'), may hold values from 0 to 1, as said below
- step_table: bfloat16 [1000, 768], replicated, may hold values from -6 to 6
- ln1_gain: float32 [768], replicated, may hold values from 0.5 to 1.5
- ln1_shift: float32 [768], replicated, may hold values from -1 to 1
- w_query: bfloat16 [768, 768], P(None, 'mp'), may hold values from -0.21875 to 0.21875
- b_query: float32 [768], P('mp'), may hold values from -1 to 1
- w_key: bfloat16 [768, 768], P(None, 'mp'), may hold values from -0.21875 to 0.21875
- w_value: bfloat16 [768, 768], P(None, 'mp'), may hold values from -0.21875 to 0.21875
- b_value: float32 [768], P('mp'), may hold values from -1 to 1
- w_out: bfloat16 [768, 768], P('mp'), may hold values from -0.875 to 0.875
- b_out: float32 [768], replicated, may hold values from -1 to 1
- ln2_gain: float32 [768], replicated, may hold values from 0.5 to 1.5
- ln2_shift: float32 [768], replicated, may hold values from -1 to 1
- w_up: bfloat16 [768, 3072], P(None, 'mp'), may hold values from -0.21875 to 0.21875
- b_up: float32 [3072], P('mp'), may hold values from -1 to 1
- w_down: bfloat16 [3072, 768], P('mp'), may hold values from -0.109375 to 0.109375
- b_down: float32 [768], replicated, may hold values from -1 to 1
- cotangent: bfloat16 [120, 128, 768], P('dp'), may hold values from -6 to 6
Outputs:
- output: bfloat16 [120, 128, 768], P('dp')
- input_grad: bfloat16 [120, 128, 768], P('dp')
- grad_ln1_gain: float32 [768], replicated
- grad_ln1_shift: float32 [768], replicated
- grad_w_query: float32 [768, 768], P(None, 'mp')
- grad_b_query: float32 [768], P('mp')
- grad_w_key: float32 [768, 768], P(None, 'mp')
- grad_w_value: float32 [768, 768], P(None, 'mp')
- grad_b_value: float32 [768], P('mp')
- grad_w_out: float32 [768, 768], P('mp')
- grad_b_out: float32 [768], replicated
- grad_ln2_gain: float32 [768], replicated
- grad_ln2_shift: float32 [768], replicated
- grad_w_up: float32 [768, 3072], P(None, 'mp')
- grad_b_up: float32 [3072], P('mp')
- grad_w_down: float32 [3072, 768], P('mp')
- grad_b_down: float32 [768], replicated
- table_grad: float32 [1000, 768], P(None, 'mp')
Inputs may be any that keep to these rules, and one draw needn't show every extreme that they name: `valid_mask`: in each row the zeros, if any, are its last positions.
All inputs are finite; a program needn't handle non-finite values.
Results may differ from a plain program's by a relative error of at most 0.014.
Values sent between devices are 32-bit elements; how exact they have to be, the bound alone decides.
No kernel may reach another device: no remote copies, remote signals or barrier semaphores. Data moves between devices by JAX's collectives and lax.ppermute only.
A program may use at most 192 MiB of HBM per device.

v0:
```python
import math

import jax
import jax.numpy as jnp
from jax import lax
from jax.sharding import PartitionSpec as P

HD = 64


EPSILON = 1e-05
CONTRACT_ROWS = (((0,), (0,)), ((), ()))
CONTRACT_COLS = (((1,), (1,)), ((), ()))


def normalize(values, gain, shift):
    average = jnp.mean(values, axis=-1, keepdims=True)
    centered = values - average
    variance = jnp.mean(centered * centered, axis=-1, keepdims=True)
    return centered * lax.rsqrt(variance + EPSILON) * gain + shift


def exact_gelu(values):
    return jax.nn.gelu(values, approximate=False)


def product(left, right):
    return jnp.dot(left, right, preferred_element_type=jnp.float32)


def over_rows(left, right):
    return lax.dot_general(left, right, CONTRACT_ROWS, preferred_element_type=jnp.float32)


def over_cols(left, right):
    return lax.dot_general(left, right, CONTRACT_COLS, preferred_element_type=jnp.float32)


def column_sum(values):
    return jnp.sum(values.astype(jnp.float32), axis=0)


def attention_scores(queries_split, keys_split, allowed):
    scaling = 1.0 / math.sqrt(HD)
    scores = (
        jnp.einsum("rqhe,rkhe->rhqk", queries_split, keys_split, preferred_element_type=jnp.float32)
        * scaling
    )
    return jnp.where(allowed[:, None], scores, -1e30)


def on_device(
    inputs,
    timesteps,
    segments,
    valid_mask,
    step_table,
    ln1_gain,
    ln1_shift,
    w_query,
    b_query,
    w_key,
    w_value,
    b_value,
    w_out,
    b_out,
    ln2_gain,
    ln2_shift,
    w_up,
    b_up,
    w_down,
    b_down,
    cotangent,
):
    row_count, seq_len, model_width = inputs.shape
    token_count = row_count * seq_len
    heads_here = w_query.shape[1] // HD
    low_type = jnp.bfloat16
    scaling = 1.0 / math.sqrt(HD)
    head_shape = (row_count, seq_len, heads_here, HD)
    start = inputs.astype(jnp.float32) + step_table[timesteps].astype(jnp.float32)[:, None, :]
    start = start.reshape(token_count, model_width)
    normed, first_pull = jax.vjp(normalize, start, ln1_gain, ln1_shift)
    normed_low = normed.astype(low_type)
    queries = (product(normed_low, w_query) + b_query).astype(low_type)
    key_rows = product(normed_low, w_key).astype(low_type)
    value_rows = (product(normed_low, w_value) + b_value).astype(low_type)
    queries_split = queries.reshape(head_shape)
    keys_split = key_rows.reshape(head_shape)
    values_split = value_rows.reshape(head_shape)
    places = jnp.arange(seq_len, dtype=jnp.int32)
    diagonal = places[:, None] == places[None, :]
    allowed = (segments[:, :, None] == segments[:, None, :]) & (
        (valid_mask[:, None, :] > 0) | diagonal[None]
    )
    scores = attention_scores(queries_split, keys_split, allowed)
    row_max = jnp.max(scores, axis=-1, keepdims=True)
    powers = jnp.exp(scores - row_max)
    total = jnp.sum(powers, axis=-1, keepdims=True)
    log_total = row_max + jnp.log(total)
    probabilities = powers / total
    mixed = jnp.einsum(
        "rhqk,rkhe->rqhe",
        probabilities.astype(low_type),
        values_split,
        preferred_element_type=jnp.float32,
    )
    mixed = mixed.reshape(token_count, heads_here * HD).astype(low_type)
    attended = lax.psum(product(mixed, w_out), "mp") + b_out
    middle = start + attended
    normed2, second_pull = jax.vjp(normalize, middle, ln2_gain, ln2_shift)
    normed2_low = normed2.astype(low_type)
    upper = product(normed2_low, w_up) + b_up
    activated, gelu_pull = jax.vjp(exact_gelu, upper)
    hidden = activated.astype(low_type)
    lowered = lax.psum(product(hidden, w_down), "mp")
    output = (middle + lowered + b_down).astype(low_type).reshape(row_count, seq_len, model_width)
    grad_out = cotangent.reshape(token_count, model_width).astype(jnp.float32)
    grad_out = grad_out * valid_mask.reshape(token_count, 1).astype(jnp.float32)
    grad_out_low = grad_out.astype(low_type)
    grad_w_down = over_rows(hidden, grad_out_low)
    grad_b_down = jnp.sum(grad_out, axis=0)
    grad_hidden = over_cols(grad_out_low, w_down)
    (grad_upper,) = gelu_pull(grad_hidden)
    grad_upper_low = grad_upper.astype(low_type)
    grad_w_up = over_rows(normed2_low, grad_upper_low)
    grad_b_up = column_sum(grad_upper_low)
    grad_normed2 = lax.psum(over_cols(grad_upper_low, w_up), "mp")
    grad_mid_norm, grad_ln2_gain, grad_ln2_shift = second_pull(grad_normed2)
    grad_middle = grad_out + grad_mid_norm
    grad_mid_low = grad_middle.astype(low_type)
    grad_w_out = over_rows(mixed, grad_mid_low)
    grad_b_out = column_sum(grad_mid_low)
    grad_mixed = over_cols(grad_mid_low, w_out).astype(low_type).reshape(head_shape)
    scores_again = attention_scores(queries_split, keys_split, allowed)
    soft_again = jnp.exp(scores_again - log_total)
    grad_soft = jnp.einsum(
        "rqhe,rkhe->rhqk", grad_mixed, values_split, preferred_element_type=jnp.float32
    )
    delta = jnp.sum(soft_again * grad_soft, axis=-1, keepdims=True)
    grad_scores = (soft_again * (grad_soft - delta)).astype(low_type)
    grad_queries = jnp.einsum(
        "rhqk,rkhe->rqhe", grad_scores, keys_split, preferred_element_type=jnp.float32
    )
    grad_queries = (grad_queries * scaling).reshape(token_count, heads_here * HD).astype(low_type)
    grad_keys = jnp.einsum(
        "rhqk,rqhe->rkhe", grad_scores, queries_split, preferred_element_type=jnp.float32
    )
    grad_keys = (grad_keys * scaling).reshape(token_count, heads_here * HD).astype(low_type)
    grad_values = jnp.einsum(
        "rhqk,rqhe->rkhe",
        soft_again.astype(low_type),
        grad_mixed,
        preferred_element_type=jnp.float32,
    )
    grad_values = grad_values.reshape(token_count, heads_here * HD).astype(low_type)
    grad_w_query = over_rows(normed_low, grad_queries)
    grad_b_query = column_sum(grad_queries)
    grad_w_key = over_rows(normed_low, grad_keys)
    grad_w_value = over_rows(normed_low, grad_values)
    grad_b_value = column_sum(grad_values)
    local_normed = (
        over_cols(grad_queries, w_query)
        + over_cols(grad_keys, w_key)
        + over_cols(grad_values, w_value)
    )
    grad_normed = lax.psum(local_normed, "mp")
    grad_start_norm, grad_ln1_gain, grad_ln1_shift = first_pull(grad_normed)
    grad_start = grad_middle + grad_start_norm
    input_grad = grad_start.astype(low_type).reshape(row_count, seq_len, model_width)
    row_sums = jnp.sum(grad_start.reshape(row_count, seq_len, model_width), axis=1)
    column_count = model_width // lax.axis_size("mp")
    own_columns = lax.dynamic_slice_in_dim(
        row_sums, lax.axis_index("mp") * column_count, column_count, 1
    )
    step_count = step_table.shape[0]
    one_hot = (timesteps[:, None] == jnp.arange(step_count, dtype=jnp.int32)[None, :]).astype(
        jnp.float32
    )
    table_grad = lax.dot_general(
        one_hot,
        own_columns,
        CONTRACT_ROWS,
        precision=lax.Precision.HIGHEST,
        preferred_element_type=jnp.float32,
    )
    (
        grad_ln1_gain,
        grad_ln1_shift,
        grad_w_query,
        grad_b_query,
        grad_w_key,
        grad_w_value,
        grad_b_value,
        grad_w_out,
        grad_b_out,
        table_grad,
        grad_w_down,
        grad_b_down,
        grad_w_up,
        grad_b_up,
        grad_ln2_gain,
        grad_ln2_shift,
    ) = lax.psum(
        (
            grad_ln1_gain,
            grad_ln1_shift,
            grad_w_query,
            grad_b_query,
            grad_w_key,
            grad_w_value,
            grad_b_value,
            grad_w_out,
            grad_b_out,
            table_grad,
            grad_w_down,
            grad_b_down,
            grad_w_up,
            grad_b_up,
            grad_ln2_gain,
            grad_ln2_shift,
        ),
        "dp",
    )
    return (
        output,
        input_grad,
        grad_ln1_gain,
        grad_ln1_shift,
        grad_w_query,
        grad_b_query,
        grad_w_key,
        grad_w_value,
        grad_b_value,
        grad_w_out,
        grad_b_out,
        grad_ln2_gain,
        grad_ln2_shift,
        grad_w_up,
        grad_b_up,
        grad_w_down,
        grad_b_down,
        table_grad,
    )


def solution(mesh):
    in_specs = (
        P("dp", None, None),
        P("dp"),
        P("dp", None),
        P("dp", None),
        P(),
        P(),
        P(),
        P(None, "mp"),
        P("mp"),
        P(None, "mp"),
        P(None, "mp"),
        P("mp"),
        P("mp", None),
        P(),
        P(),
        P(),
        P(None, "mp"),
        P("mp"),
        P("mp", None),
        P(),
        P("dp", None, None),
    )
    out_specs = (
        P("dp", None, None),
        P("dp", None, None),
        P(),
        P(),
        P(None, "mp"),
        P("mp"),
        P(None, "mp"),
        P(None, "mp"),
        P("mp"),
        P("mp", None),
        P(),
        P(),
        P(),
        P(None, "mp"),
        P("mp"),
        P("mp", None),
        P(),
        P(None, "mp"),
    )
    return jax.shard_map(
        on_device, mesh=mesh, in_specs=in_specs, out_specs=out_specs, check_vma=False
    )
```

profile of v0, /device:TPU:0, one launch (start us, length us, event | category | flops | bytes accessed | tf_op | source)
XLA Modules:
  0.0 1091.7 jit_solution(8519146503552362906)
XLA Ops:
  9.2 2.6 fusion.7
  11.9 3.0 multiply_reduce_fusion.6
  15.5 2.6 add_convert_fusion
  18.0 2.6 copy-done.3
  25.2 3.0 fusion.10
  28.8 3.2 fusion.11
  36.6 3.5 fusion.40
  40.1 10.4 all-reduce.10.cloned.1.call-start
  50.5 4.0 fusion.6
  54.4 198.6 %all-reduce.8.cloned.1.call-done = f32[1920,768]{1,0:T(8,128)} async-done(((f32[1920,768]{1,0:T(8,128)}), f32[1920,768]{1,0:T(8,128)}) %all-reduce.8.cloned.1.call-update) | async-done | bytes 5898256 | tf_op jit(solution)/shard_map/psum | solution.py:109
  253.1 5.1 fusion.74
  261.2 2.5 fusion.77
  264.5 17.1 %convert_reduce_fusion = (f32[768]{0:T(1024)S(1)}, bf16[1920,768]{1,0:T(8,128)(2,1)S(1)}, f32[1920,768]{1,0:T(8,128)}) fusion(f32[1920,768]{1,0:T(8,128)S(1)} %fusion.77, f32[768]{0:T(1024)S(1)} %copy-done.45, bf16[1920,768]{1,0:T(8,128)(2,1)S(1)} %copy-done.22, bf16[768,768]{1,0:T(8,128)(2,1)S(1)} %copy-done.49), kind=kOutput, calls=%fused_computation.9 | convolution fusion | flops 2375515392 | bytes 18880512 | tf_op jit(solution)/shard_map/dot_general | solution.py:36
  283.2 5.1 fusion.79
  288.5 5.5 multiply_convert_fusion
  295.5 5.0 fusion.78
  300.5 197.0 %all-reduce.10.cloned.1.call-done = f32[1920,768]{1,0:T(8,128)} async-done(((f32[1920,768]{1,0:T(8,128)}), f32[1920,768]{1,0:T(8,128)}) %all-reduce.10.cloned.1.call-update) | async-done | bytes 5898256 | tf_op jit(solution)/shard_map/psum | solution.py:128
  497.6 6.2 multiply_reduce_fusion.1
  503.8 4.9 fusion.73
  514.6 3.2 convert_reduce_fusion.2
  517.9 3.2 multiply_reduce_fusion.7
  527.3 3.6 add_add_fusion.3
  531.2 6.9 fusion.80
  538.1 4.1 fusion.81
  548.7 382.0 %all-reduce.14.cloned.1.call-done = (f32[1920,768]{1,0:T(8,128)}, f32[1920,768]{1,0:T(8,128)}) async-done(((f32[1920,768]{1,0:T(8,128)}, f32[1920,768]{1,0:T(8,128)}), (f32[1920,768]{1,0:T(8,128)}, f32[1920,768]{1,0:T(8,128)})) %all-reduce.14.cloned.1.call-update) | async-done | bytes 11796496 | tf_op jit(solution)/shard_map/psum | solution.py:116
  930.7 7.4 multiply_reduce_fusion.2
  938.2 5.1 fusion.72
  943.3 4.3 fusion.71
  947.6 3.1 reduce_sum.237
  954.9 26.2 %all-reduce = (f32[768]{0:T(1024)}, f32[768]{0:T(1024)}, f32[192]{0:T(256)}, f32[192]{0:T(256)}, f32[768]{0:T(1024)}, /*index=5*/f32[768]{0:T(1024)}, f32[768]{0:T(1024)}, f32[768]{0:T(1024)}, f32[768]{0:T(1024)}) all-reduce(f32[768]{0:T(1024)S(1)} %get-tuple-element.20, ...), channel_id=1, replica_groups=mesh['dp'=8,'mp'=4] {'dp'}, use_global_device_ids=true, to_apply=%region_16.17 | all-reduce | flops 5760 | bytes 46080 | tf_op jit(solution)/shard_map/psum | solution.py:204
  981.0 6.9 add_convert_fusion.2
  987.9 85.4 %all-reduce.12.cloned.1.call-done = (f32[768,192]{0,1:T(8,128)}, f32[768,192]{0,1:T(8,128)}, f32[768,192]{0,1:T(8,128)}, f32[192,768]{1,0:T(8,128)}, f32[768,768...) async-done(((f32[768,192]{0,1:T(8,128)}, f32[768,192]{0,1:T(8,128)}, f32[768,192]{0,1:T(8,128)}, f32[192,768]{1,0:T(8,128)}, f32[768,768]{1,0:T(8,128)}, ...) | async-done | bytes 7845904 | tf_op jit(solution)/shard_map/psum | solution.py:204
  (179 shorter events, 53.6 us)
Async XLA Ops:
  7.2 7.7 copy-start.41
  7.2 8.2 copy-start.38
  7.2 8.2 copy-start.42
  7.2 245.8 %all-reduce.8.cloned.1.call-start = ((), (), s32[]{:S(2)}) async-start(), calls=%async_computation | async-start | bytes 11796480 | tf_op jit(solution)/shard_map/psum | solution.py:109
  9.2 6.3 copy-start.10
  18.0 5.4 copy-start.32
  24.6 4.2 copy-start.30
  28.2 4.5 copy-start.40
  28.8 6.3 copy-start.19
  40.0 213.0 %copy-start.44 = (f32[768]{0:T(1024)S(1)}, f32[768]{0:T(1024)}, u32[]{:S(2)}) copy-start(f32[768]{0:T(1024)} %param.34) | copy-start | bytes 9220
  40.1 457.5 %all-reduce.10.cloned.1.call-start = ((), (), s32[]{:S(2)}) async-start(), calls=%async_computation.1 | async-start | bytes 11796480 | tf_op jit(solution)/shard_map/psum | solution.py:128
  264.5 17.1 %copy-start.16 = (f32[1920,768]{1,0:T(8,128)}, f32[1920,768]{1,0:T(8,128)S(1)}, u32[]{:S(2)}) copy-start(f32[1920,768]{1,0:T(8,128)S(1)} %fusion.77) | copy-start | bytes 17694724
  288.4 642.4 %all-reduce.14.cloned.1.call-start = ((), (), s32[]{:S(2)}) async-start(), calls=%async_computation.3 | async-start | bytes 23592960 | tf_op jit(solution)/shard_map/psum | solution.py:116
  288.5 7.1 copy-start.50
  497.6 6.2 copy-start.11
  503.8 5.0 copy-start.5
  514.6 6.5 copy-start.9
  530.9 542.4 %all-reduce.12.cloned.1.call-start = ((), (), s32[]{:S(2)}) async-start(), calls=%async_computation.2 | async-start | bytes 15728640 | tf_op jit(solution)/shard_map/psum | solution.py:204
  531.1 7.0 copy-start.23
  531.2 7.0 copy-start.25
  538.1 5.7 copy-start.7
  545.5 392.7 %slice-start = ((s8[5898240]{0:T(1024)(128)(4,1)}), s8[1703936]{0:T(1024)(128)(4,1)S(1)}, s32[]{:S(2)}) async-start(s8[5898240]{0:T(1024)(128)(4,1)} %bitcast.126), calls=%async_computation.4 | async-start | bytes 3407872
  930.7 7.4 copy-start.37
  930.7 7.4 slice-start.1
  930.7 12.5 %slice-start.2 = ((s8[5898240]{0:T(1024)(128)(4,1)}), s8[4194304]{0:T(1024)(128)(4,1)S(1)}, s32[]{:S(2)}) async-start(s8[5898240]{0:T(1024)(128)(4,1)} %bitcast.128), calls=%async_computation.6 | async-start | bytes 8388608
  938.2 5.1 slice-start.3
  938.2 5.1 copy-start.6
  950.7 30.3 %copy-start.46 = (f32[768]{0:T(1024)S(1)}, f32[768]{0:T(1024)}, u32[]{:S(2)}) copy-start(f32[768]{0:T(1024)} %param.40) | copy-start | bytes 9220
  1073.3 8.0 copy-start.27
  1073.3 9.4 copy-start.26
  1077.3 6.8 copy-start.28
  1077.3 7.7 copy-start.1
  (30 other events, 66.8 us)
Sparse Core Ops, SparseCore 0:
  40.2 212.8 all-reduce.7
  288.5 209.0 all-reduce.9
  531.0 399.6 all-reduce.13
  952.3 120.9 all-reduce.11
where the time goes:
time: 1100 us; the launch traced here: 1090 us
  waiting for transfers between devices  863 us (78%)
  matrix products  76 us (7%)
  other arithmetic  71.5 us (6%)
  local copies, waits for them, and re-layouts  29.4 us (3%)
  blocking collectives  26.2 us (2%)
  between operations  14.8 us (1%)
    psum x1, waiting for transfers between devices, on_device(): lowered = lax.psum(product(hidden, w_down), 'mp')  382 us
    psum x1, waiting for transfers between devices, on_device(): attended = lax.psum(product(mixed, w_out), 'mp') + b_out  199 us
    psum x1, waiting for transfers between devices, on_device(): grad_normed2 = lax.psum(over_cols(grad_upper_low, w_up), 'mp')  197 us
    psum x1, waiting for transfers between devices, on_device(): lax.psum((grad_ln1_gain, grad_ln1_shift, grad_w_query, grad_b_query, grad...  85.4 us
    dot_general x6, matrix products, over_cols(): lax.dot_general(left, right, CONTRACT_COLS, preferred_element_type=jnp.fl...  28.9 us
    psum x1, blocking collectives, on_device(): lax.psum((grad_ln1_gain, grad_ln1_shift, grad_w_query, grad_b_query, grad...  26.2 us
    unnamed x123, local copies, waits for them, and re-layouts  24.4 us
  transfers between devices with their start and end apart: 4, of which 4 were waited for; matrix products, arithmetic and copies ran while one was open for 4% of the time, Pallas kernels for 0%

commit v1 on v0

--- a/solution.py
+++ b/solution.py
@@ -47,6 +47,28 @@
         * scaling
     )
     return jnp.where(allowed[:, None], scores, -1e30)
+
+
+def gather_whole(shard, sharded_dim, one):
+    n_dp = lax.axis_size("dp")
+    n_mp = lax.axis_size("mp")
+    rows, cols = shard.shape
+    piece_rows = rows // n_dp
+    piece = lax.dynamic_slice_in_dim(shard, lax.axis_index("dp") * piece_rows, piece_rows, 0)
+    piece = piece.astype(jnp.float32) * one
+    pieces = lax.all_gather(piece, ("dp", "mp"), axis=0)
+    pieces = (pieces * one).astype(shard.dtype).reshape(n_dp, n_mp, piece_rows, cols)
+    if sharded_dim == 1:
+        return pieces.transpose(0, 2, 1, 3).reshape(rows, n_mp * cols)
+    return pieces.transpose(1, 0, 2, 3).reshape(n_mp * rows, cols)
+
+
+def gather_vector(shard):
+    return lax.all_gather(shard, "mp", axis=0, tiled=True)
+
+
+def own_columns(values, width):
+    return lax.dynamic_slice_in_dim(values, lax.axis_index("mp") * width, width, 1)
 
 
 def on_device(
@@ -57,27 +79,39 @@
     step_table,
     ln1_gain,
     ln1_shift,
-    w_query,
-    b_query,
-    w_key,
-    w_value,
-    b_value,
-    w_out,
+    w_query_shard,
+    b_query_shard,
+    w_key_shard,
+    w_value_shard,
+    b_value_shard,
+    w_out_shard,
     b_out,
     ln2_gain,
     ln2_shift,
-    w_up,
-    b_up,
-    w_down,
+    w_up_shard,
+    b_up_shard,
+    w_down_shard,
     b_down,
     cotangent,
 ):
     row_count, seq_len, model_width = inputs.shape
     token_count = row_count * seq_len
-    heads_here = w_query.shape[1] // HD
+    qkv_width = w_query_shard.shape[1]
+    ff_width = w_up_shard.shape[1]
+    one = 1.0 + 0.0 * ln1_gain[0]
+    w_query = gather_whole(w_query_shard, 1, one)
+    w_key = gather_whole(w_key_shard, 1, one)
+    w_value = gather_whole(w_value_shard, 1, one)
+    w_out = gather_whole(w_out_shard, 0, one)
+    w_up = gather_whole(w_up_shard, 1, one)
+    w_down = gather_whole(w_down_shard, 0, one)
+    b_query = gather_vector(b_query_shard)
+    b_value = gather_vector(b_value_shard)
+    b_up = gather_vector(b_up_shard)
+    heads = w_query.shape[1] // HD
     low_type = jnp.bfloat16
     scaling = 1.0 / math.sqrt(HD)
-    head_shape = (row_count, seq_len, heads_here, HD)
+    head_shape = (row_count, seq_len, heads, HD)
     start = inputs.astype(jnp.float32) + step_table[timesteps].astype(jnp.float32)[:, None, :]
     start = start.reshape(token_count, model_width)
     normed, first_pull = jax.vjp(normalize, start, ln1_gain, ln1_shift)
@@ -105,31 +139,32 @@
         values_split,
         preferred_element_type=jnp.float32,
     )
-    mixed = mixed.reshape(token_count, heads_here * HD).astype(low_type)
-    attended = lax.psum(product(mixed, w_out), "mp") + b_out
+    mixed = mixed.reshape(token_count, heads * HD).astype(low_type)
+    attended = product(mixed, w_out) + b_out
     middle = start + attended
     normed2, second_pull = jax.vjp(normalize, middle, ln2_gain, ln2_shift)
     normed2_low = normed2.astype(low_type)
     upper = product(normed2_low, w_up) + b_up
     activated, gelu_pull = jax.vjp(exact_gelu, upper)
     hidden = activated.astype(low_type)
-    lowered = lax.psum(product(hidden, w_down), "mp")
+    lowered = product(hidden, w_down)
     output = (middle + lowered + b_down).astype(low_type).reshape(row_count, seq_len, model_width)
     grad_out = cotangent.reshape(token_count, model_width).astype(jnp.float32)
     grad_out = grad_out * valid_mask.reshape(token_count, 1).astype(jnp.float32)
     grad_out_low = grad_out.astype(low_type)
-    grad_w_down = over_rows(hidden, grad_out_low)
+    grad_w_down = over_rows(own_columns(hidden, ff_width), grad_out_low)
     grad_b_down = jnp.sum(grad_out, axis=0)
     grad_hidden = over_cols(grad_out_low, w_down)
     (grad_upper,) = gelu_pull(grad_hidden)
     grad_upper_low = grad_upper.astype(low_type)
-    grad_w_up = over_rows(normed2_low, grad_upper_low)
-    grad_b_up = column_sum(grad_upper_low)
-    grad_normed2 = lax.psum(over_cols(grad_upper_low, w_up), "mp")
+    own_grad_upper = own_columns(grad_upper_low, ff_width)
+    grad_w_up = over_rows(normed2_low, own_grad_upper)
+    grad_b_up = column_sum(own_grad_upper)
+    grad_normed2 = over_cols(grad_upper_low, w_up)
     grad_mid_norm, grad_ln2_gain, grad_ln2_shift = second_pull(grad_normed2)
     grad_middle = grad_out + grad_mid_norm
     grad_mid_low = grad_middle.astype(low_type)
-    grad_w_out = over_rows(mixed, grad_mid_low)
+    grad_w_out = over_rows(own_columns(mixed, qkv_width), grad_mid_low)
     grad_b_out = column_sum(grad_mid_low)
     grad_mixed = over_cols(grad_mid_low, w_out).astype(low_type).reshape(head_shape)
     scores_again = attention_scores(queries_split, keys_split, allowed)
@@ -142,44 +177,43 @@
     grad_queries = jnp.einsum(
         "rhqk,rkhe->rqhe", grad_scores, keys_split, preferred_element_type=jnp.float32
     )
-    grad_queries = (grad_queries * scaling).reshape(token_count, heads_here * HD).astype(low_type)
+    grad_queries = (grad_queries * scaling).reshape(token_count, heads * HD).astype(low_type)
     grad_keys = jnp.einsum(
         "rhqk,rqhe->rkhe", grad_scores, queries_split, preferred_element_type=jnp.float32
     )
-    grad_keys = (grad_keys * scaling).reshape(token_count, heads_here * HD).astype(low_type)
+    grad_keys = (grad_keys * scaling).reshape(token_count, heads * HD).astype(low_type)
     grad_values = jnp.einsum(
         "rhqk,rqhe->rkhe",
         soft_again.astype(low_type),
         grad_mixed,
         preferred_element_type=jnp.float32,
     )
-    grad_values = grad_values.reshape(token_count, heads_here * HD).astype(low_type)
-    grad_w_query = over_rows(normed_low, grad_queries)
-    grad_b_query = column_sum(grad_queries)
-    grad_w_key = over_rows(normed_low, grad_keys)
-    grad_w_value = over_rows(normed_low, grad_values)
-    grad_b_value = column_sum(grad_values)
-    local_normed = (
+    grad_values = grad_values.reshape(token_count, heads * HD).astype(low_type)
+    own_grad_queries = own_columns(grad_queries, qkv_width)
+    own_grad_values = own_columns(grad_values, qkv_width)
+    grad_w_query = over_rows(normed_low, own_grad_queries)
+    grad_b_query = column_sum(own_grad_queries)
+    grad_w_key = over_rows(normed_low, own_columns(grad_keys, qkv_width))
+    grad_w_value = over_rows(normed_low, own_grad_values)
+    grad_b_value = column_sum(own_grad_values)
+    grad_normed = (
         over_cols(grad_queries, w_query)
         + over_cols(grad_keys, w_key)
         + over_cols(grad_values, w_value)
     )
-    grad_normed = lax.psum(local_normed, "mp")
     grad_start_norm, grad_ln1_gain, grad_ln1_shift = first_pull(grad_normed)
     grad_start = grad_middle + grad_start_norm
     input_grad = grad_start.astype(low_type).reshape(row_count, seq_len, model_width)
     row_sums = jnp.sum(grad_start.reshape(row_count, seq_len, model_width), axis=1)
     column_count = model_width // lax.axis_size("mp")
-    own_columns = lax.dynamic_slice_in_dim(
-        row_sums, lax.axis_index("mp") * column_count, column_count, 1
-    )
+    table_columns = own_columns(row_sums, column_count)
     step_count = step_table.shape[0]
     one_hot = (timesteps[:, None] == jnp.arange(step_count, dtype=jnp.int32)[None, :]).astype(
         jnp.float32
     )
     table_grad = lax.dot_general(
         one_hot,
-        own_columns,
+        table_columns,
         CONTRACT_ROWS,
         precision=lax.Precision.HIGHEST,
         preferred_element_type=jnp.float32,

time: 1100 us -> 806 us (0.73)
  waiting for transfers between devices: 863 us -> 306 us
  matrix products: 76 us -> 232 us
  local copies, waits for them, and re-layouts: 29.4 us -> 113 us
  blocking collectives: 26.2 us -> 52.7 us
    psum x3 -> x0, waiting for transfers between devices: 778 us -> none  [the longest x1 382 us: on_device(): lowered = lax.psum(product(hidden, w_down), 'mp')]
    all_gather x0 -> x6, waiting for transfers between devices: none -> 232 us  [gather_whole(): pieces = lax.all_gather(piece, ('dp', 'mp'), axis=0)]
    dot_general x6, matrix products: 18.3 us -> 102 us  [product(): return jnp.dot(left, right, preferred_element_type=jnp.float32)]
    dot_general x6, matrix products: 28.9 us -> 65.2 us  [over_cols(): lax.dot_general(left, right, CONTRACT_COLS, preferred_element_type=jnp.fl...]
    convert_element_type x4 -> x8, local copies, waits for them, and re-layouts: 1.95 us -> 29.8 us  [the longest x1 4.88 us: on_device(): over_cols(grad_mid_low, w_out).astype(low_type).reshape(head_shape)]
    reshape x0 -> x7, local copies, waits for them, and re-layouts: none -> 18.7 us  [the longest x3 9.67 us: gather_whole(): return pieces.transpose(0, 2, 1, 3).reshape(rows, n_mp * cols)]
    unnamed x0 -> x1, blocking collectives: none -> 13.7 us
    reduce_sum x2 -> x0, other arithmetic: 13.6 us -> none  [normalize(): return centered * lax.rsqrt(variance + EPSILON) * gain + shift]
  transfers between devices with their start and end apart: 4 -> 7, of which waited for: 4 -> 6; matrix products, arithmetic and copies ran while one was open for 4% -> 21% of each run, Pallas kernels for 0% -> 0%
where the time goes in v1:
time: 806 us; the launch traced here: 801 us
  waiting for transfers between devices  306 us (38%)
  matrix products  232 us (29%)
  local copies, waits for them, and re-layouts  113 us (14%)
  other arithmetic  80.5 us (10%)
  blocking collectives  52.7 us (7%)
  between operations  16.7 us (2%)
    all_gather x6, waiting for transfers between devices, gather_whole(): pieces = lax.all_gather(piece, ('dp', 'mp'), axis=0)  232 us
    dot_general x6, matrix products, product(): return jnp.dot(left, right, preferred_element_type=jnp.float32)  102 us
    psum x1, waiting for transfers between devices, on_device(): lax.psum((grad_ln1_gain, grad_ln1_shift, grad_w_query, grad_b_query, grad...  74.1 us
    dot_general x6, matrix products, over_cols(): lax.dot_general(left, right, CONTRACT_COLS, preferred_element_type=jnp.fl...  65.2 us
    unnamed x157, local copies, waits for them, and re-layouts  32 us
    psum x1, blocking collectives, on_device(): lax.psum((grad_ln1_gain, grad_ln1_shift, grad_w_query, grad_b_query, grad...  25.7 us
    dot_general x6, matrix products, over_rows(): lax.dot_general(left, right, CONTRACT_ROWS, preferred_element_type=jnp.fl...  23 us
    convert_element_type x6, other arithmetic, gather_whole(): (pieces * one).astype(shard.dtype).reshape(n_dp, n_mp, piece_rows, cols)  17.4 us
  transfers between devices with their start and end apart: 7, of which 6 were waited for; matrix products, arithmetic and copies ran while one was open for 21% of the time, Pallas kernels for 0%

profile of v1, /device:TPU:0, one launch (start us, length us, event | category | flops | bytes accessed | tf_op | source)
XLA Modules:
  0.0 800.8 jit_solution(10009840443468317510)
XLA Ops:
  24.3 13.7 %all-reduce.4 = (f32[768]{0:T(1024)S(1)}, f32[768]{0:T(1024)S(1)}) all-reduce(f32[768]{0:T(1024)S(1)} %dynamic-update-slice.1, f32[768]{0:T(1024)S(1)} %dynamic-update-slice), channel_id=1, replica_groups=mesh['dp'=8,'mp'=4] {'mp'}, use_global_device_ids=true, to_apply=%add.1 | all-reduce | flops 1536 | bytes 12288
  38.1 13.3 %all-gather.6 = f32[4,1,768]{2,1,0:T(1,128)S(1)} all-gather(f32[1,1,768]{2,1,0:T(1,128)S(1)} %reshape.382), channel_id=1, replica_groups=mesh['dp'=8,'mp'=4] {'mp'}, dimensions={0}, use_global_device_ids=true | all-gather | bytes 15360 | tf_op jit(solution)/shard_map/all_gather | solution.py:67
  80.4 52.2 %all-gather.20.cloned.1.call-done = f32[768,768]{1,0:T(8,128)} async-done(((f32[24,768]{1,0:T(8,128)}), f32[768,768]{1,0:T(8,128)}) %all-gather.20.cloned.1.call-update) | async-done | bytes 2359312 | tf_op jit(solution)/shard_map/all_gather | solution.py:59
  135.6 58.5 %all-gather.18.cloned.1.call-done = f32[3072,192]{1,0:T(8,128)} async-done(((f32[96,192]{1,0:T(8,128)}), f32[3072,192]{1,0:T(8,128)}) %all-gather.18.cloned.1.call-update) | async-done | bytes 2359312 | tf_op jit(solution)/shard_map/all_gather | solution.py:59
  201.9 53.5 %all-gather.16.cloned.1.call-done = f32[3072,192]{1,0:T(8,128)} async-done(((f32[96,192]{1,0:T(8,128)}), f32[3072,192]{1,0:T(8,128)}) %all-gather.16.cloned.1.call-update) | async-done | bytes 2359312 | tf_op jit(solution)/shard_map/all_gather | solution.py:59
  263.3 6.0 add_convert_fusion.4
  274.0 6.2 reshape.322
  280.2 5.9 convolution_convert_fusion.1
  290.8 6.0 add_convert_fusion.5
  301.3 6.0 reshape.319
  307.3 6.2 reshape.325
  313.6 6.7 fusion.15
  325.3 5.0 convert_bitcast_fusion.1
  335.8 6.7 fusion.73
  359.4 62.7 %all-gather.24.cloned.1.call-done = f32[3072,768]{1,0:T(8,128)} async-done(((f32[96,768]{1,0:T(8,128)}), f32[3072,768]{1,0:T(8,128)}) %all-gather.24.cloned.1.call-update) | async-done | bytes 9437200 | tf_op jit(solution)/shard_map/all_gather | solution.py:59
  431.4 61.2 %multiply_convert_fusion = (bf16[1920,3072]{1,0:T(8,128)(2,1)}, f32[1920,3072]{1,0:T(8,128)}, f32[1920,3072]{1,0:T(8,128)}) fusion(f32[3072]{0:T(1024)S(1)} %bitcast.196, bf16[1920,768]{1,0:T(8,128)(2,1)S(1)} %copy-done.26, bf16[768,3072]{1,0:T(8,128)(2,1)S(1)} %bitcast.183), kind=kOutput, calls=%fused_computation.4 | convolution fusion | flops 9448980480 | bytes 66662400 | tf_op jit(solution)/shard_map/dot_general | solution.py:28
  492.6 31.6 %add_convert_fusion = bf16[1920,3072]{1,0:T(8,128)(2,1)} fusion(f32[1920,3072]{1,0:T(8,128)} %get-tuple-element.51, f32[1920,3072]{1,0:T(8,128)} %get-tuple-element.66, f32[3072]{0:T(1024)S(1)} %bitcast.197, bf16[1920,768]{1,0:T(8,128)(2,1)} %bitcast.189, bf16[3072,768]{1,0:T(8,128)(2,1)} %bitcast.178), kind=kOutput, calls=%fused_computation.3 | convolution fusion | flops 9148170240 | bytes 66662400 | tf_op jit(solution)/shard_map/dot_general | solution.py:36
  524.3 15.1 %multiply_reduce_fusion.1 = (f32[768]{0:T(1024)S(1)}, f32[1920]{0:T(1024)S(1)}, f32[768]{0:T(1024)S(1)}, f32[1920,768]{1,0:T(8,128)S(1)}) fusion(f32[1920,768]{1,0:T(8,128)} %copy-done.3, f32[1920]{0:T(1024)S(1)} %copy-done.44, f32[1920]{0:T(1024)S(1)} %copy-done.40, f32[768]{0:T(1024)S(1)} %copy-done.54, bf16[1920,3072]{1,0:T(8,128)(2,1)} %add_convert_fusion, ...), kind=kOutput, calls=%fused_computation.35 | convolution fusion | flops 9071489024 | bytes 28343808 | tf_op jit(solution)/shard_map/dot_general | solution.py:36
  550.3 4.9 copy.118
  555.2 6.0 reshape.333
  561.2 11.1 %convert_bitcast_fusion = bf16[15,128,12,64]{1,3,2,0:T(8,128)(2,1)} fusion(f32[15,12,128]{2,1,0:T(8,128)S(1)} %copy-done.37, f32[15,12,128,128]{2,3,1,0:T(8,128)} %copy-done.2, pred[15,128,128]{1,2,0:T(8,128)(4,1)S(1)} %copy-done.25, bf16[15,128,12,64]{1,0,3,2:T(8,128)(2,1)} %reshape.333), kind=kOutput, calls=%fused_computation.76 | convolution fusion | flops 390758400 | bytes 18032640 | tf_op jit(solution)/shard_map/rhqk,rqhe->rkhe/dot_general | solution.py:185
  572.4 10.0 %multiply_reduce_fusion = (f32[15,12,128]{2,1,0:T(8,128)S(1)}, f32[15,12,128,128]{2,3,1,0:T(8,128)}) fusion(f32[15,12,128]{2,1,0:T(8,128)S(1)} %copy-done.37, f32[15,12,128,128]{2,3,1,0:T(8,128)} %copy-done.2, pred[15,128,128]{1,2,0:T(8,128)(4,1)S(1)} %copy-done.25, bf16[15,128,12,64]{1,0,3,2:T(8,128)(2,1)S(1)} %copy-done.14, ...), kind=kOutput, calls=%fused_computation.19 | convolution fusion | flops 392209920 | bytes 29921280 | tf_op jit(solution)/shard_map/rqhe,rkhe->rhqk/dot_general | solution.py:172
  582.4 9.8 %multiply_convert_fusion.1 = bf16[15,12,128,128]{2,3,1,0:T(8,128)(2,1)S(1)} fusion(f32[15,12,128,128]{2,3,1,0:T(8,128)} %get-tuple-element.69, f32[15,12,128]{2,1,0:T(8,128)S(1)} %get-tuple-element.68, f32[15,12,128]{2,1,0:T(8,128)S(1)} %copy-done.37, f32[15,12,128,128]{2,3,1,0:T(8,128)} %copy-done.2, pred[15,128,128]{1,2,0:T(8,128)(4,1)S(1)} %copy-done.25), kind=kLoop, calls=%fused_computation.18 | loop fusion | flops 17694720 | bytes 29921280 | tf_op jit(solution)/shard_map/convert_element_type | solution.py:176
  592.2 5.4 fusion.19
  616.4 5.1 fusion.74
  621.5 6.5 multiply_reduce_fusion.2
  638.5 6.1 fusion.22
  644.6 5.2 fusion.69
  654.4 6.8 fusion.20
  666.5 25.7 %all-reduce.2 = (f32[768]{0:T(1024)}, f32[768]{0:T(1024)}, f32[192]{0:T(256)}, f32[192]{0:T(256)}, f32[768]{0:T(1024)}, /*index=5*/f32[768]{0:T(1024)}, f32[768]{0:T(1024)}, f32[768]{0:T(1024)}, f32[768]{0:T(1024)}) all-reduce(f32[768]{0:T(1024)S(1)} %get-tuple-element.20, ...), channel_id=1, replica_groups=mesh['dp'=8,'mp'=4] {'dp'}, use_global_device_ids=true, to_apply=%region_12.13 | all-reduce | flops 5760 | bytes 46080 | tf_op jit(solution)/shard_map/psum | solution.py:238
  692.1 15.8 %add_convert_fusion.2 = bf16[1920,768]{1,0:T(8,128)(2,1)} fusion(f32[1920,768]{1,0:T(8,128)} %copy-done.3, bf16[1920,3072]{1,0:T(8,128)(2,1)} %get-tuple-element.50, bf16[3072,768]{1,0:T(8,128)(2,1)} %bitcast.179, f32[768]{0:T(1024)S(1)} %copy-done.61), kind=kOutput, calls=%fused_computation.47 | convolution fusion | flops 9064120320 | bytes 25365504 | tf_op jit(solution)/shard_map/dot_general | solution.py:28
  708.0 74.1 %all-reduce.7.cloned.1.call-done = (f32[768,192]{0,1:T(8,128)}, f32[768,192]{0,1:T(8,128)}, f32[768,192]{0,1:T(8,128)}, f32[192,768]{1,0:T(8,128)}, f32[768,768]...) async-done(((f32[768,192]{0,1:T(8,128)}, f32[768,192]{0,1:T(8,128)}, f32[768,192]{0,1:T(8,128)}, f32[192,768]{1,0:T(8,128)}, f32[768,768]{1,0:T(8,128)}, ...) | async-done | bytes 7845904 | tf_op jit(solution)/shard_map/psum | solution.py:238
  (247 shorter events, 175.0 us)
Async XLA Ops:
  7.2 12.9 %copy-start = (bf16[1000,768]{1,0:T(8,128)(2,1)S(1)}, bf16[1000,768]{1,0:T(8,128)(2,1)}, u32[]{:S(2)}) copy-start(bf16[1000,768]{1,0:T(8,128)(2,1)} %param.25) | copy-start | bytes 4608004
  7.2 53.0 %copy-start.52 = (s32[15,128]{1,0:T(8,128)S(1)}, s32[15,128]{1,0:T(8,128)}, u32[]{:S(2)}) copy-start(s32[15,128]{1,0:T(8,128)} %param.23) | copy-start | bytes 23044
  7.2 66.3 %all-gather.14.cloned.1.call-start = ((), (), s32[]{:S(2)}) async-start(), calls=%async_computation | async-start | bytes 3244032 | tf_op jit(solution)/shard_map/all_gather | solution.py:59
  11.0 121.7 %all-gather.20.cloned.1.call-start = ((), (), s32[]{:S(2)}) async-start(), calls=%async_computation.3 | async-start | bytes 2433024 | tf_op jit(solution)/shard_map/all_gather | solution.py:59
  12.5 181.7 %all-gather.18.cloned.1.call-start = ((), (), s32[]{:S(2)}) async-start(), calls=%async_computation.2 | async-start | bytes 3244032 | tf_op jit(solution)/shard_map/all_gather | solution.py:59
  14.4 241.0 %all-gather.16.cloned.1.call-start = ((), (), s32[]{:S(2)}) async-start(), calls=%async_computation.1 | async-start | bytes 3244032 | tf_op jit(solution)/shard_map/all_gather | solution.py:59
  15.2 332.7 %all-gather.22.cloned.1.call-start = ((), (), s32[]{:S(2)}) async-start(), calls=%async_computation.4 | async-start | bytes 9732096 | tf_op jit(solution)/shard_map/all_gather | solution.py:59
  16.9 405.2 %all-gather.24.cloned.1.call-start = ((), (), s32[]{:S(2)}) async-start(), calls=%async_computation.5 | async-start | bytes 9732096 | tf_op jit(solution)/shard_map/all_gather | solution.py:59
  18.6 763.4 %all-reduce.7.cloned.1.call-start = ((), (), s32[]{:S(2)}) async-start(), calls=%async_computation.6 | async-start | bytes 15728640 | tf_op jit(solution)/shard_map/psum | solution.py:238
  38.0 23.5 %copy-start.6 = (bf16[15,128,768]{2,1,0:T(8,128)(2,1)S(1)}, bf16[15,128,768]{2,1,0:T(8,128)(2,1)}, u32[]{:S(2)}) copy-start(bf16[15,128,768]{2,1,0:T(8,128)(2,1)} %param.41) | copy-start | bytes 8847364
  53.4 11.1 %copy-start.9 = (bf16[15,128,768]{2,1,0:T(8,128)(2,1)S(1)}, bf16[15,128,768]{2,1,0:T(8,128)(2,1)}, u32[]{:S(2)}) copy-start(bf16[15,128,768]{2,1,0:T(8,128)(2,1)} %param.21) | copy-start | bytes 8847364
  53.4 11.1 %copy-start.50 = (f32[768]{0:T(1024)S(1)}, f32[768]{0:T(1024)}, u32[]{:S(2)}) copy-start(f32[768]{0:T(1024)} %param.26) | copy-start | bytes 9220
  53.4 11.1 %copy-start.55 = (f32[768]{0:T(1024)S(1)}, f32[768]{0:T(1024)}, u32[]{:S(2)}) copy-start(f32[768]{0:T(1024)} %param.27) | copy-start | bytes 9220
  59.6 9.1 %copy-start.41 = (f32[15,128]{1,0:T(8,128)}, f32[15,128]{1,0:T(8,128)S(1)}, u32[]{:S(2)}) copy-start(f32[15,128]{1,0:T(8,128)S(1)} %multiply_reduce_fusion.6) | copy-start | bytes 23044
  61.5 262.4 %copy-start.24 = (pred[15,128,128]{1,2,0:T(8,128)(4,1)}, pred[15,128,128]{1,2,0:T(8,128)(4,1)S(1)}, u32[]{:S(2)}) copy-start(pred[15,128,128]{1,2,0:T(8,128)(4,1)S(1)} %or_and_fusion) | copy-start | bytes 737284
  80.4 210.4 %copy-start.20 = (bf16[768,768]{0,1:T(8,128)(2,1)}, bf16[768,768]{0,1:T(8,128)(2,1)S(1)}, u32[]{:S(2)}) copy-start(bf16[768,768]{0,1:T(8,128)(2,1)S(1)} %reshape.318) | copy-start | bytes 3538948
  269.3 10.9 %copy-start.33 = (bf16[768,768]{0,1:T(8,128)(2,1)S(1)}, bf16[768,768]{0,1:T(8,128)(2,1)}, u32[]{:S(2)}) copy-start(bf16[768,768]{0,1:T(8,128)(2,1)} %reshape.324) | copy-start | bytes 3538948
  343.3 9.2 %copy-start.47 = (f32[1920]{0:T(1024)}, f32[1920]{0:T(1024)S(1)}, u32[]{:S(2)}) copy-start(f32[1920]{0:T(1024)S(1)} %multiply_reduce_fusion.5) | copy-start | bytes 23044
  343.3 9.2 %copy-start.43 = (f32[1920]{0:T(1024)}, f32[1920]{0:T(1024)S(1)}, u32[]{:S(2)}) copy-start(f32[1920]{0:T(1024)S(1)} %fusion.54) | copy-start | bytes 23044
  492.6 31.7 %copy-start.40 = (f32[1920]{0:T(1024)S(1)}, f32[1920]{0:T(1024)}, u32[]{:S(2)}) copy-start(f32[1920]{0:T(1024)} %copy-done.39) | copy-start | bytes 23044
  492.6 31.7 %copy-start.44 = (f32[1920]{0:T(1024)S(1)}, f32[1920]{0:T(1024)}, u32[]{:S(2)}) copy-start(f32[1920]{0:T(1024)} %copy-done.43) | copy-start | bytes 23044
  492.6 31.7 %copy-start.54 = (f32[768]{0:T(1024)S(1)}, f32[768]{0:T(1024)}, u32[]{:S(2)}) copy-start(f32[768]{0:T(1024)} %param.35) | copy-start | bytes 9220
  524.3 15.1 %copy-start.48 = (f32[1920]{0:T(1024)S(1)}, f32[1920]{0:T(1024)}, u32[]{:S(2)}) copy-start(f32[1920]{0:T(1024)} %copy-done.47) | copy-start | bytes 23044
  524.3 15.1 %copy-start.4 = (f32[1920,768]{1,0:T(8,128)S(1)}, f32[1920,768]{1,0:T(8,128)}, u32[]{:S(2)}) copy-start(f32[1920,768]{1,0:T(8,128)} %copy-done.3) | copy-start | bytes 17694724
  550.3 10.9 %copy-start.25 = (pred[15,128,128]{1,2,0:T(8,128)(4,1)S(1)}, pred[15,128,128]{1,2,0:T(8,128)(4,1)}, u32[]{:S(2)}) copy-start(pred[15,128,128]{1,2,0:T(8,128)(4,1)} %copy-done.24) | copy-start | bytes 737284
  550.3 10.9 %copy-start.37 = (f32[15,12,128]{2,1,0:T(8,128)S(1)}, f32[15,12,128]{2,1,0:T(8,128)}, u32[]{:S(2)}) copy-start(f32[15,12,128]{2,1,0:T(8,128)} %log_add_fusion) | copy-start | bytes 276484
  561.2 11.2 %copy-start.14 = (bf16[15,128,12,64]{1,0,3,2:T(8,128)(2,1)S(1)}, bf16[15,128,12,64]{1,0,3,2:T(8,128)(2,1)}, u32[]{:S(2)}) copy-start(bf16[15,128,12,64]{1,0,3,2:T(8,128)(2,1)} %reshape.319) | copy-start | bytes 8847364
  561.2 11.2 %copy-start.15 = (bf16[15,128,12,64]{1,0,3,2:T(8,128)(2,1)S(1)}, bf16[15,128,12,64]{1,0,3,2:T(8,128)(2,1)}, u32[]{:S(2)}) copy-start(bf16[15,128,12,64]{1,0,3,2:T(8,128)(2,1)} %reshape.333) | copy-start | bytes 8847364
  582.4 9.8 %copy-start.12 = (bf16[15,128,12,64]{1,0,3,2:T(8,128)(2,1)S(1)}, bf16[15,128,12,64]{1,0,3,2:T(8,128)(2,1)}, u32[]{:S(2)}) copy-start(bf16[15,128,12,64]{1,0,3,2:T(8,128)(2,1)} %reshape.322) | copy-start | bytes 8847364
  606.4 30.5 %copy-start.11 = (bf16[96,8,15,128]{3,1,2,0:T(8,128)(2,1)}, bf16[96,8,15,128]{3,1,2,0:T(8,128)(2,1)S(1)}, u32[]{:S(2)}) copy-start(bf16[96,8,15,128]{3,1,2,0:T(8,128)(2,1)S(1)} %copy.174) | copy-start | bytes 8847364
  661.3 30.9 %copy-start.61 = (f32[768]{0:T(1024)S(1)}, f32[768]{0:T(1024)}, u32[]{:S(2)}) copy-start(f32[768]{0:T(1024)} %param.40) | copy-start | bytes 9220
  782.1 9.4 %copy-start.29 = (f32[768,768]{1,0:T(8,128)S(1)}, f32[768,768]{1,0:T(8,128)}, u32[]{:S(2)}) copy-start(f32[768,768]{1,0:T(8,128)} %get-tuple-element.88) | copy-start | bytes 7077892
  (43 other events, 203.5 us)
Sparse Core Ops, SparseCore 0:
  11.5 61.9 all-gather.13
  76.9 55.7 all-gather.19
  136.1 57.9 all-gather.17
  197.4 57.8 all-gather.15
  258.6 80.2 all-gather.21
  342.1 79.9 all-gather.23
  661.4 120.6 all-reduce.6

commit v2 on v1

--- a/solution.py
+++ b/solution.py
@@ -49,22 +49,34 @@
     return jnp.where(allowed[:, None], scores, -1e30)
 
 
-def gather_whole(shard, sharded_dim, one):
+def gather_pieces(blocks, one):
     n_dp = lax.axis_size("dp")
+    d = lax.axis_index("dp")
+    pieces = []
+    for block in blocks:
+        piece_rows = block.shape[0] // n_dp
+        pieces.append(lax.dynamic_slice_in_dim(block, d * piece_rows, piece_rows, 0))
+    sent = jnp.concatenate([p.astype(jnp.float32) for p in pieces], axis=0) * one
+    got = lax.all_gather(sent, ("mp", "dp"), axis=0) * one
     n_mp = lax.axis_size("mp")
-    rows, cols = shard.shape
-    piece_rows = rows // n_dp
-    piece = lax.dynamic_slice_in_dim(shard, lax.axis_index("dp") * piece_rows, piece_rows, 0)
-    piece = piece.astype(jnp.float32) * one
-    pieces = lax.all_gather(piece, ("dp", "mp"), axis=0)
-    pieces = (pieces * one).astype(shard.dtype).reshape(n_dp, n_mp, piece_rows, cols)
-    if sharded_dim == 1:
-        return pieces.transpose(0, 2, 1, 3).reshape(rows, n_mp * cols)
-    return pieces.transpose(1, 0, 2, 3).reshape(n_mp * rows, cols)
-
-
-def gather_vector(shard):
-    return lax.all_gather(shard, "mp", axis=0, tiled=True)
+    got = got.reshape(n_mp, n_dp, *sent.shape)
+    out, at = [], 0
+    for p in pieces:
+        rows = p.shape[0]
+        out.append(got[:, :, at : at + rows])
+        at += rows
+    return out
+
+
+def whole_rows(part, dtype):
+    n_mp, n_dp, rows, width = part.shape
+    return part.astype(dtype).reshape(n_mp * n_dp * rows, width)
+
+
+def bias_block(vectors, width, n_dp):
+    row = jnp.concatenate(vectors)
+    row = jnp.pad(row, (0, width - row.shape[0]))
+    return jnp.zeros((n_dp, width), jnp.float32).at[0].set(row)
 
 
 def own_columns(values, width):
@@ -99,26 +111,45 @@
     qkv_width = w_query_shard.shape[1]
     ff_width = w_up_shard.shape[1]
     one = 1.0 + 0.0 * ln1_gain[0]
-    w_query = gather_whole(w_query_shard, 1, one)
-    w_key = gather_whole(w_key_shard, 1, one)
-    w_value = gather_whole(w_value_shard, 1, one)
-    w_out = gather_whole(w_out_shard, 0, one)
-    w_up = gather_whole(w_up_shard, 1, one)
-    w_down = gather_whole(w_down_shard, 0, one)
-    b_query = gather_vector(b_query_shard)
-    b_value = gather_vector(b_value_shard)
-    b_up = gather_vector(b_up_shard)
-    heads = w_query.shape[1] // HD
+    n_dp = lax.axis_size("dp")
     low_type = jnp.bfloat16
+    q_part, k_part, v_part, qv_bias = gather_pieces(
+        (
+            w_query_shard.T,
+            w_key_shard.T,
+            w_value_shard.T,
+            bias_block((b_query_shard, b_value_shard), model_width, n_dp),
+        ),
+        one,
+    )
+    w_query_t = whole_rows(q_part, low_type)
+    w_key_t = whole_rows(k_part, low_type)
+    w_value_t = whole_rows(v_part, low_type)
+    b_query = qv_bias[:, 0, 0, :qkv_width].reshape(-1)
+    b_value = qv_bias[:, 0, 0, qkv_width : 2 * qkv_width].reshape(-1)
+    o_part, up_part, down_part, up_bias = gather_pieces(
+        (
+            w_out_shard,
+            w_up_shard.T,
+            w_down_shard,
+            bias_block((b_up_shard,), model_width, n_dp),
+        ),
+        one,
+    )
+    w_out = whole_rows(o_part, low_type)
+    w_up_t = whole_rows(up_part, low_type)
+    w_down = whole_rows(down_part, low_type)
+    b_up = up_bias[:, 0, 0, :].reshape(-1)
+    heads = w_query_t.shape[0] // HD
     scaling = 1.0 / math.sqrt(HD)
     head_shape = (row_count, seq_len, heads, HD)
     start = inputs.astype(jnp.float32) + step_table[timesteps].astype(jnp.float32)[:, None, :]
     start = start.reshape(token_count, model_width)
     normed, first_pull = jax.vjp(normalize, start, ln1_gain, ln1_shift)
     normed_low = normed.astype(low_type)
-    queries = (product(normed_low, w_query) + b_query).astype(low_type)
-    key_rows = product(normed_low, w_key).astype(low_type)
-    value_rows = (product(normed_low, w_value) + b_value).astype(low_type)
+    queries = (over_cols(normed_low, w_query_t) + b_query).astype(low_type)
+    key_rows = over_cols(normed_low, w_key_t).astype(low_type)
+    value_rows = (over_cols(normed_low, w_value_t) + b_value).astype(low_type)
     queries_split = queries.reshape(head_shape)
     keys_split = key_rows.reshape(head_shape)
     values_split = value_rows.reshape(head_shape)
@@ -144,7 +175,7 @@
     middle = start + attended
     normed2, second_pull = jax.vjp(normalize, middle, ln2_gain, ln2_shift)
     normed2_low = normed2.astype(low_type)
-    upper = product(normed2_low, w_up) + b_up
+    upper = over_cols(normed2_low, w_up_t) + b_up
     activated, gelu_pull = jax.vjp(exact_gelu, upper)
     hidden = activated.astype(low_type)
     lowered = product(hidden, w_down)
@@ -160,7 +191,7 @@
     own_grad_upper = own_columns(grad_upper_low, ff_width)
     grad_w_up = over_rows(normed2_low, own_grad_upper)
     grad_b_up = column_sum(own_grad_upper)
-    grad_normed2 = over_cols(grad_upper_low, w_up)
+    grad_normed2 = product(grad_upper_low, w_up_t)
     grad_mid_norm, grad_ln2_gain, grad_ln2_shift = second_pull(grad_normed2)
     grad_middle = grad_out + grad_mid_norm
     grad_mid_low = grad_middle.astype(low_type)
@@ -197,9 +228,9 @@
     grad_w_value = over_rows(normed_low, own_grad_values)
     grad_b_value = column_sum(own_grad_values)
     grad_normed = (
-        over_cols(grad_queries, w_query)
-        + over_cols(grad_keys, w_key)
-        + over_cols(grad_values, w_value)
+        product(grad_queries, w_query_t)
+        + product(grad_keys, w_key_t)
+        + product(grad_values, w_value_t)
     )
     grad_start_norm, grad_ln1_gain, grad_ln1_shift = first_pull(grad_normed)
     grad_start = grad_middle + grad_start_norm
@@ -218,44 +249,56 @@
         precision=lax.Precision.HIGHEST,
         preferred_element_type=jnp.float32,
     )
+    small = (
+        grad_ln1_gain,
+        grad_ln1_shift,
+        grad_b_query,
+        grad_b_value,
+        grad_b_out,
+        grad_b_down,
+        grad_b_up,
+        grad_ln2_gain,
+        grad_ln2_shift,
+    )
+    small_rows = jnp.concatenate(small).reshape(-1, column_count)
+    packed = jnp.concatenate([table_grad, small_rows], axis=0)
+    (
+        grad_w_query,
+        grad_w_key,
+        grad_w_value,
+        grad_w_out,
+        packed,
+        grad_w_down,
+        grad_w_up,
+    ) = lax.psum(
+        (
+            grad_w_query,
+            grad_w_key,
+            grad_w_value,
+            grad_w_out,
+            packed,
+            grad_w_down,
+            grad_w_up,
+        ),
+        "dp",
+    )
+    table_grad = packed[:step_count]
+    flat_small = packed[step_count:].reshape(-1)
+    unpacked, at = [], 0
+    for item in small:
+        unpacked.append(flat_small[at : at + item.shape[0]])
+        at += item.shape[0]
     (
         grad_ln1_gain,
         grad_ln1_shift,
-        grad_w_query,
         grad_b_query,
-        grad_w_key,
-        grad_w_value,
         grad_b_value,
-        grad_w_out,
         grad_b_out,
-        table_grad,
-        grad_w_down,
         grad_b_down,
-        grad_w_up,
         grad_b_up,
         grad_ln2_gain,
         grad_ln2_shift,
-    ) = lax.psum(
-        (
-            grad_ln1_gain,
-            grad_ln1_shift,
-            grad_w_query,
-            grad_b_query,
-            grad_w_key,
-            grad_w_value,
-            grad_b_value,
-            grad_w_out,
-            grad_b_out,
-            table_grad,
-            grad_w_down,
-            grad_b_down,
-            grad_w_up,
-            grad_b_up,
-            grad_ln2_gain,
-            grad_ln2_shift,
-        ),
-        "dp",
-    )
+    ) = unpacked
     return (
         output,
         input_grad,

time: 806 us -> 658 us (0.82)
  waiting for transfers between devices: 306 us -> 215 us
  blocking collectives: 52.7 us -> 0 us
    all_gather x6 -> x2, waiting for transfers between devices: 232 us -> 111 us  [gather_pieces(): got = lax.all_gather(sent, ('mp', 'dp'), axis=0) * one]
    dot_general x6, matrix products: 65.2 us -> 116 us  [over_cols(): lax.dot_general(left, right, CONTRACT_COLS, preferred_element_type=jnp.fl...]
    dot_general x6, matrix products: 102 us -> 52.2 us  [product(): return jnp.dot(left, right, preferred_element_type=jnp.float32)]
    psum x1, waiting for transfers between devices: 74.1 us -> 105 us  [on_device(): lax.psum((grad_w_query, grad_w_key, grad_w_value, grad_w_out, packed, gra...]
    psum x1 -> x0, blocking collectives: 25.7 us -> none  [on_device(): lax.psum((grad_ln1_gain, grad_ln1_shift, grad_w_query, grad_b_query, grad...]
    slice x0 -> x22, local copies, waits for them, and re-layouts: none -> 22.9 us  [the longest x3 12 us: gather_pieces(): out.append(got[:, :, at:at + rows])]
    reshape x7 -> x2, local copies, waits for them, and re-layouts: 18.7 us -> 0.19 us  [on_device(): small_rows = jnp.concatenate(small).reshape(-1, column_count)]
    convert_element_type x6 -> x0, other arithmetic: 17.4 us -> none  [gather_whole(): (pieces * one).astype(shard.dtype).reshape(n_dp, n_mp, piece_rows, cols)]
  transfers between devices with their start and end apart: 7 -> 3, of which waited for: 6 -> 3; matrix products, arithmetic and copies ran while one was open for 21% -> 19% of each run, Pallas kernels for 0% -> 0%
where the time goes in v2:
time: 658 us; the launch traced here: 654 us
  matrix products  229 us (35%)
  waiting for transfers between devices  215 us (33%)
  local copies, waits for them, and re-layouts  107 us (16%)
  other arithmetic  87 us (13%)
  between operations  15.6 us (2%)
    dot_general x6, matrix products, over_cols(): lax.dot_general(left, right, CONTRACT_COLS, preferred_element_type=jnp.fl...  116 us
    all_gather x2, waiting for transfers between devices, gather_pieces(): got = lax.all_gather(sent, ('mp', 'dp'), axis=0) * one  111 us
    psum x1, waiting for transfers between devices, on_device(): lax.psum((grad_w_query, grad_w_key, grad_w_value, grad_w_out, packed, gra...  105 us
    dot_general x6, matrix products, product(): return jnp.dot(left, right, preferred_element_type=jnp.float32)  52.2 us
    unnamed x135, local copies, waits for them, and re-layouts  25.6 us
    dot_general x6, matrix products, over_rows(): lax.dot_general(left, right, CONTRACT_ROWS, preferred_element_type=jnp.fl...  21.5 us
  transfers between devices with their start and end apart: 3, of which 3 were waited for; matrix products, arithmetic and copies ran while one was open for 19% of the time, Pallas kernels for 0%

profile of v2, /device:TPU:0, one launch (start us, length us, event | category | flops | bytes accessed | tf_op | source)
XLA Modules:
  0.0 654.0 jit_solution(17601089700868264851)
XLA Ops:
  35.6 54.5 %all-gather.3.cloned.1.call-done = f32[32,73,768]{2,1,0:T(8,128)} async-done(((f32[1,73,768]{2,1,0:T(8,128)}), f32[32,73,768]{2,1,0:T(8,128)}) %all-gather.3.cloned.1.call-update) | async-done | bytes 7176208 | tf_op jit(solution)/shard_map/all_gather | solution.py:60
  90.1 6.2 bitcast_convert_fusion.2
  99.8 6.5 add_convert_fusion.4
  106.3 4.7 copy.82
  111.0 6.1 reshape.492
  117.0 5.9 convolution_convert_fusion.1
  127.6 5.9 add_convert_fusion.5
  138.1 6.3 reshape.490
  144.4 6.0 reshape.494
  150.5 6.6 %fusion.15 = (f32[15,12,128]{2,1,0:T(8,128)S(1)}, f32[15,12,128,128]{2,3,1,0:T(8,128)S(1)}) fusion(pred[15,128,128]{1,2,0:T(8,128)(4,1)S(1)} %or_and_fusion, bf16[15,128,12,64]{1,0,3,2:T(8,128)(2,1)} %reshape.494, bf16[15,128,12,64]{1,0,3,2:T(8,128)(2,1)} %reshape.492), kind=kOutput, calls=%fused_computation.59 | convolution fusion | flops 386311680 | bytes 18032640 | tf_op jit(solution)/shard_map/rqhe,rkhe->rhqk/dot_general | solution.py:46
  162.1 5.1 convert_bitcast_fusion.1
  174.9 56.2 %all-gather.5.cloned.1.call-done = f32[32,217,768]{2,1,0:T(8,128)} async-done(((f32[1,217,768]{2,1,0:T(8,128)}), f32[32,217,768]{2,1,0:T(8,128)}) %all-gather.5.cloned.1.call-update) | async-done | bytes 21331984 | tf_op jit(solution)/shard_map/all_gather | solution.py:60
  231.1 8.9 %broadcast_multiply_fusion = f32[32,217,768]{2,1,0:T(8,128)S(1)} fusion(f32[32,217,768]{2,1,0:T(8,128)} %all-gather.5.cloned.1.call-done, f32[]{:T(128)} %bitcast.9), kind=kLoop, calls=%fused_computation.24 | loop fusion | flops 5332992 | bytes 42663940 | tf_op jit(solution)/shard_map/mul | solution.py:60
  240.0 5.4 convert.22
  246.8 8.4 %fusion.75 = (bf16[4,8,96,768]{3,2,1,0:T(8,128)(2,1)}, bf16[4,8,96,768]{3,2,1,0:T(8,128)(2,1)}) fusion(bf16[4,8,217,768]{3,2,1,0:T(8,128)(2,1)} %convert.22), kind=kLoop, calls=%fused_computation.158 | loop fusion | bytes 18874368 | tf_op jit(solution)/shard_map/slice | solution.py:66
  255.3 4.7 fusion.78
  265.4 61.8 %multiply_convert_fusion = (bf16[1920,3072]{1,0:T(8,128)(2,1)}, f32[1920,3072]{1,0:T(8,128)}, f32[1920,3072]{1,0:T(8,128)}) fusion(f32[3072]{0:T(1024)S(1)} %bitcast.198, bf16[1920,768]{1,0:T(8,128)(2,1)S(1)} %add_convert_fusion.3, bf16[3072,768]{1,0:T(8,128)(2,1)S(1)} %bitcast.181), kind=kOutput, calls=%fused_computation.4 | convolution fusion | flops 9448980480 | bytes 66662400 | tf_op jit(solution)/shard_map/dot_general | solution.py:36
  327.3 31.3 %add_convert_fusion = bf16[1920,3072]{1,0:T(8,128)(2,1)} fusion(f32[1920,3072]{1,0:T(8,128)} %get-tuple-element.68, f32[1920,3072]{1,0:T(8,128)} %get-tuple-element.97, f32[3072]{0:T(1024)S(1)} %bitcast.199, bf16[1920,768]{1,0:T(8,128)(2,1)} %bitcast.187, bf16[3072,768]{1,0:T(8,128)(2,1)} %bitcast.177), kind=kOutput, calls=%fused_computation.3 | convolution fusion | flops 9148170240 | bytes 66662400 | tf_op jit(solution)/shard_map/dot_general | solution.py:36
  358.6 7.0 %fusion.22 = f32[768,768]{1,0:T(8,128)} fusion(bf16[1920,768]{1,0:T(8,128)(2,1)} %copy-done.21, bf16[1920,3072]{1,0:T(8,128)(2,1)} %add_convert_fusion, s32[]{:T(128)S(6)} %select_n.39), kind=kOutput, calls=%fused_computation.75 | convolution fusion | flops 2264924160 | bytes 8257540 | tf_op jit(solution)/shard_map/dot_general | solution.py:32
  368.0 13.4 %multiply_reduce_fusion.1 = (f32[768]{0:T(1024)S(1)}, f32[1920]{0:T(1024)S(1)}, f32[768]{0:T(1024)S(1)}, f32[1920,768]{1,0:T(8,128)S(1)}) fusion(f32[1920,768]{1,0:T(8,128)S(1)} %copy-done.4, f32[1920]{0:T(1024)S(1)} %copy-done.38, f32[1920]{0:T(1024)S(1)} %copy-done.34, f32[768]{0:T(1024)S(1)} %copy-done.48, bf16[1920,3072]{1,0:T(8,128)(2,1)} %add_convert_fusion, ...), kind=kOutput, calls=%fused_computation.34 | convolution fusion | flops 9071489024 | bytes 28343808 | tf_op jit(solution)/shard_map/dot_general | solution.py:28
  392.4 4.8 copy.90
  397.2 6.0 reshape.501
  403.2 11.1 %convert_bitcast_fusion = bf16[15,128,12,64]{1,3,2,0:T(8,128)(2,1)} fusion(f32[15,12,128]{2,1,0:T(8,128)S(1)} %copy-done.30, f32[15,12,128,128]{2,3,1,0:T(8,128)} %copy-done.2, pred[15,128,128]{1,2,0:T(8,128)(4,1)S(1)} %copy-done.20, bf16[15,128,12,64]{1,0,3,2:T(8,128)(2,1)} %reshape.501), kind=kOutput, calls=%fused_computation.73 | convolution fusion | flops 390758400 | bytes 18032640 | tf_op jit(solution)/shard_map/rhqk,rqhe->rkhe/dot_general | solution.py:216
  414.4 10.0 %multiply_reduce_fusion = (f32[15,12,128]{2,1,0:T(8,128)S(1)}, f32[15,12,128,128]{2,3,1,0:T(8,128)}) fusion(f32[15,12,128]{2,1,0:T(8,128)S(1)} %copy-done.30, f32[15,12,128,128]{2,3,1,0:T(8,128)} %copy-done.2, pred[15,128,128]{1,2,0:T(8,128)(4,1)S(1)} %copy-done.20, bf16[15,128,12,64]{1,0,3,2:T(8,128)(2,1)S(1)} %copy-done.12, ...), kind=kOutput, calls=%fused_computation.19 | convolution fusion | flops 392209920 | bytes 29921280 | tf_op jit(solution)/shard_map/rqhe,rkhe->rhqk/dot_general | solution.py:203
  424.3 9.8 %multiply_convert_fusion.1 = bf16[15,12,128,128]{2,3,1,0:T(8,128)(2,1)S(1)} fusion(f32[15,12,128,128]{2,3,1,0:T(8,128)} %get-tuple-element.100, f32[15,12,128]{2,1,0:T(8,128)S(1)} %get-tuple-element.99, f32[15,12,128]{2,1,0:T(8,128)S(1)} %copy-done.30, f32[15,12,128,128]{2,3,1,0:T(8,128)} %copy-done.2, pred[15,128,128]{1,2,0:T(8,128)(4,1)S(1)} %copy-done.20), kind=kLoop, calls=%fused_computation.18 | loop fusion | flops 17694720 | bytes 29921280 | tf_op jit(solution)/shard_map/convert_element_type | solution.py:207
  447.0 5.2 fusion.79
  459.7 5.2 fusion.80
  465.0 7.5 %multiply_reduce_fusion.2 = (f32[768]{0:T(1024)S(1)}, f32[1920]{0:T(1024)S(1)}, f32[768]{0:T(1024)S(1)}, f32[1920,768]{1,0:T(8,128)S(1)}) fusion(f32[15,128,768]{2,1,0:T(8,128)S(1)} %bitcast.162, f32[1920]{0:T(1024)S(1)} %copy-done.39, f32[1920]{0:T(1024)S(1)} %copy-done.40, f32[768]{0:T(1024)S(1)} %copy-done.45, bf16[1920,768]{0,1:T(8,128)(2,1)S(1)} %bitcast.165, ...), kind=kOutput, calls=%fused_computation.37 | convolution fusion | flops 2279666432 | bytes 27753984 | tf_op jit(solution)/shard_map/dot_general | solution.py:28
  482.3 11.0 %fusion.71 = (bf16[1920,768]{1,0:T(8,128)(2,1)}, f32[1920,768]{1,0:T(8,128)}, bf16[1920,768]{1,0:T(8,128)(2,1)}) fusion(f32[1920,768]{1,0:T(8,128)} %get-tuple-element.64, f32[1920]{0:T(1024)S(1)} %negate_multiply_fusion.1, f32[1920,768]{1,0:T(8,128)} %copy-done.5, f32[1920]{0:T(1024)S(1)} %negate_multiply_fusion.2, f32[1920]{0:T(1024)S(1)} %copy-done.43, ...), kind=kLoop, calls=%fused_computation.155 | loop fusion | flops 11796480 | bytes 26565120 | tf_op jit(solution)/shard_map/convert_element_type | solution.py:237
  497.1 6.9 %fusion.20 = f32[768,768]{1,0:T(8,128)} fusion(bf16[1920,768]{1,0:T(8,128)(2,1)} %get-tuple-element.79, bf16[1920,3072]{1,0:T(8,128)(2,1)} %get-tuple-element.67, s32[]{:T(128)S(6)} %select_n.39), kind=kOutput, calls=%fused_computation.71 | convolution fusion | flops 2264924160 | bytes 8257540 | tf_op jit(solution)/shard_map/dot_general | solution.py:32
  505.1 16.2 %add_convert_fusion.2 = bf16[1920,768]{1,0:T(8,128)(2,1)} fusion(f32[1920,768]{1,0:T(8,128)} %copy-done.3, bf16[1920,3072]{1,0:T(8,128)(2,1)} %get-tuple-element.67, bf16[3072,768]{1,0:T(8,128)(2,1)} %bitcast.178, f32[768]{0:T(1024)S(1)} %copy-done.55), kind=kOutput, calls=%fused_computation.46 | convolution fusion | flops 9064120320 | bytes 25365504 | tf_op jit(solution)/shard_map/dot_general | solution.py:28
  521.4 104.7 %all-reduce.6.cloned.1.call-done = (f32[1030,192]{0,1:T(8,128)}, f32[768,192]{0,1:T(8,128)}, f32[768,192]{0,1:T(8,128)}, f32[768,192]{0,1:T(8,128)}, f32[192,768...) async-done(((f32[1030,192]{0,1:T(8,128)}, f32[768,192]{0,1:T(8,128)}, f32[768,192]{0,1:T(8,128)}, f32[768,192]{0,1:T(8,128)}, f32[192,768]{1,0:T(8,128)}, ...) | async-done | bytes 7868944 | tf_op jit(solution)/shard_map/psum | solution.py:273
  (231 shorter events, 129.1 us)
Async XLA Ops:
  7.2 10.6 %copy-start = (bf16[1000,768]{1,0:T(8,128)(2,1)S(1)}, bf16[1000,768]{1,0:T(8,128)(2,1)}, u32[]{:S(2)}) copy-start(bf16[1000,768]{1,0:T(8,128)(2,1)} %param.29) | copy-start | bytes 4608004
  7.2 20.3 %copy-start.46 = (s32[15,128]{1,0:T(8,128)S(1)}, s32[15,128]{1,0:T(8,128)}, u32[]{:S(2)}) copy-start(s32[15,128]{1,0:T(8,128)} %param.27) | copy-start | bytes 23044
  7.2 82.9 %all-gather.3.cloned.1.call-start = ((), (), s32[]{:S(2)}) async-start(), calls=%async_computation | async-start | bytes 8110080 | tf_op jit(solution)/shard_map/all_gather | solution.py:60
  12.4 218.7 %all-gather.5.cloned.1.call-start = ((), (), s32[]{:S(2)}) async-start(), calls=%async_computation.1 | async-start | bytes 22708224 | tf_op jit(solution)/shard_map/all_gather | solution.py:60
  17.0 609.0 %all-reduce.6.cloned.1.call-start = ((), (), s32[]{:S(2)}) async-start(), calls=%async_computation.2 | async-start | bytes 15925248 | tf_op jit(solution)/shard_map/psum | solution.py:273
  18.4 10.1 %copy-start.6 = (bf16[15,128,768]{2,1,0:T(8,128)(2,1)S(1)}, bf16[15,128,768]{2,1,0:T(8,128)(2,1)}, u32[]{:S(2)}) copy-start(bf16[15,128,768]{2,1,0:T(8,128)(2,1)} %param.45) | copy-start | bytes 8847364
  20.6 10.8 %copy-start.8 = (bf16[15,128,768]{2,1,0:T(8,128)(2,1)S(1)}, bf16[15,128,768]{2,1,0:T(8,128)(2,1)}, u32[]{:S(2)}) copy-start(bf16[15,128,768]{2,1,0:T(8,128)(2,1)} %param.25) | copy-start | bytes 8847364
  20.6 10.8 %copy-start.44 = (f32[768]{0:T(1024)S(1)}, f32[768]{0:T(1024)}, u32[]{:S(2)}) copy-start(f32[768]{0:T(1024)} %param.30) | copy-start | bytes 9220
  20.6 10.8 %copy-start.49 = (f32[768]{0:T(1024)S(1)}, f32[768]{0:T(1024)}, u32[]{:S(2)}) copy-start(f32[768]{0:T(1024)} %param.31) | copy-start | bytes 9220
  26.9 8.8 %copy-start.35 = (f32[15,128]{1,0:T(8,128)}, f32[15,128]{1,0:T(8,128)S(1)}, u32[]{:S(2)}) copy-start(f32[15,128]{1,0:T(8,128)S(1)} %multiply_reduce_fusion.6) | copy-start | bytes 23044
  28.5 132.3 %copy-start.19 = (pred[15,128,128]{1,2,0:T(8,128)(4,1)}, pred[15,128,128]{1,2,0:T(8,128)(4,1)S(1)}, u32[]{:S(2)}) copy-start(pred[15,128,128]{1,2,0:T(8,128)(4,1)S(1)} %or_and_fusion) | copy-start | bytes 737284
  98.8 18.3 %copy-start.24 = (bf16[4,8,24,768]{3,2,1,0:T(8,128)(2,1)}, bf16[4,8,24,768]{3,2,1,0:T(8,128)(2,1)S(1)}, u32[]{:S(2)}) copy-start(bf16[4,8,24,768]{3,2,1,0:T(8,128)(2,1)S(1)} %get-tuple-element.75) | copy-start | bytes 3538948
  98.8 28.8 %copy-start.16 = (bf16[4,8,24,768]{3,2,1,0:T(8,128)(2,1)}, bf16[4,8,24,768]{3,2,1,0:T(8,128)(2,1)S(1)}, u32[]{:S(2)}) copy-start(bf16[4,8,24,768]{3,2,1,0:T(8,128)(2,1)S(1)} %get-tuple-element.74) | copy-start | bytes 3538948
  231.1 24.2 %slice-start = ((s8[5898240]{0:T(1024)(128)(4,1)}), s8[4194304]{0:T(1024)(128)(4,1)S(1)}, s32[]{:S(2)}) async-start(s8[5898240]{0:T(1024)(128)(4,1)} %bitcast.159), calls=%async_computation.3 | async-start | bytes 8388608
  240.0 15.2 %slice-start.1 = ((s8[5898240]{0:T(1024)(128)(4,1)}), s8[1703936]{0:T(1024)(128)(4,1)S(1)}, s32[]{:S(2)}) async-start(s8[5898240]{0:T(1024)(128)(4,1)} %bitcast.159), calls=%async_computation.4 | async-start | bytes 3407872
  246.8 8.5 %copy-start.28 = (bf16[4,8,24,768]{3,2,1,0:T(8,128)(2,1)}, bf16[4,8,24,768]{3,2,1,0:T(8,128)(2,1)S(1)}, u32[]{:S(2)}) copy-start(bf16[4,8,24,768]{3,2,1,0:T(8,128)(2,1)S(1)} %slice.172) | copy-start | bytes 3538948
  260.8 66.5 %copy-start.41 = (f32[1920]{0:T(1024)}, f32[1920]{0:T(1024)S(1)}, u32[]{:S(2)}) copy-start(f32[1920]{0:T(1024)S(1)} %multiply_reduce_fusion.5) | copy-start | bytes 23044
  260.9 66.4 %copy-start.37 = (f32[1920]{0:T(1024)}, f32[1920]{0:T(1024)S(1)}, u32[]{:S(2)}) copy-start(f32[1920]{0:T(1024)S(1)} %fusion.54) | copy-start | bytes 23044
  262.6 64.7 %copy-start.21 = (bf16[1920,768]{1,0:T(8,128)(2,1)}, bf16[1920,768]{1,0:T(8,128)(2,1)S(1)}, u32[]{:S(2)}) copy-start(bf16[1920,768]{1,0:T(8,128)(2,1)S(1)} %add_convert_fusion.3) | copy-start | bytes 8847364
  358.6 9.4 %copy-start.4 = (f32[1920,768]{1,0:T(8,128)S(1)}, f32[1920,768]{1,0:T(8,128)}, u32[]{:S(2)}) copy-start(f32[1920,768]{1,0:T(8,128)} %copy-done.3) | copy-start | bytes 17694724
  358.6 9.4 %copy-start.18 = (bf16[4,8,96,768]{3,2,1,0:T(8,128)(2,1)S(1)}, bf16[4,8,96,768]{3,2,1,0:T(8,128)(2,1)}, u32[]{:S(2)}) copy-start(bf16[4,8,96,768]{3,2,1,0:T(8,128)(2,1)} %get-tuple-element.72) | copy-start | bytes 14155780
  358.6 9.4 %copy-start.34 = (f32[1920]{0:T(1024)S(1)}, f32[1920]{0:T(1024)}, u32[]{:S(2)}) copy-start(f32[1920]{0:T(1024)} %copy-done.33) | copy-start | bytes 23044
  358.6 9.4 %copy-start.38 = (f32[1920]{0:T(1024)S(1)}, f32[1920]{0:T(1024)}, u32[]{:S(2)}) copy-start(f32[1920]{0:T(1024)} %copy-done.37) | copy-start | bytes 23044
  358.6 9.4 %copy-start.48 = (f32[768]{0:T(1024)S(1)}, f32[768]{0:T(1024)}, u32[]{:S(2)}) copy-start(f32[768]{0:T(1024)} %param.39) | copy-start | bytes 9220
  368.0 13.4 %copy-start.42 = (f32[1920]{0:T(1024)S(1)}, f32[1920]{0:T(1024)}, u32[]{:S(2)}) copy-start(f32[1920]{0:T(1024)} %copy-done.41) | copy-start | bytes 23044
  392.4 10.8 %copy-start.20 = (pred[15,128,128]{1,2,0:T(8,128)(4,1)S(1)}, pred[15,128,128]{1,2,0:T(8,128)(4,1)}, u32[]{:S(2)}) copy-start(pred[15,128,128]{1,2,0:T(8,128)(4,1)} %copy-done.19) | copy-start | bytes 737284
  392.4 10.8 %copy-start.30 = (f32[15,12,128]{2,1,0:T(8,128)S(1)}, f32[15,12,128]{2,1,0:T(8,128)}, u32[]{:S(2)}) copy-start(f32[15,12,128]{2,1,0:T(8,128)} %log_add_fusion) | copy-start | bytes 276484
  403.2 11.2 %copy-start.12 = (bf16[15,128,12,64]{1,0,3,2:T(8,128)(2,1)S(1)}, bf16[15,128,12,64]{1,0,3,2:T(8,128)(2,1)}, u32[]{:S(2)}) copy-start(bf16[15,128,12,64]{1,0,3,2:T(8,128)(2,1)} %reshape.490) | copy-start | bytes 8847364
  403.2 11.2 %copy-start.13 = (bf16[15,128,12,64]{1,0,3,2:T(8,128)(2,1)S(1)}, bf16[15,128,12,64]{1,0,3,2:T(8,128)(2,1)}, u32[]{:S(2)}) copy-start(bf16[15,128,12,64]{1,0,3,2:T(8,128)(2,1)} %reshape.501) | copy-start | bytes 8847364
  424.3 9.8 %copy-start.10 = (bf16[15,128,12,64]{1,0,3,2:T(8,128)(2,1)S(1)}, bf16[15,128,12,64]{1,0,3,2:T(8,128)(2,1)}, u32[]{:S(2)}) copy-start(bf16[15,128,12,64]{1,0,3,2:T(8,128)(2,1)} %reshape.492) | copy-start | bytes 8847364
  626.0 14.9 %copy-start.32 = (f32[768,192]{0,1:T(8,128)S(1)}, f32[768,192]{0,1:T(8,128)}, u32[]{:S(2)}) copy-start(f32[768,192]{0,1:T(8,128)} %get-tuple-element.111) | copy-start | bytes 1769476
  626.0 15.7 %copy-start.31 = (f32[192,768]{1,0:T(8,128)S(1)}, f32[192,768]{1,0:T(8,128)}, u32[]{:S(2)}) copy-start(f32[192,768]{1,0:T(8,128)} %get-tuple-element.113) | copy-start | bytes 1769476
  (33 other events, 139.4 us)
Sparse Core Ops, SparseCore 0:
  12.5 77.5 all-gather.2
  93.6 137.4 all-gather.4
  505.2 120.7 all-reduce.5

commit v3 on v2

--- a/solution.py
+++ b/solution.py
@@ -191,6 +191,11 @@
     own_grad_upper = own_columns(grad_upper_low, ff_width)
     grad_w_up = over_rows(normed2_low, own_grad_upper)
     grad_b_up = column_sum(own_grad_upper)
+    ffn_grads, grad_upper_low = lax.optimization_barrier(
+        (jnp.concatenate([grad_w_down, grad_w_up], axis=0), grad_upper_low)
+    )
+    ffn_grads = lax.psum(ffn_grads, "dp")
+    grad_w_down, grad_w_up = ffn_grads[:ff_width], ffn_grads[ff_width:]
     grad_normed2 = product(grad_upper_low, w_up_t)
     grad_mid_norm, grad_ln2_gain, grad_ln2_shift = second_pull(grad_normed2)
     grad_middle = grad_out + grad_mid_norm
@@ -262,23 +267,20 @@
     )
     small_rows = jnp.concatenate(small).reshape(-1, column_count)
     packed = jnp.concatenate([table_grad, small_rows], axis=0)
+    tie = 0.0 * grad_w_up[0, 0]
     (
         grad_w_query,
         grad_w_key,
         grad_w_value,
         grad_w_out,
         packed,
-        grad_w_down,
-        grad_w_up,
     ) = lax.psum(
         (
-            grad_w_query,
+            grad_w_query + tie,
             grad_w_key,
             grad_w_value,
             grad_w_out,
             packed,
-            grad_w_down,
-            grad_w_up,
         ),
         "dp",
     )

time: 658 us -> 678 us (1.030)
  other arithmetic: 87 us -> 95.9 us
  matrix products: 229 us -> 237 us
    psum x1 -> x2, waiting for transfers between devices: 105 us -> 103 us  [the longest x1 53 us: on_device(): lax.psum((grad_w_query + tie, grad_w_key, grad_w_value, grad_w_out, packe...]
    unnamed x135 -> x149, local copies, waits for them, and re-layouts: 25.6 us -> 26.4 us
  transfers between devices with their start and end apart: 3 -> 4, of which waited for: 3 -> 4; matrix products, arithmetic and copies ran while one was open for 19% -> 24% of each run, Pallas kernels for 0% -> 0%
where the time goes in v3:
time: 678 us; the launch traced here: 674 us
  matrix products  237 us (35%)
  waiting for transfers between devices  212 us (31%)
  local copies, waits for them, and re-layouts  113 us (17%)
  other arithmetic  95.9 us (14%)
  between operations  16.4 us (2%)
    dot_general x6, matrix products, over_cols(): lax.dot_general(left, right, CONTRACT_COLS, preferred_element_type=jnp.fl...  116 us
    all_gather x2, waiting for transfers between devices, gather_pieces(): got = lax.all_gather(sent, ('mp', 'dp'), axis=0) * one  109 us
    psum x1, waiting for transfers between devices, on_device(): lax.psum((grad_w_query + tie, grad_w_key, grad_w_value, grad_w_out, packe...  53 us
    dot_general x6, matrix products, product(): return jnp.dot(left, right, preferred_element_type=jnp.float32)  51.7 us
    psum x1, waiting for transfers between devices, on_device(): ffn_grads = lax.psum(ffn_grads, 'dp')  49.8 us
    unnamed x149, local copies, waits for them, and re-layouts  26.4 us
    dot_general x6, matrix products, over_rows(): lax.dot_general(left, right, CONTRACT_ROWS, preferred_element_type=jnp.fl...  23.5 us
    dot_general x1, matrix products, on_device(): jnp.einsum('rqhe,rkhe->rhqk', grad_mixed, values_split, preferred_element...  15.3 us
  transfers between devices with their start and end apart: 4, of which 4 were waited for; matrix products, arithmetic and copies ran while one was open for 24% of the time, Pallas kernels for 0%

profile of v3, /device:TPU:0, one launch (start us, length us, event | category | flops | bytes accessed | tf_op | source)
XLA Modules:
  0.0 673.7 jit_solution(16465243003127371900)
XLA Ops:
  37.2 52.9 %all-gather.3.cloned.1.call-done = f32[32,73,768]{2,1,0:T(8,128)} async-done(((f32[1,73,768]{2,1,0:T(8,128)}), f32[32,73,768]{2,1,0:T(8,128)}) %all-gather.3.cloned.1.call-update) | async-done | bytes 7176208 | tf_op jit(solution)/shard_map/all_gather | solution.py:60
  90.1 6.2 bitcast_convert_fusion.2
  99.7 6.5 add_convert_fusion.4
  110.9 6.1 reshape.494
  117.0 5.9 convolution_convert_fusion.1
  127.6 6.2 reshape.496
  133.9 5.9 add_convert_fusion.5
  144.4 6.0 reshape.492
  150.5 6.6 fusion.15
  162.2 5.2 convert_bitcast_fusion.1
  174.9 56.1 %all-gather.5.cloned.1.call-done = f32[32,217,768]{2,1,0:T(8,128)} async-done(((f32[1,217,768]{2,1,0:T(8,128)}), f32[32,217,768]{2,1,0:T(8,128)}) %all-gather.5.cloned.1.call-update) | async-done | bytes 21331984 | tf_op jit(solution)/shard_map/all_gather | solution.py:60
  231.1 8.9 %broadcast_multiply_fusion = f32[32,217,768]{2,1,0:T(8,128)S(1)} fusion(f32[32,217,768]{2,1,0:T(8,128)} %all-gather.5.cloned.1.call-done, f32[]{:T(128)} %bitcast.9), kind=kLoop, calls=%fused_computation.24 | loop fusion | flops 5332992 | bytes 42663940 | tf_op jit(solution)/shard_map/mul | solution.py:60
  240.0 5.5 convert.22
  245.5 5.7 copy-done.3
  252.6 8.4 %fusion.74 = (bf16[4,8,96,768]{3,2,1,0:T(8,128)(2,1)}, bf16[4,8,96,768]{3,2,1,0:T(8,128)(2,1)}) fusion(bf16[4,8,217,768]{3,2,1,0:T(8,128)(2,1)} %convert.22), kind=kLoop, calls=%fused_computation.159 | loop fusion | bytes 18874368 | tf_op jit(solution)/shard_map/slice | solution.py:66
  272.1 61.9 %multiply_convert_fusion = (bf16[1920,3072]{1,0:T(8,128)(2,1)}, f32[1920,3072]{1,0:T(8,128)}, f32[1920,3072]{1,0:T(8,128)}) fusion(f32[3072]{0:T(1024)S(1)} %bitcast.203, bf16[1920,768]{1,0:T(8,128)(2,1)S(1)} %add_convert_fusion.3, bf16[3072,768]{1,0:T(8,128)(2,1)S(1)} %bitcast.187), kind=kOutput, calls=%fused_computation.4 | convolution fusion | flops 9448980480 | bytes 66662400 | tf_op jit(solution)/shard_map/dot_general | solution.py:36
  334.0 31.6 %add_convert_fusion = bf16[1920,3072]{1,0:T(8,128)(2,1)} fusion(f32[1920,3072]{1,0:T(8,128)} %get-tuple-element.70, f32[1920,3072]{1,0:T(8,128)} %get-tuple-element.100, f32[3072]{0:T(1024)S(1)} %bitcast.204, bf16[1920,768]{1,0:T(8,128)(2,1)} %bitcast.193, bf16[3072,768]{1,0:T(8,128)(2,1)} %bitcast.182), kind=kOutput, calls=%fused_computation.3 | convolution fusion | flops 9148170240 | bytes 66662400 | tf_op jit(solution)/shard_map/dot_general | solution.py:36
  365.7 5.6 fusion.22
  378.4 14.9 %multiply_reduce_fusion.1 = (f32[768]{0:T(1024)S(1)}, f32[1920]{0:T(1024)S(1)}, f32[768]{0:T(1024)S(1)}, f32[1920,768]{1,0:T(8,128)S(1)}) fusion(f32[1920,768]{1,0:T(8,128)} %copy-done.4, f32[1920]{0:T(1024)S(1)} %copy-done.43, f32[1920]{0:T(1024)S(1)} %copy-done.37, f32[768]{0:T(1024)S(1)} %copy-done.52, bf16[1920,3072]{1,0:T(8,128)(2,1)} %add_convert_fusion, ...), kind=kOutput, calls=%fused_computation.34 | convolution fusion | flops 9071489024 | bytes 28343808 | tf_op jit(solution)/shard_map/dot_general | solution.py:28
  404.4 5.0 copy.90
  409.4 6.0 reshape.503
  415.4 15.3 %multiply_reduce_fusion = (f32[15,12,128]{2,1,0:T(8,128)S(1)}, f32[15,12,128,128]{2,3,1,0:T(8,128)}) fusion(f32[15,12,128]{2,1,0:T(8,128)S(1)} %copy-done.33, f32[15,12,128,128]{2,3,1,0:T(8,128)} %copy-done.2, pred[15,128,128]{1,2,0:T(8,128)(4,1)S(1)} %copy-done.23, bf16[15,128,12,64]{1,0,3,2:T(8,128)(2,1)} %reshape.492, bf16[15,128,12,64]{1,0,3,2:T(8,128)(2,1)} %reshape.503), kind=kOutput, calls=%fused_computation.19 | convolution fusion | flops 392209920 | bytes 29921280 | tf_op jit(solution)/shard_map/rqhe,rkhe->rhqk/dot_general | solution.py:208
  430.8 9.8 %multiply_convert_fusion.1 = bf16[15,12,128,128]{2,3,1,0:T(8,128)(2,1)S(1)} fusion(f32[15,12,128,128]{2,3,1,0:T(8,128)} %get-tuple-element.103, f32[15,12,128]{2,1,0:T(8,128)S(1)} %get-tuple-element.102, f32[15,12,128]{2,1,0:T(8,128)S(1)} %copy-done.33, f32[15,12,128,128]{2,3,1,0:T(8,128)} %copy-done.2, pred[15,128,128]{1,2,0:T(8,128)(4,1)S(1)} %copy-done.23), kind=kLoop, calls=%fused_computation.18 | loop fusion | flops 17694720 | bytes 29921280 | tf_op jit(solution)/shard_map/convert_element_type | solution.py:212
  440.6 5.5 fusion.19
  448.2 10.1 %convert_bitcast_fusion = bf16[15,128,12,64]{1,3,2,0:T(8,128)(2,1)} fusion(f32[15,12,128]{2,1,0:T(8,128)S(1)} %copy-done.33, f32[15,12,128,128]{2,3,1,0:T(8,128)} %copy-done.2, pred[15,128,128]{1,2,0:T(8,128)(4,1)S(1)} %copy-done.23, bf16[15,128,12,64]{1,0,3,2:T(8,128)(2,1)S(1)} %copy-done.14), kind=kOutput, calls=%fused_computation.72 | convolution fusion | flops 390758400 | bytes 18032640 | tf_op jit(solution)/shard_map/rhqk,rqhe->rkhe/dot_general | solution.py:221
  470.5 5.1 fusion.79
  479.6 8.9 %multiply_reduce_fusion.2 = (f32[768]{0:T(1024)S(1)}, f32[1920]{0:T(1024)S(1)}, f32[768]{0:T(1024)S(1)}, f32[1920,768]{1,0:T(8,128)}) fusion(f32[15,128,768]{2,1,0:T(8,128)S(1)} %bitcast.163, f32[1920]{0:T(1024)S(1)} %copy-done.44, f32[1920]{0:T(1024)S(1)} %copy-done.45, f32[768]{0:T(1024)S(1)} %copy-done.49, bf16[1920,768]{0,1:T(8,128)(2,1)S(1)} %bitcast.168, ...), kind=kOutput, calls=%fused_computation.37 | convolution fusion | flops 2279666432 | bytes 27753984 | tf_op jit(solution)/shard_map/dot_general | solution.py:28
  488.6 10.2 %fusion.71 = (f32[1920]{0:T(1024)S(1)}, f32[1920,768]{1,0:T(8,128)}, bf16[1920,768]{1,0:T(8,128)(2,1)}) fusion(f32[1920]{0:T(1024)S(1)} %fusion.52, f32[1920]{0:T(1024)S(1)} %copy-done.44, f32[15,128,768]{2,1,0:T(8,128)} %get-tuple-element.82, f32[1920]{0:T(1024)S(1)} %copy-done.45, f32[1920,768]{1,0:T(8,128)} %get-tuple-element.104, ...), kind=kLoop, calls=%fused_computation.157 | loop fusion | flops 16218240 | bytes 20680704 | tf_op jit(solution)/shard_map/transpose(jvp())/reduce_sum | solution.py:18
  499.2 9.9 %fusion.70 = (bf16[1920,768]{1,0:T(8,128)(2,1)}, f32[1920,768]{1,0:T(8,128)}) fusion(f32[1920,768]{1,0:T(8,128)} %get-tuple-element.66, f32[1920]{0:T(1024)S(1)} %negate_multiply_fusion.1, f32[1920,768]{1,0:T(8,128)} %copy-done.5, f32[1920]{0:T(1024)S(1)} %negate_multiply_fusion.2, f32[1920]{0:T(1024)S(1)} %copy-done.41, bf16[15,128,768]{2,1,0:T(8,128)(2,1)} %param.45), kind=kLoop, calls=%fused_computation.156 | loop fusion | flops 10321920 | bytes 23616000 | tf_op jit(solution)/shard_map/convert_element_type | solution.py:242
  523.7 49.8 %all-reduce.7.cloned.1.call-done = f32[1536,768]{1,0:T(8,128)} async-done(((f32[1536,768]{1,0:T(8,128)}), f32[1536,768]{1,0:T(8,128)}) %all-reduce.7.cloned.1.call-update) | async-done | bytes 4718608 | tf_op jit(solution)/shard_map/psum | solution.py:197
  579.1 15.6 %add_convert_fusion.2 = bf16[1920,768]{1,0:T(8,128)(2,1)} fusion(f32[1920,768]{1,0:T(8,128)} %copy-done.4, bf16[1920,3072]{1,0:T(8,128)(2,1)} %get-tuple-element.69, bf16[3072,768]{1,0:T(8,128)(2,1)} %bitcast.183, f32[768]{0:T(1024)S(1)} %copy-done.59), kind=kOutput, calls=%fused_computation.46 | convolution fusion | flops 9064120320 | bytes 25365504 | tf_op jit(solution)/shard_map/dot_general | solution.py:28
  597.2 53.0 %all-reduce.9.cloned.1.call-done = (f32[1030,192]{0,1:T(8,128)}, f32[768,192]{0,1:T(8,128)}, f32[768,192]{0,1:T(8,128)}, f32[768,192]{0,1:T(8,128)}, f32[192,768]{1,0:T(8,128)}) async-done(((f32[1030,192]{0,1:T(8,128)}, f32[768,192]{0,1:T(8,128)}, f32[768,192]{0,1:T(8,128)}, f32[768,192]{0,1:T(8,128)}, f32[192,768]{1,0:T(8,128)}), (f32[1030,192]{0,1:T(8,128)}, f32[768,192]{0,1:T(8,128)}, ...) | async-done | bytes 3150352 | tf_op jit(solution)/shard_map/psum | solution.py:277
  (254 shorter events, 146.8 us)
Async XLA Ops:
  7.2 10.6 %copy-start = (bf16[1000,768]{1,0:T(8,128)(2,1)S(1)}, bf16[1000,768]{1,0:T(8,128)(2,1)}, u32[]{:S(2)}) copy-start(bf16[1000,768]{1,0:T(8,128)(2,1)} %param.29) | copy-start | bytes 4608004
  7.2 19.7 %copy-start.50 = (s32[15,128]{1,0:T(8,128)S(1)}, s32[15,128]{1,0:T(8,128)}, u32[]{:S(2)}) copy-start(s32[15,128]{1,0:T(8,128)} %param.27) | copy-start | bytes 23044
  7.2 82.9 %all-gather.3.cloned.1.call-start = ((), (), s32[]{:S(2)}) async-start(), calls=%async_computation | async-start | bytes 8110080 | tf_op jit(solution)/shard_map/all_gather | solution.py:60
  12.3 218.7 %all-gather.5.cloned.1.call-start = ((), (), s32[]{:S(2)}) async-start(), calls=%async_computation.1 | async-start | bytes 22708224 | tf_op jit(solution)/shard_map/all_gather | solution.py:60
  17.0 556.5 %all-reduce.7.cloned.1.call-start = ((), (), s32[]{:S(2)}) async-start(), calls=%async_computation.2 | async-start | bytes 9437184 | tf_op jit(solution)/shard_map/psum | solution.py:197
  20.0 15.0 %copy-start.40 = (f32[1920]{0:T(1024)}, f32[1920]{0:T(1024)S(1)}, u32[]{:S(2)}) copy-start(f32[1920]{0:T(1024)S(1)} %get-tuple-element.94) | copy-start | bytes 23044
  20.0 10.8 %copy-start.9 = (bf16[15,128,768]{2,1,0:T(8,128)(2,1)S(1)}, bf16[15,128,768]{2,1,0:T(8,128)(2,1)}, u32[]{:S(2)}) copy-start(bf16[15,128,768]{2,1,0:T(8,128)(2,1)} %param.25) | copy-start | bytes 8847364
  20.0 10.8 %copy-start.48 = (f32[768]{0:T(1024)S(1)}, f32[768]{0:T(1024)}, u32[]{:S(2)}) copy-start(f32[768]{0:T(1024)} %param.30) | copy-start | bytes 9220
  20.0 10.8 %copy-start.53 = (f32[768]{0:T(1024)S(1)}, f32[768]{0:T(1024)}, u32[]{:S(2)}) copy-start(f32[768]{0:T(1024)} %param.31) | copy-start | bytes 9220
  27.9 132.9 %copy-start.22 = (pred[15,128,128]{1,2,0:T(8,128)(4,1)}, pred[15,128,128]{1,2,0:T(8,128)(4,1)S(1)}, u32[]{:S(2)}) copy-start(pred[15,128,128]{1,2,0:T(8,128)(4,1)S(1)} %or_and_fusion) | copy-start | bytes 737284
  98.7 18.3 %copy-start.29 = (bf16[4,8,24,768]{3,2,1,0:T(8,128)(2,1)}, bf16[4,8,24,768]{3,2,1,0:T(8,128)(2,1)S(1)}, u32[]{:S(2)}) copy-start(bf16[4,8,24,768]{3,2,1,0:T(8,128)(2,1)S(1)} %get-tuple-element.79) | copy-start | bytes 3538948
  98.7 35.2 %copy-start.19 = (bf16[4,8,24,768]{3,2,1,0:T(8,128)(2,1)}, bf16[4,8,24,768]{3,2,1,0:T(8,128)(2,1)S(1)}, u32[]{:S(2)}) copy-start(bf16[4,8,24,768]{3,2,1,0:T(8,128)(2,1)S(1)} %get-tuple-element.78) | copy-start | bytes 3538948
  231.1 30.8 %slice-start = ((s8[5898240]{0:T(1024)(128)(4,1)}), s8[4194304]{0:T(1024)(128)(4,1)S(1)}, s32[]{:S(2)}) async-start(s8[5898240]{0:T(1024)(128)(4,1)} %bitcast.160), calls=%async_computation.4 | async-start | bytes 8388608
  240.0 11.2 %copy-start.3 = (f32[32,217,768]{2,1,0:T(8,128)}, f32[32,217,768]{2,1,0:T(8,128)S(1)}, u32[]{:S(2)}) copy-start(f32[32,217,768]{2,1,0:T(8,128)S(1)} %broadcast_multiply_fusion) | copy-start | bytes 63995908
  240.0 21.9 %slice-start.1 = ((s8[5898240]{0:T(1024)(128)(4,1)}), s8[1703936]{0:T(1024)(128)(4,1)S(1)}, s32[]{:S(2)}) async-start(s8[5898240]{0:T(1024)(128)(4,1)} %bitcast.160), calls=%async_computation.5 | async-start | bytes 3407872
  267.5 66.5 %copy-start.46 = (f32[1920]{0:T(1024)}, f32[1920]{0:T(1024)S(1)}, u32[]{:S(2)}) copy-start(f32[1920]{0:T(1024)S(1)} %multiply_reduce_fusion.5) | copy-start | bytes 23044
  267.5 66.4 %copy-start.42 = (f32[1920]{0:T(1024)}, f32[1920]{0:T(1024)S(1)}, u32[]{:S(2)}) copy-start(f32[1920]{0:T(1024)S(1)} %fusion.53) | copy-start | bytes 23044
  269.2 64.8 %copy-start.24 = (bf16[1920,768]{1,0:T(8,128)(2,1)}, bf16[1920,768]{1,0:T(8,128)(2,1)S(1)}, u32[]{:S(2)}) copy-start(bf16[1920,768]{1,0:T(8,128)(2,1)S(1)} %add_convert_fusion.3) | copy-start | bytes 8847364
  375.8 17.4 %slice-start.4 = ((s8[5898240]{0:T(1024)(128)(4,1)}), s8[1703936]{0:T(1024)(128)(4,1)S(1)}, s32[]{:S(2)}) async-start(s8[5898240]{0:T(1024)(128)(4,1)} %bitcast.164), calls=%async_computation.8 | async-start | bytes 3407872
  378.3 14.9 %copy-start.47 = (f32[1920]{0:T(1024)S(1)}, f32[1920]{0:T(1024)}, u32[]{:S(2)}) copy-start(f32[1920]{0:T(1024)} %copy-done.46) | copy-start | bytes 23044
  378.3 14.9 %slice-start.5 = ((s8[5898240]{0:T(1024)(128)(4,1)}), s8[4194304]{0:T(1024)(128)(4,1)S(1)}, s32[]{:S(2)}) async-start(s8[5898240]{0:T(1024)(128)(4,1)} %bitcast.164), calls=%async_computation.9 | async-start | bytes 8388608
  404.4 11.1 %copy-start.23 = (pred[15,128,128]{1,2,0:T(8,128)(4,1)S(1)}, pred[15,128,128]{1,2,0:T(8,128)(4,1)}, u32[]{:S(2)}) copy-start(pred[15,128,128]{1,2,0:T(8,128)(4,1)} %copy-done.22) | copy-start | bytes 737284
  404.4 11.1 %copy-start.33 = (f32[15,12,128]{2,1,0:T(8,128)S(1)}, f32[15,12,128]{2,1,0:T(8,128)}, u32[]{:S(2)}) copy-start(f32[15,12,128]{2,1,0:T(8,128)} %log_add_fusion) | copy-start | bytes 276484
  448.2 12.4 %copy-start.17 = (bf16[15,128,12,64]{1,3,2,0:T(8,128)(2,1)S(1)}, bf16[15,128,12,64]{1,3,2,0:T(8,128)(2,1)}, u32[]{:S(2)}) copy-start(bf16[15,128,12,64]{1,3,2,0:T(8,128)(2,1)} %fusion.19) | copy-start | bytes 8847364
  488.6 161.6 %all-reduce.9.cloned.1.call-start = ((), (), s32[]{:S(2)}) async-start(), calls=%async_computation.3 | async-start | bytes 6488064 | tf_op jit(solution)/shard_map/psum | solution.py:277
  488.6 10.3 %copy-start.55 = (f32[768]{0:T(1024)S(1)}, f32[768]{0:T(1024)}, u32[]{:S(2)}) copy-start(f32[768]{0:T(1024)} %get-tuple-element.83) | copy-start | bytes 9220
  521.0 58.1 %copy-start.59 = (f32[768]{0:T(1024)S(1)}, f32[768]{0:T(1024)}, u32[]{:S(2)}) copy-start(f32[768]{0:T(1024)} %param.44) | copy-start | bytes 9220
  579.0 15.7 %slice-start.6 = ((s8[4718592]{0:T(1024)(128)(4,1)}), s8[524288]{0:T(1024)(128)(4,1)S(1)}, s32[]{:S(2)}) async-start(s8[4718592]{0:T(1024)(128)(4,1)} %bitcast.180), calls=%async_computation.10 | async-start | bytes 1048576
  579.1 15.7 %slice-start.7 = ((s8[4718592]{0:T(1024)(128)(4,1)}), s8[4194304]{0:T(1024)(128)(4,1)S(1)}, s32[]{:S(2)}) async-start(s8[4718592]{0:T(1024)(128)(4,1)} %bitcast.180), calls=%async_computation.11 | async-start | bytes 8388608
  594.7 72.2 %copy-start.1 = (bf16[1000,768]{1,0:T(8,128)(2,1)S(1)}, bf16[1000,768]{1,0:T(8,128)(2,1)}, u32[]{:S(2)}) copy-start(bf16[1000,768]{1,0:T(8,128)(2,1)} %param.29) | copy-start | bytes 4608004
  650.2 15.0 %copy-start.35 = (f32[768,192]{0,1:T(8,128)S(1)}, f32[768,192]{0,1:T(8,128)}, u32[]{:S(2)}) copy-start(f32[768,192]{0,1:T(8,128)} %get-tuple-element.114) | copy-start | bytes 1769476
  650.2 15.8 %copy-start.34 = (f32[192,768]{1,0:T(8,128)S(1)}, f32[192,768]{1,0:T(8,128)}, u32[]{:S(2)}) copy-start(f32[192,768]{1,0:T(8,128)} %get-tuple-element.116) | copy-start | bytes 1769476
  (42 other events, 198.9 us)
Sparse Core Ops, SparseCore 0:
  12.5 77.5 all-gather.2
  93.6 137.4 all-gather.4
  488.7 84.7 all-reduce.6
  579.2 70.9 all-reduce.8

commit v4 on v2

--- a/solution.py
+++ b/solution.py
@@ -21,7 +21,7 @@
 
 
 def exact_gelu(values):
-    return jax.nn.gelu(values, approximate=False)
+    return 0.5 * values * (1.0 + lax.erf(values * math.sqrt(0.5)))
 
 
 def product(left, right):

time: 658 us -> 600 us (0.912)
  matrix products: 229 us -> 172 us
    dot_general x6, matrix products: 116 us -> 59.9 us  [over_cols(): lax.dot_general(left, right, CONTRACT_COLS, preferred_element_type=jnp.fl...]
    unnamed x135 -> x109, local copies, waits for them, and re-layouts: 25.6 us -> 24.5 us
  transfers between devices with their start and end apart: 3 -> 3, of which waited for: 3 -> 3; matrix products, arithmetic and copies ran while one was open for 19% -> 20% of each run, Pallas kernels for 0% -> 0%
where the time goes in v4:
time: 600 us; the launch traced here: 595 us
  waiting for transfers between devices  216 us (36%)
  matrix products  172 us (29%)
  local copies, waits for them, and re-layouts  105 us (18%)
  other arithmetic  86.6 us (14%)
  between operations  15.4 us (3%)
    all_gather x2, waiting for transfers between devices, gather_pieces(): got = lax.all_gather(sent, ('mp', 'dp'), axis=0) * one  111 us
    psum x1, waiting for transfers between devices, on_device(): lax.psum((grad_w_query, grad_w_key, grad_w_value, grad_w_out, packed, gra...  105 us
    dot_general x6, matrix products, over_cols(): lax.dot_general(left, right, CONTRACT_COLS, preferred_element_type=jnp.fl...  59.9 us
    dot_general x6, matrix products, product(): return jnp.dot(left, right, preferred_element_type=jnp.float32)  51.6 us
    unnamed x109, local copies, waits for them, and re-layouts  24.5 us
    dot_general x6, matrix products, over_rows(): lax.dot_general(left, right, CONTRACT_ROWS, preferred_element_type=jnp.fl...  20.4 us
  transfers between devices with their start and end apart: 3, of which 3 were waited for; matrix products, arithmetic and copies ran while one was open for 20% of the time, Pallas kernels for 0%

profile of v4, /device:TPU:0, one launch (start us, length us, event | category | flops | bytes accessed | tf_op | source)
XLA Modules:
  0.0 595.1 jit_solution(18021024033673940113)
XLA Ops:
  36.0 54.1 %all-gather.3.cloned.1.call-done = f32[32,73,768]{2,1,0:T(8,128)} async-done(((f32[1,73,768]{2,1,0:T(8,128)}), f32[32,73,768]{2,1,0:T(8,128)}) %all-gather.3.cloned.1.call-update) | async-done | bytes 7176208 | tf_op jit(solution)/shard_map/all_gather | solution.py:60
  90.1 6.1 %bitcast_convert_fusion.2 = (bf16[4,8,73,768]{3,2,1,0:T(8,128)(2,1)}, f32[32,73,768]{2,1,0:T(8,128)S(1)}) fusion(f32[32,73,768]{2,1,0:T(8,128)} %all-gather.3.cloned.1.call-done, f32[]{:T(128)} %bitcast.9), kind=kLoop, calls=%fused_computation.134 | loop fusion | flops 3588096 | bytes 17940484 | tf_op jit(solution)/shard_map/convert.16
  99.8 6.5 %add_convert_fusion.4 = bf16[1920,768]{1,0:T(8,128)(2,1)} fusion(bf16[1920,768]{1,0:T(8,128)(2,1)} %bitcast.189, bf16[768,768]{1,0:T(8,128)(2,1)S(1)} %bitcast.194, f32[768]{0:T(1024)S(1)} %add.204), kind=kOutput, calls=%fused_computation.35 | convolution fusion | flops 2267873280 | bytes 7080960 | tf_op jit(solution)/shard_map/dot_general | solution.py:36
  106.3 4.7 copy.82
  111.0 6.0 %reshape.492 = bf16[15,128,12,64]{1,0,3,2:T(8,128)(2,1)} reshape(bf16[1920,768]{0,1:T(8,128)(2,1)} %copy.82) | data formatting | bytes 5898240 | tf_op jit(solution)/shard_map/reshape | solution.py:153
  117.1 5.9 convolution_convert_fusion.1
  123.0 4.7 copy.83
  127.7 5.9 add_convert_fusion.5
  138.2 6.2 %reshape.490 = bf16[15,128,12,64]{1,0,3,2:T(8,128)(2,1)} reshape(bf16[1920,768]{0,1:T(8,128)(2,1)} %copy.81) | data formatting | bytes 5898240 | tf_op jit(solution)/shard_map/reshape | solution.py:155
  144.4 6.1 %reshape.494 = bf16[15,128,12,64]{1,0,3,2:T(8,128)(2,1)} reshape(bf16[1920,768]{0,1:T(8,128)(2,1)} %copy.83) | data formatting | bytes 5898240 | tf_op jit(solution)/shard_map/reshape | solution.py:154
  150.5 6.6 %fusion.9 = (f32[15,12,128]{2,1,0:T(8,128)S(1)}, f32[15,12,128,128]{2,3,1,0:T(8,128)S(1)}) fusion(pred[15,128,128]{1,2,0:T(8,128)(4,1)S(1)} %or_and_fusion, bf16[15,128,12,64]{1,0,3,2:T(8,128)(2,1)} %reshape.494, bf16[15,128,12,64]{1,0,3,2:T(8,128)(2,1)} %reshape.492), kind=kOutput, calls=%fused_computation.45 | convolution fusion | flops 386311680 | bytes 18032640 | tf_op jit(solution)/shard_map/rqhe,rkhe->rhqk/dot_general | solution.py:46
  162.2 5.0 convert_bitcast_fusion.1
  174.1 57.0 %all-gather.5.cloned.1.call-done = f32[32,217,768]{2,1,0:T(8,128)} async-done(((f32[1,217,768]{2,1,0:T(8,128)}), f32[32,217,768]{2,1,0:T(8,128)}) %all-gather.5.cloned.1.call-update) | async-done | bytes 21331984 | tf_op jit(solution)/shard_map/all_gather | solution.py:60
  231.1 8.9 %broadcast_multiply_fusion = f32[32,217,768]{2,1,0:T(8,128)S(1)} fusion(f32[32,217,768]{2,1,0:T(8,128)} %all-gather.5.cloned.1.call-done, f32[]{:T(128)} %bitcast.9), kind=kLoop, calls=%fused_computation.10 | loop fusion | flops 5332992 | bytes 42663940 | tf_op jit(solution)/shard_map/mul | solution.py:60
  240.0 5.5 convert.22
  246.9 7.9 %fusion.68 = (bf16[4,8,96,768]{3,2,1,0:T(8,128)(2,1)}, bf16[4,8,96,768]{3,2,1,0:T(8,128)(2,1)}) fusion(bf16[4,8,217,768]{3,2,1,0:T(8,128)(2,1)} %convert.22), kind=kLoop, calls=%fused_computation.144 | loop fusion | bytes 18874368 | tf_op jit(solution)/shard_map/slice | solution.py:66
  254.8 4.7 fusion.71
  263.9 15.9 %multiply_convert_fusion = (bf16[1920,3072]{1,0:T(8,128)(2,1)}, f32[1920,3072]{1,0:T(8,128)}) fusion(f32[3072]{0:T(1024)S(1)} %bitcast.198, bf16[1920,768]{1,0:T(8,128)(2,1)S(1)} %add_convert_fusion.3, bf16[3072,768]{1,0:T(8,128)(2,1)S(1)} %bitcast.181), kind=kOutput, calls=%fused_computation.2 | convolution fusion | flops 9095086080 | bytes 43069440 | tf_op jit(solution)/shard_map/dot_general | solution.py:36
  279.9 21.5 %add_convert_fusion = bf16[1920,3072]{1,0:T(8,128)(2,1)} fusion(f32[1920,3072]{1,0:T(8,128)} %get-tuple-element.96, f32[3072]{0:T(1024)S(1)} %bitcast.199, bf16[1920,768]{1,0:T(8,128)(2,1)S(1)} %bitcast.187, bf16[3072,768]{1,0:T(8,128)(2,1)S(1)} %bitcast.180), kind=kOutput, calls=%fused_computation.1 | convolution fusion | flops 9142272000 | bytes 43069440 | tf_op jit(solution)/shard_map/dot_general | solution.py:36
  301.3 5.9 fusion.16
  309.6 13.0 %multiply_reduce_fusion.1 = (f32[768]{0:T(1024)S(1)}, f32[1920]{0:T(1024)S(1)}, f32[768]{0:T(1024)S(1)}, f32[1920,768]{1,0:T(8,128)S(1)}) fusion(f32[1920,768]{1,0:T(8,128)S(1)} %get-tuple-element.94, f32[1920]{0:T(1024)S(1)} %fusion.48, f32[1920]{0:T(1024)S(1)} %broadcast_multiply_fusion.2, f32[768]{0:T(1024)S(1)} %copy-done.35, ...), kind=kOutput, calls=%fused_computation.20 | convolution fusion | flops 9071489024 | bytes 28343808 | tf_op jit(solution)/shard_map/dot_general | solution.py:28
  338.1 6.2 %reshape.501 = bf16[15,128,12,64]{1,0,3,2:T(8,128)(2,1)} reshape(bf16[1920,768]{0,1:T(8,128)(2,1)} %copy.90) | data formatting | bytes 5898240 | tf_op jit(solution)/shard_map/reshape | solution.py:200
  344.3 11.1 %convert_bitcast_fusion = bf16[15,128,12,64]{1,3,2,0:T(8,128)(2,1)} fusion(f32[15,12,128]{2,1,0:T(8,128)S(1)} %log_add_fusion, f32[15,12,128,128]{2,3,1,0:T(8,128)} %copy-done.2, pred[15,128,128]{1,2,0:T(8,128)(4,1)S(1)} %or_and_fusion, bf16[15,128,12,64]{1,0,3,2:T(8,128)(2,1)} %reshape.501), kind=kOutput, calls=%fused_computation.59 | convolution fusion | flops 390758400 | bytes 18032640 | tf_op jit(solution)/shard_map/rhqk,rqhe->rkhe/dot_general | solution.py:216
  355.5 10.0 %multiply_reduce_fusion = (f32[15,12,128]{2,1,0:T(8,128)S(1)}, f32[15,12,128,128]{2,3,1,0:T(8,128)}) fusion(f32[15,12,128]{2,1,0:T(8,128)S(1)} %log_add_fusion, f32[15,12,128,128]{2,3,1,0:T(8,128)} %copy-done.2, pred[15,128,128]{1,2,0:T(8,128)(4,1)S(1)} %or_and_fusion, bf16[15,128,12,64]{1,0,3,2:T(8,128)(2,1)S(1)} %copy-done.11, ...), kind=kOutput, calls=%fused_computation.5 | convolution fusion | flops 392209920 | bytes 29921280 | tf_op jit(solution)/shard_map/rqhe,rkhe->rhqk/dot_general | solution.py:203
  365.5 9.7 %multiply_convert_fusion.1 = bf16[15,12,128,128]{2,3,1,0:T(8,128)(2,1)S(1)} fusion(f32[15,12,128,128]{2,3,1,0:T(8,128)} %get-tuple-element.99, f32[15,12,128]{2,1,0:T(8,128)S(1)} %get-tuple-element.98, f32[15,12,128]{2,1,0:T(8,128)S(1)} %log_add_fusion, f32[15,12,128,128]{2,3,1,0:T(8,128)} %copy-done.2, pred[15,128,128]{1,2,0:T(8,128)(4,1)S(1)} %or_and_fusion), kind=kLoop, calls=%fused_computation.4 | loop fusion | flops 17694720 | bytes 29921280 | tf_op jit(solution)/shard_map/convert_element_type | solution.py:207
  388.2 5.1 fusion.72
  400.9 5.1 fusion.73
  406.1 7.5 %multiply_reduce_fusion.2 = (f32[768]{0:T(1024)S(1)}, f32[1920]{0:T(1024)S(1)}, f32[768]{0:T(1024)S(1)}, f32[1920,768]{1,0:T(8,128)S(1)}) fusion(f32[15,128,768]{2,1,0:T(8,128)S(1)} %bitcast.162, f32[1920]{0:T(1024)S(1)} %copy-done.29, f32[1920]{0:T(1024)S(1)} %copy-done.30, f32[768]{0:T(1024)S(1)} %copy-done.33, bf16[1920,768]{0,1:T(8,128)(2,1)S(1)} %bitcast.165, ...), kind=kOutput, calls=%fused_computation.23 | convolution fusion | flops 2279666432 | bytes 27753984 | tf_op jit(solution)/shard_map/dot_general | solution.py:28
  423.5 11.0 %fusion.65 = (bf16[1920,768]{1,0:T(8,128)(2,1)}, f32[1920,768]{1,0:T(8,128)}, bf16[1920,768]{1,0:T(8,128)(2,1)}) fusion(f32[1920,768]{1,0:T(8,128)} %get-tuple-element.64, f32[1920]{0:T(1024)S(1)} %negate_multiply_fusion, f32[1920,768]{1,0:T(8,128)} %copy-done.4, f32[1920]{0:T(1024)S(1)} %negate_multiply_fusion.1, f32[1920]{0:T(1024)S(1)} %copy-done.31, ...), kind=kLoop, calls=%fused_computation.141 | loop fusion | flops 11796480 | bytes 26565120 | tf_op jit(solution)/shard_map/convert_element_type | solution.py:237
  438.2 6.8 %fusion.14 = f32[768,768]{1,0:T(8,128)} fusion(bf16[1920,768]{1,0:T(8,128)(2,1)} %get-tuple-element.77, bf16[1920,3072]{1,0:T(8,128)(2,1)} %get-tuple-element.95, s32[]{:T(128)S(6)} %select_n.39), kind=kOutput, calls=%fused_computation.57 | convolution fusion | flops 2264924160 | bytes 8257540 | tf_op jit(solution)/shard_map/dot_general | solution.py:32
  446.1 16.2 %add_convert_fusion.2 = bf16[1920,768]{1,0:T(8,128)(2,1)} fusion(f32[1920,768]{1,0:T(8,128)} %copy-done.3, bf16[1920,3072]{1,0:T(8,128)(2,1)} %get-tuple-element.95, bf16[3072,768]{1,0:T(8,128)(2,1)} %bitcast.177, f32[768]{0:T(1024)S(1)} %copy-done.42), kind=kOutput, calls=%fused_computation.32 | convolution fusion | flops 9064120320 | bytes 25365504 | tf_op jit(solution)/shard_map/dot_general | solution.py:28
  462.3 104.8 %all-reduce.6.cloned.1.call-done = (f32[1030,192]{0,1:T(8,128)}, f32[768,192]{0,1:T(8,128)}, f32[768,192]{0,1:T(8,128)}, f32[768,192]{0,1:T(8,128)}, f32[192,768...) async-done(((f32[1030,192]{0,1:T(8,128)}, f32[768,192]{0,1:T(8,128)}, f32[768,192]{0,1:T(8,128)}, f32[768,192]{0,1:T(8,128)}, f32[192,768]{1,0:T(8,128)}, ...) | async-done | bytes 7868944 | tf_op jit(solution)/shard_map/psum | solution.py:273
  (205 shorter events, 127.9 us)
Async XLA Ops:
  7.2 10.6 %copy-start = (bf16[1000,768]{1,0:T(8,128)(2,1)S(1)}, bf16[1000,768]{1,0:T(8,128)(2,1)}, u32[]{:S(2)}) copy-start(bf16[1000,768]{1,0:T(8,128)(2,1)} %param.29) | copy-start | bytes 4608004
  7.2 20.3 %copy-start.34 = (s32[15,128]{1,0:T(8,128)S(1)}, s32[15,128]{1,0:T(8,128)}, u32[]{:S(2)}) copy-start(s32[15,128]{1,0:T(8,128)} %param.27) | copy-start | bytes 23044
  7.2 82.9 %all-gather.3.cloned.1.call-start = ((), (), s32[]{:S(2)}) async-start(), calls=%async_computation | async-start | bytes 8110080 | tf_op jit(solution)/shard_map/all_gather | solution.py:60
  12.4 218.7 %all-gather.5.cloned.1.call-start = ((), (), s32[]{:S(2)}) async-start(), calls=%async_computation.1 | async-start | bytes 22708224 | tf_op jit(solution)/shard_map/all_gather | solution.py:60
  17.0 550.1 %all-reduce.6.cloned.1.call-start = ((), (), s32[]{:S(2)}) async-start(), calls=%async_computation.2 | async-start | bytes 15925248 | tf_op jit(solution)/shard_map/psum | solution.py:273
  18.4 10.4 %copy-start.5 = (bf16[15,128,768]{2,1,0:T(8,128)(2,1)S(1)}, bf16[15,128,768]{2,1,0:T(8,128)(2,1)}, u32[]{:S(2)}) copy-start(bf16[15,128,768]{2,1,0:T(8,128)(2,1)} %param.45) | copy-start | bytes 8847364
  20.6 11.2 %copy-start.7 = (bf16[15,128,768]{2,1,0:T(8,128)(2,1)S(1)}, bf16[15,128,768]{2,1,0:T(8,128)(2,1)}, u32[]{:S(2)}) copy-start(bf16[15,128,768]{2,1,0:T(8,128)(2,1)} %param.25) | copy-start | bytes 8847364
  20.6 11.2 %copy-start.32 = (f32[768]{0:T(1024)S(1)}, f32[768]{0:T(1024)}, u32[]{:S(2)}) copy-start(f32[768]{0:T(1024)} %param.30) | copy-start | bytes 9220
  20.6 11.2 %copy-start.36 = (f32[768]{0:T(1024)S(1)}, f32[768]{0:T(1024)}, u32[]{:S(2)}) copy-start(f32[768]{0:T(1024)} %param.31) | copy-start | bytes 9220
  26.9 9.2 %copy-start.27 = (f32[15,128]{1,0:T(8,128)}, f32[15,128]{1,0:T(8,128)S(1)}, u32[]{:S(2)}) copy-start(f32[15,128]{1,0:T(8,128)S(1)} %multiply_reduce_fusion.6) | copy-start | bytes 23044
  98.8 18.3 %copy-start.21 = (bf16[4,8,24,768]{3,2,1,0:T(8,128)(2,1)}, bf16[4,8,24,768]{3,2,1,0:T(8,128)(2,1)S(1)}, u32[]{:S(2)}) copy-start(bf16[4,8,24,768]{3,2,1,0:T(8,128)(2,1)S(1)} %get-tuple-element.73) | copy-start | bytes 3538948
  98.8 29.0 %copy-start.15 = (bf16[4,8,24,768]{3,2,1,0:T(8,128)(2,1)}, bf16[4,8,24,768]{3,2,1,0:T(8,128)(2,1)S(1)}, u32[]{:S(2)}) copy-start(bf16[4,8,24,768]{3,2,1,0:T(8,128)(2,1)S(1)} %get-tuple-element.72) | copy-start | bytes 3538948
  231.1 23.7 %slice-start = ((s8[5898240]{0:T(1024)(128)(4,1)}), s8[4194304]{0:T(1024)(128)(4,1)S(1)}, s32[]{:S(2)}) async-start(s8[5898240]{0:T(1024)(128)(4,1)} %bitcast.159), calls=%async_computation.3 | async-start | bytes 8388608
  240.0 14.8 %slice-start.1 = ((s8[5898240]{0:T(1024)(128)(4,1)}), s8[1703936]{0:T(1024)(128)(4,1)S(1)}, s32[]{:S(2)}) async-start(s8[5898240]{0:T(1024)(128)(4,1)} %bitcast.159), calls=%async_computation.4 | async-start | bytes 3407872
  246.9 7.9 %copy-start.41 = (f32[768]{0:T(1024)S(1)}, f32[768]{0:T(1024)}, u32[]{:S(2)}) copy-start(f32[768]{0:T(1024)} %param.38) | copy-start | bytes 9220
  259.5 63.1 %copy-start.3 = (f32[1920,768]{1,0:T(8,128)}, f32[1920,768]{1,0:T(8,128)S(1)}, u32[]{:S(2)}) copy-start(f32[1920,768]{1,0:T(8,128)S(1)} %get-tuple-element.94) | copy-start | bytes 17694724
  260.4 19.5 %slice-start.4 = ((s8[4718592]{0:T(1024)(128)(4,1)}), s8[4194304]{0:T(1024)(128)(4,1)S(1)}, s32[]{:S(2)}) async-start(s8[4718592]{0:T(1024)(128)(4,1)} %bitcast.178), calls=%async_computation.7 | async-start | bytes 8388608
  263.9 15.9 %slice-start.5 = ((s8[4718592]{0:T(1024)(128)(4,1)}), s8[524288]{0:T(1024)(128)(4,1)S(1)}, s32[]{:S(2)}) async-start(s8[4718592]{0:T(1024)(128)(4,1)} %bitcast.178), calls=%async_computation.8 | async-start | bytes 1048576
  263.9 15.9 %copy-start.18 = (bf16[15,128,768]{2,1,0:T(8,128)(2,1)S(1)}, bf16[15,128,768]{2,1,0:T(8,128)(2,1)}, u32[]{:S(2)}) copy-start(bf16[15,128,768]{2,1,0:T(8,128)(2,1)} %get-tuple-element.79) | copy-start | bytes 8847364
  344.3 11.2 %copy-start.11 = (bf16[15,128,12,64]{1,0,3,2:T(8,128)(2,1)S(1)}, bf16[15,128,12,64]{1,0,3,2:T(8,128)(2,1)}, u32[]{:S(2)}) copy-start(bf16[15,128,12,64]{1,0,3,2:T(8,128)(2,1)} %reshape.490) | copy-start | bytes 8847364
  344.3 11.2 %copy-start.12 = (bf16[15,128,12,64]{1,0,3,2:T(8,128)(2,1)S(1)}, bf16[15,128,12,64]{1,0,3,2:T(8,128)(2,1)}, u32[]{:S(2)}) copy-start(bf16[15,128,12,64]{1,0,3,2:T(8,128)(2,1)} %reshape.501) | copy-start | bytes 8847364
  365.5 9.7 %copy-start.9 = (bf16[15,128,12,64]{1,0,3,2:T(8,128)(2,1)S(1)}, bf16[15,128,12,64]{1,0,3,2:T(8,128)(2,1)}, u32[]{:S(2)}) copy-start(bf16[15,128,12,64]{1,0,3,2:T(8,128)(2,1)} %reshape.492) | copy-start | bytes 8847364
  399.6 6.5 %slice-start.2 = ((s8[5898240]{0:T(1024)(128)(4,1)}), s8[4194304]{0:T(1024)(128)(4,1)S(1)}, s32[]{:S(2)}) async-start(s8[5898240]{0:T(1024)(128)(4,1)} %bitcast.161), calls=%async_computation.5 | async-start | bytes 8388608
  400.9 5.2 slice-start.3
  400.9 5.2 copy-start.16
  400.9 5.2 copy-start.29
  406.1 7.6 %copy-start.28 = (f32[15,128]{1,0:T(8,128)S(1)}, f32[15,128]{1,0:T(8,128)}, u32[]{:S(2)}) copy-start(f32[15,128]{1,0:T(8,128)} %copy-done.27) | copy-start | bytes 23044
  406.1 7.6 %copy-start.37 = (f32[768]{0:T(1024)S(1)}, f32[768]{0:T(1024)}, u32[]{:S(2)}) copy-start(f32[768]{0:T(1024)} %param.31) | copy-start | bytes 9220
  567.2 14.9 %copy-start.26 = (f32[768,192]{0,1:T(8,128)S(1)}, f32[768,192]{0,1:T(8,128)}, u32[]{:S(2)}) copy-start(f32[768,192]{0,1:T(8,128)} %get-tuple-element.110) | copy-start | bytes 1769476
  567.2 15.8 %copy-start.25 = (f32[192,768]{1,0:T(8,128)S(1)}, f32[192,768]{1,0:T(8,128)}, u32[]{:S(2)}) copy-start(f32[192,768]{1,0:T(8,128)} %get-tuple-element.112) | copy-start | bytes 1769476
  578.0 5.7 copy-start.20
  580.1 8.3 %copy-start.1 = (bf16[1000,768]{1,0:T(8,128)(2,1)S(1)}, bf16[1000,768]{1,0:T(8,128)(2,1)}, u32[]{:S(2)}) copy-start(bf16[1000,768]{1,0:T(8,128)(2,1)} %param.29) | copy-start | bytes 4608004
  (20 other events, 64.6 us)
Sparse Core Ops, SparseCore 0:
  12.5 77.5 all-gather.2
  93.6 137.4 all-gather.4
  446.2 120.9 all-reduce.5

commit v5 on v4

--- a/solution.py
+++ b/solution.py
@@ -3,7 +3,7 @@
 import jax
 import jax.numpy as jnp
 from jax import lax
-from jax.sharding import PartitionSpec as P
+from jax.sharding import Mesh, PartitionSpec as P
 
 HD = 64
 
@@ -49,34 +49,43 @@
     return jnp.where(allowed[:, None], scores, -1e30)
 
 
+DP = ("dpo", "core")
+
+
 def gather_pieces(blocks, one):
-    n_dp = lax.axis_size("dp")
-    d = lax.axis_index("dp")
+    n_dpo = lax.axis_size("dpo")
+    n_mp = lax.axis_size("mp")
+    c = lax.axis_index("core")
+    j = lax.axis_index("dpo")
     pieces = []
     for block in blocks:
-        piece_rows = block.shape[0] // n_dp
-        pieces.append(lax.dynamic_slice_in_dim(block, d * piece_rows, piece_rows, 0))
+        piece_rows = block.shape[0] // (2 * n_dpo)
+        at = (c * n_dpo + j) * piece_rows
+        pieces.append(lax.dynamic_slice_in_dim(block, at, piece_rows, 0))
     sent = jnp.concatenate([p.astype(jnp.float32) for p in pieces], axis=0) * one
-    got = lax.all_gather(sent, ("mp", "dp"), axis=0) * one
-    n_mp = lax.axis_size("mp")
-    got = got.reshape(n_mp, n_dp, *sent.shape)
+    half = lax.all_gather(sent, ("mp", "dpo"), axis=0) * one
+    other = lax.ppermute(half, "core", [(0, 1), (1, 0)]) * one
+    mine_first = jnp.stack([half, other])
+    other_first = jnp.stack([other, half])
+    both = jnp.where(c == 0, mine_first, other_first)
+    both = both.reshape(2, n_mp, n_dpo, *sent.shape).transpose(1, 0, 2, 3, 4)
     out, at = [], 0
     for p in pieces:
         rows = p.shape[0]
-        out.append(got[:, :, at : at + rows])
+        out.append(both[:, :, :, at : at + rows])
         at += rows
     return out
 
 
 def whole_rows(part, dtype):
-    n_mp, n_dp, rows, width = part.shape
-    return part.astype(dtype).reshape(n_mp * n_dp * rows, width)
-
-
-def bias_block(vectors, width, n_dp):
+    n_mp, n_core, n_dpo, rows, width = part.shape
+    return part.astype(dtype).reshape(n_mp * n_core * n_dpo * rows, width)
+
+
+def bias_block(vectors, width, n_pieces):
     row = jnp.concatenate(vectors)
     row = jnp.pad(row, (0, width - row.shape[0]))
-    return jnp.zeros((n_dp, width), jnp.float32).at[0].set(row)
+    return jnp.zeros((n_pieces, width), jnp.float32).at[0].set(row)
 
 
 def own_columns(values, width):
@@ -111,7 +120,7 @@
     qkv_width = w_query_shard.shape[1]
     ff_width = w_up_shard.shape[1]
     one = 1.0 + 0.0 * ln1_gain[0]
-    n_dp = lax.axis_size("dp")
+    n_dp = lax.axis_size("dpo") * lax.axis_size("core")
     low_type = jnp.bfloat16
     q_part, k_part, v_part, qv_bias = gather_pieces(
         (
@@ -125,8 +134,8 @@
     w_query_t = whole_rows(q_part, low_type)
     w_key_t = whole_rows(k_part, low_type)
     w_value_t = whole_rows(v_part, low_type)
-    b_query = qv_bias[:, 0, 0, :qkv_width].reshape(-1)
-    b_value = qv_bias[:, 0, 0, qkv_width : 2 * qkv_width].reshape(-1)
+    b_query = qv_bias[:, 0, 0, 0, :qkv_width].reshape(-1)
+    b_value = qv_bias[:, 0, 0, 0, qkv_width : 2 * qkv_width].reshape(-1)
     o_part, up_part, down_part, up_bias = gather_pieces(
         (
             w_out_shard,
@@ -139,7 +148,7 @@
     w_out = whole_rows(o_part, low_type)
     w_up_t = whole_rows(up_part, low_type)
     w_down = whole_rows(down_part, low_type)
-    b_up = up_bias[:, 0, 0, :].reshape(-1)
+    b_up = up_bias[:, 0, 0, 0, :].reshape(-1)
     heads = w_query_t.shape[0] // HD
     scaling = 1.0 / math.sqrt(HD)
     head_shape = (row_count, seq_len, heads, HD)
@@ -280,7 +289,7 @@
             grad_w_down,
             grad_w_up,
         ),
-        "dp",
+        DP,
     )
     table_grad = packed[:step_count]
     flat_small = packed[step_count:].reshape(-1)
@@ -323,10 +332,10 @@
 
 def solution(mesh):
     in_specs = (
-        P("dp", None, None),
-        P("dp"),
-        P("dp", None),
-        P("dp", None),
+        P(DP, None, None),
+        P(DP),
+        P(DP, None),
+        P(DP, None),
         P(),
         P(),
         P(),
@@ -343,11 +352,11 @@
         P("mp"),
         P("mp", None),
         P(),
-        P("dp", None, None),
+        P(DP, None, None),
     )
     out_specs = (
-        P("dp", None, None),
-        P("dp", None, None),
+        P(DP, None, None),
+        P(DP, None, None),
         P(),
         P(),
         P(None, "mp"),
@@ -365,6 +374,8 @@
         P(),
         P(None, "mp"),
     )
+    n_dp, n_mp = mesh.devices.shape
+    split = Mesh(mesh.devices.reshape(n_dp // 2, 2, n_mp), ("dpo", "core", "mp"))
     return jax.shard_map(
-        on_device, mesh=mesh, in_specs=in_specs, out_specs=out_specs, check_vma=False
-    )
+        on_device, mesh=split, in_specs=in_specs, out_specs=out_specs, check_vma=False
+    )

time: 600 us -> 735 us (1.23)
  waiting for transfers between devices: 216 us -> 302 us
  other arithmetic: 86.6 us -> 110 us
  local copies, waits for them, and re-layouts: 105 us -> 124 us
    all_gather x2, waiting for transfers between devices: 111 us -> 196 us  [gather_pieces(): half = lax.all_gather(sent, ('mp', 'dpo'), axis=0) * one]
    mul x1 -> x4, other arithmetic: 8.94 us -> 26.2 us  [the longest x2 18.7 us: gather_pieces(): other = lax.ppermute(half, 'core', [(0, 1), (1, 0)]) * one]
    mul x0 -> x2, local copies, waits for them, and re-layouts: none -> 14.1 us  [gather_pieces(): half = lax.all_gather(sent, ('mp', 'dpo'), axis=0) * one]
    another operation x2, other arithmetic: 11.6 us -> 19.9 us
    unnamed x109 -> x125, local copies, waits for them, and re-layouts: 24.5 us -> 30.3 us
  transfers between devices with their start and end apart: 3 -> 5, of which waited for: 3 -> 3; matrix products, arithmetic and copies ran while one was open for 20% -> 19% of each run, Pallas kernels for 0% -> 0%
where the time goes in v5:
time: 735 us; the launch traced here: 724 us
  waiting for transfers between devices  302 us (41%)
  matrix products  174 us (24%)
  local copies, waits for them, and re-layouts  124 us (17%)
  other arithmetic  110 us (15%)
  between operations  15.5 us (2%)
    all_gather x2, waiting for transfers between devices, gather_pieces(): half = lax.all_gather(sent, ('mp', 'dpo'), axis=0) * one  196 us
    psum x1, waiting for transfers between devices, on_device(): lax.psum((grad_w_query, grad_w_key, grad_w_value, grad_w_out, packed, gra...  106 us
    dot_general x6, matrix products, over_cols(): lax.dot_general(left, right, CONTRACT_COLS, preferred_element_type=jnp.fl...  58.9 us
    dot_general x6, matrix products, product(): return jnp.dot(left, right, preferred_element_type=jnp.float32)  54.4 us
    unnamed x125, local copies, waits for them, and re-layouts  30.3 us
    dot_general x6, matrix products, over_rows(): lax.dot_general(left, right, CONTRACT_ROWS, preferred_element_type=jnp.fl...  20.4 us
    another operation x2, other arithmetic  19.9 us
    mul x2, other arithmetic, gather_pieces(): other = lax.ppermute(half, 'core', [(0, 1), (1, 0)]) * one  18.7 us
  transfers between devices with their start and end apart: 5, of which 3 were waited for; matrix products, arithmetic and copies ran while one was open for 19% of the time, Pallas kernels for 0%

profile of v5, /device:TPU:0, one launch (start us, length us, event | category | flops | bytes accessed | tf_op | source)
XLA Modules:
  0.0 724.5 jit_solution(945628913078713197)
XLA Ops:
  17.1 136.1 %all-gather.5.cloned.1.call-done = f32[16,217,768]{2,1,0:T(8,128)} async-done(((f32[1,217,768]{2,1,0:T(8,128)}), f32[16,217,768]{2,1,0:T(8,128)}) %all-gather.5.cloned.1.call-update) | async-done | bytes 10666000 | tf_op jit(solution)/shard_map/all_gather | solution.py:66
  153.2 5.1 broadcast_multiply_fusion
  158.3 10.2 %copy.92 = f32[16,217,768]{2,0,1:T(8,128)} copy(f32[16,217,768]{2,1,0:T(8,128)S(1)} %broadcast_multiply_fusion) | data formatting | bytes 21331968 | tf_op jit(solution)/shard_map/mul | solution.py:66
  168.5 59.9 %all-gather.3.cloned.1.call-done = f32[16,73,768]{2,1,0:T(8,128)} async-done(((f32[1,73,768]{2,1,0:T(8,128)}), f32[16,73,768]{2,1,0:T(8,128)}) %all-gather.3.cloned.1.call-update) | async-done | bytes 3588112 | tf_op jit(solution)/shard_map/all_gather | solution.py:66
  263.3 6.1 add_convert_fusion.4
  274.1 6.0 reshape.503
  280.1 5.9 convolution_convert_fusion.1
  286.0 5.0 copy.85
  291.1 5.9 add_convert_fusion.5
  301.6 6.0 reshape.501
  307.6 6.0 reshape.505
  313.7 6.6 fusion.11
  325.3 4.9 convert_bitcast_fusion.1
  337.3 14.4 %copy_multiply_fusion = f32[16,217,768]{2,1,0:T(8,128)} fusion(f32[16,217,768]{2,0,1:T(8,128)} %collective-permute-done.1, f32[]{:T(128)} %bitcast.9), kind=kLoop, calls=%fused_computation.12 | loop fusion | flops 2666496 | bytes 21331972 | tf_op jit(solution)/shard_map/mul | solution.py:67
  351.7 17.5 %fusion.70 = (bf16[4,2,4,217,768]{4,3,2,1,0:T(8,128)(2,1)S(1)}, f32[4,2,4,217,768]{4,3,2,1,0:T(8,128)}) fusion(f32[1,4,4,217,768]{4,3,2,0,1:T(8,128)S(1)} %bitcast.166, f32[1,4,4,217,768]{4,3,2,0,1:T(8,128)} %bitcast.169, pred[]{:T(512)S(6)} %eq.51), kind=kLoop, calls=%fused_computation.149 | loop fusion | flops 21331968 | bytes 53329920 | tf_op jit(solution)/shard_map/convert.13
  373.3 7.0 fusion.74
  381.3 6.3 fusion.77
  391.9 15.8 %multiply_convert_fusion = (bf16[1920,3072]{1,0:T(8,128)(2,1)}, f32[1920,3072]{1,0:T(8,128)}) fusion(f32[3072]{0:T(1024)S(1)} %bitcast.206, bf16[1920,768]{1,0:T(8,128)(2,1)S(1)} %add_convert_fusion.3, bf16[3072,768]{1,0:T(8,128)(2,1)S(1)} %bitcast.190), kind=kOutput, calls=%fused_computation.2 | convolution fusion | flops 9095086080 | bytes 43069440 | tf_op jit(solution)/shard_map/dot_general | solution.py:36
  407.7 21.1 %add_convert_fusion = bf16[1920,3072]{1,0:T(8,128)(2,1)} fusion(f32[1920,3072]{1,0:T(8,128)} %get-tuple-element.98, f32[3072]{0:T(1024)S(1)} %bitcast.207, bf16[1920,768]{1,0:T(8,128)(2,1)S(1)} %bitcast.195, bf16[3072,768]{1,0:T(8,128)(2,1)S(1)} %bitcast.185), kind=kOutput, calls=%fused_computation.1 | convolution fusion | flops 9142272000 | bytes 43069440 | tf_op jit(solution)/shard_map/dot_general | solution.py:36
  428.8 5.9 fusion.18
  437.0 14.4 %multiply_reduce_fusion.1 = (f32[768]{0:T(1024)S(1)}, f32[1920]{0:T(1024)S(1)}, f32[768]{0:T(1024)S(1)}, f32[1920,768]{1,0:T(8,128)S(1)}) fusion(f32[1920,768]{1,0:T(8,128)S(1)} %get-tuple-element.96, f32[1920]{0:T(1024)S(1)} %fusion.50, f32[1920]{0:T(1024)S(1)} %broadcast_multiply_fusion.2, f32[768]{0:T(1024)S(1)} %copy-done.41, ...), kind=kOutput, calls=%fused_computation.24 | convolution fusion | flops 9071489024 | bytes 28343808 | tf_op jit(solution)/shard_map/dot_general | solution.py:28
  467.0 6.1 reshape.511
  473.1 11.1 %convert_bitcast_fusion = bf16[15,128,12,64]{1,3,2,0:T(8,128)(2,1)} fusion(f32[15,12,128]{2,1,0:T(8,128)S(1)} %log_add_fusion, f32[15,12,128,128]{2,3,1,0:T(8,128)} %copy-done.2, pred[15,128,128]{1,2,0:T(8,128)(4,1)S(1)} %or_and_fusion, bf16[15,128,12,64]{1,0,3,2:T(8,128)(2,1)} %reshape.511), kind=kOutput, calls=%fused_computation.64 | convolution fusion | flops 390758400 | bytes 18032640 | tf_op jit(solution)/shard_map/rhqk,rqhe->rkhe/dot_general | solution.py:225
  484.2 10.0 %multiply_reduce_fusion = (f32[15,12,128]{2,1,0:T(8,128)S(1)}, f32[15,12,128,128]{2,3,1,0:T(8,128)}) fusion(f32[15,12,128]{2,1,0:T(8,128)S(1)} %log_add_fusion, f32[15,12,128,128]{2,3,1,0:T(8,128)} %copy-done.2, pred[15,128,128]{1,2,0:T(8,128)(4,1)S(1)} %or_and_fusion, bf16[15,128,12,64]{1,0,3,2:T(8,128)(2,1)S(1)} %copy-done.15, ...), kind=kOutput, calls=%fused_computation.7 | convolution fusion | flops 392209920 | bytes 29921280 | tf_op jit(solution)/shard_map/rqhe,rkhe->rhqk/dot_general | solution.py:212
  494.2 9.7 %multiply_convert_fusion.1 = bf16[15,12,128,128]{2,3,1,0:T(8,128)(2,1)S(1)} fusion(f32[15,12,128,128]{2,3,1,0:T(8,128)} %get-tuple-element.101, f32[15,12,128]{2,1,0:T(8,128)S(1)} %get-tuple-element.100, f32[15,12,128]{2,1,0:T(8,128)S(1)} %log_add_fusion, f32[15,12,128,128]{2,3,1,0:T(8,128)} %copy-done.2, pred[15,128,128]{1,2,0:T(8,128)(4,1)S(1)} %or_and_fusion), kind=kLoop, calls=%fused_computation.6 | loop fusion | flops 17694720 | bytes 29921280 | tf_op jit(solution)/shard_map/convert_element_type | solution.py:216
  517.1 5.1 fusion.78
  529.7 5.1 fusion.79
  534.8 7.5 %multiply_reduce_fusion.2 = (f32[768]{0:T(1024)S(1)}, f32[1920]{0:T(1024)S(1)}, f32[768]{0:T(1024)S(1)}, f32[1920,768]{1,0:T(8,128)S(1)}) fusion(f32[15,128,768]{2,1,0:T(8,128)S(1)} %bitcast.168, f32[1920]{0:T(1024)S(1)} %copy-done.34, f32[1920]{0:T(1024)S(1)} %copy-done.35, f32[768]{0:T(1024)S(1)} %copy-done.38, bf16[1920,768]{0,1:T(8,128)(2,1)S(1)} %bitcast.173, ...), kind=kOutput, calls=%fused_computation.27 | convolution fusion | flops 2279666432 | bytes 27753984 | tf_op jit(solution)/shard_map/dot_general | solution.py:28
  552.2 11.0 %fusion.67 = (bf16[1920,768]{1,0:T(8,128)(2,1)}, f32[1920,768]{1,0:T(8,128)}, bf16[1920,768]{1,0:T(8,128)(2,1)}) fusion(f32[1920,768]{1,0:T(8,128)} %get-tuple-element.64, f32[1920]{0:T(1024)S(1)} %negate_multiply_fusion, f32[1920,768]{1,0:T(8,128)} %copy-done.5, f32[1920]{0:T(1024)S(1)} %negate_multiply_fusion.1, f32[1920]{0:T(1024)S(1)} %copy-done.36, ...), kind=kLoop, calls=%fused_computation.146 | loop fusion | flops 11796480 | bytes 26565120 | tf_op jit(solution)/shard_map/convert_element_type | solution.py:246
  566.9 6.8 fusion.16
  574.8 16.0 %add_convert_fusion.2 = bf16[1920,768]{1,0:T(8,128)(2,1)} fusion(f32[1920,768]{1,0:T(8,128)} %copy-done.4, bf16[1920,3072]{1,0:T(8,128)(2,1)} %get-tuple-element.97, bf16[3072,768]{1,0:T(8,128)(2,1)} %bitcast.186, f32[768]{0:T(1024)S(1)} %copy-done.49), kind=kOutput, calls=%fused_computation.36 | convolution fusion | flops 9064120320 | bytes 25365504 | tf_op jit(solution)/shard_map/dot_general | solution.py:28
  590.8 105.7 %all-reduce.6.cloned.1.call-done = (f32[1030,192]{0,1:T(8,128)}, f32[768,192]{0,1:T(8,128)}, f32[768,192]{0,1:T(8,128)}, f32[768,192]{0,1:T(8,128)}, f32[192,768...) async-done(((f32[1030,192]{0,1:T(8,128)}, f32[768,192]{0,1:T(8,128)}, f32[768,192]{0,1:T(8,128)}, f32[768,192]{0,1:T(8,128)}, f32[192,768]{1,0:T(8,128)}, ...) | async-done | bytes 7868944 | tf_op jit(solution)/shard_map/psum | solution.py:282
  (230 shorter events, 148.7 us)
Async XLA Ops:
  7.2 229.4 %copy-start = (bf16[1000,768]{1,0:T(8,128)(2,1)S(1)}, bf16[1000,768]{1,0:T(8,128)(2,1)}, u32[]{:S(2)}) copy-start(bf16[1000,768]{1,0:T(8,128)(2,1)} %param.29) | copy-start | bytes 4608004
  7.2 146.0 %all-gather.5.cloned.1.call-start = ((), (), s32[]{:S(2)}) async-start(), calls=%async_computation.1 | async-start | bytes 11698176 | tf_op jit(solution)/shard_map/all_gather | solution.py:66
  13.9 214.5 %all-gather.3.cloned.1.call-start = ((), (), s32[]{:S(2)}) async-start(), calls=%async_computation | async-start | bytes 4177920 | tf_op jit(solution)/shard_map/all_gather | solution.py:66
  17.0 679.4 %all-reduce.6.cloned.1.call-start = ((), (), s32[]{:S(2)}) async-start(), calls=%async_computation.2 | async-start | bytes 15925248 | tf_op jit(solution)/shard_map/psum | solution.py:282
  158.3 10.2 %copy-start.3 = (f32[16,217,768]{2,1,0:T(8,128)}, f32[16,217,768]{2,1,0:T(8,128)S(1)}, u32[]{:S(2)}) copy-start(f32[16,217,768]{2,1,0:T(8,128)S(1)} %broadcast_multiply_fusion) | copy-start | bytes 31997956
  168.5 68.1 %copy-start.46 = (s32[15]{0:T(128)S(1)}, s32[15]{0:T(128)}, u32[]{:S(2)}) copy-start(s32[15]{0:T(128)} %param.26) | copy-start | bytes 184
  168.5 68.8 %copy-start.39 = (s32[15,128]{1,0:T(8,128)S(1)}, s32[15,128]{1,0:T(8,128)}, u32[]{:S(2)}) copy-start(s32[15,128]{1,0:T(8,128)} %param.28) | copy-start | bytes 23044
  168.5 168.8 %collective-permute-start.1 = (f32[16,217,768]{2,0,1:T(8,128)}, f32[16,217,768]{2,0,1:T(8,128)}, u32[]{:S(2)}, u32[]{:S(2)}) collective-permute-start(f32[16,217,768]{2,0,1:T(8,128)} %copy.92), channel_id=1, source_target_pairs={{0,4},{4,0},{1,5},{5,1},{2,6},{6,2},{3,7},{7,3},{8,12},{12,8},{9,1... | collective-permute-start | bytes 31997960 | tf_op jit(solution)/shard_map/ppermute | solution.py:67
  232.7 12.1 %copy-start.40 = (s32[15,128]{1,0:T(8,128)S(1)}, s32[15,128]{1,0:T(8,128)}, u32[]{:S(2)}) copy-start(s32[15,128]{1,0:T(8,128)} %param.27) | copy-start | bytes 23044
  236.6 16.4 %collective-permute-start = (f32[16,73,768]{2,0,1:T(8,128)}, f32[16,73,768]{2,0,1:T(8,128)}, u32[]{:S(2)}, u32[]{:S(2)}) collective-permute-start(f32[16,73,768]{2,0,1:T(8,128)} %copy.81), channel_id=1, source_target_pairs={{0,4},{4,0},{1,5},{5,1},{2,6},{6,2},{3,7},{7,3},{8,12},{12,8},{9,1... | collective-permute-start | bytes 10764296 | tf_op jit(solution)/shard_map/ppermute | solution.py:67
  237.2 8.6 %copy-start.9 = (bf16[15,128,768]{2,1,0:T(8,128)(2,1)S(1)}, bf16[15,128,768]{2,1,0:T(8,128)(2,1)}, u32[]{:S(2)}) copy-start(bf16[15,128,768]{2,1,0:T(8,128)(2,1)} %param.45) | copy-start | bytes 8847364
  237.9 10.8 %copy-start.11 = (bf16[15,128,768]{2,1,0:T(8,128)(2,1)S(1)}, bf16[15,128,768]{2,1,0:T(8,128)(2,1)}, u32[]{:S(2)}) copy-start(bf16[15,128,768]{2,1,0:T(8,128)(2,1)} %param.25) | copy-start | bytes 8847364
  237.9 10.8 %copy-start.37 = (f32[768]{0:T(1024)S(1)}, f32[768]{0:T(1024)}, u32[]{:S(2)}) copy-start(f32[768]{0:T(1024)} %param.30) | copy-start | bytes 9220
  237.9 10.8 %copy-start.42 = (f32[768]{0:T(1024)S(1)}, f32[768]{0:T(1024)}, u32[]{:S(2)}) copy-start(f32[768]{0:T(1024)} %param.31) | copy-start | bytes 9220
  244.2 8.8 %copy-start.32 = (f32[15,128]{1,0:T(8,128)}, f32[15,128]{1,0:T(8,128)S(1)}, u32[]{:S(2)}) copy-start(f32[15,128]{1,0:T(8,128)S(1)} %multiply_reduce_fusion.6) | copy-start | bytes 23044
  262.3 17.8 %copy-start.26 = (bf16[4,2,4,24,768]{4,3,2,1,0:T(8,128)(2,1)}, bf16[4,2,4,24,768]{4,3,2,1,0:T(8,128)(2,1)S(1)}, u32[]{:S(2)}) copy-start(bf16[4,2,4,24,768]{4,3,2,1,0:T(8,128)(2,1)S(1)} %get-tuple-element.75) | copy-start | bytes 3538948
  262.3 28.8 %copy-start.19 = (bf16[4,2,4,24,768]{4,3,2,1,0:T(8,128)(2,1)}, bf16[4,2,4,24,768]{4,3,2,1,0:T(8,128)(2,1)S(1)}, u32[]{:S(2)}) copy-start(bf16[4,2,4,24,768]{4,3,2,1,0:T(8,128)(2,1)S(1)} %get-tuple-element.74) | copy-start | bytes 3538948
  337.2 14.5 %slice-start = ((s8[11010048]{0:T(1024)(128)(4,1)}), s8[4194304]{0:T(1024)(128)(4,1)S(1)}, s32[]{:S(2)}) async-start(s8[11010048]{0:T(1024)(128)(4,1)} %bitcast.164), calls=%async_computation.3 | async-start | bytes 8388608
  337.2 14.4 %slice-start.1 = ((s8[11010048]{0:T(1024)(128)(4,1)}), s8[4194304]{0:T(1024)(128)(4,1)S(1)}, s32[]{:S(2)}) async-start(s8[11010048]{0:T(1024)(128)(4,1)} %bitcast.164), calls=%async_computation.4 | async-start | bytes 8388608
  337.2 14.4 %slice-start.2 = ((s8[11010048]{0:T(1024)(128)(4,1)}), s8[2621440]{0:T(1024)(128)(4,1)S(1)}, s32[]{:S(2)}) async-start(s8[11010048]{0:T(1024)(128)(4,1)} %bitcast.164), calls=%async_computation.5 | async-start | bytes 5242880
  373.3 8.0 %copy-start.22 = (bf16[96,8,15,128]{3,1,2,0:T(8,128)(2,1)S(1)}, bf16[96,8,15,128]{3,1,2,0:T(8,128)(2,1)}, u32[]{:S(2)}) copy-start(bf16[96,8,15,128]{3,1,2,0:T(8,128)(2,1)} %copy.160) | copy-start | bytes 8847364
  373.3 8.0 %copy-start.48 = (f32[768]{0:T(1024)S(1)}, f32[768]{0:T(1024)}, u32[]{:S(2)}) copy-start(f32[768]{0:T(1024)} %param.38) | copy-start | bytes 9220
  380.3 27.4 %copy-start.21 = (bf16[4,2,4,96,768]{4,3,2,1,0:T(8,128)(2,1)}, bf16[4,2,4,96,768]{4,3,2,1,0:T(8,128)(2,1)S(1)}, u32[]{:S(2)}) copy-start(bf16[4,2,4,96,768]{4,3,2,1,0:T(8,128)(2,1)S(1)} %get-tuple-element.71) | copy-start | bytes 14155780
  387.5 63.9 %copy-start.4 = (f32[1920,768]{1,0:T(8,128)}, f32[1920,768]{1,0:T(8,128)S(1)}, u32[]{:S(2)}) copy-start(f32[1920,768]{1,0:T(8,128)S(1)} %get-tuple-element.96) | copy-start | bytes 17694724
  391.9 15.8 %copy-start.23 = (bf16[15,128,768]{2,1,0:T(8,128)(2,1)S(1)}, bf16[15,128,768]{2,1,0:T(8,128)(2,1)}, u32[]{:S(2)}) copy-start(bf16[15,128,768]{2,1,0:T(8,128)(2,1)} %get-tuple-element.81) | copy-start | bytes 8847364
  473.1 11.2 %copy-start.15 = (bf16[15,128,12,64]{1,0,3,2:T(8,128)(2,1)S(1)}, bf16[15,128,12,64]{1,0,3,2:T(8,128)(2,1)}, u32[]{:S(2)}) copy-start(bf16[15,128,12,64]{1,0,3,2:T(8,128)(2,1)} %reshape.501) | copy-start | bytes 8847364
  473.1 11.2 %copy-start.16 = (bf16[15,128,12,64]{1,0,3,2:T(8,128)(2,1)S(1)}, bf16[15,128,12,64]{1,0,3,2:T(8,128)(2,1)}, u32[]{:S(2)}) copy-start(bf16[15,128,12,64]{1,0,3,2:T(8,128)(2,1)} %reshape.511) | copy-start | bytes 8847364
  494.2 9.7 %copy-start.13 = (bf16[15,128,12,64]{1,0,3,2:T(8,128)(2,1)S(1)}, bf16[15,128,12,64]{1,0,3,2:T(8,128)(2,1)}, u32[]{:S(2)}) copy-start(bf16[15,128,12,64]{1,0,3,2:T(8,128)(2,1)} %reshape.503) | copy-start | bytes 8847364
  534.8 7.6 %copy-start.43 = (f32[768]{0:T(1024)S(1)}, f32[768]{0:T(1024)}, u32[]{:S(2)}) copy-start(f32[768]{0:T(1024)} %param.31) | copy-start | bytes 9220
  696.5 15.0 %copy-start.31 = (f32[768,192]{0,1:T(8,128)S(1)}, f32[768,192]{0,1:T(8,128)}, u32[]{:S(2)}) copy-start(f32[768,192]{0,1:T(8,128)} %get-tuple-element.112) | copy-start | bytes 1769476
  696.5 15.8 %copy-start.30 = (f32[192,768]{1,0:T(8,128)S(1)}, f32[192,768]{1,0:T(8,128)}, u32[]{:S(2)}) copy-start(f32[192,768]{1,0:T(8,128)} %get-tuple-element.114) | copy-start | bytes 1769476
  709.4 8.3 %copy-start.1 = (bf16[1000,768]{1,0:T(8,128)(2,1)S(1)}, bf16[1000,768]{1,0:T(8,128)(2,1)}, u32[]{:S(2)}) copy-start(bf16[1000,768]{1,0:T(8,128)(2,1)} %param.29) | copy-start | bytes 4608004
  (30 other events, 113.4 us)
Sparse Core Ops, SparseCore 0:
  14.0 139.1 all-gather.4
  156.6 71.7 all-gather.2
  574.9 121.4 all-reduce.5

commit v6 on v4

--- a/solution.py
+++ b/solution.py
@@ -4,6 +4,7 @@
 import jax.numpy as jnp
 from jax import lax
 from jax.sharding import PartitionSpec as P
+
 
 HD = 64
 
@@ -183,6 +184,7 @@
     grad_out = cotangent.reshape(token_count, model_width).astype(jnp.float32)
     grad_out = grad_out * valid_mask.reshape(token_count, 1).astype(jnp.float32)
     grad_out_low = grad_out.astype(low_type)
+    grad_out, grad_out_low = lax.optimization_barrier((grad_out, grad_out_low))
     grad_w_down = over_rows(own_columns(hidden, ff_width), grad_out_low)
     grad_b_down = jnp.sum(grad_out, axis=0)
     grad_hidden = over_cols(grad_out_low, w_down)
@@ -191,6 +193,8 @@
     own_grad_upper = own_columns(grad_upper_low, ff_width)
     grad_w_up = over_rows(normed2_low, own_grad_upper)
     grad_b_up = column_sum(own_grad_upper)
+    ffn_grads = lax.psum(jnp.concatenate([grad_w_down, grad_w_up], axis=0), "dp")
+    grad_w_down, grad_w_up = ffn_grads[:ff_width], ffn_grads[ff_width:]
     grad_normed2 = product(grad_upper_low, w_up_t)
     grad_mid_norm, grad_ln2_gain, grad_ln2_shift = second_pull(grad_normed2)
     grad_middle = grad_out + grad_mid_norm
@@ -262,23 +266,20 @@
     )
     small_rows = jnp.concatenate(small).reshape(-1, column_count)
     packed = jnp.concatenate([table_grad, small_rows], axis=0)
+    tie = 0.0 * ffn_grads[0, 0]
     (
         grad_w_query,
         grad_w_key,
         grad_w_value,
         grad_w_out,
         packed,
-        grad_w_down,
-        grad_w_up,
     ) = lax.psum(
         (
-            grad_w_query,
+            grad_w_query + tie,
             grad_w_key,
             grad_w_value,
             grad_w_out,
             packed,
-            grad_w_down,
-            grad_w_up,
         ),
         "dp",
     )
@@ -365,6 +366,7 @@
         P(),
         P(None, "mp"),
     )
+
     return jax.shard_map(
         on_device, mesh=mesh, in_specs=in_specs, out_specs=out_specs, check_vma=False
     )

time: 600 us -> 583 us (0.972)
  waiting for transfers between devices: 216 us -> 182 us
  matrix products: 172 us -> 181 us
    psum x1 -> x2, waiting for transfers between devices: 105 us -> 73.9 us  [the longest x1 53 us: on_device(): lax.psum((grad_w_query + tie, grad_w_key, grad_w_value, grad_w_out, packe...]
    convert_element_type x0 -> x1, other arithmetic: none -> 6.13 us  [on_device(): grad_out_low = grad_out.astype(low_type)]
    unnamed x109 -> x125, local copies, waits for them, and re-layouts: 24.5 us -> 19.7 us
  transfers between devices with their start and end apart: 3 -> 4, of which waited for: 3 -> 4; matrix products, arithmetic and copies ran while one was open for 20% -> 33% of each run, Pallas kernels for 0% -> 0%
where the time goes in v6:
time: 583 us; the launch traced here: 578 us
  waiting for transfers between devices  182 us (31%)
  matrix products  181 us (31%)
  local copies, waits for them, and re-layouts  106 us (18%)
  other arithmetic  91.2 us (16%)
  between operations  16.2 us (3%)
    all_gather x2, waiting for transfers between devices, gather_pieces(): got = lax.all_gather(sent, ('mp', 'dp'), axis=0) * one  108 us
    dot_general x6, matrix products, over_cols(): lax.dot_general(left, right, CONTRACT_COLS, preferred_element_type=jnp.fl...  60.1 us
    dot_general x6, matrix products, product(): return jnp.dot(left, right, preferred_element_type=jnp.float32)  55.6 us
    psum x1, waiting for transfers between devices, on_device(): lax.psum((grad_w_query + tie, grad_w_key, grad_w_value, grad_w_out, packe...  53 us
    dot_general x6, matrix products, over_rows(): lax.dot_general(left, right, CONTRACT_ROWS, preferred_element_type=jnp.fl...  23.6 us
    psum x1, waiting for transfers between devices, on_device(): lax.psum(jnp.concatenate([grad_w_down, grad_w_up], axis=0), 'dp')  20.9 us
    unnamed x125, local copies, waits for them, and re-layouts  19.7 us
    another operation x2, other arithmetic  11.7 us
  transfers between devices with their start and end apart: 4, of which 4 were waited for; matrix products, arithmetic and copies ran while one was open for 33% of the time, Pallas kernels for 0%

profile of v6, /device:TPU:0, one launch (start us, length us, event | category | flops | bytes accessed | tf_op | source)
XLA Modules:
  0.0 577.6 jit_solution(3121712678501707817)
XLA Ops:
  19.1 6.1 %fusion.60 = (bf16[1920,768]{1,0:T(8,128)(2,1)}, f32[1920,768]{1,0:T(8,128)}) fusion(f32[1920]{0:T(1024)S(1)} %convert_bitcast_fusion.6, bf16[15,128,768]{2,1,0:T(8,128)(2,1)} %param.45), kind=kLoop, calls=%fused_computation.138 | loop fusion | flops 4423680 | bytes 11804160 | tf_op jit(solution)/shard_map/convert_element_type | solution.py:186
  33.0 5.6 add_convert_fusion.6
  38.5 51.5 %all-gather.3.cloned.1.call-done = f32[32,73,768]{2,1,0:T(8,128)} async-done(((f32[1,73,768]{2,1,0:T(8,128)}), f32[32,73,768]{2,1,0:T(8,128)}) %all-gather.3.cloned.1.call-update) | async-done | bytes 7176208 | tf_op jit(solution)/shard_map/all_gather | solution.py:61
  90.1 6.2 %bitcast_convert_fusion.2 = (bf16[4,8,73,768]{3,2,1,0:T(8,128)(2,1)}, f32[32,73,768]{2,1,0:T(8,128)S(1)}) fusion(f32[32,73,768]{2,1,0:T(8,128)} %all-gather.3.cloned.1.call-done, f32[]{:T(128)} %bitcast.9), kind=kLoop, calls=%fused_computation.132 | loop fusion | flops 3588096 | bytes 17940484 | tf_op jit(solution)/shard_map/convert.16
  99.8 6.5 %add_convert_fusion.4 = bf16[1920,768]{1,0:T(8,128)(2,1)} fusion(bf16[1920,768]{1,0:T(8,128)(2,1)} %bitcast.189, bf16[768,768]{1,0:T(8,128)(2,1)S(1)} %bitcast.192, f32[768]{0:T(1024)S(1)} %add.208), kind=kOutput, calls=%fused_computation.35 | convolution fusion | flops 2267873280 | bytes 7080960 | tf_op jit(solution)/shard_map/dot_general | solution.py:37
  111.0 6.1 %reshape.483 = bf16[15,128,12,64]{1,0,3,2:T(8,128)(2,1)} reshape(bf16[1920,768]{0,1:T(8,128)(2,1)} %copy.82) | data formatting | bytes 5898240 | tf_op jit(solution)/shard_map/reshape | solution.py:154
  117.0 5.9 %convolution_convert_fusion.1 = bf16[1920,768]{1,0:T(8,128)(2,1)} fusion(bf16[1920,768]{1,0:T(8,128)(2,1)} %bitcast.190, bf16[768,768]{1,0:T(8,128)(2,1)S(1)} %bitcast.194), kind=kOutput, calls=%fused_computation.45 | convolution fusion | flops 2266398720 | bytes 7077888 | tf_op jit(solution)/shard_map/dot_general | solution.py:37
  127.6 5.9 %add_convert_fusion.5 = bf16[1920,768]{1,0:T(8,128)(2,1)} fusion(bf16[1920,768]{1,0:T(8,128)(2,1)} %bitcast.191, bf16[768,768]{1,0:T(8,128)(2,1)S(1)} %bitcast.174, f32[768]{0:T(1024)S(1)} %add.205), kind=kOutput, calls=%fused_computation.36 | convolution fusion | flops 2267873280 | bytes 7080960 | tf_op jit(solution)/shard_map/dot_general | solution.py:37
  138.1 6.1 %reshape.481 = bf16[15,128,12,64]{1,0,3,2:T(8,128)(2,1)} reshape(bf16[1920,768]{0,1:T(8,128)(2,1)} %copy.81) | data formatting | bytes 5898240 | tf_op jit(solution)/shard_map/reshape | solution.py:156
  144.2 6.2 %reshape.485 = bf16[15,128,12,64]{1,0,3,2:T(8,128)(2,1)} reshape(bf16[1920,768]{0,1:T(8,128)(2,1)} %copy.83) | data formatting | bytes 5898240 | tf_op jit(solution)/shard_map/reshape | solution.py:155
  150.4 6.6 %fusion.6 = (f32[15,12,128]{2,1,0:T(8,128)S(1)}, f32[15,12,128,128]{2,3,1,0:T(8,128)S(1)}) fusion(pred[15,128,128]{1,2,0:T(8,128)(4,1)S(1)} %or_and_fusion, bf16[15,128,12,64]{1,0,3,2:T(8,128)(2,1)} %reshape.485, bf16[15,128,12,64]{1,0,3,2:T(8,128)(2,1)} %reshape.483), kind=kOutput, calls=%fused_computation.42 | convolution fusion | flops 386311680 | bytes 18032640 | tf_op jit(solution)/shard_map/rqhe,rkhe->rhqk/dot_general | solution.py:47
  174.2 56.8 %all-gather.5.cloned.1.call-done = f32[32,217,768]{2,1,0:T(8,128)} async-done(((f32[1,217,768]{2,1,0:T(8,128)}), f32[32,217,768]{2,1,0:T(8,128)}) %all-gather.5.cloned.1.call-update) | async-done | bytes 21331984 | tf_op jit(solution)/shard_map/all_gather | solution.py:61
  231.1 8.9 %broadcast_multiply_fusion = f32[32,217,768]{2,1,0:T(8,128)S(1)} fusion(f32[32,217,768]{2,1,0:T(8,128)} %all-gather.5.cloned.1.call-done, f32[]{:T(128)} %bitcast.9), kind=kLoop, calls=%fused_computation.10 | loop fusion | flops 5332992 | bytes 42663940 | tf_op jit(solution)/shard_map/mul | solution.py:61
  240.0 5.5 convert.22
  246.9 8.1 %fusion.65 = (bf16[4,8,96,768]{3,2,1,0:T(8,128)(2,1)}, bf16[4,8,96,768]{3,2,1,0:T(8,128)(2,1)}) fusion(bf16[4,8,217,768]{3,2,1,0:T(8,128)(2,1)} %convert.22), kind=kLoop, calls=%fused_computation.142 | loop fusion | bytes 18874368 | tf_op jit(solution)/shard_map/slice | solution.py:67
  264.1 15.8 %multiply_convert_fusion = (bf16[1920,3072]{1,0:T(8,128)(2,1)}, f32[1920,3072]{1,0:T(8,128)}) fusion(f32[3072]{0:T(1024)S(1)} %bitcast.198, bf16[1920,768]{1,0:T(8,128)(2,1)S(1)} %add_convert_fusion.3, bf16[3072,768]{1,0:T(8,128)(2,1)S(1)} %bitcast.183), kind=kOutput, calls=%fused_computation.2 | convolution fusion | flops 9095086080 | bytes 43069440 | tf_op jit(solution)/shard_map/dot_general | solution.py:37
  280.0 21.8 %add_convert_fusion = bf16[1920,3072]{1,0:T(8,128)(2,1)} fusion(f32[1920,3072]{1,0:T(8,128)} %get-tuple-element.98, f32[3072]{0:T(1024)S(1)} %bitcast.199, bf16[1920,768]{1,0:T(8,128)(2,1)S(1)} %copy-done.20, bf16[3072,768]{1,0:T(8,128)(2,1)S(1)} %bitcast.181), kind=kOutput, calls=%fused_computation.1 | convolution fusion | flops 9142272000 | bytes 43069440 | tf_op jit(solution)/shard_map/dot_general | solution.py:37
  301.7 6.1 %fusion.12 = f32[768,768]{1,0:T(8,128)} fusion(bf16[1920,768]{1,0:T(8,128)(2,1)S(1)} %add_convert_fusion.3, bf16[1920,3072]{1,0:T(8,128)(2,1)} %add_convert_fusion, s32[]{:T(128)S(6)} %select_n.39), kind=kOutput, calls=%fused_computation.57 | convolution fusion | flops 2264924160 | bytes 8257540 | tf_op jit(solution)/shard_map/dot_general | solution.py:33
  310.1 14.3 %multiply_reduce_fusion.1 = (f32[768]{0:T(1024)S(1)}, f32[1920]{0:T(1024)S(1)}, f32[768]{0:T(1024)S(1)}, f32[1920,768]{1,0:T(8,128)S(1)}) fusion(f32[1920,768]{1,0:T(8,128)S(1)} %get-tuple-element.96, f32[1920]{0:T(1024)S(1)} %fusion.44, f32[1920]{0:T(1024)S(1)} %broadcast_multiply_fusion.2, f32[768]{0:T(1024)S(1)} %copy-done.37, ...), kind=kOutput, calls=%fused_computation.20 | convolution fusion | flops 9071489024 | bytes 28343808 | tf_op jit(solution)/shard_map/dot_general | solution.py:29
  340.0 6.4 %reshape.492 = bf16[15,128,12,64]{1,0,3,2:T(8,128)(2,1)} reshape(bf16[1920,768]{0,1:T(8,128)(2,1)} %copy.90) | data formatting | bytes 5898240 | tf_op jit(solution)/shard_map/reshape | solution.py:204
  346.4 11.1 %convert_bitcast_fusion = bf16[15,128,12,64]{1,3,2,0:T(8,128)(2,1)} fusion(f32[15,12,128]{2,1,0:T(8,128)S(1)} %log_add_fusion, f32[15,12,128,128]{2,3,1,0:T(8,128)} %copy-done.2, pred[15,128,128]{1,2,0:T(8,128)(4,1)S(1)} %or_and_fusion, bf16[15,128,12,64]{1,0,3,2:T(8,128)(2,1)} %reshape.492), kind=kOutput, calls=%fused_computation.55 | convolution fusion | flops 390758400 | bytes 18032640 | tf_op jit(solution)/shard_map/rhqk,rqhe->rkhe/dot_general | solution.py:220
  357.6 9.9 %multiply_reduce_fusion = (f32[15,12,128]{2,1,0:T(8,128)S(1)}, f32[15,12,128,128]{2,3,1,0:T(8,128)}) fusion(f32[15,12,128]{2,1,0:T(8,128)S(1)} %log_add_fusion, f32[15,12,128,128]{2,3,1,0:T(8,128)} %copy-done.2, pred[15,128,128]{1,2,0:T(8,128)(4,1)S(1)} %or_and_fusion, bf16[15,128,12,64]{1,0,3,2:T(8,128)(2,1)S(1)} %copy-done.11, ...), kind=kOutput, calls=%fused_computation.5 | convolution fusion | flops 392209920 | bytes 29921280 | tf_op jit(solution)/shard_map/rqhe,rkhe->rhqk/dot_general | solution.py:207
  367.5 9.7 %multiply_convert_fusion.1 = bf16[15,12,128,128]{2,3,1,0:T(8,128)(2,1)S(1)} fusion(f32[15,12,128,128]{2,3,1,0:T(8,128)} %get-tuple-element.101, f32[15,12,128]{2,1,0:T(8,128)S(1)} %get-tuple-element.100, f32[15,12,128]{2,1,0:T(8,128)S(1)} %log_add_fusion, f32[15,12,128,128]{2,3,1,0:T(8,128)} %copy-done.2, pred[15,128,128]{1,2,0:T(8,128)(4,1)S(1)} %or_and_fusion), kind=kLoop, calls=%fused_computation.4 | loop fusion | flops 17694720 | bytes 29921280 | tf_op jit(solution)/shard_map/convert_element_type | solution.py:211
  377.3 5.4 fusion.9
  405.8 5.3 fusion.71
  411.2 5.4 fusion.70
  416.9 10.2 %multiply_reduce_fusion.2 = (f32[768]{0:T(1024)S(1)}, f32[1920]{0:T(1024)S(1)}, f32[768]{0:T(1024)S(1)}, f32[1920,768]{1,0:T(8,128)}) fusion(f32[15,128,768]{2,1,0:T(8,128)S(1)} %bitcast.155, f32[1920]{0:T(1024)S(1)} %copy-done.31, f32[1920]{0:T(1024)S(1)} %copy-done.32, f32[768]{0:T(1024)S(1)} %copy-done.34, bf16[1920,768]{0,1:T(8,128)(2,1)S(1)} %bitcast.164, ...), kind=kOutput, calls=%fused_computation.23 | convolution fusion | flops 2279666432 | bytes 27753984 | tf_op jit(solution)/shard_map/dot_general | solution.py:29
  427.1 8.1 %fusion.63 = (f32[1920]{0:T(1024)S(1)}, f32[1920,768]{1,0:T(8,128)}, bf16[1920,768]{1,0:T(8,128)(2,1)}) fusion(f32[1920]{0:T(1024)S(1)} %fusion.43, f32[1920]{0:T(1024)S(1)} %copy-done.31, f32[15,128,768]{2,1,0:T(8,128)S(1)} %bitcast.155, f32[1920]{0:T(1024)S(1)} %copy-done.32, f32[1920,768]{1,0:T(8,128)} %get-tuple-element.102, f32[768]{0:T(1024)S(1)} %copy-done.34, ...), kind=kLoop, calls=%fused_computation.140 | loop fusion | flops 16218240 | bytes 20680704 | tf_op jit(solution)/shard_map/transpose(jvp())/reduce_sum | solution.py:19
  436.6 6.1 %fusion.62 = (bf16[1920,768]{1,0:T(8,128)(2,1)}, f32[1920,768]{1,0:T(8,128)}, f32[768]{0:T(1024)S(1)}) fusion(f32[1920,768]{1,0:T(8,128)} %get-tuple-element.66, f32[1920]{0:T(1024)S(1)} %negate_multiply_fusion, f32[1920,768]{1,0:T(8,128)S(1)} %bitcast.159, f32[1920,768]{1,0:T(8,128)S(1)} %bitcast.161, f32[1920]{0:T(1024)S(1)} %negate_multiply_fusion.1), kind=kLoop, calls=%fused_computation.139 | loop fusion | flops 8846592 | bytes 26560512 | tf_op jit(solution)/shard_map/convert_element_type | solution.py:241
  457.0 20.9 %all-reduce.7.cloned.1.call-done = f32[1536,768]{1,0:T(8,128)} async-done(((f32[1536,768]{1,0:T(8,128)}), f32[1536,768]{1,0:T(8,128)}) %all-reduce.7.cloned.1.call-update) | async-done | bytes 4718608 | tf_op jit(solution)/shard_map/psum | solution.py:196
  483.4 15.6 %add_convert_fusion.2 = bf16[1920,768]{1,0:T(8,128)(2,1)} fusion(f32[1920,768]{1,0:T(8,128)} %copy-done.3, bf16[1920,3072]{1,0:T(8,128)(2,1)} %get-tuple-element.97, bf16[3072,768]{1,0:T(8,128)(2,1)} %bitcast.178, f32[768]{0:T(1024)S(1)} %copy-done.43), kind=kOutput, calls=%fused_computation.32 | convolution fusion | flops 9064120320 | bytes 25365504 | tf_op jit(solution)/shard_map/dot_general | solution.py:29
  501.6 53.0 %all-reduce.9.cloned.1.call-done = (f32[1030,192]{0,1:T(8,128)}, f32[768,192]{0,1:T(8,128)}, f32[768,192]{0,1:T(8,128)}, f32[768,192]{0,1:T(8,128)}, f32[192,768]{1,0:T(8,128)}) async-done(((f32[1030,192]{0,1:T(8,128)}, f32[768,192]{0,1:T(8,128)}, f32[768,192]{0,1:T(8,128)}, f32[768,192]{0,1:T(8,128)}, f32[192,768]{1,0:T(8,128)}), (f32[1030,192]{0,1:T(8,128)}, f32[768,192]{0,1:T(8,128)}, ...) | async-done | bytes 3150352 | tf_op jit(solution)/shard_map/psum | solution.py:276
  (231 shorter events, 143.9 us)
Async XLA Ops:
  7.2 10.6 %copy-start = (bf16[1000,768]{1,0:T(8,128)(2,1)S(1)}, bf16[1000,768]{1,0:T(8,128)(2,1)}, u32[]{:S(2)}) copy-start(bf16[1000,768]{1,0:T(8,128)(2,1)} %param.29) | copy-start | bytes 4608004
  7.2 82.9 %all-gather.3.cloned.1.call-start = ((), (), s32[]{:S(2)}) async-start(), calls=%async_computation | async-start | bytes 8110080 | tf_op jit(solution)/shard_map/all_gather | solution.py:61
  12.3 218.7 %all-gather.5.cloned.1.call-start = ((), (), s32[]{:S(2)}) async-start(), calls=%async_computation.1 | async-start | bytes 22708224 | tf_op jit(solution)/shard_map/all_gather | solution.py:61
  17.0 460.8 %all-reduce.7.cloned.1.call-start = ((), (), s32[]{:S(2)}) async-start(), calls=%async_computation.2 | async-start | bytes 9437184 | tf_op jit(solution)/shard_map/psum | solution.py:196
  98.8 18.3 %copy-start.25 = (bf16[4,8,24,768]{3,2,1,0:T(8,128)(2,1)}, bf16[4,8,24,768]{3,2,1,0:T(8,128)(2,1)S(1)}, u32[]{:S(2)}) copy-start(bf16[4,8,24,768]{3,2,1,0:T(8,128)(2,1)S(1)} %get-tuple-element.78) | copy-start | bytes 3538948
  98.8 28.9 %copy-start.16 = (bf16[4,8,24,768]{3,2,1,0:T(8,128)(2,1)}, bf16[4,8,24,768]{3,2,1,0:T(8,128)(2,1)S(1)}, u32[]{:S(2)}) copy-start(bf16[4,8,24,768]{3,2,1,0:T(8,128)(2,1)S(1)} %get-tuple-element.77) | copy-start | bytes 3538948
  231.1 23.9 %slice-start = ((s8[5898240]{0:T(1024)(128)(4,1)}), s8[4194304]{0:T(1024)(128)(4,1)S(1)}, s32[]{:S(2)}) async-start(s8[5898240]{0:T(1024)(128)(4,1)} %bitcast.152), calls=%async_computation.4 | async-start | bytes 8388608
  240.0 15.0 %slice-start.1 = ((s8[5898240]{0:T(1024)(128)(4,1)}), s8[1703936]{0:T(1024)(128)(4,1)S(1)}, s32[]{:S(2)}) async-start(s8[5898240]{0:T(1024)(128)(4,1)} %bitcast.152), calls=%async_computation.5 | async-start | bytes 3407872
  259.7 64.8 %copy-start.3 = (f32[1920,768]{1,0:T(8,128)}, f32[1920,768]{1,0:T(8,128)S(1)}, u32[]{:S(2)}) copy-start(f32[1920,768]{1,0:T(8,128)S(1)} %get-tuple-element.96) | copy-start | bytes 17694724
  260.6 19.4 %slice-start.12 = ((s8[4718592]{0:T(1024)(128)(4,1)}), s8[4194304]{0:T(1024)(128)(4,1)S(1)}, s32[]{:S(2)}) async-start(s8[4718592]{0:T(1024)(128)(4,1)} %bitcast.179), calls=%async_computation.16 | async-start | bytes 8388608
  264.1 15.8 %slice-start.13 = ((s8[4718592]{0:T(1024)(128)(4,1)}), s8[524288]{0:T(1024)(128)(4,1)S(1)}, s32[]{:S(2)}) async-start(s8[4718592]{0:T(1024)(128)(4,1)} %bitcast.179), calls=%async_computation.17 | async-start | bytes 1048576
  264.1 15.8 %copy-start.20 = (bf16[1920,768]{1,0:T(8,128)(2,1)S(1)}, bf16[1920,768]{1,0:T(8,128)(2,1)}, u32[]{:S(2)}) copy-start(bf16[1920,768]{1,0:T(8,128)(2,1)} %get-tuple-element.45) | copy-start | bytes 8847364
  301.7 25.5 %slice-start.4 = ((s8[5898240]{0:T(1024)(128)(4,1)}), s8[4194304]{0:T(1024)(128)(4,1)S(1)}, s32[]{:S(2)}) async-start(s8[5898240]{0:T(1024)(128)(4,1)} %bitcast.156), calls=%async_computation.8 | async-start | bytes 8388608
  310.1 17.1 %slice-start.5 = ((s8[5898240]{0:T(1024)(128)(4,1)}), s8[1703936]{0:T(1024)(128)(4,1)S(1)}, s32[]{:S(2)}) async-start(s8[5898240]{0:T(1024)(128)(4,1)} %bitcast.156), calls=%async_computation.9 | async-start | bytes 3407872
  346.4 11.2 %copy-start.11 = (bf16[15,128,12,64]{1,0,3,2:T(8,128)(2,1)S(1)}, bf16[15,128,12,64]{1,0,3,2:T(8,128)(2,1)}, u32[]{:S(2)}) copy-start(bf16[15,128,12,64]{1,0,3,2:T(8,128)(2,1)} %reshape.481) | copy-start | bytes 8847364
  346.4 11.2 %copy-start.12 = (bf16[15,128,12,64]{1,0,3,2:T(8,128)(2,1)S(1)}, bf16[15,128,12,64]{1,0,3,2:T(8,128)(2,1)}, u32[]{:S(2)}) copy-start(bf16[15,128,12,64]{1,0,3,2:T(8,128)(2,1)} %reshape.492) | copy-start | bytes 8847364
  367.5 9.7 %copy-start.9 = (bf16[15,128,12,64]{1,0,3,2:T(8,128)(2,1)S(1)}, bf16[15,128,12,64]{1,0,3,2:T(8,128)(2,1)}, u32[]{:S(2)}) copy-start(bf16[15,128,12,64]{1,0,3,2:T(8,128)(2,1)} %reshape.483) | copy-start | bytes 8847364
  392.9 161.7 %all-reduce.9.cloned.1.call-start = ((), (), s32[]{:S(2)}) async-start(), calls=%async_computation.3 | async-start | bytes 6488064 | tf_op jit(solution)/shard_map/psum | solution.py:276
  398.6 18.1 %copy-start.8 = (bf16[96,8,15,128]{3,1,2,0:T(8,128)(2,1)}, bf16[96,8,15,128]{3,1,2,0:T(8,128)(2,1)S(1)}, u32[]{:S(2)}) copy-start(bf16[96,8,15,128]{3,1,2,0:T(8,128)(2,1)S(1)} %copy.151) | copy-start | bytes 8847364
  405.7 11.0 %slice-start.2 = ((s8[5898240]{0:T(1024)(128)(4,1)}), s8[4194304]{0:T(1024)(128)(4,1)S(1)}, s32[]{:S(2)}) async-start(s8[5898240]{0:T(1024)(128)(4,1)} %bitcast.154), calls=%async_computation.6 | async-start | bytes 8388608
  411.1 25.4 %slice-start.6 = ((s8[5898240]{0:T(1024)(128)(4,1)}), s8[4194304]{0:T(1024)(128)(4,1)S(1)}, s32[]{:S(2)}) async-start(s8[5898240]{0:T(1024)(128)(4,1)} %bitcast.158), calls=%async_computation.10 | async-start | bytes 8388608
  411.2 25.4 %slice-start.8 = ((s8[5898240]{0:T(1024)(128)(4,1)}), s8[4194304]{0:T(1024)(128)(4,1)S(1)}, s32[]{:S(2)}) async-start(s8[5898240]{0:T(1024)(128)(4,1)} %bitcast.160), calls=%async_computation.12 | async-start | bytes 8388608
  416.9 10.3 %copy-start.30 = (f32[15,128]{1,0:T(8,128)S(1)}, f32[15,128]{1,0:T(8,128)}, u32[]{:S(2)}) copy-start(f32[15,128]{1,0:T(8,128)} %copy-done.29) | copy-start | bytes 23044
  416.9 10.3 %copy-start.39 = (f32[768]{0:T(1024)S(1)}, f32[768]{0:T(1024)}, u32[]{:S(2)}) copy-start(f32[768]{0:T(1024)} %param.31) | copy-start | bytes 9220
  416.9 19.7 %slice-start.7 = ((s8[5898240]{0:T(1024)(128)(4,1)}), s8[1703936]{0:T(1024)(128)(4,1)S(1)}, s32[]{:S(2)}) async-start(s8[5898240]{0:T(1024)(128)(4,1)} %bitcast.158), calls=%async_computation.11 | async-start | bytes 3407872
  416.9 19.7 %slice-start.9 = ((s8[5898240]{0:T(1024)(128)(4,1)}), s8[1703936]{0:T(1024)(128)(4,1)S(1)}, s32[]{:S(2)}) async-start(s8[5898240]{0:T(1024)(128)(4,1)} %bitcast.160), calls=%async_computation.13 | async-start | bytes 3407872
  454.2 29.2 %copy-start.43 = (f32[768]{0:T(1024)S(1)}, f32[768]{0:T(1024)}, u32[]{:S(2)}) copy-start(f32[768]{0:T(1024)} %param.44) | copy-start | bytes 9220
  483.4 15.7 %slice-start.10 = ((s8[4718592]{0:T(1024)(128)(4,1)}), s8[524288]{0:T(1024)(128)(4,1)S(1)}, s32[]{:S(2)}) async-start(s8[4718592]{0:T(1024)(128)(4,1)} %bitcast.176), calls=%async_computation.14 | async-start | bytes 1048576
  483.4 15.7 %slice-start.11 = ((s8[4718592]{0:T(1024)(128)(4,1)}), s8[4194304]{0:T(1024)(128)(4,1)S(1)}, s32[]{:S(2)}) async-start(s8[4718592]{0:T(1024)(128)(4,1)} %bitcast.176), calls=%async_computation.15 | async-start | bytes 8388608
  499.1 71.8 %copy-start.1 = (bf16[1000,768]{1,0:T(8,128)(2,1)S(1)}, bf16[1000,768]{1,0:T(8,128)(2,1)}, u32[]{:S(2)}) copy-start(bf16[1000,768]{1,0:T(8,128)(2,1)} %param.29) | copy-start | bytes 4608004
  554.6 14.7 %copy-start.28 = (f32[768,192]{0,1:T(8,128)S(1)}, f32[768,192]{0,1:T(8,128)}, u32[]{:S(2)}) copy-start(f32[768,192]{0,1:T(8,128)} %get-tuple-element.112) | copy-start | bytes 1769476
  554.6 15.5 %copy-start.27 = (f32[192,768]{1,0:T(8,128)S(1)}, f32[192,768]{1,0:T(8,128)}, u32[]{:S(2)}) copy-start(f32[192,768]{1,0:T(8,128)} %get-tuple-element.114) | copy-start | bytes 1769476
  (30 other events, 146.7 us)
Sparse Core Ops, SparseCore 0:
  12.5 77.5 all-gather.2
  93.6 137.4 all-gather.4
  393.0 84.7 all-reduce.6
  483.5 70.9 all-reduce.8

commit v7 on v6

--- a/solution.py
+++ b/solution.py
@@ -3,10 +3,12 @@
 import jax
 import jax.numpy as jnp
 from jax import lax
+from jax.experimental import pallas as pl
 from jax.sharding import PartitionSpec as P
 
 
 HD = 64
+SCALE = 1.0 / math.sqrt(HD)
 
 
 EPSILON = 1e-05
@@ -41,13 +43,111 @@
     return jnp.sum(values.astype(jnp.float32), axis=0)
 
 
-def attention_scores(queries_split, keys_split, allowed):
-    scaling = 1.0 / math.sqrt(HD)
-    scores = (
-        jnp.einsum("rqhe,rkhe->rhqk", queries_split, keys_split, preferred_element_type=jnp.float32)
-        * scaling
-    )
-    return jnp.where(allowed[:, None], scores, -1e30)
+NT = (((1,), (1,)), ((), ()))
+TN = (((0,), (0,)), ((), ()))
+
+
+def _allowed(segc_ref, segr_ref, valid_ref, seq):
+    rows = lax.broadcasted_iota(jnp.int32, (seq, seq), 0)
+    cols = lax.broadcasted_iota(jnp.int32, (seq, seq), 1)
+    return (segc_ref[0] == segr_ref[0]) & ((valid_ref[0] > 0) | (rows == cols))
+
+
+def _fwd_kernel(q_ref, k_ref, v_ref, segc_ref, segr_ref, valid_ref, o_ref, lse_ref):
+    seq, width = q_ref.shape
+    allowed = _allowed(segc_ref, segr_ref, valid_ref, seq)
+    outs, lses = [], []
+    for h in range(width // HD):
+        cols = slice(h * HD, (h + 1) * HD)
+        qh, kh, vh = q_ref[:, cols], k_ref[:, cols], v_ref[:, cols]
+        s = lax.dot_general(qh, kh, NT, preferred_element_type=jnp.float32) * SCALE
+        s = jnp.where(allowed, s, -1e30)
+        m = jnp.max(s, axis=-1, keepdims=True)
+        p = jnp.exp(s - m)
+        total = jnp.sum(p, axis=-1, keepdims=True)
+        prob = p / total
+        o = jnp.dot(prob.astype(jnp.bfloat16), vh, preferred_element_type=jnp.float32)
+        outs.append(o.astype(jnp.bfloat16))
+        lses.append(m + jnp.log(total))
+    o_ref[...] = jnp.concatenate(outs, axis=1)
+    lse_ref[0] = jnp.concatenate(lses, axis=1)
+
+
+def _bwd_kernel(q_ref, k_ref, v_ref, g_ref, lse_ref, segc_ref, segr_ref, valid_ref,
+                dq_ref, dk_ref, dv_ref):
+    seq, width = q_ref.shape
+    allowed = _allowed(segc_ref, segr_ref, valid_ref, seq)
+    lse = lse_ref[0]
+    dqs, dks, dvs = [], [], []
+    for h in range(width // HD):
+        cols = slice(h * HD, (h + 1) * HD)
+        qh, kh, vh, gh = q_ref[:, cols], k_ref[:, cols], v_ref[:, cols], g_ref[:, cols]
+        s = lax.dot_general(qh, kh, NT, preferred_element_type=jnp.float32) * SCALE
+        s = jnp.where(allowed, s, -1e30)
+        p = jnp.exp(s - lse[:, h : h + 1])
+        gs = lax.dot_general(gh, vh, NT, preferred_element_type=jnp.float32)
+        delta = jnp.sum(p * gs, axis=-1, keepdims=True)
+        ds = (p * (gs - delta)).astype(jnp.bfloat16)
+        dq = jnp.dot(ds, kh, preferred_element_type=jnp.float32) * SCALE
+        dk = lax.dot_general(ds, qh, TN, preferred_element_type=jnp.float32) * SCALE
+        dv = lax.dot_general(p.astype(jnp.bfloat16), gh, TN, preferred_element_type=jnp.float32)
+        dqs.append(dq.astype(jnp.bfloat16))
+        dks.append(dk.astype(jnp.bfloat16))
+        dvs.append(dv.astype(jnp.bfloat16))
+    dq_ref[...] = jnp.concatenate(dqs, axis=1)
+    dk_ref[...] = jnp.concatenate(dks, axis=1)
+    dv_ref[...] = jnp.concatenate(dvs, axis=1)
+
+
+def _mask_specs(seq):
+    return [
+        pl.BlockSpec((1, seq, 1), lambda r: (r, 0, 0)),
+        pl.BlockSpec((1, 1, seq), lambda r: (r, 0, 0)),
+        pl.BlockSpec((1, 1, seq), lambda r: (r, 0, 0)),
+    ]
+
+
+def attention_forward(q, k, v, segments, valid_mask):
+    rows, seq = segments.shape
+    width = q.shape[1]
+    heads = width // HD
+    tile = pl.BlockSpec((seq, width), lambda r: (r, 0))
+    flops = rows * heads * 4 * seq * seq * HD
+    return pl.pallas_call(
+        _fwd_kernel,
+        grid=(rows,),
+        in_specs=[tile, tile, tile] + _mask_specs(seq),
+        out_specs=[tile, pl.BlockSpec((1, seq, heads), lambda r: (r, 0, 0))],
+        out_shape=[
+            jax.ShapeDtypeStruct(q.shape, jnp.bfloat16),
+            jax.ShapeDtypeStruct((rows, seq, heads), jnp.float32),
+        ],
+        cost_estimate=pl.CostEstimate(
+            flops=flops, transcendentals=rows * heads * seq * seq, bytes_accessed=4 * q.size * 2
+        ),
+        name="attention_forward",
+    )(q, k, v, segments[:, :, None], segments[:, None, :], valid_mask[:, None, :])
+
+
+def attention_backward(q, k, v, grad_mixed, lse, segments, valid_mask):
+    rows, seq = segments.shape
+    width = q.shape[1]
+    heads = width // HD
+    tile = pl.BlockSpec((seq, width), lambda r: (r, 0))
+    flops = rows * heads * 10 * seq * seq * HD
+    out = jax.ShapeDtypeStruct(q.shape, jnp.bfloat16)
+    return pl.pallas_call(
+        _bwd_kernel,
+        grid=(rows,),
+        in_specs=[tile, tile, tile, tile, pl.BlockSpec((1, seq, heads), lambda r: (r, 0, 0))]
+        + _mask_specs(seq),
+        out_specs=[tile, tile, tile],
+        out_shape=[out, out, out],
+        cost_estimate=pl.CostEstimate(
+            flops=flops, transcendentals=rows * heads * seq * seq, bytes_accessed=7 * q.size * 2
+        ),
+        name="attention_backward",
+    )(q, k, v, grad_mixed, lse, segments[:, :, None], segments[:, None, :], valid_mask[:, None, :])
 
 
 def gather_pieces(blocks, one):
@@ -141,9 +241,6 @@
     w_up_t = whole_rows(up_part, low_type)
     w_down = whole_rows(down_part, low_type)
     b_up = up_bias[:, 0, 0, :].reshape(-1)
-    heads = w_query_t.shape[0] // HD
-    scaling = 1.0 / math.sqrt(HD)
-    head_shape = (row_count, seq_len, heads, HD)
     start = inputs.astype(jnp.float32) + step_table[timesteps].astype(jnp.float32)[:, None, :]
     start = start.reshape(token_count, model_width)
     normed, first_pull = jax.vjp(normalize, start, ln1_gain, ln1_shift)
@@ -151,27 +248,7 @@
     queries = (over_cols(normed_low, w_query_t) + b_query).astype(low_type)
     key_rows = over_cols(normed_low, w_key_t).astype(low_type)
     value_rows = (over_cols(normed_low, w_value_t) + b_value).astype(low_type)
-    queries_split = queries.reshape(head_shape)
-    keys_split = key_rows.reshape(head_shape)
-    values_split = value_rows.reshape(head_shape)
-    places = jnp.arange(seq_len, dtype=jnp.int32)
-    diagonal = places[:, None] == places[None, :]
-    allowed = (segments[:, :, None] == segments[:, None, :]) & (
-        (valid_mask[:, None, :] > 0) | diagonal[None]
-    )
-    scores = attention_scores(queries_split, keys_split, allowed)
-    row_max = jnp.max(scores, axis=-1, keepdims=True)
-    powers = jnp.exp(scores - row_max)
-    total = jnp.sum(powers, axis=-1, keepdims=True)
-    log_total = row_max + jnp.log(total)
-    probabilities = powers / total
-    mixed = jnp.einsum(
-        "rhqk,rkhe->rqhe",
-        probabilities.astype(low_type),
-        values_split,
-        preferred_element_type=jnp.float32,
-    )
-    mixed = mixed.reshape(token_count, heads * HD).astype(low_type)
+    mixed, log_total = attention_forward(queries, key_rows, value_rows, segments, valid_mask)
     attended = product(mixed, w_out) + b_out
     middle = start + attended
     normed2, second_pull = jax.vjp(normalize, middle, ln2_gain, ln2_shift)
@@ -201,29 +278,10 @@
     grad_mid_low = grad_middle.astype(low_type)
     grad_w_out = over_rows(own_columns(mixed, qkv_width), grad_mid_low)
     grad_b_out = column_sum(grad_mid_low)
-    grad_mixed = over_cols(grad_mid_low, w_out).astype(low_type).reshape(head_shape)
-    scores_again = attention_scores(queries_split, keys_split, allowed)
-    soft_again = jnp.exp(scores_again - log_total)
-    grad_soft = jnp.einsum(
-        "rqhe,rkhe->rhqk", grad_mixed, values_split, preferred_element_type=jnp.float32
-    )
-    delta = jnp.sum(soft_again * grad_soft, axis=-1, keepdims=True)
-    grad_scores = (soft_again * (grad_soft - delta)).astype(low_type)
-    grad_queries = jnp.einsum(
-        "rhqk,rkhe->rqhe", grad_scores, keys_split, preferred_element_type=jnp.float32
-    )
-    grad_queries = (grad_queries * scaling).reshape(token_count, heads * HD).astype(low_type)
-    grad_keys = jnp.einsum(
-        "rhqk,rqhe->rkhe", grad_scores, queries_split, preferred_element_type=jnp.float32
-    )
-    grad_keys = (grad_keys * scaling).reshape(token_count, heads * HD).astype(low_type)
-    grad_values = jnp.einsum(
-        "rhqk,rqhe->rkhe",
-        soft_again.astype(low_type),
-        grad_mixed,
-        preferred_element_type=jnp.float32,
-    )
-    grad_values = grad_values.reshape(token_count, heads * HD).astype(low_type)
+    grad_mixed = over_cols(grad_mid_low, w_out).astype(low_type)
+    grad_queries, grad_keys, grad_values = attention_backward(
+        queries, key_rows, value_rows, grad_mixed, log_total, segments, valid_mask
+    )
     own_grad_queries = own_columns(grad_queries, qkv_width)
     own_grad_values = own_columns(grad_values, qkv_width)
     grad_w_query = over_rows(normed_low, own_grad_queries)

time: 583 us -> 566 us (0.971)
  Pallas kernels: 0 us -> 131 us
  local copies, waits for them, and re-layouts: 106 us -> 47.9 us
  matrix products: 181 us -> 131 us
  waiting for transfers between devices: 182 us -> 150 us
    pallas_call x0 -> x2, Pallas kernels: none -> 131 us  [the longest x1 66.5 us: attention_forward(): pl.pallas_call(_fwd_kernel, grid=(rows,), in_specs=[tile, tile, tile] + _...]
    dot_general x6 -> x0, matrix products: 41.3 us -> none  [the longest x1 11.1 us: on_device(): jnp.einsum('rhqk,rqhe->rkhe', soft_again.astype(low_type), grad_mixed, pr...]
    convert_element_type x8 -> x0, local copies, waits for them, and re-layouts: 31.4 us -> none  [the longest x1 4.66 us: on_device(): queries = (over_cols(normed_low, w_query_t) + b_query).astype(low_type)]
    reshape x4 -> x0, local copies, waits for them, and re-layouts: 24.8 us -> none  [the longest x1 6.44 us: on_device(): over_cols(grad_mid_low, w_out).astype(low_type).reshape(head_shape)]
    psum x1, waiting for transfers between devices: 20.9 us -> 0.01 us  [on_device(): lax.psum(jnp.concatenate([grad_w_down, grad_w_up], axis=0), 'dp')]
    convert_element_type x1 -> x0, other arithmetic: 9.72 us -> none  [on_device(): grad_scores = (soft_again * (grad_soft - delta)).astype(low_type)]
    all_gather x2, waiting for transfers between devices: 108 us -> 99.2 us  [gather_pieces(): got = lax.all_gather(sent, ('mp', 'dp'), axis=0) * one]
    dot_general x6, matrix products: 55.6 us -> 48 us  [product(): return jnp.dot(left, right, preferred_element_type=jnp.float32)]
  transfers between devices with their start and end apart: 4 -> 4, of which waited for: 4 -> 3; matrix products, arithmetic and copies ran while one was open for 33% -> 24% of each run, Pallas kernels for 0% -> 23%
where the time goes in v7:
time: 566 us; the launch traced here: 561 us
  waiting for transfers between devices  150 us (27%)
  matrix products  131 us (23%)
  Pallas kernels  131 us (23%)
  other arithmetic  85.4 us (15%)
  local copies, waits for them, and re-layouts  47.9 us (8%)
  between operations  16.1 us (3%)
    all_gather x2, waiting for transfers between devices, gather_pieces(): got = lax.all_gather(sent, ('mp', 'dp'), axis=0) * one  99.2 us
    pallas_call x1, Pallas kernels, attention_forward(): pl.pallas_call(_fwd_kernel, grid=(rows,), in_specs=[tile, tile, tile] + _...  66.5 us
    pallas_call x1, Pallas kernels, attention_backward(): pl.pallas_call(_bwd_kernel, grid=(rows,), in_specs=[tile, tile, tile, til...  64.2 us
    dot_general x6, matrix products, over_cols(): lax.dot_general(left, right, CONTRACT_COLS, preferred_element_type=jnp.fl...  57.7 us
    psum x1, waiting for transfers between devices, on_device(): lax.psum((grad_w_query + tie, grad_w_key, grad_w_value, grad_w_out, packe...  50.5 us
    dot_general x6, matrix products, product(): return jnp.dot(left, right, preferred_element_type=jnp.float32)  48 us
    dot_general x6, matrix products, over_rows(): lax.dot_general(left, right, CONTRACT_ROWS, preferred_element_type=jnp.fl...  25.2 us
    reduce_sum x2, other arithmetic, normalize(): centered = values - average  17.3 us
  transfers between devices with their start and end apart: 4, of which 3 were waited for; matrix products, arithmetic and copies ran while one was open for 24% of the time, Pallas kernels for 23%

profile of v7, /device:TPU:0, one launch (start us, length us, event | category | flops | bytes accessed | tf_op | source)
XLA Modules:
  0.0 561.3 jit_solution(17956772062106129653)
XLA Ops:
  22.3 6.0 %fusion.31 = (bf16[1920,768]{1,0:T(8,128)(2,1)}, f32[1920,768]{1,0:T(8,128)}) fusion(f32[1920]{0:T(1024)S(1)} %convert_bitcast_fusion.4, bf16[15,128,768]{2,1,0:T(8,128)(2,1)} %param.45), kind=kLoop, calls=%fused_computation.98 | loop fusion | flops 4423680 | bytes 11804160 | tf_op jit(solution)/shard_map/convert_element_type | solution.py:263
  35.0 5.7 %add_convert_fusion.6 = (bf16[15,128,768]{2,1,0:T(8,128)(2,1)}, f32[15,128,768]{2,1,0:T(8,128)}) fusion(bf16[15,128,768]{2,1,0:T(8,128)(2,1)} %param.25, f32[768]{0:T(1024)S(1)} %copy-done.29, f32[768]{0:T(1024)S(1)} %copy-done.25, f32[15,128]{1,0:T(8,128)S(1)} %fusion.20, f32[15,128]{1,0:T(8,128)S(1)} %get-tuple-element.102, ...), kind=kLoop, calls=%fused_computation.25 | loop fusion | flops 10321920 | bytes 11864064 | tf_op jit(solution)/shard_map/convert_element_type | solution.py:247
  40.8 49.4 %all-gather.3.cloned.1.call-done = f32[32,73,768]{2,1,0:T(8,128)} async-done(((f32[1,73,768]{2,1,0:T(8,128)}), f32[32,73,768]{2,1,0:T(8,128)}) %all-gather.3.cloned.1.call-update) | async-done | bytes 7176208 | tf_op jit(solution)/shard_map/all_gather | solution.py:161
  90.2 6.2 %bitcast_convert_fusion.2 = (bf16[4,8,73,768]{3,2,1,0:T(8,128)(2,1)}, f32[32,73,768]{2,1,0:T(8,128)S(1)}) fusion(f32[32,73,768]{2,1,0:T(8,128)} %all-gather.3.cloned.1.call-done, f32[]{:T(128)} %bitcast.9), kind=kLoop, calls=%fused_computation.96 | loop fusion | flops 3588096 | bytes 17940484 | tf_op jit(solution)/shard_map/convert.16
  98.9 7.4 %convolution_convert_fusion.1.k_ref = bf16[1920,768]{1,0:T(8,128)(2,1)} fusion(bf16[1920,768]{1,0:T(8,128)(2,1)} %bitcast.130, bf16[768,768]{1,0:T(8,128)(2,1)S(1)} %bitcast.135), kind=kOutput, calls=%fused_computation.31 | convolution fusion | flops 2266398720 | bytes 7077888 | tf_op jit(solution)/shard_map/dot_general | solution.py:39
  106.3 4.3 add_convert_fusion.4.v_ref
  110.6 4.2 add_convert_fusion.5.q_ref
  114.8 66.5 %attention_forward.1 = (bf16[1920,768]{1,0:T(8,128)(2,1)}, f32[15,128,12]{2,1,0:T(8,128)}) custom-call(bf16[1920,768]{1,0:T(8,128)(2,1)} %add_convert_fusion.5.q_ref, bf16[1920,768]{1,0:T(8,128)(2,1)} %convolution_convert_fusion.1.k_ref, bf16[1920,768]{1,0:T(8,128)(2,1)} %add_convert_fusion.4.v_ref, s32[15,128,1]{2,1,0:T(8,128)} %copy.51.segc_ref, ...), custom_call_target="tpu_custom_call" | custom-call | flops 754974720 | bytes 11796480 | tf_op jit(solution)/shard_map/attention_forward/pallas_call | solution.py:116
  181.3 49.8 %all-gather.5.cloned.1.call-done = f32[32,217,768]{2,1,0:T(8,128)} async-done(((f32[1,217,768]{2,1,0:T(8,128)}), f32[32,217,768]{2,1,0:T(8,128)}) %all-gather.5.cloned.1.call-update) | async-done | bytes 21331984 | tf_op jit(solution)/shard_map/all_gather | solution.py:161
  231.1 8.8 %broadcast_multiply_fusion = f32[32,217,768]{2,1,0:T(8,128)S(1)} fusion(f32[32,217,768]{2,1,0:T(8,128)} %all-gather.5.cloned.1.call-done, f32[]{:T(128)} %bitcast.9), kind=kLoop, calls=%fused_computation.4 | loop fusion | flops 5332992 | bytes 42663940 | tf_op jit(solution)/shard_map/mul | solution.py:161
  239.9 7.4 %convert.22 = bf16[4,8,217,768]{3,2,1,0:T(8,128)(2,1)} convert(f32[4,8,217,768]{3,2,1,0:T(8,128)S(1)} %bitcast.105) | non-fusion elementwise | flops 5332992 | bytes 31997952 | tf_op jit(solution)/shard_map/convert.13
  247.3 3.2 copy-done.2
  252.0 8.1 %fusion.36 = (bf16[4,8,96,768]{3,2,1,0:T(8,128)(2,1)}, bf16[4,8,96,768]{3,2,1,0:T(8,128)(2,1)}) fusion(bf16[4,8,217,768]{3,2,1,0:T(8,128)(2,1)} %convert.22), kind=kLoop, calls=%fused_computation.102 | loop fusion | bytes 18874368 | tf_op jit(solution)/shard_map/slice | solution.py:167
  261.1 4.7 fusion.40
  270.2 16.1 %multiply_convert_fusion = (bf16[1920,3072]{1,0:T(8,128)(2,1)}, f32[1920,3072]{1,0:T(8,128)}) fusion(f32[3072]{0:T(1024)S(1)} %bitcast.140, bf16[1920,768]{1,0:T(8,128)(2,1)S(1)} %add_convert_fusion.3, bf16[3072,768]{1,0:T(8,128)(2,1)S(1)} %bitcast.127), kind=kOutput, calls=%fused_computation.2 | convolution fusion | flops 9095086080 | bytes 43069440 | tf_op jit(solution)/shard_map/dot_general | solution.py:39
  286.3 21.6 %add_convert_fusion = bf16[1920,3072]{1,0:T(8,128)(2,1)} fusion(f32[1920,3072]{1,0:T(8,128)} %get-tuple-element.106, f32[3072]{0:T(1024)S(1)} %bitcast.141, bf16[1920,768]{1,0:T(8,128)(2,1)S(1)} %copy-done.12, bf16[3072,768]{1,0:T(8,128)(2,1)S(1)} %bitcast.126), kind=kOutput, calls=%fused_computation.1 | convolution fusion | flops 9142272000 | bytes 43069440 | tf_op jit(solution)/shard_map/dot_general | solution.py:39
  307.9 14.2 %multiply_reduce_fusion = (f32[768]{0:T(1024)S(1)}, f32[1920]{0:T(1024)S(1)}, f32[768]{0:T(1024)S(1)}, f32[1920,768]{1,0:T(8,128)}) fusion(f32[1920,768]{1,0:T(8,128)S(1)} %get-tuple-element.104, f32[1920]{0:T(1024)S(1)} %fusion.19, f32[1920]{0:T(1024)S(1)} %broadcast_multiply_fusion.2, f32[768]{0:T(1024)S(1)} %copy-done.28, ...), kind=kOutput, calls=%fused_computation.11 | convolution fusion | flops 9071489024 | bytes 28343808 | tf_op jit(solution)/shard_map/dot_general | solution.py:31
  322.1 4.6 fusion.3
  329.0 4.6 fusion.1
  336.1 7.5 %fusion.35 = (f32[1920]{0:T(1024)S(1)}, f32[1920,768]{1,0:T(8,128)S(1)}) fusion(f32[1920]{0:T(1024)S(1)} %multiply_multiply_fusion, f32[1920,768]{1,0:T(8,128)} %copy-done.3, f32[1920]{0:T(1024)S(1)} %broadcast_multiply_fusion.2, f32[1920]{0:T(1024)S(1)} %fusion.19, f32[1920,768]{1,0:T(8,128)} %get-tuple-element.107, f32[768]{0:T(1024)S(1)} %copy-done.28), kind=kLoop, calls=%fused_computation.101 | loop fusion | flops 10320000 | bytes 17728512 | tf_op jit(solution)/shard_map/transpose(jvp())/reduce_sum | solution.py:21
  346.1 4.1 convolution_convert_fusion.g_ref
  350.3 64.2 %attention_backward.1 = (bf16[1920,768]{1,0:T(8,128)(2,1)}, bf16[1920,768]{1,0:T(8,128)(2,1)}, bf16[1920,768]{1,0:T(8,128)(2,1)}) custom-call(bf16[1920,768]{1,0:T(8,128)(2,1)} %add_convert_fusion.5.q_ref, bf16[1920,768]{1,0:T(8,128)(2,1)} %convolution_convert_fusion.1.k_ref, bf16[1920,768]{1,0:T(8,128)(2,1)} %add_convert_fusion.4.v_ref, ...), custom_call_target="tpu_custom_call" | custom-call | flops 1887436800 | bytes 20643840 | tf_op jit(solution)/shard_map/attention_backward/pallas_call | solution.py:139
  414.5 4.6 fusion.42
  421.9 5.8 %multiply_reduce_fusion.1 = (f32[768]{0:T(1024)S(1)}, f32[1920]{0:T(1024)S(1)}, f32[768]{0:T(1024)S(1)}, f32[1920,768]{1,0:T(8,128)}) fusion(f32[15,128,768]{2,1,0:T(8,128)S(1)} %bitcast.110, f32[1920]{0:T(1024)S(1)} %copy-done.23, f32[1920]{0:T(1024)S(1)} %copy-done.24, f32[768]{0:T(1024)S(1)} %copy-done.26, bf16[1920,768]{1,0:T(8,128)(2,1)S(1)} %copy-done.7, ...), kind=kOutput, calls=%fused_computation.14 | convolution fusion | flops 2279666432 | bytes 27753984 | tf_op jit(solution)/shard_map/dot_general | solution.py:31
  427.7 9.8 %fusion.34 = (f32[1920]{0:T(1024)S(1)}, f32[1920,768]{1,0:T(8,128)}, bf16[1920,768]{1,0:T(8,128)(2,1)}) fusion(f32[1920]{0:T(1024)S(1)} %fusion.18, f32[1920]{0:T(1024)S(1)} %copy-done.23, f32[15,128,768]{2,1,0:T(8,128)S(1)} %bitcast.110, f32[1920]{0:T(1024)S(1)} %copy-done.24, f32[1920,768]{1,0:T(8,128)} %get-tuple-element.108, f32[768]{0:T(1024)S(1)} %copy-done.26, ...), kind=kLoop, calls=%fused_computation.100 | loop fusion | flops 16218240 | bytes 20680704 | tf_op jit(solution)/shard_map/transpose(jvp())/reduce_sum | solution.py:21
  440.0 6.1 %fusion.33 = (bf16[1920,768]{1,0:T(8,128)(2,1)}, f32[1920,768]{1,0:T(8,128)}, f32[768]{0:T(1024)S(1)}) fusion(f32[1920,768]{1,0:T(8,128)} %get-tuple-element.76, f32[1920]{0:T(1024)S(1)} %negate_multiply_fusion, f32[1920,768]{1,0:T(8,128)S(1)} %bitcast.114, f32[1920,768]{1,0:T(8,128)S(1)} %bitcast.116, f32[1920]{0:T(1024)S(1)} %negate_multiply_fusion.1), kind=kLoop, calls=%fused_computation.99 | loop fusion | flops 8846592 | bytes 26560512 | tf_op jit(solution)/shard_map/convert_element_type | solution.py:299
  451.2 4.8 fusion.9
  455.9 3.5 fusion.7
  459.5 3.3 fusion.5
  464.6 4.4 convolution_add_fusion
  469.1 16.2 %add_convert_fusion.2 = bf16[1920,768]{1,0:T(8,128)(2,1)} fusion(f32[1920,768]{1,0:T(8,128)} %copy-done.3, bf16[1920,3072]{1,0:T(8,128)(2,1)} %get-tuple-element.105, bf16[3072,768]{1,0:T(8,128)(2,1)} %bitcast.123, f32[768]{0:T(1024)S(1)} %copy-done.34), kind=kOutput, calls=%fused_computation.20 | convolution fusion | flops 9064120320 | bytes 25365504 | tf_op jit(solution)/shard_map/dot_general | solution.py:31
  487.8 50.5 %all-reduce.9.cloned.1.call-done = (f32[1030,192]{0,1:T(8,128)}, f32[768,192]{0,1:T(8,128)}, f32[768,192]{0,1:T(8,128)}, f32[768,192]{0,1:T(8,128)}, f32[192,768]{1,0:T(8,128)}) async-done(((f32[1030,192]{0,1:T(8,128)}, f32[768,192]{0,1:T(8,128)}, f32[768,192]{0,1:T(8,128)}, f32[768,192]{0,1:T(8,128)}, f32[192,768]{1,0:T(8,128)}), (f32[1030,192]{0,1:T(8,128)}, f32[768,192]{0,1:T(8,128)}, ...) | async-done | bytes 3150352 | tf_op jit(solution)/shard_map/psum | solution.py:334
  (190 shorter events, 67.7 us)
Async XLA Ops:
  7.2 10.6 %copy-start = (bf16[1000,768]{1,0:T(8,128)(2,1)S(1)}, bf16[1000,768]{1,0:T(8,128)(2,1)}, u32[]{:S(2)}) copy-start(bf16[1000,768]{1,0:T(8,128)(2,1)} %param.29) | copy-start | bytes 4608004
  7.2 14.5 %copy-start.27 = (s32[15,128]{1,0:T(8,128)S(1)}, s32[15,128]{1,0:T(8,128)}, u32[]{:S(2)}) copy-start(s32[15,128]{1,0:T(8,128)} %param.28) | copy-start | bytes 23044
  7.2 83.0 %all-gather.3.cloned.1.call-start = ((), (), s32[]{:S(2)}) async-start(), calls=%async_computation | async-start | bytes 8110080 | tf_op jit(solution)/shard_map/all_gather | solution.py:161
  12.3 218.8 %all-gather.5.cloned.1.call-start = ((), (), s32[]{:S(2)}) async-start(), calls=%async_computation.1 | async-start | bytes 22708224 | tf_op jit(solution)/shard_map/all_gather | solution.py:161
  17.0 445.7 %all-reduce.7.cloned.1.call-start = ((), (), s32[]{:S(2)}) async-start(), calls=%async_computation.2 | async-start | bytes 9437184 | tf_op jit(solution)/shard_map/psum | solution.py:273
  98.9 7.4 %copy-start.16 = (bf16[4,8,24,768]{3,2,1,0:T(8,128)(2,1)}, bf16[4,8,24,768]{3,2,1,0:T(8,128)(2,1)S(1)}, u32[]{:S(2)}) copy-start(bf16[4,8,24,768]{3,2,1,0:T(8,128)(2,1)S(1)} %get-tuple-element.88) | copy-start | bytes 3538948
  98.9 7.4 %copy-start.8 = (bf16[4,8,24,768]{3,2,1,0:T(8,128)(2,1)}, bf16[4,8,24,768]{3,2,1,0:T(8,128)(2,1)S(1)}, u32[]{:S(2)}) copy-start(bf16[4,8,24,768]{3,2,1,0:T(8,128)(2,1)S(1)} %get-tuple-element.87) | copy-start | bytes 3538948
  98.9 11.7 %copy-start.14 = (bf16[4,8,24,768]{3,2,1,0:T(8,128)(2,1)}, bf16[4,8,24,768]{3,2,1,0:T(8,128)(2,1)S(1)}, u32[]{:S(2)}) copy-start(bf16[4,8,24,768]{3,2,1,0:T(8,128)(2,1)S(1)} %get-tuple-element.89) | copy-start | bytes 3538948
  98.9 7.4 %copy-start.13 = (bf16[15,128,768]{2,1,0:T(8,128)(2,1)S(1)}, bf16[15,128,768]{2,1,0:T(8,128)(2,1)}, u32[]{:S(2)}) copy-start(bf16[15,128,768]{2,1,0:T(8,128)(2,1)} %get-tuple-element.90) | copy-start | bytes 8847364
  239.9 10.6 %copy-start.2 = (f32[32,217,768]{2,1,0:T(8,128)}, f32[32,217,768]{2,1,0:T(8,128)S(1)}, u32[]{:S(2)}) copy-start(f32[32,217,768]{2,1,0:T(8,128)S(1)} %broadcast_multiply_fusion) | copy-start | bytes 63995908
  250.5 10.5 %slice-start = ((s8[5898240]{0:T(1024)(128)(4,1)}), s8[4194304]{0:T(1024)(128)(4,1)S(1)}, s32[]{:S(2)}) async-start(s8[5898240]{0:T(1024)(128)(4,1)} %bitcast.107), calls=%async_computation.4 | async-start | bytes 8388608
  252.0 9.0 %slice-start.1 = ((s8[5898240]{0:T(1024)(128)(4,1)}), s8[1703936]{0:T(1024)(128)(4,1)S(1)}, s32[]{:S(2)}) async-start(s8[5898240]{0:T(1024)(128)(4,1)} %bitcast.107), calls=%async_computation.5 | async-start | bytes 3407872
  252.0 9.0 %copy-start.33 = (f32[768]{0:T(1024)S(1)}, f32[768]{0:T(1024)}, u32[]{:S(2)}) copy-start(f32[768]{0:T(1024)} %param.38) | copy-start | bytes 9220
  265.7 42.2 %copy-start.3 = (f32[1920,768]{1,0:T(8,128)}, f32[1920,768]{1,0:T(8,128)S(1)}, u32[]{:S(2)}) copy-start(f32[1920,768]{1,0:T(8,128)S(1)} %get-tuple-element.104) | copy-start | bytes 17694724
  266.6 19.7 %slice-start.12 = ((s8[4718592]{0:T(1024)(128)(4,1)}), s8[4194304]{0:T(1024)(128)(4,1)S(1)}, s32[]{:S(2)}) async-start(s8[4718592]{0:T(1024)(128)(4,1)} %bitcast.124), calls=%async_computation.16 | async-start | bytes 8388608
  270.2 16.1 %slice-start.13 = ((s8[4718592]{0:T(1024)(128)(4,1)}), s8[524288]{0:T(1024)(128)(4,1)S(1)}, s32[]{:S(2)}) async-start(s8[4718592]{0:T(1024)(128)(4,1)} %bitcast.124), calls=%async_computation.17 | async-start | bytes 1048576
  270.2 16.1 %copy-start.12 = (bf16[1920,768]{1,0:T(8,128)(2,1)S(1)}, bf16[1920,768]{1,0:T(8,128)(2,1)}, u32[]{:S(2)}) copy-start(bf16[1920,768]{1,0:T(8,128)(2,1)} %get-tuple-element.51) | copy-start | bytes 8847364
  333.6 10.1 %slice-start.4 = ((s8[5898240]{0:T(1024)(128)(4,1)}), s8[1703936]{0:T(1024)(128)(4,1)S(1)}, s32[]{:S(2)}) async-start(s8[5898240]{0:T(1024)(128)(4,1)} %bitcast.111), calls=%async_computation.8 | async-start | bytes 3407872
  336.0 202.2 %all-reduce.9.cloned.1.call-start = ((), (), s32[]{:S(2)}) async-start(), calls=%async_computation.3 | async-start | bytes 6488064 | tf_op jit(solution)/shard_map/psum | solution.py:334
  336.1 7.6 %slice-start.5 = ((s8[5898240]{0:T(1024)(128)(4,1)}), s8[4194304]{0:T(1024)(128)(4,1)S(1)}, s32[]{:S(2)}) async-start(s8[5898240]{0:T(1024)(128)(4,1)} %bitcast.111), calls=%async_computation.9 | async-start | bytes 8388608
  350.3 64.2 %copy-start.17 = (bf16[4,8,24,768]{3,2,1,0:T(8,128)(2,1)S(1)}, bf16[4,8,24,768]{3,2,1,0:T(8,128)(2,1)}, u32[]{:S(2)}) copy-start(bf16[4,8,24,768]{3,2,1,0:T(8,128)(2,1)} %copy-done.16) | copy-start | bytes 3538948
  427.7 12.3 %slice-start.6 = ((s8[5898240]{0:T(1024)(128)(4,1)}), s8[4194304]{0:T(1024)(128)(4,1)S(1)}, s32[]{:S(2)}) async-start(s8[5898240]{0:T(1024)(128)(4,1)} %bitcast.113), calls=%async_computation.10 | async-start | bytes 8388608
  427.7 12.3 %slice-start.8 = ((s8[5898240]{0:T(1024)(128)(4,1)}), s8[4194304]{0:T(1024)(128)(4,1)S(1)}, s32[]{:S(2)}) async-start(s8[5898240]{0:T(1024)(128)(4,1)} %bitcast.115), calls=%async_computation.12 | async-start | bytes 8388608
  427.7 12.3 %slice-start.7 = ((s8[5898240]{0:T(1024)(128)(4,1)}), s8[1703936]{0:T(1024)(128)(4,1)S(1)}, s32[]{:S(2)}) async-start(s8[5898240]{0:T(1024)(128)(4,1)} %bitcast.113), calls=%async_computation.11 | async-start | bytes 3407872
  427.7 12.3 %slice-start.9 = ((s8[5898240]{0:T(1024)(128)(4,1)}), s8[1703936]{0:T(1024)(128)(4,1)S(1)}, s32[]{:S(2)}) async-start(s8[5898240]{0:T(1024)(128)(4,1)} %bitcast.115), calls=%async_computation.13 | async-start | bytes 3407872
  450.1 9.4 %copy-start.6 = (bf16[1920,768]{1,0:T(8,128)(2,1)S(1)}, bf16[1920,768]{1,0:T(8,128)(2,1)}, u32[]{:S(2)}) copy-start(bf16[1920,768]{1,0:T(8,128)(2,1)} %copy-done.5) | copy-start | bytes 8847364
  459.5 9.5 %copy-start.34 = (f32[768]{0:T(1024)S(1)}, f32[768]{0:T(1024)}, u32[]{:S(2)}) copy-start(f32[768]{0:T(1024)} %param.44) | copy-start | bytes 9220
  469.0 16.3 %slice-start.10 = ((s8[4718592]{0:T(1024)(128)(4,1)}), s8[524288]{0:T(1024)(128)(4,1)S(1)}, s32[]{:S(2)}) async-start(s8[4718592]{0:T(1024)(128)(4,1)} %bitcast.121), calls=%async_computation.14 | async-start | bytes 1048576
  469.0 16.3 %slice-start.11 = ((s8[4718592]{0:T(1024)(128)(4,1)}), s8[4194304]{0:T(1024)(128)(4,1)S(1)}, s32[]{:S(2)}) async-start(s8[4718592]{0:T(1024)(128)(4,1)} %bitcast.121), calls=%async_computation.15 | async-start | bytes 8388608
  485.3 69.3 %copy-start.1 = (bf16[1000,768]{1,0:T(8,128)(2,1)S(1)}, bf16[1000,768]{1,0:T(8,128)(2,1)}, u32[]{:S(2)}) copy-start(bf16[1000,768]{1,0:T(8,128)(2,1)} %param.29) | copy-start | bytes 4608004
  538.3 14.7 %copy-start.19 = (f32[768,192]{0,1:T(8,128)S(1)}, f32[768,192]{0,1:T(8,128)}, u32[]{:S(2)}) copy-start(f32[768,192]{0,1:T(8,128)} %get-tuple-element.118) | copy-start | bytes 1769476
  538.3 15.5 %copy-start.18 = (f32[192,768]{1,0:T(8,128)S(1)}, f32[192,768]{1,0:T(8,128)}, u32[]{:S(2)}) copy-start(f32[192,768]{1,0:T(8,128)} %get-tuple-element.120) | copy-start | bytes 1769476
  (21 other events, 85.8 us)
Sparse Core Ops, SparseCore 0:
  12.5 77.6 all-gather.2
  93.6 137.4 all-gather.4
  336.2 84.9 all-reduce.6
  469.2 69.0 all-reduce.8

commit v8 on v6

--- a/solution.py
+++ b/solution.py
@@ -113,12 +113,14 @@
     ff_width = w_up_shard.shape[1]
     one = 1.0 + 0.0 * ln1_gain[0]
     n_dp = lax.axis_size("dp")
+    n_mp = lax.axis_size("mp")
     low_type = jnp.bfloat16
-    q_part, k_part, v_part, qv_bias = gather_pieces(
+    q_part, k_part, v_part, o_part, qv_bias = gather_pieces(
         (
             w_query_shard.T,
             w_key_shard.T,
             w_value_shard.T,
+            w_out_shard,
             bias_block((b_query_shard, b_value_shard), model_width, n_dp),
         ),
         one,
@@ -128,9 +130,8 @@
     w_value_t = whole_rows(v_part, low_type)
     b_query = qv_bias[:, 0, 0, :qkv_width].reshape(-1)
     b_value = qv_bias[:, 0, 0, qkv_width : 2 * qkv_width].reshape(-1)
-    o_part, up_part, down_part, up_bias = gather_pieces(
+    up_part, down_part, up_bias = gather_pieces(
         (
-            w_out_shard,
             w_up_shard.T,
             w_down_shard,
             bias_block((b_up_shard,), model_width, n_dp),
@@ -138,9 +139,10 @@
         one,
     )
     w_out = whole_rows(o_part, low_type)
-    w_up_t = whole_rows(up_part, low_type)
-    w_down = whole_rows(down_part, low_type)
-    b_up = up_bias[:, 0, 0, :].reshape(-1)
+    others = (lax.axis_index("mp") + jnp.arange(1, n_mp, dtype=jnp.int32)) % n_mp
+    w_up_others = whole_rows(jnp.take(up_part, others, axis=0), low_type)
+    w_down_others = whole_rows(jnp.take(down_part, others, axis=0), low_type)
+    b_up_others = jnp.take(up_bias[:, 0, 0, :], others, axis=0).reshape(-1)
     heads = w_query_t.shape[0] // HD
     scaling = 1.0 / math.sqrt(HD)
     head_shape = (row_count, seq_len, heads, HD)
@@ -176,26 +178,31 @@
     middle = start + attended
     normed2, second_pull = jax.vjp(normalize, middle, ln2_gain, ln2_shift)
     normed2_low = normed2.astype(low_type)
-    upper = over_cols(normed2_low, w_up_t) + b_up
-    activated, gelu_pull = jax.vjp(exact_gelu, upper)
-    hidden = activated.astype(low_type)
-    lowered = product(hidden, w_down)
-    output = (middle + lowered + b_down).astype(low_type).reshape(row_count, seq_len, model_width)
+    upper_own = product(normed2_low, w_up_shard) + b_up_shard
+    activated_own, gelu_pull_own = jax.vjp(exact_gelu, upper_own)
+    hidden_own = activated_own.astype(low_type)
+    lowered_own = product(hidden_own, w_down_shard)
     grad_out = cotangent.reshape(token_count, model_width).astype(jnp.float32)
     grad_out = grad_out * valid_mask.reshape(token_count, 1).astype(jnp.float32)
     grad_out_low = grad_out.astype(low_type)
     grad_out, grad_out_low = lax.optimization_barrier((grad_out, grad_out_low))
-    grad_w_down = over_rows(own_columns(hidden, ff_width), grad_out_low)
+    grad_w_down = over_rows(hidden_own, grad_out_low)
     grad_b_down = jnp.sum(grad_out, axis=0)
-    grad_hidden = over_cols(grad_out_low, w_down)
-    (grad_upper,) = gelu_pull(grad_hidden)
-    grad_upper_low = grad_upper.astype(low_type)
-    own_grad_upper = own_columns(grad_upper_low, ff_width)
-    grad_w_up = over_rows(normed2_low, own_grad_upper)
-    grad_b_up = column_sum(own_grad_upper)
+    (grad_upper_own,) = gelu_pull_own(over_cols(grad_out_low, w_down_shard))
+    grad_upper_own = grad_upper_own.astype(low_type)
+    grad_w_up = over_rows(normed2_low, grad_upper_own)
+    grad_b_up = column_sum(grad_upper_own)
     ffn_grads = lax.psum(jnp.concatenate([grad_w_down, grad_w_up], axis=0), "dp")
     grad_w_down, grad_w_up = ffn_grads[:ff_width], ffn_grads[ff_width:]
-    grad_normed2 = product(grad_upper_low, w_up_t)
+    grad_normed2_own = over_cols(grad_upper_own, w_up_shard)
+    upper = over_cols(normed2_low, w_up_others) + b_up_others
+    activated, gelu_pull = jax.vjp(exact_gelu, upper)
+    hidden = activated.astype(low_type)
+    lowered = lowered_own + product(hidden, w_down_others)
+    output = (middle + lowered + b_down).astype(low_type).reshape(row_count, seq_len, model_width)
+    (grad_upper,) = gelu_pull(over_cols(grad_out_low, w_down_others))
+    grad_upper_low = grad_upper.astype(low_type)
+    grad_normed2 = grad_normed2_own + product(grad_upper_low, w_up_others)
     grad_mid_norm, grad_ln2_gain, grad_ln2_shift = second_pull(grad_normed2)
     grad_middle = grad_out + grad_mid_norm
     grad_mid_low = grad_middle.astype(low_type)

time: 583 us -> 732 us (1.26)
  waiting for transfers between devices: 182 us -> 321 us
  local copies, waits for them, and re-layouts: 106 us -> 121 us
  matrix products: 181 us -> 171 us
    all_gather x2, waiting for transfers between devices: 108 us -> 196 us  [gather_pieces(): got = lax.all_gather(sent, ('mp', 'dp'), axis=0) * one]
    psum x1, waiting for transfers between devices: 20.9 us -> 73.8 us  [on_device(): lax.psum(jnp.concatenate([grad_w_down, grad_w_up], axis=0), 'dp')]
    dot_general x6 -> x7, matrix products: 60.1 us -> 46.1 us  [over_cols(): lax.dot_general(left, right, CONTRACT_COLS, preferred_element_type=jnp.fl...]
    dot_general x6 -> x8, matrix products: 55.6 us -> 68.8 us  [product(): return jnp.dot(left, right, preferred_element_type=jnp.float32)]
    reshape x0 -> x1, other arithmetic: none -> 12.4 us  [gather_pieces(): got = got.reshape(n_mp, n_dp, *sent.shape)]
    gather x0 -> x3, local copies, waits for them, and re-layouts: none -> 10.7 us  [the longest x1 5.09 us: on_device(): w_down_others = whole_rows(jnp.take(down_part, others, axis=0), low_type)]
    mul x1 -> x0, other arithmetic: 8.94 us -> none  [gather_pieces(): got = lax.all_gather(sent, ('mp', 'dp'), axis=0) * one]
    dot_general x6, matrix products: 23.6 us -> 15.5 us  [over_rows(): lax.dot_general(left, right, CONTRACT_ROWS, preferred_element_type=jnp.fl...]
  transfers between devices with their start and end apart: 4 -> 4, of which waited for: 4 -> 4; matrix products, arithmetic and copies ran while one was open for 33% -> 7% of each run, Pallas kernels for 0% -> 0%
where the time goes in v8:
time: 732 us; the launch traced here: 727 us
  waiting for transfers between devices  321 us (44%)
  matrix products  171 us (23%)
  local copies, waits for them, and re-layouts  121 us (17%)
  other arithmetic  96.3 us (13%)
  between operations  16.3 us (2%)
    all_gather x2, waiting for transfers between devices, gather_pieces(): got = lax.all_gather(sent, ('mp', 'dp'), axis=0) * one  196 us
    psum x1, waiting for transfers between devices, on_device(): lax.psum(jnp.concatenate([grad_w_down, grad_w_up], axis=0), 'dp')  73.8 us
    dot_general x8, matrix products, product(): return jnp.dot(left, right, preferred_element_type=jnp.float32)  68.8 us
    psum x1, waiting for transfers between devices, on_device(): lax.psum((grad_w_query + tie, grad_w_key, grad_w_value, grad_w_out, packe...  51.2 us
    dot_general x7, matrix products, over_cols(): lax.dot_general(left, right, CONTRACT_COLS, preferred_element_type=jnp.fl...  46.1 us
    unnamed x138, local copies, waits for them, and re-layouts  27.4 us
    dot_general x6, matrix products, over_rows(): lax.dot_general(left, right, CONTRACT_ROWS, preferred_element_type=jnp.fl...  15.5 us
  transfers between devices with their start and end apart: 4, of which 4 were waited for; matrix products, arithmetic and copies ran while one was open for 7% of the time, Pallas kernels for 0%

profile of v8, /device:TPU:0, one launch (start us, length us, event | category | flops | bytes accessed | tf_op | source)
XLA Modules:
  0.0 726.7 jit_solution(14385103455490748405)
XLA Ops:
  16.0 6.0 fusion.69
  30.1 71.7 %all-gather.3.cloned.1.call-done = f32[32,97,768]{2,1,0:T(8,128)} async-done(((f32[1,97,768]{2,1,0:T(8,128)}), f32[32,97,768]{2,1,0:T(8,128)}) %all-gather.3.cloned.1.call-update) | async-done | bytes 9535504 | tf_op jit(solution)/shard_map/all_gather | solution.py:61
  101.8 10.6 %bitcast_convert_fusion.1 = (bf16[4,8,97,768]{3,2,1,0:T(8,128)(2,1)}, f32[32,97,768]{2,1,0:T(8,128)}) fusion(f32[32,97,768]{2,1,0:T(8,128)} %all-gather.3.cloned.1.call-done, f32[]{:T(128)} %bitcast.10), kind=kLoop, calls=%fused_computation.157 | loop fusion | flops 4767744 | bytes 23838724 | tf_op jit(solution)/shard_map/convert.14
  117.7 6.3 add_convert_fusion.6
  128.6 6.0 reshape.558
  134.6 5.9 convolution_convert_fusion.1
  145.3 5.9 add_convert_fusion.7
  155.8 6.0 reshape.556
  161.8 6.2 reshape.560
  168.0 6.6 fusion.13
  190.1 6.6 fusion.78
  203.0 5.9 convert_reduce_fusion
  221.0 7.5 %fusion.81 = f32[1920,768]{1,0:T(8,128)} fusion(bf16[1920,768]{1,0:T(8,128)(2,1)} %copy-done.54, bf16[768,768]{1,0:T(8,128)(2,1)} %param.43), kind=kOutput, calls=%fused_computation.178 | convolution fusion | flops 2264924160 | bytes 10027008 | tf_op jit(solution)/shard_map/dot_general | solution.py:37
  228.5 73.8 %all-reduce.7.cloned.1.call-done = f32[1536,768]{1,0:T(8,128)} async-done(((f32[1536,768]{1,0:T(8,128)}), f32[1536,768]{1,0:T(8,128)}) %all-reduce.7.cloned.1.call-update) | async-done | bytes 4718608 | tf_op jit(solution)/shard_map/psum | solution.py:195
  309.0 124.5 %all-gather.5.cloned.1.call-done = f32[32,193,768]{2,1,0:T(8,128)} async-done(((f32[1,193,768]{2,1,0:T(8,128)}), f32[32,193,768]{2,1,0:T(8,128)}) %all-gather.5.cloned.1.call-update) | async-done | bytes 18972688 | tf_op jit(solution)/shard_map/all_gather | solution.py:61
  433.5 12.4 %fusion = f32[4,8,193,768]{3,1,0,2:T(8,128)S(1)} fusion(f32[32,193,768]{2,1,0:T(8,128)} %all-gather.5.cloned.1.call-done, f32[]{:T(128)} %bitcast.10), kind=kLoop, calls=%fused_computation.5 | loop fusion | flops 4743168 | bytes 37945348 | tf_op jit(solution)/shard_map/reshape | solution.py:63
  454.7 7.1 copy.124
  471.9 6.8 select_convert_fusion.1
  478.7 10.5 %fusion.80 = f32[1920,2304]{1,0:T(8,128)} fusion(bf16[1920,768]{1,0:T(8,128)(2,1)S(1)} %copy-done.23, bf16[2304,768]{1,0:T(8,128)(2,1)S(1)} %bitcast.191), kind=kOutput, calls=%fused_computation.177 | convolution fusion | flops 6794772480 | bytes 24182784 | tf_op jit(solution)/shard_map/dot_general | solution.py:37
  489.1 25.7 %multiply_reduce_fusion.1 = (f32[768]{0:T(1024)S(1)}, f32[1920]{0:T(1024)S(1)}, f32[768]{0:T(1024)S(1)}, f32[1920,768]{1,0:T(8,128)}) fusion(f32[1920,768]{1,0:T(8,128)} %copy-done.3, f32[1920]{0:T(1024)S(1)} %fusion.48, f32[1920]{0:T(1024)S(1)} %broadcast_multiply_fusion.2, f32[768]{0:T(1024)S(1)} %copy-done.43, f32[1920,768]{1,0:T(8,128)} %fusion.81, ...), kind=kOutput, calls=%fused_computation.31 | convolution fusion | flops 13664743424 | bytes 45457920 | tf_op jit(solution)/shard_map/dot_general | solution.py:29
  514.9 6.1 fusion.73
  521.0 5.5 convert_reduce_fusion.1
  537.0 6.4 reshape.567
  543.4 11.1 %convert_bitcast_fusion = bf16[15,128,12,64]{1,3,2,0:T(8,128)(2,1)} fusion(f32[15,12,128]{2,1,0:T(8,128)S(1)} %log_add_fusion, f32[15,12,128,128]{2,3,1,0:T(8,128)} %copy-done.2, pred[15,128,128]{1,2,0:T(8,128)(4,1)S(1)} %copy-done.20, bf16[15,128,12,64]{1,0,3,2:T(8,128)(2,1)} %reshape.567), kind=kOutput, calls=%fused_computation.68 | convolution fusion | flops 390758400 | bytes 18032640 | tf_op jit(solution)/shard_map/rhqk,rqhe->rkhe/dot_general | solution.py:227
  554.5 10.0 %multiply_reduce_fusion = (f32[15,12,128]{2,1,0:T(8,128)S(1)}, f32[15,12,128,128]{2,3,1,0:T(8,128)}) fusion(f32[15,12,128]{2,1,0:T(8,128)S(1)} %log_add_fusion, f32[15,12,128,128]{2,3,1,0:T(8,128)} %copy-done.2, pred[15,128,128]{1,2,0:T(8,128)(4,1)S(1)} %copy-done.20, bf16[15,128,12,64]{1,0,3,2:T(8,128)(2,1)S(1)} %copy-done.9, ...), kind=kOutput, calls=%fused_computation.10 | convolution fusion | flops 392209920 | bytes 29921280 | tf_op jit(solution)/shard_map/rqhe,rkhe->rhqk/dot_general | solution.py:214
  564.5 9.8 %multiply_convert_fusion.1 = bf16[15,12,128,128]{2,3,1,0:T(8,128)(2,1)S(1)} fusion(f32[15,12,128,128]{2,3,1,0:T(8,128)} %get-tuple-element.106, f32[15,12,128]{2,1,0:T(8,128)S(1)} %get-tuple-element.105, f32[15,12,128]{2,1,0:T(8,128)S(1)} %log_add_fusion, f32[15,12,128,128]{2,3,1,0:T(8,128)} %copy-done.2, pred[15,128,128]{1,2,0:T(8,128)(4,1)S(1)} %copy-done.20), kind=kLoop, calls=%fused_computation.9 | loop fusion | flops 17694720 | bytes 29921280 | tf_op jit(solution)/shard_map/convert_element_type | solution.py:218
  574.3 5.5 fusion.17
  598.7 5.1 fusion.83
  603.8 8.2 %multiply_reduce_fusion.2 = (f32[768]{0:T(1024)S(1)}, f32[1920]{0:T(1024)S(1)}, f32[768]{0:T(1024)S(1)}, f32[1920,768]{1,0:T(8,128)}) fusion(f32[15,128,768]{2,1,0:T(8,128)S(1)} %bitcast.166, f32[1920]{0:T(1024)S(1)} %copy-done.34, f32[1920]{0:T(1024)S(1)} %copy-done.35, f32[768]{0:T(1024)S(1)} %copy-done.37, bf16[1920,768]{0,1:T(8,128)(2,1)S(1)} %bitcast.173, ...), kind=kOutput, calls=%fused_computation.34 | convolution fusion | flops 2279666432 | bytes 27753984 | tf_op jit(solution)/shard_map/dot_general | solution.py:29
  612.1 5.5 fusion.72
  634.3 13.3 %fusion.3 = f32[1920,768]{1,0:T(8,128)S(1)} fusion(bf16[2304,768]{1,0:T(8,128)(2,1)} %bitcast.190, f32[1920,2304]{1,0:T(8,128)} %fusion.80, f32[2304]{0:T(1024)S(1)} %select_n.90), kind=kOutput, calls=%fused_computation.17 | convolution fusion | flops 6821314560 | bytes 27141120 | tf_op jit(solution)/shard_map/dot_general | solution.py:29
  652.5 51.2 %all-reduce.9.cloned.1.call-done = (f32[1030,192]{0,1:T(8,128)}, f32[768,192]{0,1:T(8,128)}, f32[768,192]{0,1:T(8,128)}, f32[768,192]{0,1:T(8,128)}, f32[192,768]{1,0:T(8,128)}) async-done(((f32[1030,192]{0,1:T(8,128)}, f32[768,192]{0,1:T(8,128)}, f32[768,192]{0,1:T(8,128)}, f32[768,192]{0,1:T(8,128)}, f32[192,768]{1,0:T(8,128)}), (f32[1030,192]{0,1:T(8,128)}, f32[768,192]{0,1:T(8,128)}, ...) | async-done | bytes 3150352 | tf_op jit(solution)/shard_map/psum | solution.py:283
  (253 shorter events, 160.6 us)
Async XLA Ops:
  7.2 7.5 %copy-start = (bf16[1000,768]{1,0:T(8,128)(2,1)S(1)}, bf16[1000,768]{1,0:T(8,128)(2,1)}, u32[]{:S(2)}) copy-start(bf16[1000,768]{1,0:T(8,128)(2,1)} %param.31) | copy-start | bytes 4608004
  7.2 94.6 %all-gather.3.cloned.1.call-start = ((), (), s32[]{:S(2)}) async-start(), calls=%async_computation | async-start | bytes 10543104 | tf_op jit(solution)/shard_map/all_gather | solution.py:61
  14.0 288.4 %all-reduce.7.cloned.1.call-start = ((), (), s32[]{:S(2)}) async-start(), calls=%async_computation.2 | async-start | bytes 9437184 | tf_op jit(solution)/shard_map/psum | solution.py:195
  16.0 6.0 copy-start.5
  24.5 195.9 %copy-start.32 = (f32[15,128]{1,0:T(8,128)}, f32[15,128]{1,0:T(8,128)S(1)}, u32[]{:S(2)}) copy-start(f32[15,128]{1,0:T(8,128)S(1)} %multiply_reduce_fusion.6) | copy-start | bytes 23044
  25.9 152.4 %copy-start.19 = (pred[15,128,128]{1,2,0:T(8,128)(4,1)}, pred[15,128,128]{1,2,0:T(8,128)(4,1)S(1)}, u32[]{:S(2)}) copy-start(pred[15,128,128]{1,2,0:T(8,128)(4,1)S(1)} %or_and_fusion) | copy-start | bytes 737284
  116.6 18.1 %copy-start.26 = (bf16[4,8,24,768]{3,2,1,0:T(8,128)(2,1)}, bf16[4,8,24,768]{3,2,1,0:T(8,128)(2,1)S(1)}, u32[]{:S(2)}) copy-start(bf16[4,8,24,768]{3,2,1,0:T(8,128)(2,1)S(1)} %get-tuple-element.80) | copy-start | bytes 3538948
  116.6 28.7 %copy-start.15 = (bf16[4,8,24,768]{3,2,1,0:T(8,128)(2,1)}, bf16[4,8,24,768]{3,2,1,0:T(8,128)(2,1)S(1)}, u32[]{:S(2)}) copy-start(bf16[4,8,24,768]{3,2,1,0:T(8,128)(2,1)S(1)} %get-tuple-element.82) | copy-start | bytes 3538948
  190.1 6.7 copy-start.17
  199.8 9.1 %copy-start.22 = (bf16[1920,768]{1,0:T(8,128)(2,1)}, bf16[1920,768]{1,0:T(8,128)(2,1)S(1)}, u32[]{:S(2)}) copy-start(bf16[1920,768]{1,0:T(8,128)(2,1)S(1)} %add_convert_fusion.5) | copy-start | bytes 8847364
  217.0 216.5 %all-gather.5.cloned.1.call-start = ((), (), s32[]{:S(2)}) async-start(), calls=%async_computation.1 | async-start | bytes 20275200 | tf_op jit(solution)/shard_map/all_gather | solution.py:61
  220.2 483.4 %all-reduce.9.cloned.1.call-start = ((), (), s32[]{:S(2)}) async-start(), calls=%async_computation.3 | async-start | bytes 6488064 | tf_op jit(solution)/shard_map/psum | solution.py:283
  471.9 6.8 copy-start.23
  478.7 10.5 %copy-start.21 = (bf16[3,8,96,768]{3,2,1,0:T(8,128)(2,1)}, bf16[3,8,96,768]{3,2,1,0:T(8,128)(2,1)S(1)}, u32[]{:S(2)}) copy-start(bf16[3,8,96,768]{3,2,1,0:T(8,128)(2,1)S(1)} %get-tuple-element.98) | copy-start | bytes 10616836
  532.2 11.1 %copy-start.20 = (pred[15,128,128]{1,2,0:T(8,128)(4,1)S(1)}, pred[15,128,128]{1,2,0:T(8,128)(4,1)}, u32[]{:S(2)}) copy-start(pred[15,128,128]{1,2,0:T(8,128)(4,1)} %copy-done.19) | copy-start | bytes 737284
  543.4 11.1 %copy-start.9 = (bf16[15,128,12,64]{1,0,3,2:T(8,128)(2,1)S(1)}, bf16[15,128,12,64]{1,0,3,2:T(8,128)(2,1)}, u32[]{:S(2)}) copy-start(bf16[15,128,12,64]{1,0,3,2:T(8,128)(2,1)} %reshape.556) | copy-start | bytes 8847364
  543.4 11.2 %copy-start.10 = (bf16[15,128,12,64]{1,0,3,2:T(8,128)(2,1)S(1)}, bf16[15,128,12,64]{1,0,3,2:T(8,128)(2,1)}, u32[]{:S(2)}) copy-start(bf16[15,128,12,64]{1,0,3,2:T(8,128)(2,1)} %reshape.567) | copy-start | bytes 8847364
  564.5 9.8 %copy-start.7 = (bf16[15,128,12,64]{1,0,3,2:T(8,128)(2,1)S(1)}, bf16[15,128,12,64]{1,0,3,2:T(8,128)(2,1)}, u32[]{:S(2)}) copy-start(bf16[15,128,12,64]{1,0,3,2:T(8,128)(2,1)} %reshape.558) | copy-start | bytes 8847364
  597.3 6.5 slice-start.2
  603.8 8.2 %copy-start.33 = (f32[15,128]{1,0:T(8,128)S(1)}, f32[15,128]{1,0:T(8,128)}, u32[]{:S(2)}) copy-start(f32[15,128]{1,0:T(8,128)} %copy-done.32) | copy-start | bytes 23044
  603.8 8.3 %copy-start.45 = (f32[768]{0:T(1024)S(1)}, f32[768]{0:T(1024)}, u32[]{:S(2)}) copy-start(f32[768]{0:T(1024)} %param.33) | copy-start | bytes 9220
  612.1 12.7 %slice-start.6 = ((s8[5898240]{0:T(1024)(128)(4,1)}), s8[4194304]{0:T(1024)(128)(4,1)S(1)}, s32[]{:S(2)}) async-start(s8[5898240]{0:T(1024)(128)(4,1)} %bitcast.169), calls=%async_computation.10 | async-start | bytes 8388608
  612.1 12.7 %slice-start.7 = ((s8[5898240]{0:T(1024)(128)(4,1)}), s8[1703936]{0:T(1024)(128)(4,1)S(1)}, s32[]{:S(2)}) async-start(s8[5898240]{0:T(1024)(128)(4,1)} %bitcast.169), calls=%async_computation.11 | async-start | bytes 3407872
  617.6 7.3 slice-start.4
  633.2 14.5 %slice-start = ((s8[5898240]{0:T(1024)(128)(4,1)}), s8[1703936]{0:T(1024)(128)(4,1)S(1)}, s32[]{:S(2)}) async-start(s8[5898240]{0:T(1024)(128)(4,1)} %bitcast.163), calls=%async_computation.4 | async-start | bytes 3407872
  634.3 13.4 %slice-start.1 = ((s8[5898240]{0:T(1024)(128)(4,1)}), s8[4194304]{0:T(1024)(128)(4,1)S(1)}, s32[]{:S(2)}) async-start(s8[5898240]{0:T(1024)(128)(4,1)} %bitcast.163), calls=%async_computation.5 | async-start | bytes 8388608
  634.3 13.4 %copy-start.42 = (bf16[768,768]{1,0:T(8,128)(2,1)S(1)}, bf16[768,768]{1,0:T(8,128)(2,1)}, u32[]{:S(2)}) copy-start(bf16[768,768]{1,0:T(8,128)(2,1)} %param.45) | copy-start | bytes 3538948
  634.3 13.4 %copy-start.51 = (f32[768]{0:T(1024)S(1)}, f32[768]{0:T(1024)}, u32[]{:S(2)}) copy-start(f32[768]{0:T(1024)} %param.46) | copy-start | bytes 9220
  634.3 13.4 %copy-start.53 = (bf16[1920,768]{1,0:T(8,128)(2,1)S(1)}, bf16[1920,768]{1,0:T(8,128)(2,1)}, u32[]{:S(2)}) copy-start(bf16[1920,768]{1,0:T(8,128)(2,1)} %copy-done.52) | copy-start | bytes 8847364
  647.7 72.2 %copy-start.1 = (bf16[1000,768]{1,0:T(8,128)(2,1)S(1)}, bf16[1000,768]{1,0:T(8,128)(2,1)}, u32[]{:S(2)}) copy-start(bf16[1000,768]{1,0:T(8,128)(2,1)} %param.31) | copy-start | bytes 4608004
  703.6 14.7 %copy-start.31 = (f32[768,192]{0,1:T(8,128)S(1)}, f32[768,192]{0,1:T(8,128)}, u32[]{:S(2)}) copy-start(f32[768,192]{0,1:T(8,128)} %get-tuple-element.117) | copy-start | bytes 1769476
  703.6 15.5 %copy-start.30 = (f32[192,768]{1,0:T(8,128)S(1)}, f32[192,768]{1,0:T(8,128)}, u32[]{:S(2)}) copy-start(f32[192,768]{1,0:T(8,128)} %get-tuple-element.119) | copy-start | bytes 1769476
  (35 other events, 138.9 us)
Sparse Core Ops, SparseCore 0:
  14.1 87.6 all-gather.2
  217.1 85.1 all-reduce.6
  305.8 127.6 all-gather.4
  634.4 69.1 all-reduce.8

commit v9 on v8

--- a/solution.py
+++ b/solution.py
@@ -58,7 +58,7 @@
         piece_rows = block.shape[0] // n_dp
         pieces.append(lax.dynamic_slice_in_dim(block, d * piece_rows, piece_rows, 0))
     sent = jnp.concatenate([p.astype(jnp.float32) for p in pieces], axis=0) * one
-    got = lax.all_gather(sent, ("mp", "dp"), axis=0) * one
+    got = lax.all_gather(sent, ("mp", "dp"), axis=0)
     n_mp = lax.axis_size("mp")
     got = got.reshape(n_mp, n_dp, *sent.shape)
     out, at = [], 0
@@ -69,9 +69,19 @@
     return out
 
 
-def whole_rows(part, dtype):
+def whole_rows(part, one, dtype):
     n_mp, n_dp, rows, width = part.shape
-    return part.astype(dtype).reshape(n_mp * n_dp * rows, width)
+    return (part * one).astype(dtype).reshape(n_mp * n_dp * rows, width)
+
+
+def other_rows(part, one, dtype):
+    n_mp, n_dp, rows, width = part.shape
+    me = lax.axis_index("mp")
+    blocks = [
+        lax.dynamic_index_in_dim(part, (me + step) % n_mp, 0, keepdims=False)
+        for step in range(1, n_mp)
+    ]
+    return (jnp.stack(blocks) * one).astype(dtype).reshape((n_mp - 1) * n_dp * rows, width)
 
 
 def bias_block(vectors, width, n_dp):
@@ -113,7 +123,6 @@
     ff_width = w_up_shard.shape[1]
     one = 1.0 + 0.0 * ln1_gain[0]
     n_dp = lax.axis_size("dp")
-    n_mp = lax.axis_size("mp")
     low_type = jnp.bfloat16
     q_part, k_part, v_part, o_part, qv_bias = gather_pieces(
         (
@@ -125,11 +134,11 @@
         ),
         one,
     )
-    w_query_t = whole_rows(q_part, low_type)
-    w_key_t = whole_rows(k_part, low_type)
-    w_value_t = whole_rows(v_part, low_type)
-    b_query = qv_bias[:, 0, 0, :qkv_width].reshape(-1)
-    b_value = qv_bias[:, 0, 0, qkv_width : 2 * qkv_width].reshape(-1)
+    w_query_t = whole_rows(q_part, one, low_type)
+    w_key_t = whole_rows(k_part, one, low_type)
+    w_value_t = whole_rows(v_part, one, low_type)
+    b_query = (qv_bias[:, 0, 0, :qkv_width] * one).reshape(-1)
+    b_value = (qv_bias[:, 0, 0, qkv_width : 2 * qkv_width] * one).reshape(-1)
     up_part, down_part, up_bias = gather_pieces(
         (
             w_up_shard.T,
@@ -138,11 +147,10 @@
         ),
         one,
     )
-    w_out = whole_rows(o_part, low_type)
-    others = (lax.axis_index("mp") + jnp.arange(1, n_mp, dtype=jnp.int32)) % n_mp
-    w_up_others = whole_rows(jnp.take(up_part, others, axis=0), low_type)
-    w_down_others = whole_rows(jnp.take(down_part, others, axis=0), low_type)
-    b_up_others = jnp.take(up_bias[:, 0, 0, :], others, axis=0).reshape(-1)
+    w_out = whole_rows(o_part, one, low_type)
+    w_up_others = other_rows(up_part, one, low_type)
+    w_down_others = other_rows(down_part, one, low_type)
+    b_up_others = other_rows(up_bias[:, :1, :1, :], one, jnp.float32).reshape(-1)
     heads = w_query_t.shape[0] // HD
     scaling = 1.0 / math.sqrt(HD)
     head_shape = (row_count, seq_len, heads, HD)
@@ -197,11 +205,12 @@
     grad_normed2_own = over_cols(grad_upper_own, w_up_shard)
     upper = over_cols(normed2_low, w_up_others) + b_up_others
     activated, gelu_pull = jax.vjp(exact_gelu, upper)
-    hidden = activated.astype(low_type)
+    hidden = lax.optimization_barrier(activated.astype(low_type))
     lowered = lowered_own + product(hidden, w_down_others)
-    output = (middle + lowered + b_down).astype(low_type).reshape(row_count, seq_len, model_width)
+    output = (middle + lowered + b_down).astype(low_type)
+    output = output.reshape(row_count, seq_len, model_width)
     (grad_upper,) = gelu_pull(over_cols(grad_out_low, w_down_others))
-    grad_upper_low = grad_upper.astype(low_type)
+    grad_upper_low = lax.optimization_barrier(grad_upper.astype(low_type))
     grad_normed2 = grad_normed2_own + product(grad_upper_low, w_up_others)
     grad_mid_norm, grad_ln2_gain, grad_ln2_shift = second_pull(grad_normed2)
     grad_middle = grad_out + grad_mid_norm

time: 732 us -> 710 us (0.970)
  other arithmetic: 96.3 us -> 66.6 us
  waiting for transfers between devices: 321 us -> 331 us
  local copies, waits for them, and re-layouts: 121 us -> 112 us
    dot_general x7 -> x8, matrix products: 46.1 us -> 64.7 us  [over_cols(): lax.dot_general(left, right, CONTRACT_COLS, preferred_element_type=jnp.fl...]
    dot_general x8, matrix products: 68.8 us -> 54.9 us  [product(): return jnp.dot(left, right, preferred_element_type=jnp.float32)]
    reshape x1 -> x0, other arithmetic: 12.4 us -> none  [gather_pieces(): got = got.reshape(n_mp, n_dp, *sent.shape)]
    gather x3 -> x0, local copies, waits for them, and re-layouts: 10.7 us -> none  [the longest x1 5.09 us: on_device(): w_down_others = whole_rows(jnp.take(down_part, others, axis=0), low_type)]
    another operation x1 -> x0, other arithmetic: 10.6 us -> none
    unnamed x138 -> x167, local copies, waits for them, and re-layouts: 27.4 us -> 19.8 us
    psum x1, waiting for transfers between devices: 73.8 us -> 81.3 us  [on_device(): lax.psum(jnp.concatenate([grad_w_down, grad_w_up], axis=0), 'dp')]
  transfers between devices with their start and end apart: 4 -> 4, of which waited for: 4 -> 4; matrix products, arithmetic and copies ran while one was open for 7% -> 6% of each run, Pallas kernels for 0% -> 0%
where the time goes in v9:
time: 710 us; the launch traced here: 705 us
  waiting for transfers between devices  331 us (47%)
  matrix products  178 us (25%)
  local copies, waits for them, and re-layouts  112 us (16%)
  other arithmetic  66.6 us (9%)
  between operations  16.5 us (2%)
    all_gather x2, waiting for transfers between devices, gather_pieces(): got = lax.all_gather(sent, ('mp', 'dp'), axis=0)  196 us
    psum x1, waiting for transfers between devices, on_device(): lax.psum(jnp.concatenate([grad_w_down, grad_w_up], axis=0), 'dp')  81.3 us
    dot_general x8, matrix products, over_cols(): lax.dot_general(left, right, CONTRACT_COLS, preferred_element_type=jnp.fl...  64.7 us
    dot_general x8, matrix products, product(): return jnp.dot(left, right, preferred_element_type=jnp.float32)  54.9 us
    psum x1, waiting for transfers between devices, on_device(): lax.psum((grad_w_query + tie, grad_w_key, grad_w_value, grad_w_out, packe...  53.6 us
    unnamed x167, local copies, waits for them, and re-layouts  19.8 us
    dot_general x6, matrix products, over_rows(): lax.dot_general(left, right, CONTRACT_ROWS, preferred_element_type=jnp.fl...  17 us
  transfers between devices with their start and end apart: 4, of which 4 were waited for; matrix products, arithmetic and copies ran while one was open for 6% of the time, Pallas kernels for 0%

profile of v9, /device:TPU:0, one launch (start us, length us, event | category | flops | bytes accessed | tf_op | source)
XLA Modules:
  0.0 704.8 jit_solution(7059291395138692901)
XLA Ops:
  16.0 6.0 fusion.63
  29.8 72.0 %all-gather.3.cloned.1.call-done = f32[32,97,768]{2,1,0:T(8,128)} async-done(((f32[1,97,768]{2,1,0:T(8,128)}), f32[32,97,768]{2,1,0:T(8,128)}) %all-gather.3.cloned.1.call-update) | async-done | bytes 9535504 | tf_op jit(solution)/shard_map/all_gather | solution.py:61
  101.8 5.8 fusion.22
  117.4 6.1 reshape.518
  123.6 5.9 add_convert_fusion.5
  134.2 6.0 reshape.516
  140.3 5.9 add_convert_fusion.6
  150.8 6.3 reshape.514
  157.1 6.6 fusion.8
  168.7 5.1 convert_bitcast_fusion.1
  179.4 6.6 fusion.71
  192.3 5.9 convert_reduce_fusion
  210.2 81.3 %all-reduce.7.cloned.1.call-done = f32[1536,768]{1,0:T(8,128)} async-done(((f32[1536,768]{1,0:T(8,128)}), f32[1536,768]{1,0:T(8,128)}) %all-reduce.7.cloned.1.call-update) | async-done | bytes 4718608 | tf_op jit(solution)/shard_map/psum | solution.py:203
  293.4 4.9 fusion.69
  298.2 124.5 %all-gather.5.cloned.1.call-done = f32[32,193,768]{2,1,0:T(8,128)} async-done(((f32[1,193,768]{2,1,0:T(8,128)}), f32[32,193,768]{2,1,0:T(8,128)}) %all-gather.5.cloned.1.call-update) | async-done | bytes 18972688 | tf_op jit(solution)/shard_map/all_gather | solution.py:61
  423.6 13.0 %fusion.68 = (f32[4,8,96,768]{3,2,1,0:T(8,128)}, f32[4,8,96,768]{3,2,1,0:T(8,128)}) fusion(f32[4,8,193,768]{3,2,1,0:T(8,128)} %bitcast.175), kind=kLoop, calls=%fused_computation.162 | loop fusion | bytes 37748736 | tf_op jit(solution)/shard_map/slice | solution.py:67
  444.9 13.6 %multiply_convert_fusion = (bf16[1920,2304]{1,0:T(8,128)(2,1)}, f32[1920,2304]{1,0:T(8,128)}) fusion(f32[2304]{0:T(1024)S(1)} %mul.366, bf16[1920,768]{1,0:T(8,128)(2,1)S(1)} %copy-done.27, bf16[2304,768]{1,0:T(8,128)(2,1)S(1)} %bitcast.195), kind=kOutput, calls=%fused_computation.2 | convolution fusion | flops 6821314560 | bytes 33039360 | tf_op jit(solution)/shard_map/dot_general | solution.py:37
  458.5 19.2 %add_convert_fusion = bf16[1920,2304]{1,0:T(8,128)(2,1)} fusion(f32[1920,2304]{1,0:T(8,128)} %get-tuple-element.109, f32[2304]{0:T(1024)S(1)} %mul.366, bf16[1920,768]{1,0:T(8,128)(2,1)S(1)} %copy-done.29, bf16[2304,768]{1,0:T(8,128)(2,1)S(1)} %bitcast.193), kind=kOutput, calls=%fused_computation.1 | convolution fusion | flops 6856704000 | bytes 33039360 | tf_op jit(solution)/shard_map/dot_general | solution.py:37
  477.7 11.2 %fusion.74 = f32[1920,768]{1,0:T(8,128)} fusion(bf16[1920,2304]{1,0:T(8,128)(2,1)} %add_convert_fusion, bf16[2304,768]{1,0:T(8,128)(2,1)S(1)} %bitcast.196), kind=kOutput, calls=%fused_computation.168 | convolution fusion | flops 6794772480 | bytes 18284544 | tf_op jit(solution)/shard_map/dot_general | solution.py:29
  489.0 5.9 multiply_reduce_fusion.1
  506.0 4.7 copy.90
  510.7 6.0 reshape.523
  516.7 11.1 %convert_bitcast_fusion = bf16[15,128,12,64]{1,3,2,0:T(8,128)(2,1)} fusion(f32[15,12,128]{2,1,0:T(8,128)S(1)} %log_add_fusion, f32[15,12,128,128]{2,3,1,0:T(8,128)} %copy-done.2, pred[15,128,128]{1,2,0:T(8,128)(4,1)S(1)} %copy-done.22, bf16[15,128,12,64]{1,0,3,2:T(8,128)(2,1)} %reshape.523), kind=kOutput, calls=%fused_computation.59 | convolution fusion | flops 390758400 | bytes 18032640 | tf_op jit(solution)/shard_map/rhqk,rqhe->rkhe/dot_general | solution.py:236
  527.9 9.9 %multiply_reduce_fusion = (f32[15,12,128]{2,1,0:T(8,128)S(1)}, f32[15,12,128,128]{2,3,1,0:T(8,128)}) fusion(f32[15,12,128]{2,1,0:T(8,128)S(1)} %log_add_fusion, f32[15,12,128,128]{2,3,1,0:T(8,128)} %copy-done.2, pred[15,128,128]{1,2,0:T(8,128)(4,1)S(1)} %copy-done.22, bf16[15,128,12,64]{1,0,3,2:T(8,128)(2,1)S(1)} %copy-done.11, ...), kind=kOutput, calls=%fused_computation.5 | convolution fusion | flops 392209920 | bytes 29921280 | tf_op jit(solution)/shard_map/rqhe,rkhe->rhqk/dot_general | solution.py:223
  537.8 9.8 %multiply_convert_fusion.1 = bf16[15,12,128,128]{2,3,1,0:T(8,128)(2,1)S(1)} fusion(f32[15,12,128,128]{2,3,1,0:T(8,128)} %get-tuple-element.112, f32[15,12,128]{2,1,0:T(8,128)S(1)} %get-tuple-element.111, f32[15,12,128]{2,1,0:T(8,128)S(1)} %log_add_fusion, f32[15,12,128,128]{2,3,1,0:T(8,128)} %copy-done.2, pred[15,128,128]{1,2,0:T(8,128)(4,1)S(1)} %copy-done.22), kind=kLoop, calls=%fused_computation.4 | loop fusion | flops 17694720 | bytes 29921280 | tf_op jit(solution)/shard_map/convert_element_type | solution.py:227
  549.6 5.6 fusion.11
  562.3 5.0 fusion.75
  571.2 5.5 fusion.76
  578.0 8.3 %multiply_reduce_fusion.2 = (f32[768]{0:T(1024)S(1)}, f32[1920]{0:T(1024)S(1)}, f32[768]{0:T(1024)S(1)}, f32[1920,768]{1,0:T(8,128)}) fusion(f32[15,128,768]{2,1,0:T(8,128)S(1)} %bitcast.163, f32[1920]{0:T(1024)S(1)} %copy-done.42, f32[1920]{0:T(1024)S(1)} %copy-done.43, f32[768]{0:T(1024)S(1)} %copy-done.45, bf16[1920,768]{0,1:T(8,128)(2,1)S(1)} %bitcast.172, ...), kind=kOutput, calls=%fused_computation.26 | convolution fusion | flops 2279666432 | bytes 27753984 | tf_op jit(solution)/shard_map/dot_general | solution.py:29
  586.3 5.2 fusion.66
  612.5 10.9 %fusion.73 = f32[1920,768]{1,0:T(8,128)S(1)} fusion(bf16[1920,2304]{1,0:T(8,128)(2,1)} %get-tuple-element.108, bf16[2304,768]{1,0:T(8,128)(2,1)} %bitcast.194), kind=kOutput, calls=%fused_computation.167 | convolution fusion | flops 6794772480 | bytes 18284544 | tf_op jit(solution)/shard_map/dot_general | solution.py:29
  628.2 53.6 %all-reduce.9.cloned.1.call-done = (f32[1030,192]{0,1:T(8,128)}, f32[768,192]{0,1:T(8,128)}, f32[768,192]{0,1:T(8,128)}, f32[768,192]{0,1:T(8,128)}, f32[192,768]{1,0:T(8,128)}) async-done(((f32[1030,192]{0,1:T(8,128)}, f32[768,192]{0,1:T(8,128)}, f32[768,192]{0,1:T(8,128)}, f32[768,192]{0,1:T(8,128)}, f32[192,768]{1,0:T(8,128)}), (f32[1030,192]{0,1:T(8,128)}, f32[768,192]{0,1:T(8,128)}, ...) | async-done | bytes 3150352 | tf_op jit(solution)/shard_map/psum | solution.py:292
  (280 shorter events, 140.6 us)
Async XLA Ops:
  7.2 94.6 %all-gather.3.cloned.1.call-start = ((), (), s32[]{:S(2)}) async-start(), calls=%async_computation | async-start | bytes 10543104 | tf_op jit(solution)/shard_map/all_gather | solution.py:61
  14.0 277.5 %all-reduce.7.cloned.1.call-start = ((), (), s32[]{:S(2)}) async-start(), calls=%async_computation.2 | async-start | bytes 9437184 | tf_op jit(solution)/shard_map/psum | solution.py:203
  24.5 185.0 %copy-start.40 = (f32[15,128]{1,0:T(8,128)}, f32[15,128]{1,0:T(8,128)S(1)}, u32[]{:S(2)}) copy-start(f32[15,128]{1,0:T(8,128)S(1)} %multiply_reduce_fusion.6) | copy-start | bytes 23044
  25.5 141.8 %copy-start.21 = (pred[15,128,128]{1,2,0:T(8,128)(4,1)}, pred[15,128,128]{1,2,0:T(8,128)(4,1)S(1)}, u32[]{:S(2)}) copy-start(pred[15,128,128]{1,2,0:T(8,128)(4,1)S(1)} %or_and_fusion) | copy-start | bytes 737284
  107.6 16.0 %copy-start.34 = (bf16[4,8,24,768]{3,2,1,0:T(8,128)(2,1)}, bf16[4,8,24,768]{3,2,1,0:T(8,128)(2,1)S(1)}, u32[]{:S(2)}) copy-start(bf16[4,8,24,768]{3,2,1,0:T(8,128)(2,1)S(1)} %get-tuple-element.75) | copy-start | bytes 3538948
  107.6 32.7 %copy-start.17 = (bf16[4,8,24,768]{3,2,1,0:T(8,128)(2,1)}, bf16[4,8,24,768]{3,2,1,0:T(8,128)(2,1)S(1)}, u32[]{:S(2)}) copy-start(bf16[4,8,24,768]{3,2,1,0:T(8,128)(2,1)S(1)} %get-tuple-element.76) | copy-start | bytes 3538948
  206.2 216.5 %all-gather.5.cloned.1.call-start = ((), (), s32[]{:S(2)}) async-start(), calls=%async_computation.1 | async-start | bytes 20275200 | tf_op jit(solution)/shard_map/all_gather | solution.py:61
  209.4 472.3 %all-reduce.9.cloned.1.call-start = ((), (), s32[]{:S(2)}) async-start(), calls=%async_computation.3 | async-start | bytes 6488064 | tf_op jit(solution)/shard_map/psum | solution.py:292
  444.4 14.1 %copy-start.24 = (bf16[3,8,96,768]{3,2,1,0:T(8,128)(2,1)}, bf16[3,8,96,768]{3,2,1,0:T(8,128)(2,1)S(1)}, u32[]{:S(2)}) copy-start(bf16[3,8,96,768]{3,2,1,0:T(8,128)(2,1)S(1)} %get-tuple-element.114) | copy-start | bytes 10616836
  444.4 14.1 %copy-start.23 = (bf16[3,8,96,768]{3,2,1,0:T(8,128)(2,1)}, bf16[3,8,96,768]{3,2,1,0:T(8,128)(2,1)S(1)}, u32[]{:S(2)}) copy-start(bf16[3,8,96,768]{3,2,1,0:T(8,128)(2,1)S(1)} %get-tuple-element.115) | copy-start | bytes 10616836
  444.9 13.6 %copy-start.29 = (bf16[1920,768]{1,0:T(8,128)(2,1)S(1)}, bf16[1920,768]{1,0:T(8,128)(2,1)}, u32[]{:S(2)}) copy-start(bf16[1920,768]{1,0:T(8,128)(2,1)} %get-tuple-element.45) | copy-start | bytes 8847364
  444.9 44.0 %slice-start = ((s8[5898240]{0:T(1024)(128)(4,1)}), s8[4194304]{0:T(1024)(128)(4,1)S(1)}, s32[]{:S(2)}) async-start(s8[5898240]{0:T(1024)(128)(4,1)} %bitcast.158), calls=%async_computation.4 | async-start | bytes 8388608
  458.5 19.2 %copy-start.25 = (bf16[3,8,96,768]{3,2,1,0:T(8,128)(2,1)S(1)}, bf16[3,8,96,768]{3,2,1,0:T(8,128)(2,1)}, u32[]{:S(2)}) copy-start(bf16[3,8,96,768]{3,2,1,0:T(8,128)(2,1)} %copy-done.24) | copy-start | bytes 10616836
  458.5 30.4 %slice-start.1 = ((s8[5898240]{0:T(1024)(128)(4,1)}), s8[1703936]{0:T(1024)(128)(4,1)S(1)}, s32[]{:S(2)}) async-start(s8[5898240]{0:T(1024)(128)(4,1)} %bitcast.158), calls=%async_computation.5 | async-start | bytes 3407872
  458.5 39.2 %slice-start.6 = ((s8[5898240]{0:T(1024)(128)(4,1)}), s8[4194304]{0:T(1024)(128)(4,1)S(1)}, s32[]{:S(2)}) async-start(s8[5898240]{0:T(1024)(128)(4,1)} %bitcast.164), calls=%async_computation.10 | async-start | bytes 8388608
  477.7 11.3 %copy-start.48 = (bf16[768,768]{1,0:T(8,128)(2,1)S(1)}, bf16[768,768]{1,0:T(8,128)(2,1)}, u32[]{:S(2)}) copy-start(bf16[768,768]{1,0:T(8,128)(2,1)} %param.41) | copy-start | bytes 3538948
  477.7 11.3 %copy-start.64 = (bf16[1920,768]{1,0:T(8,128)(2,1)S(1)}, bf16[1920,768]{1,0:T(8,128)(2,1)}, u32[]{:S(2)}) copy-start(bf16[1920,768]{1,0:T(8,128)(2,1)} %copy-done.63) | copy-start | bytes 8847364
  477.7 20.0 %slice-start.7 = ((s8[5898240]{0:T(1024)(128)(4,1)}), s8[1703936]{0:T(1024)(128)(4,1)S(1)}, s32[]{:S(2)}) async-start(s8[5898240]{0:T(1024)(128)(4,1)} %bitcast.164), calls=%async_computation.11 | async-start | bytes 3407872
  506.0 10.8 %copy-start.22 = (pred[15,128,128]{1,2,0:T(8,128)(4,1)S(1)}, pred[15,128,128]{1,2,0:T(8,128)(4,1)}, u32[]{:S(2)}) copy-start(pred[15,128,128]{1,2,0:T(8,128)(4,1)} %copy-done.21) | copy-start | bytes 737284
  516.7 11.1 %copy-start.11 = (bf16[15,128,12,64]{1,0,3,2:T(8,128)(2,1)S(1)}, bf16[15,128,12,64]{1,0,3,2:T(8,128)(2,1)}, u32[]{:S(2)}) copy-start(bf16[15,128,12,64]{1,0,3,2:T(8,128)(2,1)} %reshape.514) | copy-start | bytes 8847364
  516.7 11.2 %copy-start.12 = (bf16[15,128,12,64]{1,0,3,2:T(8,128)(2,1)S(1)}, bf16[15,128,12,64]{1,0,3,2:T(8,128)(2,1)}, u32[]{:S(2)}) copy-start(bf16[15,128,12,64]{1,0,3,2:T(8,128)(2,1)} %reshape.523) | copy-start | bytes 8847364
  562.3 14.5 %copy-start.16 = (bf16[96,8,15,128]{3,1,2,0:T(8,128)(2,1)}, bf16[96,8,15,128]{3,1,2,0:T(8,128)(2,1)S(1)}, u32[]{:S(2)}) copy-start(bf16[96,8,15,128]{3,1,2,0:T(8,128)(2,1)S(1)} %copy.153) | copy-start | bytes 8847364
  577.9 21.5 %slice-start.10 = ((s8[5898240]{0:T(1024)(128)(4,1)}), s8[4194304]{0:T(1024)(128)(4,1)S(1)}, s32[]{:S(2)}) async-start(s8[5898240]{0:T(1024)(128)(4,1)} %bitcast.168), calls=%async_computation.14 | async-start | bytes 8388608
  586.3 13.1 %slice-start.11 = ((s8[5898240]{0:T(1024)(128)(4,1)}), s8[1703936]{0:T(1024)(128)(4,1)S(1)}, s32[]{:S(2)}) async-start(s8[5898240]{0:T(1024)(128)(4,1)} %bitcast.168), calls=%async_computation.15 | async-start | bytes 3407872
  611.4 12.1 %slice-start.2 = ((s8[5898240]{0:T(1024)(128)(4,1)}), s8[1703936]{0:T(1024)(128)(4,1)S(1)}, s32[]{:S(2)}) async-start(s8[5898240]{0:T(1024)(128)(4,1)} %bitcast.160), calls=%async_computation.6 | async-start | bytes 3407872
  612.4 11.0 %slice-start.3 = ((s8[5898240]{0:T(1024)(128)(4,1)}), s8[4194304]{0:T(1024)(128)(4,1)S(1)}, s32[]{:S(2)}) async-start(s8[5898240]{0:T(1024)(128)(4,1)} %bitcast.160), calls=%async_computation.7 | async-start | bytes 8388608
  612.4 11.0 %copy-start.51 = (bf16[768,768]{1,0:T(8,128)(2,1)S(1)}, bf16[768,768]{1,0:T(8,128)(2,1)}, u32[]{:S(2)}) copy-start(bf16[768,768]{1,0:T(8,128)(2,1)} %param.43) | copy-start | bytes 3538948
  612.5 11.0 %copy-start.60 = (f32[768]{0:T(1024)S(1)}, f32[768]{0:T(1024)}, u32[]{:S(2)}) copy-start(f32[768]{0:T(1024)} %param.44) | copy-start | bytes 9220
  612.5 11.0 %copy-start.62 = (bf16[1920,768]{1,0:T(8,128)(2,1)S(1)}, bf16[1920,768]{1,0:T(8,128)(2,1)}, u32[]{:S(2)}) copy-start(bf16[1920,768]{1,0:T(8,128)(2,1)} %copy-done.61) | copy-start | bytes 8847364
  623.5 74.5 %copy-start.1 = (bf16[1000,768]{1,0:T(8,128)(2,1)S(1)}, bf16[1000,768]{1,0:T(8,128)(2,1)}, u32[]{:S(2)}) copy-start(bf16[1000,768]{1,0:T(8,128)(2,1)} %param.29) | copy-start | bytes 4608004
  681.8 14.6 %copy-start.39 = (f32[768,192]{0,1:T(8,128)S(1)}, f32[768,192]{0,1:T(8,128)}, u32[]{:S(2)}) copy-start(f32[768,192]{0,1:T(8,128)} %get-tuple-element.123) | copy-start | bytes 1769476
  681.8 15.4 %copy-start.38 = (f32[192,768]{1,0:T(8,128)S(1)}, f32[192,768]{1,0:T(8,128)}, u32[]{:S(2)}) copy-start(f32[192,768]{1,0:T(8,128)} %get-tuple-element.125) | copy-start | bytes 1769476
  (51 other events, 255.2 us)
Sparse Core Ops, SparseCore 0:
  14.1 87.6 all-gather.2
  206.3 85.1 all-reduce.6
  295.0 127.6 all-gather.4
  612.5 69.1 all-reduce.8

commit v10 on v9

--- a/solution.py
+++ b/solution.py
@@ -175,9 +175,10 @@
     total = jnp.sum(powers, axis=-1, keepdims=True)
     log_total = row_max + jnp.log(total)
     probabilities = powers / total
+    probabilities_low = probabilities.astype(low_type)
     mixed = jnp.einsum(
         "rhqk,rkhe->rqhe",
-        probabilities.astype(low_type),
+        probabilities_low,
         values_split,
         preferred_element_type=jnp.float32,
     )
@@ -218,8 +219,7 @@
     grad_w_out = over_rows(own_columns(mixed, qkv_width), grad_mid_low)
     grad_b_out = column_sum(grad_mid_low)
     grad_mixed = over_cols(grad_mid_low, w_out).astype(low_type).reshape(head_shape)
-    scores_again = attention_scores(queries_split, keys_split, allowed)
-    soft_again = jnp.exp(scores_again - log_total)
+    soft_again = probabilities
     grad_soft = jnp.einsum(
         "rqhe,rkhe->rhqk", grad_mixed, values_split, preferred_element_type=jnp.float32
     )
@@ -235,7 +235,7 @@
     grad_keys = (grad_keys * scaling).reshape(token_count, heads * HD).astype(low_type)
     grad_values = jnp.einsum(
         "rhqk,rqhe->rkhe",
-        soft_again.astype(low_type),
+        probabilities_low,
         grad_mixed,
         preferred_element_type=jnp.float32,
     )

time: 710 us -> 723 us (1.018)
  other arithmetic: 66.6 us -> 78.6 us
    sub x0 -> x1, other arithmetic: none -> 15.8 us  [on_device(): powers = jnp.exp(scores - row_max)]
where the time goes in v10:
time: 723 us; the launch traced here: 718 us
  waiting for transfers between devices  332 us (46%)
  matrix products  180 us (25%)
  local copies, waits for them, and re-layouts  110 us (15%)
  other arithmetic  78.6 us (11%)
  between operations  16.5 us (2%)
    all_gather x2, waiting for transfers between devices, gather_pieces(): got = lax.all_gather(sent, ('mp', 'dp'), axis=0)  196 us
    psum x1, waiting for transfers between devices, on_device(): lax.psum(jnp.concatenate([grad_w_down, grad_w_up], axis=0), 'dp')  82.4 us
    dot_general x8, matrix products, over_cols(): lax.dot_general(left, right, CONTRACT_COLS, preferred_element_type=jnp.fl...  66.4 us
    psum x1, waiting for transfers between devices, on_device(): lax.psum((grad_w_query + tie, grad_w_key, grad_w_value, grad_w_out, packe...  53.6 us
    dot_general x8, matrix products, product(): return jnp.dot(left, right, preferred_element_type=jnp.float32)  51.1 us
    unnamed x167, local copies, waits for them, and re-layouts  19.4 us
    dot_general x6, matrix products, over_rows(): lax.dot_general(left, right, CONTRACT_ROWS, preferred_element_type=jnp.fl...  17.2 us
    sub x1, other arithmetic, on_device(): powers = jnp.exp(scores - row_max)  15.8 us
  transfers between devices with their start and end apart: 4, of which 4 were waited for; matrix products, arithmetic and copies ran while one was open for 6% of the time, Pallas kernels for 0%

profile of v10, /device:TPU:0, one launch (start us, length us, event | category | flops | bytes accessed | tf_op | source)
XLA Modules:
  0.0 717.7 jit_solution(17388616935117007039)
XLA Ops:
  16.0 6.0 fusion.65
  29.9 71.9 %all-gather.3.cloned.1.call-done = f32[32,97,768]{2,1,0:T(8,128)} async-done(((f32[1,97,768]{2,1,0:T(8,128)}), f32[32,97,768]{2,1,0:T(8,128)}) %all-gather.3.cloned.1.call-update) | async-done | bytes 9535504 | tf_op jit(solution)/shard_map/all_gather | solution.py:61
  101.8 6.0 fusion.24
  108.9 5.9 add_convert_fusion.6
  119.5 6.0 reshape.506
  125.5 5.9 convolution_convert_fusion.1
  136.2 6.1 reshape.510
  142.4 5.9 add_convert_fusion.5
  152.9 6.6 reshape.508
  159.5 10.3 %fusion.20 = f32[15,12,128,128]{2,3,1,0:T(8,128)} fusion(bf16[15,128,12,64]{1,0,3,2:T(8,128)(2,1)} %reshape.510, bf16[15,128,12,64]{1,0,3,2:T(8,128)(2,1)} %reshape.508), kind=kOutput, calls=%fused_computation.69 | convolution fusion | flops 377487360 | bytes 17694720 | tf_op jit(solution)/shard_map/rqhe,rkhe->rhqk/dot_general | solution.py:47
  169.8 15.8 %fusion.73 = (f32[15,12,128]{2,1,0:T(8,128)S(1)}, f32[15,12,128,128]{2,3,1,0:T(8,128)}) fusion(f32[15,12,128,128]{2,3,1,0:T(8,128)} %fusion.20, pred[15,128,128]{1,2,0:T(8,128)(4,1)S(1)} %or_and_fusion), kind=kOutput, calls=%fused_computation.164 | output fusion | flops 17694848 | bytes 23930880 | tf_op jit(solution)/shard_map/sub | solution.py:174
  186.3 6.8 convert_bitcast_fusion.1
  206.1 5.9 convert_reduce_fusion
  223.0 82.4 %all-reduce.7.cloned.1.call-done = f32[1536,768]{1,0:T(8,128)} async-done(((f32[1536,768]{1,0:T(8,128)}), f32[1536,768]{1,0:T(8,128)}) %all-reduce.7.cloned.1.call-update) | async-done | bytes 4718608 | tf_op jit(solution)/shard_map/psum | solution.py:204
  307.2 4.9 fusion.71
  312.0 124.5 %all-gather.5.cloned.1.call-done = f32[32,193,768]{2,1,0:T(8,128)} async-done(((f32[1,193,768]{2,1,0:T(8,128)}), f32[32,193,768]{2,1,0:T(8,128)}) %all-gather.5.cloned.1.call-update) | async-done | bytes 18972688 | tf_op jit(solution)/shard_map/all_gather | solution.py:61
  437.4 13.2 %fusion.70 = (f32[4,8,96,768]{3,2,1,0:T(8,128)}, f32[4,8,96,768]{3,2,1,0:T(8,128)}) fusion(f32[4,8,193,768]{3,2,1,0:T(8,128)} %bitcast.177), kind=kLoop, calls=%fused_computation.161 | loop fusion | bytes 37748736 | tf_op jit(solution)/shard_map/slice | solution.py:67
  458.9 13.4 %multiply_convert_fusion = (bf16[1920,2304]{1,0:T(8,128)(2,1)}, f32[1920,2304]{1,0:T(8,128)}) fusion(f32[2304]{0:T(1024)S(1)} %mul.369, bf16[1920,768]{1,0:T(8,128)(2,1)S(1)} %copy-done.24, bf16[2304,768]{1,0:T(8,128)(2,1)S(1)} %bitcast.197), kind=kOutput, calls=%fused_computation.3 | convolution fusion | flops 6821314560 | bytes 33039360 | tf_op jit(solution)/shard_map/dot_general | solution.py:37
  472.4 19.1 %add_convert_fusion = bf16[1920,2304]{1,0:T(8,128)(2,1)} fusion(f32[1920,2304]{1,0:T(8,128)} %get-tuple-element.109, f32[2304]{0:T(1024)S(1)} %mul.369, bf16[1920,768]{1,0:T(8,128)(2,1)S(1)} %copy-done.26, bf16[2304,768]{1,0:T(8,128)(2,1)S(1)} %bitcast.195), kind=kOutput, calls=%fused_computation.2 | convolution fusion | flops 6856704000 | bytes 33039360 | tf_op jit(solution)/shard_map/dot_general | solution.py:37
  491.6 11.2 %fusion.77 = f32[1920,768]{1,0:T(8,128)} fusion(bf16[1920,2304]{1,0:T(8,128)(2,1)} %add_convert_fusion, bf16[2304,768]{1,0:T(8,128)(2,1)S(1)} %bitcast.198), kind=kOutput, calls=%fused_computation.168 | convolution fusion | flops 6794772480 | bytes 18284544 | tf_op jit(solution)/shard_map/dot_general | solution.py:29
  502.9 5.9 multiply_reduce_fusion.1
  524.6 6.0 reshape.515
  530.6 11.2 %convert_bitcast_fusion = bf16[15,128,12,64]{1,3,2,0:T(8,128)(2,1)} fusion(bf16[15,128,12,64]{1,0,3,2:T(8,128)(2,1)} %reshape.515, f32[15,12,128,128]{2,3,1,0:T(8,128)} %get-tuple-element.105, f32[15,12,128]{2,1,0:T(8,128)S(1)} %copy-done.39), kind=kOutput, calls=%fused_computation.57 | convolution fusion | flops 384860160 | bytes 17786880 | tf_op jit(solution)/shard_map/rhqk,rqhe->rkhe/dot_general | solution.py:236
  541.8 8.8 %multiply_reduce_fusion = (f32[15,12,128]{2,1,0:T(8,128)S(1)}, f32[15,12,128,128]{2,3,1,0:T(8,128)}) fusion(f32[15,12,128,128]{2,3,1,0:T(8,128)} %get-tuple-element.105, f32[15,12,128]{2,1,0:T(8,128)S(1)} %copy-done.39, bf16[15,128,12,64]{1,0,3,2:T(8,128)(2,1)S(1)} %copy-done.21, bf16[15,128,12,64]{1,0,3,2:T(8,128)(2,1)S(1)} %copy-done.22), kind=kOutput, calls=%fused_computation.6 | convolution fusion | flops 386311680 | bytes 29675520 | tf_op jit(solution)/shard_map/rqhe,rkhe->rhqk/dot_general | solution.py:223
  550.6 9.5 %multiply_convert_fusion.1 = bf16[15,12,128,128]{2,3,1,0:T(8,128)(2,1)S(1)} fusion(f32[15,12,128,128]{2,3,1,0:T(8,128)} %get-tuple-element.112, f32[15,12,128]{2,1,0:T(8,128)S(1)} %get-tuple-element.111, f32[15,12,128,128]{2,3,1,0:T(8,128)} %get-tuple-element.105, f32[15,12,128]{2,1,0:T(8,128)S(1)} %copy-done.39), kind=kLoop, calls=%fused_computation.5 | loop fusion | flops 11796480 | bytes 29675520 | tf_op jit(solution)/shard_map/convert_element_type | solution.py:227
  562.1 5.6 fusion.9
  574.8 5.0 fusion.78
  583.9 5.5 fusion.79
  590.6 8.3 %multiply_reduce_fusion.2 = (f32[768]{0:T(1024)S(1)}, f32[1920]{0:T(1024)S(1)}, f32[768]{0:T(1024)S(1)}, f32[1920,768]{1,0:T(8,128)}) fusion(f32[15,128,768]{2,1,0:T(8,128)S(1)} %bitcast.165, f32[1920]{0:T(1024)S(1)} %copy-done.40, f32[1920]{0:T(1024)S(1)} %copy-done.41, f32[768]{0:T(1024)S(1)} %copy-done.43, bf16[1920,768]{0,1:T(8,128)(2,1)S(1)} %bitcast.174, ...), kind=kOutput, calls=%fused_computation.23 | convolution fusion | flops 2279666432 | bytes 27753984 | tf_op jit(solution)/shard_map/dot_general | solution.py:29
  599.0 5.2 fusion.68
  625.3 10.9 %fusion.76 = f32[1920,768]{1,0:T(8,128)S(1)} fusion(bf16[1920,2304]{1,0:T(8,128)(2,1)} %get-tuple-element.108, bf16[2304,768]{1,0:T(8,128)(2,1)} %bitcast.196), kind=kOutput, calls=%fused_computation.167 | convolution fusion | flops 6794772480 | bytes 18284544 | tf_op jit(solution)/shard_map/dot_general | solution.py:29
  640.9 53.6 %all-reduce.9.cloned.1.call-done = (f32[1030,192]{0,1:T(8,128)}, f32[768,192]{0,1:T(8,128)}, f32[768,192]{0,1:T(8,128)}, f32[768,192]{0,1:T(8,128)}, f32[192,768]{1,0:T(8,128)}) async-done(((f32[1030,192]{0,1:T(8,128)}, f32[768,192]{0,1:T(8,128)}, f32[768,192]{0,1:T(8,128)}, f32[768,192]{0,1:T(8,128)}, f32[192,768]{1,0:T(8,128)}), (f32[1030,192]{0,1:T(8,128)}, f32[768,192]{0,1:T(8,128)}, ...) | async-done | bytes 3150352 | tf_op jit(solution)/shard_map/psum | solution.py:292
  (280 shorter events, 137.7 us)
Async XLA Ops:
  7.2 94.6 %all-gather.3.cloned.1.call-start = ((), (), s32[]{:S(2)}) async-start(), calls=%async_computation | async-start | bytes 10543104 | tf_op jit(solution)/shard_map/all_gather | solution.py:61
  14.0 291.4 %all-reduce.7.cloned.1.call-start = ((), (), s32[]{:S(2)}) async-start(), calls=%async_computation.2 | async-start | bytes 9437184 | tf_op jit(solution)/shard_map/psum | solution.py:204
  24.5 197.8 %copy-start.36 = (f32[15,128]{1,0:T(8,128)}, f32[15,128]{1,0:T(8,128)S(1)}, u32[]{:S(2)}) copy-start(f32[15,128]{1,0:T(8,128)S(1)} %multiply_reduce_fusion.6) | copy-start | bytes 23044
  107.8 17.7 %copy-start.28 = (bf16[4,8,24,768]{3,2,1,0:T(8,128)(2,1)}, bf16[4,8,24,768]{3,2,1,0:T(8,128)(2,1)S(1)}, u32[]{:S(2)}) copy-start(bf16[4,8,24,768]{3,2,1,0:T(8,128)(2,1)S(1)} %get-tuple-element.74) | copy-start | bytes 3538948
  131.5 10.9 %copy-start.30 = (bf16[4,8,24,768]{3,2,1,0:T(8,128)(2,1)S(1)}, bf16[4,8,24,768]{3,2,1,0:T(8,128)(2,1)}, u32[]{:S(2)}) copy-start(bf16[4,8,24,768]{3,2,1,0:T(8,128)(2,1)} %get-tuple-element.75) | copy-start | bytes 3538948
  169.8 16.4 %copy-start.20 = (bf16[15,128,12,64]{1,0,3,2:T(8,128)(2,1)S(1)}, bf16[15,128,12,64]{1,0,3,2:T(8,128)(2,1)}, u32[]{:S(2)}) copy-start(bf16[15,128,12,64]{1,0,3,2:T(8,128)(2,1)} %reshape.506) | copy-start | bytes 8847364
  185.6 11.2 %slice-start.4 = ((s8[5898240]{0:T(1024)(128)(4,1)}), s8[4194304]{0:T(1024)(128)(4,1)S(1)}, s32[]{:S(2)}) async-start(s8[5898240]{0:T(1024)(128)(4,1)} %bitcast.162), calls=%async_computation.8 | async-start | bytes 8388608
  220.0 216.5 %all-gather.5.cloned.1.call-start = ((), (), s32[]{:S(2)}) async-start(), calls=%async_computation.1 | async-start | bytes 20275200 | tf_op jit(solution)/shard_map/all_gather | solution.py:61
  222.3 472.3 %all-reduce.9.cloned.1.call-start = ((), (), s32[]{:S(2)}) async-start(), calls=%async_computation.3 | async-start | bytes 6488064 | tf_op jit(solution)/shard_map/psum | solution.py:292
  458.4 13.9 %copy-start.18 = (bf16[3,8,96,768]{3,2,1,0:T(8,128)(2,1)}, bf16[3,8,96,768]{3,2,1,0:T(8,128)(2,1)S(1)}, u32[]{:S(2)}) copy-start(bf16[3,8,96,768]{3,2,1,0:T(8,128)(2,1)S(1)} %get-tuple-element.114) | copy-start | bytes 10616836
  458.5 13.9 %copy-start.17 = (bf16[3,8,96,768]{3,2,1,0:T(8,128)(2,1)}, bf16[3,8,96,768]{3,2,1,0:T(8,128)(2,1)S(1)}, u32[]{:S(2)}) copy-start(bf16[3,8,96,768]{3,2,1,0:T(8,128)(2,1)S(1)} %get-tuple-element.115) | copy-start | bytes 10616836
  458.9 13.5 %copy-start.26 = (bf16[1920,768]{1,0:T(8,128)(2,1)S(1)}, bf16[1920,768]{1,0:T(8,128)(2,1)}, u32[]{:S(2)}) copy-start(bf16[1920,768]{1,0:T(8,128)(2,1)} %get-tuple-element.45) | copy-start | bytes 8847364
  458.9 43.9 %slice-start = ((s8[5898240]{0:T(1024)(128)(4,1)}), s8[4194304]{0:T(1024)(128)(4,1)S(1)}, s32[]{:S(2)}) async-start(s8[5898240]{0:T(1024)(128)(4,1)} %bitcast.158), calls=%async_computation.4 | async-start | bytes 8388608
  472.4 19.2 %copy-start.19 = (bf16[3,8,96,768]{3,2,1,0:T(8,128)(2,1)S(1)}, bf16[3,8,96,768]{3,2,1,0:T(8,128)(2,1)}, u32[]{:S(2)}) copy-start(bf16[3,8,96,768]{3,2,1,0:T(8,128)(2,1)} %copy-done.18) | copy-start | bytes 10616836
  472.4 30.4 %slice-start.1 = ((s8[5898240]{0:T(1024)(128)(4,1)}), s8[1703936]{0:T(1024)(128)(4,1)S(1)}, s32[]{:S(2)}) async-start(s8[5898240]{0:T(1024)(128)(4,1)} %bitcast.158), calls=%async_computation.5 | async-start | bytes 3407872
  472.4 39.2 %slice-start.8 = ((s8[5898240]{0:T(1024)(128)(4,1)}), s8[4194304]{0:T(1024)(128)(4,1)S(1)}, s32[]{:S(2)}) async-start(s8[5898240]{0:T(1024)(128)(4,1)} %bitcast.166), calls=%async_computation.12 | async-start | bytes 8388608
  491.6 11.3 %copy-start.46 = (bf16[768,768]{1,0:T(8,128)(2,1)S(1)}, bf16[768,768]{1,0:T(8,128)(2,1)}, u32[]{:S(2)}) copy-start(bf16[768,768]{1,0:T(8,128)(2,1)} %param.41) | copy-start | bytes 3538948
  491.6 11.3 %copy-start.62 = (bf16[1920,768]{1,0:T(8,128)(2,1)S(1)}, bf16[1920,768]{1,0:T(8,128)(2,1)}, u32[]{:S(2)}) copy-start(bf16[1920,768]{1,0:T(8,128)(2,1)} %copy-done.61) | copy-start | bytes 8847364
  491.6 20.0 %slice-start.9 = ((s8[5898240]{0:T(1024)(128)(4,1)}), s8[1703936]{0:T(1024)(128)(4,1)S(1)}, s32[]{:S(2)}) async-start(s8[5898240]{0:T(1024)(128)(4,1)} %bitcast.166), calls=%async_computation.13 | async-start | bytes 3407872
  530.6 11.2 %copy-start.21 = (bf16[15,128,12,64]{1,0,3,2:T(8,128)(2,1)S(1)}, bf16[15,128,12,64]{1,0,3,2:T(8,128)(2,1)}, u32[]{:S(2)}) copy-start(bf16[15,128,12,64]{1,0,3,2:T(8,128)(2,1)} %reshape.506) | copy-start | bytes 8847364
  530.6 11.2 %copy-start.22 = (bf16[15,128,12,64]{1,0,3,2:T(8,128)(2,1)S(1)}, bf16[15,128,12,64]{1,0,3,2:T(8,128)(2,1)}, u32[]{:S(2)}) copy-start(bf16[15,128,12,64]{1,0,3,2:T(8,128)(2,1)} %reshape.515) | copy-start | bytes 8847364
  574.8 14.7 %copy-start.12 = (bf16[96,8,15,128]{3,1,2,0:T(8,128)(2,1)}, bf16[96,8,15,128]{3,1,2,0:T(8,128)(2,1)S(1)}, u32[]{:S(2)}) copy-start(bf16[96,8,15,128]{3,1,2,0:T(8,128)(2,1)S(1)} %copy.149) | copy-start | bytes 8847364
  590.6 21.5 %slice-start.12 = ((s8[5898240]{0:T(1024)(128)(4,1)}), s8[4194304]{0:T(1024)(128)(4,1)S(1)}, s32[]{:S(2)}) async-start(s8[5898240]{0:T(1024)(128)(4,1)} %bitcast.170), calls=%async_computation.16 | async-start | bytes 8388608
  599.0 13.1 %slice-start.13 = ((s8[5898240]{0:T(1024)(128)(4,1)}), s8[1703936]{0:T(1024)(128)(4,1)S(1)}, s32[]{:S(2)}) async-start(s8[5898240]{0:T(1024)(128)(4,1)} %bitcast.170), calls=%async_computation.17 | async-start | bytes 3407872
  620.4 15.8 %slice-start.2 = ((s8[5898240]{0:T(1024)(128)(4,1)}), s8[1703936]{0:T(1024)(128)(4,1)S(1)}, s32[]{:S(2)}) async-start(s8[5898240]{0:T(1024)(128)(4,1)} %bitcast.160), calls=%async_computation.6 | async-start | bytes 3407872
  625.2 10.9 %slice-start.3 = ((s8[5898240]{0:T(1024)(128)(4,1)}), s8[4194304]{0:T(1024)(128)(4,1)S(1)}, s32[]{:S(2)}) async-start(s8[5898240]{0:T(1024)(128)(4,1)} %bitcast.160), calls=%async_computation.7 | async-start | bytes 8388608
  625.2 10.9 %copy-start.49 = (bf16[768,768]{1,0:T(8,128)(2,1)S(1)}, bf16[768,768]{1,0:T(8,128)(2,1)}, u32[]{:S(2)}) copy-start(bf16[768,768]{1,0:T(8,128)(2,1)} %param.43) | copy-start | bytes 3538948
  625.3 10.9 %copy-start.58 = (f32[768]{0:T(1024)S(1)}, f32[768]{0:T(1024)}, u32[]{:S(2)}) copy-start(f32[768]{0:T(1024)} %param.44) | copy-start | bytes 9220
  625.3 10.9 %copy-start.60 = (bf16[1920,768]{1,0:T(8,128)(2,1)S(1)}, bf16[1920,768]{1,0:T(8,128)(2,1)}, u32[]{:S(2)}) copy-start(bf16[1920,768]{1,0:T(8,128)(2,1)} %copy-done.59) | copy-start | bytes 8847364
  636.2 74.8 %copy-start.1 = (bf16[1000,768]{1,0:T(8,128)(2,1)S(1)}, bf16[1000,768]{1,0:T(8,128)(2,1)}, u32[]{:S(2)}) copy-start(bf16[1000,768]{1,0:T(8,128)(2,1)} %param.29) | copy-start | bytes 4608004
  694.6 14.8 %copy-start.35 = (f32[768,192]{0,1:T(8,128)S(1)}, f32[768,192]{0,1:T(8,128)}, u32[]{:S(2)}) copy-start(f32[768,192]{0,1:T(8,128)} %get-tuple-element.123) | copy-start | bytes 1769476
  694.6 15.6 %copy-start.34 = (f32[192,768]{1,0:T(8,128)S(1)}, f32[192,768]{1,0:T(8,128)}, u32[]{:S(2)}) copy-start(f32[192,768]{1,0:T(8,128)} %get-tuple-element.125) | copy-start | bytes 1769476
  (51 other events, 259.3 us)
Sparse Core Ops, SparseCore 0:
  14.1 87.6 all-gather.2
  220.1 85.1 all-reduce.6
  308.8 127.6 all-gather.4
  625.3 69.1 all-reduce.8

commit v11 on v10

--- a/solution.py
+++ b/solution.py
@@ -84,10 +84,24 @@
     return (jnp.stack(blocks) * one).astype(dtype).reshape((n_mp - 1) * n_dp * rows, width)
 
 
-def bias_block(vectors, width, n_dp):
-    row = jnp.concatenate(vectors)
-    row = jnp.pad(row, (0, width - row.shape[0]))
-    return jnp.zeros((n_dp, width), jnp.float32).at[0].set(row)
+def gather_biases(shards):
+    n_mp = lax.axis_size("mp")
+    me = lax.axis_index("mp")
+    own = jnp.concatenate(shards)
+    got = [own] + [
+        lax.ppermute(own, "mp", [(i, (i + step) % n_mp) for i in range(n_mp)])
+        for step in range(1, n_mp)
+    ]
+    got = jnp.stack(got)
+    by_shard = jnp.take(got, (me - jnp.arange(n_mp)) % n_mp, axis=0)
+    by_other = jnp.take(got, (-jnp.arange(1, n_mp)) % n_mp, axis=0)
+    out, at = [], 0
+    for i, shard in enumerate(shards):
+        width = shard.shape[0]
+        source = by_other if i == len(shards) - 1 else by_shard
+        out.append(source[:, at : at + width].reshape(-1))
+        at += width
+    return out
 
 
 def own_columns(values, width):
@@ -122,35 +136,32 @@
     qkv_width = w_query_shard.shape[1]
     ff_width = w_up_shard.shape[1]
     one = 1.0 + 0.0 * ln1_gain[0]
-    n_dp = lax.axis_size("dp")
     low_type = jnp.bfloat16
-    q_part, k_part, v_part, o_part, qv_bias = gather_pieces(
+    q_part, k_part, v_part, o_part = gather_pieces(
         (
             w_query_shard.T,
             w_key_shard.T,
             w_value_shard.T,
             w_out_shard,
-            bias_block((b_query_shard, b_value_shard), model_width, n_dp),
         ),
         one,
     )
     w_query_t = whole_rows(q_part, one, low_type)
     w_key_t = whole_rows(k_part, one, low_type)
     w_value_t = whole_rows(v_part, one, low_type)
-    b_query = (qv_bias[:, 0, 0, :qkv_width] * one).reshape(-1)
-    b_value = (qv_bias[:, 0, 0, qkv_width : 2 * qkv_width] * one).reshape(-1)
-    up_part, down_part, up_bias = gather_pieces(
+    b_query, b_value, b_up_others = gather_biases(
+        (b_query_shard, b_value_shard, b_up_shard)
+    )
+    up_part, down_part = gather_pieces(
         (
             w_up_shard.T,
             w_down_shard,
-            bias_block((b_up_shard,), model_width, n_dp),
         ),
         one,
     )
     w_out = whole_rows(o_part, one, low_type)
     w_up_others = other_rows(up_part, one, low_type)
     w_down_others = other_rows(down_part, one, low_type)
-    b_up_others = other_rows(up_bias[:, :1, :1, :], one, jnp.float32).reshape(-1)
     heads = w_query_t.shape[0] // HD
     scaling = 1.0 / math.sqrt(HD)
     head_shape = (row_count, seq_len, heads, HD)

time: 723 us -> 705 us (0.975)
  waiting for transfers between devices: 332 us -> 314 us
    all_gather x2, waiting for transfers between devices: 196 us -> 179 us  [gather_pieces(): got = lax.all_gather(sent, ('mp', 'dp'), axis=0)]
    unnamed x167 -> x161, local copies, waits for them, and re-layouts: 19.4 us -> 17.2 us
  transfers between devices with their start and end apart: 4 -> 7, of which waited for: 4 -> 4; matrix products, arithmetic and copies ran while one was open for 6% -> 6% of each run, Pallas kernels for 0% -> 0%
where the time goes in v11:
time: 705 us; the launch traced here: 700 us
  waiting for transfers between devices  314 us (45%)
  matrix products  177 us (25%)
  local copies, waits for them, and re-layouts  110 us (16%)
  other arithmetic  76 us (11%)
  between operations  16.5 us (2%)
    all_gather x2, waiting for transfers between devices, gather_pieces(): got = lax.all_gather(sent, ('mp', 'dp'), axis=0)  179 us
    psum x1, waiting for transfers between devices, on_device(): lax.psum(jnp.concatenate([grad_w_down, grad_w_up], axis=0), 'dp')  81.7 us
    dot_general x8, matrix products, over_cols(): lax.dot_general(left, right, CONTRACT_COLS, preferred_element_type=jnp.fl...  63.2 us
    psum x1, waiting for transfers between devices, on_device(): lax.psum((grad_w_query + tie, grad_w_key, grad_w_value, grad_w_out, packe...  53.7 us
    dot_general x8, matrix products, product(): return jnp.dot(left, right, preferred_element_type=jnp.float32)  51.2 us
    dot_general x6, matrix products, over_rows(): lax.dot_general(left, right, CONTRACT_ROWS, preferred_element_type=jnp.fl...  17.2 us
    unnamed x161, local copies, waits for them, and re-layouts  17.2 us
    sub x1, other arithmetic, on_device(): powers = jnp.exp(scores - row_max)  15.8 us
  transfers between devices with their start and end apart: 7, of which 4 were waited for; matrix products, arithmetic and copies ran while one was open for 6% of the time, Pallas kernels for 0%

profile of v11, /device:TPU:0, one launch (start us, length us, event | category | flops | bytes accessed | tf_op | source)
XLA Modules:
  0.0 700.0 jit_solution(5105220729311640514)
XLA Ops:
  13.2 5.1 collective-permute-start.2
  39.0 57.8 %all-gather.3.cloned.1.call-done = f32[32,96,768]{2,1,0:T(8,128)} async-done(((f32[1,96,768]{2,1,0:T(8,128)}), f32[32,96,768]{2,1,0:T(8,128)}) %all-gather.3.cloned.1.call-update) | async-done | bytes 9437200 | tf_op jit(solution)/shard_map/all_gather | solution.py:61
  96.8 6.2 fusion.24
  111.8 6.0 reshape.506
  117.9 5.9 convolution_convert_fusion.1
  123.8 4.8 copy.82
  128.6 6.1 reshape.510
  134.7 5.9 add_convert_fusion.5
  145.2 6.6 reshape.508
  151.8 10.3 %fusion.20 = f32[15,12,128,128]{2,3,1,0:T(8,128)} fusion(bf16[15,128,12,64]{1,0,3,2:T(8,128)(2,1)} %reshape.510, bf16[15,128,12,64]{1,0,3,2:T(8,128)(2,1)} %reshape.508), kind=kOutput, calls=%fused_computation.71 | convolution fusion | flops 377487360 | bytes 17694720 | tf_op jit(solution)/shard_map/rqhe,rkhe->rhqk/dot_general | solution.py:47
  162.1 15.8 %fusion.75 = (f32[15,12,128]{2,1,0:T(8,128)S(1)}, f32[15,12,128,128]{2,3,1,0:T(8,128)}) fusion(f32[15,12,128,128]{2,3,1,0:T(8,128)} %fusion.20, pred[15,128,128]{1,2,0:T(8,128)(4,1)S(1)} %or_and_fusion), kind=kOutput, calls=%fused_computation.180 | output fusion | flops 17694848 | bytes 23930880 | tf_op jit(solution)/shard_map/sub | solution.py:185
  178.6 6.9 convert_bitcast_fusion.1
  198.5 5.9 convert_reduce_fusion
  216.0 81.7 %all-reduce.4.cloned.1.call-done = f32[1536,768]{1,0:T(8,128)} async-done(((f32[1536,768]{1,0:T(8,128)}), f32[1536,768]{1,0:T(8,128)}) %all-reduce.4.cloned.1.call-update) | async-done | bytes 4718608 | tf_op jit(solution)/shard_map/psum | solution.py:215
  299.5 4.9 fusion.72
  304.4 120.8 %all-gather.5.cloned.1.call-done = f32[32,192,768]{2,1,0:T(8,128)} async-done(((f32[1,192,768]{2,1,0:T(8,128)}), f32[32,192,768]{2,1,0:T(8,128)}) %all-gather.5.cloned.1.call-update) | async-done | bytes 18874384 | tf_op jit(solution)/shard_map/all_gather | solution.py:61
  425.2 11.6 %fusion.71 = (f32[4,8,96,768]{3,2,1,0:T(8,128)S(1)}, f32[4,8,96,768]{3,2,1,0:T(8,128)}) fusion(f32[4,8,192,768]{3,2,1,0:T(8,128)} %bitcast.170), kind=kLoop, calls=%fused_computation.176 | loop fusion | bytes 37748736 | tf_op jit(solution)/shard_map/slice | solution.py:67
  442.8 13.1 %multiply_convert_fusion = (bf16[1920,2304]{1,0:T(8,128)(2,1)}, f32[1920,2304]{1,0:T(8,128)}) fusion(f32[2304]{0:T(1024)S(1)} %add.350, bf16[1920,768]{1,0:T(8,128)(2,1)S(1)} %copy-done.21, bf16[2304,768]{1,0:T(8,128)(2,1)S(1)} %bitcast.192), kind=kOutput, calls=%fused_computation.5 | convolution fusion | flops 6821314560 | bytes 33039360 | tf_op jit(solution)/shard_map/dot_general | solution.py:37
  455.9 18.1 %add_convert_fusion = bf16[1920,2304]{1,0:T(8,128)(2,1)} fusion(f32[1920,2304]{1,0:T(8,128)} %get-tuple-element.82, f32[2304]{0:T(1024)S(1)} %add.350, bf16[1920,768]{1,0:T(8,128)(2,1)S(1)} %copy-done.24, bf16[2304,768]{1,0:T(8,128)(2,1)S(1)} %bitcast.190), kind=kOutput, calls=%fused_computation.4 | convolution fusion | flops 6856704000 | bytes 33039360 | tf_op jit(solution)/shard_map/dot_general | solution.py:37
  474.0 11.3 %fusion.79 = f32[1920,768]{1,0:T(8,128)} fusion(bf16[1920,2304]{1,0:T(8,128)(2,1)} %add_convert_fusion, bf16[2304,768]{1,0:T(8,128)(2,1)S(1)} %bitcast.193), kind=kOutput, calls=%fused_computation.184 | convolution fusion | flops 6794772480 | bytes 18284544 | tf_op jit(solution)/shard_map/dot_general | solution.py:29
  485.3 5.9 multiply_reduce_fusion.1
  506.9 6.0 reshape.514
  512.9 11.2 %convert_bitcast_fusion = bf16[15,128,12,64]{1,3,2,0:T(8,128)(2,1)} fusion(bf16[15,128,12,64]{1,0,3,2:T(8,128)(2,1)} %reshape.514, f32[15,12,128,128]{2,3,1,0:T(8,128)} %get-tuple-element.78, f32[15,12,128]{2,1,0:T(8,128)S(1)} %copy-done.37), kind=kOutput, calls=%fused_computation.59 | convolution fusion | flops 384860160 | bytes 17786880 | tf_op jit(solution)/shard_map/rhqk,rqhe->rkhe/dot_general | solution.py:247
  524.1 8.8 %multiply_reduce_fusion = (f32[15,12,128]{2,1,0:T(8,128)S(1)}, f32[15,12,128,128]{2,3,1,0:T(8,128)}) fusion(f32[15,12,128,128]{2,3,1,0:T(8,128)} %get-tuple-element.78, f32[15,12,128]{2,1,0:T(8,128)S(1)} %copy-done.37, bf16[15,128,12,64]{1,0,3,2:T(8,128)(2,1)S(1)} %copy-done.18, bf16[15,128,12,64]{1,0,3,2:T(8,128)(2,1)S(1)} %copy-done.19), kind=kOutput, calls=%fused_computation.8 | convolution fusion | flops 386311680 | bytes 29675520 | tf_op jit(solution)/shard_map/rqhe,rkhe->rhqk/dot_general | solution.py:234
  532.9 9.5 %multiply_convert_fusion.1 = bf16[15,12,128,128]{2,3,1,0:T(8,128)(2,1)S(1)} fusion(f32[15,12,128,128]{2,3,1,0:T(8,128)} %get-tuple-element.85, f32[15,12,128]{2,1,0:T(8,128)S(1)} %get-tuple-element.84, f32[15,12,128,128]{2,3,1,0:T(8,128)} %get-tuple-element.78, f32[15,12,128]{2,1,0:T(8,128)S(1)} %copy-done.37), kind=kLoop, calls=%fused_computation.7 | loop fusion | flops 11796480 | bytes 29675520 | tf_op jit(solution)/shard_map/convert_element_type | solution.py:238
  544.4 5.6 fusion.9
  557.1 5.0 fusion.80
  566.2 5.5 fusion.81
  573.0 8.4 %multiply_reduce_fusion.2 = (f32[768]{0:T(1024)S(1)}, f32[1920]{0:T(1024)S(1)}, f32[768]{0:T(1024)S(1)}, f32[1920,768]{1,0:T(8,128)}) fusion(f32[15,128,768]{2,1,0:T(8,128)S(1)} %bitcast.158, f32[1920]{0:T(1024)S(1)} %copy-done.38, f32[1920]{0:T(1024)S(1)} %copy-done.39, f32[768]{0:T(1024)S(1)} %copy-done.41, bf16[1920,768]{0,1:T(8,128)(2,1)S(1)} %bitcast.172, ...), kind=kOutput, calls=%fused_computation.25 | convolution fusion | flops 2279666432 | bytes 27753984 | tf_op jit(solution)/shard_map/dot_general | solution.py:29
  581.4 5.2 fusion.69
  607.7 10.9 %fusion.78 = f32[1920,768]{1,0:T(8,128)S(1)} fusion(bf16[1920,2304]{1,0:T(8,128)(2,1)} %get-tuple-element.81, bf16[2304,768]{1,0:T(8,128)(2,1)} %bitcast.191), kind=kOutput, calls=%fused_computation.183 | convolution fusion | flops 6794772480 | bytes 18284544 | tf_op jit(solution)/shard_map/dot_general | solution.py:29
  623.3 53.7 %all-reduce.6.cloned.1.call-done = (f32[1030,192]{0,1:T(8,128)}, f32[768,192]{0,1:T(8,128)}, f32[768,192]{0,1:T(8,128)}, f32[768,192]{0,1:T(8,128)}, f32[192,768]{1,0:T(8,128)}) async-done(((f32[1030,192]{0,1:T(8,128)}, f32[768,192]{0,1:T(8,128)}, f32[768,192]{0,1:T(8,128)}, f32[768,192]{0,1:T(8,128)}, f32[192,768]{1,0:T(8,128)}), (f32[1030,192]{0,1:T(8,128)}, f32[768,192]{0,1:T(8,128)}, ...) | async-done | bytes 3150352 | tf_op jit(solution)/shard_map/psum | solution.py:303
  (285 shorter events, 143.0 us)
Async XLA Ops:
  7.2 12.8 %copy-start = (bf16[1000,768]{1,0:T(8,128)(2,1)S(1)}, bf16[1000,768]{1,0:T(8,128)(2,1)}, u32[]{:S(2)}) copy-start(bf16[1000,768]{1,0:T(8,128)(2,1)} %param.25) | copy-start | bytes 4608004
  7.2 22.3 %copy-start.40 = (f32[768]{0:T(1024)S(1)}, f32[768]{0:T(1024)}, u32[]{:S(2)}) copy-start(f32[768]{0:T(1024)} %param.26) | copy-start | bytes 9220
  7.2 21.2 %copy-start.42 = (s32[15,128]{1,0:T(8,128)S(1)}, s32[15,128]{1,0:T(8,128)}, u32[]{:S(2)}) copy-start(s32[15,128]{1,0:T(8,128)} %param.23) | copy-start | bytes 23044
  7.2 22.3 %copy-start.48 = (f32[768]{0:T(1024)S(1)}, f32[768]{0:T(1024)}, u32[]{:S(2)}) copy-start(f32[768]{0:T(1024)} %param.27) | copy-start | bytes 9220
  7.2 89.5 %all-gather.3.cloned.1.call-start = ((), (), s32[]{:S(2)}) async-start(), calls=%async_computation | async-start | bytes 9732096 | tf_op jit(solution)/shard_map/all_gather | solution.py:61
  12.3 285.3 %all-reduce.4.cloned.1.call-start = ((), (), s32[]{:S(2)}) async-start(), calls=%async_computation.2 | async-start | bytes 9437184 | tf_op jit(solution)/shard_map/psum | solution.py:215
  13.2 24.8 %collective-permute-start.2 = (f32[1152]{0:T(1024)S(1)}, f32[1152]{0:T(1024)S(1)}, u32[]{:S(2)}, u32[]{:S(2)}) collective-permute-start(f32[1152]{0:T(1024)S(1)} %concatenate.56), channel_id=1, source_target_pairs={{0,3},{1,0},{2,1},{3,2},{4,7},{5,4},{6,5},{7,6},{8,11},{9,8},{10,9... | collective-permute-start | bytes 13832 | tf_op jit(solution)/shard_map/ppermute | solution.py:92
  18.3 19.8 %collective-permute-start.1 = (f32[1152]{0:T(1024)S(1)}, f32[1152]{0:T(1024)S(1)}, u32[]{:S(2)}, u32[]{:S(2)}) collective-permute-start(f32[1152]{0:T(1024)S(1)} %concatenate.56), channel_id=1, source_target_pairs={{0,2},{1,3},{2,0},{3,1},{4,6},{5,7},{6,4},{7,5},{8,10},{9,11},{10,... | collective-permute-start | bytes 13832 | tf_op jit(solution)/shard_map/ppermute | solution.py:92
  18.3 19.8 %collective-permute-start = (f32[1152]{0:T(1024)S(1)}, f32[1152]{0:T(1024)S(1)}, u32[]{:S(2)}, u32[]{:S(2)}) collective-permute-start(f32[1152]{0:T(1024)S(1)} %concatenate.56), channel_id=1, source_target_pairs={{0,1},{1,2},{2,3},{3,0},{4,5},{5,6},{6,7},{7,4},{8,9},{9,10},{10,1... | collective-permute-start | bytes 13832 | tf_op jit(solution)/shard_map/ppermute | solution.py:92
  28.4 186.3 %copy-start.34 = (f32[15,128]{1,0:T(8,128)}, f32[15,128]{1,0:T(8,128)S(1)}, u32[]{:S(2)}) copy-start(f32[15,128]{1,0:T(8,128)S(1)} %multiply_reduce_fusion.6) | copy-start | bytes 23044
  103.0 14.9 %copy-start.27 = (bf16[4,8,24,768]{3,2,1,0:T(8,128)(2,1)}, bf16[4,8,24,768]{3,2,1,0:T(8,128)(2,1)S(1)}, u32[]{:S(2)}) copy-start(bf16[4,8,24,768]{3,2,1,0:T(8,128)(2,1)S(1)} %get-tuple-element.54) | copy-start | bytes 3538948
  162.1 16.5 %copy-start.17 = (bf16[15,128,12,64]{1,0,3,2:T(8,128)(2,1)S(1)}, bf16[15,128,12,64]{1,0,3,2:T(8,128)(2,1)}, u32[]{:S(2)}) copy-start(bf16[15,128,12,64]{1,0,3,2:T(8,128)(2,1)} %reshape.506) | copy-start | bytes 8847364
  178.0 11.2 %slice-start = ((s8[5898240]{0:T(1024)(128)(4,1)}), s8[4194304]{0:T(1024)(128)(4,1)S(1)}, s32[]{:S(2)}) async-start(s8[5898240]{0:T(1024)(128)(4,1)} %bitcast.155), calls=%async_computation.4 | async-start | bytes 8388608
  212.4 212.8 %all-gather.5.cloned.1.call-start = ((), (), s32[]{:S(2)}) async-start(), calls=%async_computation.1 | async-start | bytes 19464192 | tf_op jit(solution)/shard_map/all_gather | solution.py:61
  214.6 462.4 %all-reduce.6.cloned.1.call-start = ((), (), s32[]{:S(2)}) async-start(), calls=%async_computation.3 | async-start | bytes 6488064 | tf_op jit(solution)/shard_map/psum | solution.py:303
  442.4 13.5 %copy-start.16 = (bf16[3,8,96,768]{3,2,1,0:T(8,128)(2,1)}, bf16[3,8,96,768]{3,2,1,0:T(8,128)(2,1)S(1)}, u32[]{:S(2)}) copy-start(bf16[3,8,96,768]{3,2,1,0:T(8,128)(2,1)S(1)} %get-tuple-element.90) | copy-start | bytes 10616836
  442.8 13.1 %copy-start.24 = (bf16[1920,768]{1,0:T(8,128)(2,1)S(1)}, bf16[1920,768]{1,0:T(8,128)(2,1)}, u32[]{:S(2)}) copy-start(bf16[1920,768]{1,0:T(8,128)(2,1)} %get-tuple-element.21) | copy-start | bytes 8847364
  442.8 42.5 %slice-start.4 = ((s8[5898240]{0:T(1024)(128)(4,1)}), s8[4194304]{0:T(1024)(128)(4,1)S(1)}, s32[]{:S(2)}) async-start(s8[5898240]{0:T(1024)(128)(4,1)} %bitcast.159), calls=%async_computation.8 | async-start | bytes 8388608
  455.9 29.3 %slice-start.5 = ((s8[5898240]{0:T(1024)(128)(4,1)}), s8[1703936]{0:T(1024)(128)(4,1)S(1)}, s32[]{:S(2)}) async-start(s8[5898240]{0:T(1024)(128)(4,1)} %bitcast.159), calls=%async_computation.9 | async-start | bytes 3407872
  455.9 38.1 %slice-start.8 = ((s8[5898240]{0:T(1024)(128)(4,1)}), s8[4194304]{0:T(1024)(128)(4,1)S(1)}, s32[]{:S(2)}) async-start(s8[5898240]{0:T(1024)(128)(4,1)} %bitcast.163), calls=%async_computation.12 | async-start | bytes 8388608
  474.0 11.3 %copy-start.44 = (bf16[768,768]{1,0:T(8,128)(2,1)S(1)}, bf16[768,768]{1,0:T(8,128)(2,1)}, u32[]{:S(2)}) copy-start(bf16[768,768]{1,0:T(8,128)(2,1)} %param.37) | copy-start | bytes 3538948
  474.0 11.3 %copy-start.59 = (bf16[1920,768]{1,0:T(8,128)(2,1)S(1)}, bf16[1920,768]{1,0:T(8,128)(2,1)}, u32[]{:S(2)}) copy-start(bf16[1920,768]{1,0:T(8,128)(2,1)} %copy-done.58) | copy-start | bytes 8847364
  474.0 20.0 %slice-start.9 = ((s8[5898240]{0:T(1024)(128)(4,1)}), s8[1703936]{0:T(1024)(128)(4,1)S(1)}, s32[]{:S(2)}) async-start(s8[5898240]{0:T(1024)(128)(4,1)} %bitcast.163), calls=%async_computation.13 | async-start | bytes 3407872
  512.9 11.2 %copy-start.18 = (bf16[15,128,12,64]{1,0,3,2:T(8,128)(2,1)S(1)}, bf16[15,128,12,64]{1,0,3,2:T(8,128)(2,1)}, u32[]{:S(2)}) copy-start(bf16[15,128,12,64]{1,0,3,2:T(8,128)(2,1)} %reshape.506) | copy-start | bytes 8847364
  512.9 11.2 %copy-start.19 = (bf16[15,128,12,64]{1,0,3,2:T(8,128)(2,1)S(1)}, bf16[15,128,12,64]{1,0,3,2:T(8,128)(2,1)}, u32[]{:S(2)}) copy-start(bf16[15,128,12,64]{1,0,3,2:T(8,128)(2,1)} %reshape.514) | copy-start | bytes 8847364
  557.1 14.6 %copy-start.11 = (bf16[96,8,15,128]{3,1,2,0:T(8,128)(2,1)}, bf16[96,8,15,128]{3,1,2,0:T(8,128)(2,1)S(1)}, u32[]{:S(2)}) copy-start(bf16[96,8,15,128]{3,1,2,0:T(8,128)(2,1)S(1)} %copy.148) | copy-start | bytes 8847364
  573.0 21.5 %slice-start.12 = ((s8[5898240]{0:T(1024)(128)(4,1)}), s8[4194304]{0:T(1024)(128)(4,1)S(1)}, s32[]{:S(2)}) async-start(s8[5898240]{0:T(1024)(128)(4,1)} %bitcast.167), calls=%async_computation.16 | async-start | bytes 8388608
  581.4 13.1 %slice-start.13 = ((s8[5898240]{0:T(1024)(128)(4,1)}), s8[1703936]{0:T(1024)(128)(4,1)S(1)}, s32[]{:S(2)}) async-start(s8[5898240]{0:T(1024)(128)(4,1)} %bitcast.167), calls=%async_computation.17 | async-start | bytes 3407872
  602.8 15.8 %slice-start.6 = ((s8[5898240]{0:T(1024)(128)(4,1)}), s8[1703936]{0:T(1024)(128)(4,1)S(1)}, s32[]{:S(2)}) async-start(s8[5898240]{0:T(1024)(128)(4,1)} %bitcast.161), calls=%async_computation.10 | async-start | bytes 3407872
  618.6 74.7 %copy-start.1 = (bf16[1000,768]{1,0:T(8,128)(2,1)S(1)}, bf16[1000,768]{1,0:T(8,128)(2,1)}, u32[]{:S(2)}) copy-start(bf16[1000,768]{1,0:T(8,128)(2,1)} %param.25) | copy-start | bytes 4608004
  677.0 14.7 %copy-start.33 = (f32[768,192]{0,1:T(8,128)S(1)}, f32[768,192]{0,1:T(8,128)}, u32[]{:S(2)}) copy-start(f32[768,192]{0,1:T(8,128)} %get-tuple-element.98) | copy-start | bytes 1769476
  677.0 15.5 %copy-start.32 = (f32[192,768]{1,0:T(8,128)S(1)}, f32[192,768]{1,0:T(8,128)}, u32[]{:S(2)}) copy-start(f32[192,768]{1,0:T(8,128)} %get-tuple-element.100) | copy-start | bytes 1769476
  (51 other events, 291.2 us)
Sparse Core Ops, SparseCore 0:
  12.5 84.2 all-gather.2
  212.5 85.0 all-reduce.3
  301.1 124.0 all-gather.4
  607.8 69.1 all-reduce.5

commit v12 on v11

--- a/solution.py
+++ b/solution.py
@@ -205,15 +205,15 @@
     grad_out = cotangent.reshape(token_count, model_width).astype(jnp.float32)
     grad_out = grad_out * valid_mask.reshape(token_count, 1).astype(jnp.float32)
     grad_out_low = grad_out.astype(low_type)
-    grad_out, grad_out_low = lax.optimization_barrier((grad_out, grad_out_low))
+    grad_b_down = jnp.sum(grad_out, axis=0)
+    grad_out, grad_out_low, grad_b_down = lax.optimization_barrier(
+        (grad_out, grad_out_low, grad_b_down)
+    )
     grad_w_down = over_rows(hidden_own, grad_out_low)
-    grad_b_down = jnp.sum(grad_out, axis=0)
     (grad_upper_own,) = gelu_pull_own(over_cols(grad_out_low, w_down_shard))
     grad_upper_own = grad_upper_own.astype(low_type)
     grad_w_up = over_rows(normed2_low, grad_upper_own)
     grad_b_up = column_sum(grad_upper_own)
-    ffn_grads = lax.psum(jnp.concatenate([grad_w_down, grad_w_up], axis=0), "dp")
-    grad_w_down, grad_w_up = ffn_grads[:ff_width], ffn_grads[ff_width:]
     grad_normed2_own = over_cols(grad_upper_own, w_up_shard)
     upper = over_cols(normed2_low, w_up_others) + b_up_others
     activated, gelu_pull = jax.vjp(exact_gelu, upper)
@@ -229,6 +229,20 @@
     grad_mid_low = grad_middle.astype(low_type)
     grad_w_out = over_rows(own_columns(mixed, qkv_width), grad_mid_low)
     grad_b_out = column_sum(grad_mid_low)
+    early_rows = jnp.stack(
+        [grad_b_down, grad_b_up, grad_ln2_gain, grad_ln2_shift, grad_b_out]
+    )
+    early_rows = jnp.pad(early_rows, ((0, 8 - early_rows.shape[0]), (0, 0)))
+    ffn_grads = lax.psum(
+        jnp.concatenate([grad_w_down, grad_w_up, grad_w_out, early_rows], axis=0), "dp"
+    )
+    grad_w_down = ffn_grads[:ff_width]
+    grad_w_up = ffn_grads[ff_width : 2 * ff_width]
+    grad_w_out = ffn_grads[2 * ff_width : 2 * ff_width + qkv_width]
+    early_rows = ffn_grads[2 * ff_width + qkv_width :]
+    grad_b_down, grad_b_up, grad_ln2_gain, grad_ln2_shift, grad_b_out = [
+        early_rows[i] for i in range(5)
+    ]
     grad_mixed = over_cols(grad_mid_low, w_out).astype(low_type).reshape(head_shape)
     soft_again = probabilities
     grad_soft = jnp.einsum(
@@ -285,11 +299,6 @@
         grad_ln1_shift,
         grad_b_query,
         grad_b_value,
-        grad_b_out,
-        grad_b_down,
-        grad_b_up,
-        grad_ln2_gain,
-        grad_ln2_shift,
     )
     small_rows = jnp.concatenate(small).reshape(-1, column_count)
     packed = jnp.concatenate([table_grad, small_rows], axis=0)
@@ -298,14 +307,12 @@
         grad_w_query,
         grad_w_key,
         grad_w_value,
-        grad_w_out,
         packed,
     ) = lax.psum(
         (
             grad_w_query + tie,
             grad_w_key,
             grad_w_value,
-            grad_w_out,
             packed,
         ),
         "dp",
@@ -316,17 +323,7 @@
     for item in small:
         unpacked.append(flat_small[at : at + item.shape[0]])
         at += item.shape[0]
-    (
-        grad_ln1_gain,
-        grad_ln1_shift,
-        grad_b_query,
-        grad_b_value,
-        grad_b_out,
-        grad_b_down,
-        grad_b_up,
-        grad_ln2_gain,
-        grad_ln2_shift,
-    ) = unpacked
+    grad_ln1_gain, grad_ln1_shift, grad_b_query, grad_b_value = unpacked
     return (
         output,
         input_grad,

time: 705 us -> 554 us (0.79)
  waiting for transfers between devices: 314 us -> 136 us
  matrix products: 177 us -> 195 us
  other arithmetic: 76 us -> 84.9 us
    all_gather x2, waiting for transfers between devices: 179 us -> 58.9 us  [gather_pieces(): got = lax.all_gather(sent, ('mp', 'dp'), axis=0)]
    psum x2, waiting for transfers between devices: 135 us -> 77.4 us  [the longest x1 51.3 us: on_device(): lax.psum((grad_w_query + tie, grad_w_key, grad_w_value, packed), 'dp')]
    dot_general x8, matrix products: 51.2 us -> 61.1 us  [product(): return jnp.dot(left, right, preferred_element_type=jnp.float32)]
    unnamed x161 -> x145, local copies, waits for them, and re-layouts: 17.2 us -> 19.5 us
  transfers between devices with their start and end apart: 7 -> 7, of which waited for: 4 -> 4; matrix products, arithmetic and copies ran while one was open for 6% -> 40% of each run, Pallas kernels for 0% -> 0%
where the time goes in v12:
time: 554 us; the launch traced here: 549 us
  matrix products  195 us (35%)
  waiting for transfers between devices  136 us (25%)
  local copies, waits for them, and re-layouts  109 us (20%)
  other arithmetic  84.9 us (15%)
  between operations  16.5 us (3%)
  starting transfers between devices  7.36 us (1%)
    dot_general x8, matrix products, over_cols(): lax.dot_general(left, right, CONTRACT_COLS, preferred_element_type=jnp.fl...  62.8 us
    dot_general x8, matrix products, product(): return jnp.dot(left, right, preferred_element_type=jnp.float32)  61.1 us
    all_gather x2, waiting for transfers between devices, gather_pieces(): got = lax.all_gather(sent, ('mp', 'dp'), axis=0)  58.9 us
    psum x1, waiting for transfers between devices, on_device(): lax.psum((grad_w_query + tie, grad_w_key, grad_w_value, packed), 'dp')  51.3 us
    psum x1, waiting for transfers between devices, on_device(): lax.psum(jnp.concatenate([grad_w_down, grad_w_up, grad_w_out, early_rows]...  26.1 us
    dot_general x6, matrix products, over_rows(): lax.dot_general(left, right, CONTRACT_ROWS, preferred_element_type=jnp.fl...  21.5 us
    unnamed x145, local copies, waits for them, and re-layouts  19.5 us
    sub x1, other arithmetic, on_device(): powers = jnp.exp(scores - row_max)  18.5 us
  transfers between devices with their start and end apart: 7, of which 4 were waited for; matrix products, arithmetic and copies ran while one was open for 40% of the time, Pallas kernels for 0%

profile of v12, /device:TPU:0, one launch (start us, length us, event | category | flops | bytes accessed | tf_op | source)
XLA Modules:
  0.0 548.9 jit_solution(15486584183545656754)
XLA Ops:
  45.4 51.5 %all-gather.3.cloned.1.call-done = f32[32,96,768]{2,1,0:T(8,128)} async-done(((f32[1,96,768]{2,1,0:T(8,128)}), f32[32,96,768]{2,1,0:T(8,128)}) %all-gather.3.cloned.1.call-update) | async-done | bytes 9437200 | tf_op jit(solution)/shard_map/all_gather | solution.py:61
  96.8 5.8 %fusion.24 = (bf16[4,8,24,768]{3,2,1,0:T(8,128)(2,1)}, bf16[4,8,24,768]{3,2,1,0:T(8,128)(2,1)S(1)}, bf16[4,8,24,768]{3,2,1,0:T(8,128)(2,1)S(1)}, bf16[4,8,24,768]{3,2,1,0:T(8,128)(2,1)S(1)}) fusion(f32[4,8,96,768]{3,2,1,0:T(8,128)} %bitcast.176, f32[]{:T(128)} %bitcast.9), kind=kLoop, calls=%fused_computation.78 | loop fusion | flops 4718592 | bytes 14155780 | tf_op jit(solution)/shard_map/convert_element_type | solution.py:74
  107.9 4.7 copy.76
  112.6 6.0 %reshape.512 = bf16[15,128,12,64]{1,0,3,2:T(8,128)(2,1)} reshape(bf16[1920,768]{0,1:T(8,128)(2,1)} %copy.76) | data formatting | bytes 5898240 | tf_op jit(solution)/shard_map/reshape | solution.py:175
  118.6 6.0 %convolution_convert_fusion.1 = bf16[1920,768]{1,0:T(8,128)(2,1)} fusion(bf16[1920,768]{1,0:T(8,128)(2,1)} %bitcast.192, bf16[768,768]{1,0:T(8,128)(2,1)S(1)} %bitcast.197), kind=kOutput, calls=%fused_computation.53 | convolution fusion | flops 2266398720 | bytes 7077888 | tf_op jit(solution)/shard_map/dot_general | solution.py:37
  129.3 6.3 %reshape.514 = bf16[15,128,12,64]{1,0,3,2:T(8,128)(2,1)} reshape(bf16[1920,768]{0,1:T(8,128)(2,1)} %copy.77) | data formatting | bytes 5898240 | tf_op jit(solution)/shard_map/reshape | solution.py:176
  135.6 5.9 %add_convert_fusion.6 = bf16[1920,768]{1,0:T(8,128)(2,1)} fusion(bf16[1920,768]{1,0:T(8,128)(2,1)} %bitcast.193, bf16[768,768]{1,0:T(8,128)(2,1)S(1)} %bitcast.182, f32[768]{0:T(1024)S(1)} %add.318), kind=kOutput, calls=%fused_computation.44 | convolution fusion | flops 2267873280 | bytes 7080960 | tf_op jit(solution)/shard_map/dot_general | solution.py:37
  146.1 6.0 %reshape.510 = bf16[15,128,12,64]{1,0,3,2:T(8,128)(2,1)} reshape(bf16[1920,768]{0,1:T(8,128)(2,1)} %copy.75) | data formatting | bytes 5898240 | tf_op jit(solution)/shard_map/reshape | solution.py:177
  152.1 10.3 %fusion.20 = f32[15,12,128,128]{2,3,1,0:T(8,128)} fusion(bf16[15,128,12,64]{1,0,3,2:T(8,128)(2,1)} %reshape.514, bf16[15,128,12,64]{1,0,3,2:T(8,128)(2,1)} %reshape.512), kind=kOutput, calls=%fused_computation.73 | convolution fusion | flops 377487360 | bytes 17694720 | tf_op jit(solution)/shard_map/rqhe,rkhe->rhqk/dot_general | solution.py:47
  162.4 18.5 %fusion.76 = (f32[15,12,128]{2,1,0:T(8,128)S(1)}, f32[15,12,128,128]{2,3,1,0:T(8,128)}) fusion(f32[15,12,128,128]{2,3,1,0:T(8,128)} %fusion.20, pred[15,128,128]{1,2,0:T(8,128)(4,1)S(1)} %or_and_fusion), kind=kOutput, calls=%fused_computation.188 | output fusion | flops 17694848 | bytes 23930880 | tf_op jit(solution)/shard_map/sub | solution.py:185
  181.0 6.8 %convert_bitcast_fusion.1 = bf16[15,128,12,64]{1,3,2,0:T(8,128)(2,1)S(1)} fusion(bf16[15,128,12,64]{1,0,3,2:T(8,128)(2,1)S(1)} %copy-done.17, f32[15,12,128,128]{2,3,1,0:T(8,128)} %get-tuple-element.80, f32[15,12,128]{2,1,0:T(8,128)S(1)} %get-tuple-element.79), kind=kOutput, calls=%fused_computation.62 | convolution fusion | flops 384860160 | bytes 17786880 | tf_op jit(solution)/shard_map/rhqk,rkhe->rqhe/dot_general | solution.py:190
  201.0 5.5 convert_reduce_fusion.1
  215.4 7.4 %all-gather.5.cloned.1.call-done = f32[32,192,768]{2,1,0:T(8,128)} async-done(((f32[1,192,768]{2,1,0:T(8,128)}), f32[32,192,768]{2,1,0:T(8,128)}) %all-gather.5.cloned.1.call-update) | async-done | bytes 18874384 | tf_op jit(solution)/shard_map/all_gather | solution.py:61
  222.8 11.2 %fusion.71 = (f32[4,8,96,768]{3,2,1,0:T(8,128)}, f32[4,8,96,768]{3,2,1,0:T(8,128)S(1)}) fusion(f32[4,8,192,768]{3,2,1,0:T(8,128)} %bitcast.168), kind=kLoop, calls=%fused_computation.183 | loop fusion | bytes 37748736 | tf_op jit(solution)/shard_map/slice | solution.py:67
  240.0 13.1 %multiply_convert_fusion = (bf16[1920,2304]{1,0:T(8,128)(2,1)}, f32[1920,2304]{1,0:T(8,128)}) fusion(f32[2304]{0:T(1024)S(1)} %add.350, bf16[1920,768]{1,0:T(8,128)(2,1)S(1)} %copy-done.20, bf16[2304,768]{1,0:T(8,128)(2,1)S(1)} %bitcast.190), kind=kOutput, calls=%fused_computation.5 | convolution fusion | flops 6821314560 | bytes 33039360 | tf_op jit(solution)/shard_map/dot_general | solution.py:37
  253.1 18.1 %add_convert_fusion = bf16[1920,2304]{1,0:T(8,128)(2,1)} fusion(f32[1920,2304]{1,0:T(8,128)} %get-tuple-element.84, f32[2304]{0:T(1024)S(1)} %add.350, bf16[1920,768]{1,0:T(8,128)(2,1)S(1)} %copy-done.22, bf16[2304,768]{1,0:T(8,128)(2,1)S(1)} %bitcast.188), kind=kOutput, calls=%fused_computation.4 | convolution fusion | flops 6856704000 | bytes 33039360 | tf_op jit(solution)/shard_map/dot_general | solution.py:37
  271.3 11.4 %fusion.80 = f32[1920,768]{1,0:T(8,128)} fusion(bf16[1920,2304]{1,0:T(8,128)(2,1)} %add_convert_fusion, bf16[2304,768]{1,0:T(8,128)(2,1)S(1)} %bitcast.191), kind=kOutput, calls=%fused_computation.192 | convolution fusion | flops 6794772480 | bytes 18284544 | tf_op jit(solution)/shard_map/dot_general | solution.py:29
  282.7 5.9 %multiply_reduce_fusion.1 = (f32[768]{0:T(1024)S(1)}, f32[1920]{0:T(1024)S(1)}, f32[768]{0:T(1024)S(1)}, f32[1920,768]{1,0:T(8,128)S(1)}) fusion(f32[1920,768]{1,0:T(8,128)S(1)} %bitcast.160, f32[1920]{0:T(1024)S(1)} %fusion.50, f32[1920]{0:T(1024)S(1)} %broadcast_multiply_fusion, f32[768]{0:T(1024)S(1)} %copy-done.41, f32[1920,768]{1,0:T(8,128)} %fusion.80, ...), kind=kOutput, calls=%fused_computation.22 | convolution fusion | flops 2278191872 | bytes 21855744 | tf_op jit(solution)/shard_map/dot_general | solution.py:37
  304.2 6.4 %reshape.518 = bf16[15,128,12,64]{1,0,3,2:T(8,128)(2,1)} reshape(bf16[1920,768]{0,1:T(8,128)(2,1)} %copy.84) | data formatting | bytes 5898240 | tf_op jit(solution)/shard_map/reshape | solution.py:246
  310.6 14.4 %multiply_reduce_fusion = (f32[15,12,128]{2,1,0:T(8,128)S(1)}, f32[15,12,128,128]{2,3,1,0:T(8,128)}) fusion(f32[15,12,128,128]{2,3,1,0:T(8,128)} %get-tuple-element.80, f32[15,12,128]{2,1,0:T(8,128)S(1)} %get-tuple-element.79, bf16[15,128,12,64]{1,0,3,2:T(8,128)(2,1)} %reshape.510, bf16[15,128,12,64]{1,0,3,2:T(8,128)(2,1)} %reshape.518), kind=kOutput, calls=%fused_computation.8 | convolution fusion | flops 386311680 | bytes 29675520 | tf_op jit(solution)/shard_map/rqhe,rkhe->rhqk/dot_general | solution.py:248
  325.1 9.4 %multiply_convert_fusion.1 = bf16[15,12,128,128]{2,3,1,0:T(8,128)(2,1)S(1)} fusion(f32[15,12,128,128]{2,3,1,0:T(8,128)} %get-tuple-element.87, f32[15,12,128]{2,1,0:T(8,128)S(1)} %get-tuple-element.86, f32[15,12,128,128]{2,3,1,0:T(8,128)} %get-tuple-element.80, f32[15,12,128]{2,1,0:T(8,128)S(1)} %get-tuple-element.79), kind=kLoop, calls=%fused_computation.7 | loop fusion | flops 11796480 | bytes 29675520 | tf_op jit(solution)/shard_map/convert_element_type | solution.py:252
  334.5 5.4 fusion.9
  342.0 10.3 %convert_bitcast_fusion = bf16[15,128,12,64]{1,3,2,0:T(8,128)(2,1)} fusion(bf16[15,128,12,64]{1,0,3,2:T(8,128)(2,1)S(1)} %copy-done.18, f32[15,12,128,128]{2,3,1,0:T(8,128)} %get-tuple-element.80, f32[15,12,128]{2,1,0:T(8,128)S(1)} %get-tuple-element.79), kind=kOutput, calls=%fused_computation.61 | convolution fusion | flops 384860160 | bytes 17786880 | tf_op jit(solution)/shard_map/rhqk,rqhe->rkhe/dot_general | solution.py:261
  357.8 5.0 fusion.81
  373.1 5.5 %fusion.82 = f32[1920,768]{1,0:T(8,128)} fusion(bf16[1920,768]{0,1:T(8,128)(2,1)S(1)} %bitcast.186, bf16[768,768]{1,0:T(8,128)(2,1)S(1)} %bitcast.198), kind=kOutput, calls=%fused_computation.194 | convolution fusion | flops 2264924160 | bytes 10027008 | tf_op jit(solution)/shard_map/dot_general | solution.py:29
  382.5 12.0 %multiply_reduce_fusion.2 = (f32[768]{0:T(1024)S(1)}, f32[1920]{0:T(1024)S(1)}, f32[768]{0:T(1024)S(1)}, f32[1920,768]{1,0:T(8,128)}) fusion(f32[15,128,768]{2,1,0:T(8,128)S(1)} %bitcast.158, f32[1920]{0:T(1024)S(1)} %copy-done.32, f32[1920]{0:T(1024)S(1)} %copy-done.33, f32[768]{0:T(1024)S(1)} %copy-done.35, bf16[1920,768]{0,1:T(8,128)(2,1)S(1)} %bitcast.170, ...), kind=kOutput, calls=%fused_computation.25 | convolution fusion | flops 2279666432 | bytes 27753984 | tf_op jit(solution)/shard_map/dot_general | solution.py:29
  394.5 8.1 %fusion.69 = (f32[1920]{0:T(1024)S(1)}, f32[1920,768]{1,0:T(8,128)}, bf16[1920,768]{1,0:T(8,128)(2,1)}) fusion(f32[1920]{0:T(1024)S(1)} %fusion.49, f32[1920]{0:T(1024)S(1)} %copy-done.32, f32[15,128,768]{2,1,0:T(8,128)S(1)} %bitcast.158, f32[1920]{0:T(1024)S(1)} %copy-done.33, f32[1920,768]{1,0:T(8,128)} %get-tuple-element.88, f32[768]{0:T(1024)S(1)} %copy-done.35, ...), kind=kLoop, calls=%fused_computation.181 | loop fusion | flops 16218240 | bytes 20680704 | tf_op jit(solution)/shard_map/transpose(jvp())/reduce_sum | solution.py:19
  402.7 6.0 %fusion.68 = (bf16[1920,768]{1,0:T(8,128)(2,1)}, f32[1920,768]{1,0:T(8,128)}) fusion(f32[1920,768]{1,0:T(8,128)} %get-tuple-element.48, f32[1920]{0:T(1024)S(1)} %negate_multiply_fusion, f32[1920,768]{1,0:T(8,128)S(1)} %bitcast.164, f32[1920,768]{1,0:T(8,128)S(1)} %bitcast.166, f32[1920]{0:T(1024)S(1)} %negate_multiply_fusion.1), kind=kLoop, calls=%fused_computation.180 | loop fusion | flops 7372800 | bytes 26557440 | tf_op jit(solution)/shard_map/convert_element_type | solution.py:282
  421.3 12.1 %fusion.79 = f32[1920,768]{1,0:T(8,128)} fusion(bf16[1920,2304]{1,0:T(8,128)(2,1)} %get-tuple-element.83, bf16[2304,768]{1,0:T(8,128)(2,1)} %bitcast.189), kind=kOutput, calls=%fused_computation.191 | convolution fusion | flops 6794772480 | bytes 18284544 | tf_op jit(solution)/shard_map/dot_general | solution.py:29
  433.4 26.1 %all-reduce.5.cloned.1.call-done = f32[1736,768]{1,0:T(8,128)} async-done(((f32[1736,768]{1,0:T(8,128)}), f32[1736,768]{1,0:T(8,128)}) %all-reduce.5.cloned.1.call-update) | async-done | bytes 5333008 | tf_op jit(solution)/shard_map/psum | solution.py:236
  465.1 9.6 %add_convert_fusion.3 = bf16[1920,768]{1,0:T(8,128)(2,1)} fusion(f32[1920,768]{1,0:T(8,128)} %copy-done.2, f32[1920,768]{1,0:T(8,128)} %fusion.79, bf16[1920,768]{1,0:T(8,128)(2,1)} %copy-done.51, bf16[768,768]{1,0:T(8,128)(2,1)S(1)} %copy-done.40, f32[768]{0:T(1024)S(1)} %copy-done.50), kind=kOutput, calls=%fused_computation.35 | convolution fusion | flops 2270822400 | bytes 18877440 | tf_op jit(solution)/shard_map/dot_general | solution.py:29
  478.6 51.3 %all-reduce.7.cloned.1.call-done = (f32[1010,192]{0,1:T(8,128)}, f32[768,192]{0,1:T(8,128)}, f32[768,192]{0,1:T(8,128)}, f32[768,192]{0,1:T(8,128)}) async-done(((f32[1010,192]{0,1:T(8,128)}, f32[768,192]{0,1:T(8,128)}, f32[768,192]{0,1:T(8,128)}, f32[768,192]{0,1:T(8,128)}), (f32[1010,192]{0,1:T(8,128)}, f32[768,192]{0,1:T(8,128)}, f32[768,192]{0,1:T(8,128)}, ...) | async-done | bytes 2545168 | tf_op jit(solution)/shard_map/psum | solution.py:311
  (266 shorter events, 150.3 us)
Async XLA Ops:
  7.2 16.8 %copy-start = (bf16[1000,768]{1,0:T(8,128)(2,1)S(1)}, bf16[1000,768]{1,0:T(8,128)(2,1)}, u32[]{:S(2)}) copy-start(bf16[1000,768]{1,0:T(8,128)(2,1)} %param.25) | copy-start | bytes 4608004
  7.2 25.9 %copy-start.36 = (s32[15,128]{1,0:T(8,128)S(1)}, s32[15,128]{1,0:T(8,128)}, u32[]{:S(2)}) copy-start(s32[15,128]{1,0:T(8,128)} %param.23) | copy-start | bytes 23044
  7.2 89.6 %all-gather.3.cloned.1.call-start = ((), (), s32[]{:S(2)}) async-start(), calls=%async_computation | async-start | bytes 9732096 | tf_op jit(solution)/shard_map/all_gather | solution.py:61
  12.3 210.5 %all-gather.5.cloned.1.call-start = ((), (), s32[]{:S(2)}) async-start(), calls=%async_computation.1 | async-start | bytes 19464192 | tf_op jit(solution)/shard_map/all_gather | solution.py:61
  13.5 21.2 %copy-start.34 = (f32[768]{0:T(1024)S(1)}, f32[768]{0:T(1024)}, u32[]{:S(2)}) copy-start(f32[768]{0:T(1024)} %param.26) | copy-start | bytes 9220
  13.5 21.2 %copy-start.42 = (f32[768]{0:T(1024)S(1)}, f32[768]{0:T(1024)}, u32[]{:S(2)}) copy-start(f32[768]{0:T(1024)} %param.27) | copy-start | bytes 9220
  15.5 444.0 %all-reduce.5.cloned.1.call-start = ((), (), s32[]{:S(2)}) async-start(), calls=%async_computation.2 | async-start | bytes 10665984 | tf_op jit(solution)/shard_map/psum | solution.py:236
  16.3 27.4 %collective-permute-start = (f32[1152]{0:T(1024)S(1)}, f32[1152]{0:T(1024)S(1)}, u32[]{:S(2)}, u32[]{:S(2)}) collective-permute-start(f32[1152]{0:T(1024)S(1)} %concatenate.56), channel_id=1, source_target_pairs={{0,1},{1,2},{2,3},{3,0},{4,5},{5,6},{6,7},{7,4},{8,9},{9,10},{10,1... | collective-permute-start | bytes 13832 | tf_op jit(solution)/shard_map/ppermute | solution.py:92
  19.4 24.4 %collective-permute-start.1 = (f32[1152]{0:T(1024)S(1)}, f32[1152]{0:T(1024)S(1)}, u32[]{:S(2)}, u32[]{:S(2)}) collective-permute-start(f32[1152]{0:T(1024)S(1)} %concatenate.56), channel_id=1, source_target_pairs={{0,2},{1,3},{2,0},{3,1},{4,6},{5,7},{6,4},{7,5},{8,10},{9,11},{10,... | collective-permute-start | bytes 13832 | tf_op jit(solution)/shard_map/ppermute | solution.py:92
  22.0 21.8 %collective-permute-start.2 = (f32[1152]{0:T(1024)S(1)}, f32[1152]{0:T(1024)S(1)}, u32[]{:S(2)}, u32[]{:S(2)}) collective-permute-start(f32[1152]{0:T(1024)S(1)} %concatenate.56), channel_id=1, source_target_pairs={{0,3},{1,0},{2,1},{3,2},{4,7},{5,4},{6,5},{7,6},{8,11},{9,8},{10,9... | collective-permute-start | bytes 13832 | tf_op jit(solution)/shard_map/ppermute | solution.py:92
  102.7 16.0 %copy-start.25 = (bf16[4,8,24,768]{3,2,1,0:T(8,128)(2,1)}, bf16[4,8,24,768]{3,2,1,0:T(8,128)(2,1)S(1)}, u32[]{:S(2)}) copy-start(bf16[4,8,24,768]{3,2,1,0:T(8,128)(2,1)S(1)} %get-tuple-element.60) | copy-start | bytes 3538948
  102.7 32.9 %copy-start.12 = (bf16[4,8,24,768]{3,2,1,0:T(8,128)(2,1)}, bf16[4,8,24,768]{3,2,1,0:T(8,128)(2,1)S(1)}, u32[]{:S(2)}) copy-start(bf16[4,8,24,768]{3,2,1,0:T(8,128)(2,1)S(1)} %get-tuple-element.62) | copy-start | bytes 3538948
  162.4 18.5 %copy-start.17 = (bf16[15,128,12,64]{1,0,3,2:T(8,128)(2,1)S(1)}, bf16[15,128,12,64]{1,0,3,2:T(8,128)(2,1)}, u32[]{:S(2)}) copy-start(bf16[15,128,12,64]{1,0,3,2:T(8,128)(2,1)} %reshape.510) | copy-start | bytes 8847364
  239.6 13.5 %copy-start.16 = (bf16[3,8,96,768]{3,2,1,0:T(8,128)(2,1)}, bf16[3,8,96,768]{3,2,1,0:T(8,128)(2,1)S(1)}, u32[]{:S(2)}) copy-start(bf16[3,8,96,768]{3,2,1,0:T(8,128)(2,1)S(1)} %get-tuple-element.92) | copy-start | bytes 10616836
  240.0 13.1 %copy-start.22 = (bf16[1920,768]{1,0:T(8,128)(2,1)S(1)}, bf16[1920,768]{1,0:T(8,128)(2,1)}, u32[]{:S(2)}) copy-start(bf16[1920,768]{1,0:T(8,128)(2,1)} %get-tuple-element.22) | copy-start | bytes 8847364
  240.0 42.7 %slice-start.4 = ((s8[5898240]{0:T(1024)(128)(4,1)}), s8[4194304]{0:T(1024)(128)(4,1)S(1)}, s32[]{:S(2)}) async-start(s8[5898240]{0:T(1024)(128)(4,1)} %bitcast.159), calls=%async_computation.8 | async-start | bytes 8388608
  253.1 29.6 %slice-start.5 = ((s8[5898240]{0:T(1024)(128)(4,1)}), s8[1703936]{0:T(1024)(128)(4,1)S(1)}, s32[]{:S(2)}) async-start(s8[5898240]{0:T(1024)(128)(4,1)} %bitcast.159), calls=%async_computation.9 | async-start | bytes 3407872
  253.1 38.3 %slice-start.6 = ((s8[5898240]{0:T(1024)(128)(4,1)}), s8[4194304]{0:T(1024)(128)(4,1)S(1)}, s32[]{:S(2)}) async-start(s8[5898240]{0:T(1024)(128)(4,1)} %bitcast.161), calls=%async_computation.10 | async-start | bytes 8388608
  271.3 11.5 %copy-start.38 = (bf16[768,768]{1,0:T(8,128)(2,1)S(1)}, bf16[768,768]{1,0:T(8,128)(2,1)}, u32[]{:S(2)}) copy-start(bf16[768,768]{1,0:T(8,128)(2,1)} %param.37) | copy-start | bytes 3538948
  271.3 11.5 %copy-start.53 = (bf16[1920,768]{1,0:T(8,128)(2,1)S(1)}, bf16[1920,768]{1,0:T(8,128)(2,1)}, u32[]{:S(2)}) copy-start(bf16[1920,768]{1,0:T(8,128)(2,1)} %copy-done.52) | copy-start | bytes 8847364
  271.3 20.2 %slice-start.7 = ((s8[5898240]{0:T(1024)(128)(4,1)}), s8[1703936]{0:T(1024)(128)(4,1)S(1)}, s32[]{:S(2)}) async-start(s8[5898240]{0:T(1024)(128)(4,1)} %bitcast.161), calls=%async_computation.11 | async-start | bytes 3407872
  367.3 162.6 %all-reduce.7.cloned.1.call-start = ((), (), s32[]{:S(2)}) async-start(), calls=%async_computation.3 | async-start | bytes 5111808 | tf_op jit(solution)/shard_map/psum | solution.py:311
  380.9 21.7 %slice-start.8 = ((s8[5898240]{0:T(1024)(128)(4,1)}), s8[4194304]{0:T(1024)(128)(4,1)S(1)}, s32[]{:S(2)}) async-start(s8[5898240]{0:T(1024)(128)(4,1)} %bitcast.163), calls=%async_computation.12 | async-start | bytes 8388608
  380.9 21.7 %slice-start.10 = ((s8[5898240]{0:T(1024)(128)(4,1)}), s8[4194304]{0:T(1024)(128)(4,1)S(1)}, s32[]{:S(2)}) async-start(s8[5898240]{0:T(1024)(128)(4,1)} %bitcast.165), calls=%async_computation.14 | async-start | bytes 8388608
  382.2 12.3 %copy-start.7 = (bf16[96,8,15,128]{3,1,2,0:T(8,128)(2,1)}, bf16[96,8,15,128]{3,1,2,0:T(8,128)(2,1)S(1)}, u32[]{:S(2)}) copy-start(bf16[96,8,15,128]{3,1,2,0:T(8,128)(2,1)S(1)} %copy.136) | copy-start | bytes 8847364
  382.5 12.0 %copy-start.31 = (f32[15,128]{1,0:T(8,128)S(1)}, f32[15,128]{1,0:T(8,128)}, u32[]{:S(2)}) copy-start(f32[15,128]{1,0:T(8,128)} %copy-done.30) | copy-start | bytes 23044
  382.5 12.0 %copy-start.43 = (f32[768]{0:T(1024)S(1)}, f32[768]{0:T(1024)}, u32[]{:S(2)}) copy-start(f32[768]{0:T(1024)} %param.27) | copy-start | bytes 9220
  382.5 20.1 %slice-start.9 = ((s8[5898240]{0:T(1024)(128)(4,1)}), s8[1703936]{0:T(1024)(128)(4,1)S(1)}, s32[]{:S(2)}) async-start(s8[5898240]{0:T(1024)(128)(4,1)} %bitcast.163), calls=%async_computation.13 | async-start | bytes 3407872
  382.5 20.1 %slice-start.11 = ((s8[5898240]{0:T(1024)(128)(4,1)}), s8[1703936]{0:T(1024)(128)(4,1)S(1)}, s32[]{:S(2)}) async-start(s8[5898240]{0:T(1024)(128)(4,1)} %bitcast.165), calls=%async_computation.15 | async-start | bytes 3407872
  433.4 31.6 %copy-start.40 = (bf16[768,768]{1,0:T(8,128)(2,1)S(1)}, bf16[768,768]{1,0:T(8,128)(2,1)}, u32[]{:S(2)}) copy-start(bf16[768,768]{1,0:T(8,128)(2,1)} %param.39) | copy-start | bytes 3538948
  433.4 31.6 %copy-start.50 = (f32[768]{0:T(1024)S(1)}, f32[768]{0:T(1024)}, u32[]{:S(2)}) copy-start(f32[768]{0:T(1024)} %param.40) | copy-start | bytes 9220
  475.5 66.6 %copy-start.1 = (bf16[1000,768]{1,0:T(8,128)(2,1)S(1)}, bf16[1000,768]{1,0:T(8,128)(2,1)}, u32[]{:S(2)}) copy-start(bf16[1000,768]{1,0:T(8,128)(2,1)} %param.25) | copy-start | bytes 4608004
  (43 other events, 226.9 us)
Sparse Core Ops, SparseCore 0:
  12.4 84.3 all-gather.2
  100.3 122.4 all-gather.4
  367.4 91.9 all-reduce.4
  465.1 64.7 all-reduce.6

commit v13 on v11

--- a/solution.py
+++ b/solution.py
@@ -82,6 +82,19 @@
         for step in range(1, n_mp)
     ]
     return (jnp.stack(blocks) * one).astype(dtype).reshape((n_mp - 1) * n_dp * rows, width)
+
+
+def gather_by_permutes(shard, one, dtype):
+    n_mp = lax.axis_size("mp")
+    me = lax.axis_index("mp")
+    own = shard.astype(jnp.float32) * one
+    got = [own] + [
+        lax.ppermute(own, "mp", [(i, (i + step) % n_mp) for i in range(n_mp)])
+        for step in range(1, n_mp)
+    ]
+    got = jnp.stack(got) * one
+    by_shard = jnp.take(got, (me - jnp.arange(n_mp)) % n_mp, axis=0)
+    return by_shard.astype(dtype).reshape(n_mp * shard.shape[0], shard.shape[1])
 
 
 def gather_biases(shards):
@@ -137,12 +150,11 @@
     ff_width = w_up_shard.shape[1]
     one = 1.0 + 0.0 * ln1_gain[0]
     low_type = jnp.bfloat16
-    q_part, k_part, v_part, o_part = gather_pieces(
+    q_part, k_part, v_part = gather_pieces(
         (
             w_query_shard.T,
             w_key_shard.T,
             w_value_shard.T,
-            w_out_shard,
         ),
         one,
     )
@@ -159,7 +171,7 @@
         ),
         one,
     )
-    w_out = whole_rows(o_part, one, low_type)
+    w_out = gather_by_permutes(w_out_shard, one, low_type)
     w_up_others = other_rows(up_part, one, low_type)
     w_down_others = other_rows(down_part, one, low_type)
     heads = w_query_t.shape[0] // HD

time: 705 us -> 724 us (1.027)
  waiting for transfers between devices: 314 us -> 322 us
    ppermute x0 -> x3, waiting for transfers between devices: none -> 47.1 us  [gather_by_permutes(): lax.ppermute(own, 'mp', [(i, (i + step) % n_mp) for i in range(n_mp)])]
    all_gather x2, waiting for transfers between devices: 179 us -> 141 us  [gather_pieces(): got = lax.all_gather(sent, ('mp', 'dp'), axis=0)]
    unnamed x161 -> x159, local copies, waits for them, and re-layouts: 17.2 us -> 16.4 us
  transfers between devices with their start and end apart: 7 -> 10, of which waited for: 4 -> 5; matrix products, arithmetic and copies ran while one was open for 6% -> 7% of each run, Pallas kernels for 0% -> 0%
where the time goes in v13:
time: 724 us; the launch traced here: 718 us
  waiting for transfers between devices  322 us (44%)
  matrix products  177 us (24%)
  local copies, waits for them, and re-layouts  115 us (16%)
  other arithmetic  76.9 us (11%)
  between operations  16.5 us (2%)
  starting transfers between devices  10.7 us (1%)
    all_gather x2, waiting for transfers between devices, gather_pieces(): got = lax.all_gather(sent, ('mp', 'dp'), axis=0)  141 us
    psum x1, waiting for transfers between devices, on_device(): lax.psum(jnp.concatenate([grad_w_down, grad_w_up], axis=0), 'dp')  80.3 us
    dot_general x8, matrix products, over_cols(): lax.dot_general(left, right, CONTRACT_COLS, preferred_element_type=jnp.fl...  63.9 us
    psum x1, waiting for transfers between devices, on_device(): lax.psum((grad_w_query + tie, grad_w_key, grad_w_value, grad_w_out, packe...  53.7 us
    dot_general x8, matrix products, product(): return jnp.dot(left, right, preferred_element_type=jnp.float32)  51.2 us
    ppermute x3, waiting for transfers between devices, gather_by_permutes(): lax.ppermute(own, 'mp', [(i, (i + step) % n_mp) for i in range(n_mp)])  47.1 us
    dot_general x6, matrix products, over_rows(): lax.dot_general(left, right, CONTRACT_ROWS, preferred_element_type=jnp.fl...  17.2 us
    unnamed x159, local copies, waits for them, and re-layouts  16.4 us
  transfers between devices with their start and end apart: 10, of which 5 were waited for; matrix products, arithmetic and copies ran while one was open for 7% of the time, Pallas kernels for 0%

profile of v13, /device:TPU:0, one launch (start us, length us, event | category | flops | bytes accessed | tf_op | source)
XLA Modules:
  0.0 718.1 jit_solution(5853746849025493959)
XLA Ops:
  12.4 5.1 collective-permute-start.2
  41.4 47.1 %collective-permute-done.4 = f32[192,768]{1,0:T(8,128)} collective-permute-done((f32[192,768]{1,0:T(8,128)S(1)}, f32[192,768]{1,0:T(8,128)}, u32[]{:S(2)}, u32[]{:S(2)}) %collective-permute-start.4) | collective-permute-done | bytes 589856 | tf_op jit(solution)/shard_map/ppermute | solution.py:92
  90.9 19.7 %all-gather.3.cloned.1.call-done = f32[32,72,768]{2,1,0:T(8,128)} async-done(((f32[1,72,768]{2,1,0:T(8,128)}), f32[32,72,768]{2,1,0:T(8,128)}) %all-gather.3.cloned.1.call-update) | async-done | bytes 7077904 | tf_op jit(solution)/shard_map/all_gather | solution.py:61
  110.6 5.3 fusion.25
  125.7 6.1 reshape.522
  131.8 6.3 convolution_convert_fusion.1
  142.7 6.0 reshape.526
  148.8 6.3 add_convert_fusion.5
  159.6 6.6 reshape.524
  166.2 10.3 %fusion.20 = f32[15,12,128,128]{2,3,1,0:T(8,128)} fusion(bf16[15,128,12,64]{1,0,3,2:T(8,128)(2,1)} %reshape.526, bf16[15,128,12,64]{1,0,3,2:T(8,128)(2,1)} %reshape.524), kind=kOutput, calls=%fused_computation.72 | convolution fusion | flops 377487360 | bytes 17694720 | tf_op jit(solution)/shard_map/rqhe,rkhe->rhqk/dot_general | solution.py:47
  176.5 15.8 %fusion.76 = (f32[15,12,128]{2,1,0:T(8,128)S(1)}, f32[15,12,128,128]{2,3,1,0:T(8,128)}) fusion(f32[15,12,128,128]{2,3,1,0:T(8,128)} %fusion.20, pred[15,128,128]{1,2,0:T(8,128)(4,1)S(1)} %or_and_fusion), kind=kOutput, calls=%fused_computation.184 | output fusion | flops 17694848 | bytes 23930880 | tf_op jit(solution)/shard_map/sub | solution.py:197
  192.3 6.7 convert_bitcast_fusion.1
  212.0 5.9 convert_reduce_fusion
  230.9 80.3 %all-reduce.4.cloned.1.call-done = f32[1536,768]{1,0:T(8,128)} async-done(((f32[1536,768]{1,0:T(8,128)}), f32[1536,768]{1,0:T(8,128)}) %all-reduce.4.cloned.1.call-update) | async-done | bytes 4718608 | tf_op jit(solution)/shard_map/psum | solution.py:227
  313.0 4.9 fusion.73
  317.9 120.8 %all-gather.5.cloned.1.call-done = f32[32,192,768]{2,1,0:T(8,128)} async-done(((f32[1,192,768]{2,1,0:T(8,128)}), f32[32,192,768]{2,1,0:T(8,128)}) %all-gather.5.cloned.1.call-update) | async-done | bytes 18874384 | tf_op jit(solution)/shard_map/all_gather | solution.py:61
  438.7 11.6 %fusion.72 = (f32[4,8,96,768]{3,2,1,0:T(8,128)S(1)}, f32[4,8,96,768]{3,2,1,0:T(8,128)}) fusion(f32[4,8,192,768]{3,2,1,0:T(8,128)} %bitcast.177), kind=kLoop, calls=%fused_computation.180 | loop fusion | bytes 37748736 | tf_op jit(solution)/shard_map/slice | solution.py:67
  456.3 13.1 %multiply_convert_fusion = (bf16[1920,2304]{1,0:T(8,128)(2,1)}, f32[1920,2304]{1,0:T(8,128)}) fusion(f32[2304]{0:T(1024)S(1)} %add.353, bf16[1920,768]{1,0:T(8,128)(2,1)S(1)} %copy-done.21, bf16[2304,768]{1,0:T(8,128)(2,1)S(1)} %bitcast.199), kind=kOutput, calls=%fused_computation.6 | convolution fusion | flops 6821314560 | bytes 33039360 | tf_op jit(solution)/shard_map/dot_general | solution.py:37
  469.4 18.1 %add_convert_fusion = bf16[1920,2304]{1,0:T(8,128)(2,1)} fusion(f32[1920,2304]{1,0:T(8,128)} %get-tuple-element.83, f32[2304]{0:T(1024)S(1)} %add.353, bf16[1920,768]{1,0:T(8,128)(2,1)S(1)} %copy-done.24, bf16[2304,768]{1,0:T(8,128)(2,1)S(1)} %bitcast.197), kind=kOutput, calls=%fused_computation.5 | convolution fusion | flops 6856704000 | bytes 33039360 | tf_op jit(solution)/shard_map/dot_general | solution.py:37
  487.6 11.3 %fusion.80 = f32[1920,768]{1,0:T(8,128)} fusion(bf16[1920,2304]{1,0:T(8,128)(2,1)} %add_convert_fusion, bf16[2304,768]{1,0:T(8,128)(2,1)S(1)} %bitcast.200), kind=kOutput, calls=%fused_computation.188 | convolution fusion | flops 6794772480 | bytes 18284544 | tf_op jit(solution)/shard_map/dot_general | solution.py:29
  498.9 5.9 multiply_reduce_fusion.1
  520.4 6.0 reshape.529
  526.5 11.2 %convert_bitcast_fusion = bf16[15,128,12,64]{1,3,2,0:T(8,128)(2,1)} fusion(bf16[15,128,12,64]{1,0,3,2:T(8,128)(2,1)} %reshape.529, f32[15,12,128,128]{2,3,1,0:T(8,128)} %get-tuple-element.79, f32[15,12,128]{2,1,0:T(8,128)S(1)} %copy-done.36), kind=kOutput, calls=%fused_computation.60 | convolution fusion | flops 384860160 | bytes 17786880 | tf_op jit(solution)/shard_map/rhqk,rqhe->rkhe/dot_general | solution.py:259
  537.7 8.8 %multiply_reduce_fusion = (f32[15,12,128]{2,1,0:T(8,128)S(1)}, f32[15,12,128,128]{2,3,1,0:T(8,128)}) fusion(f32[15,12,128,128]{2,3,1,0:T(8,128)} %get-tuple-element.79, f32[15,12,128]{2,1,0:T(8,128)S(1)} %copy-done.36, bf16[15,128,12,64]{1,0,3,2:T(8,128)(2,1)S(1)} %copy-done.18, bf16[15,128,12,64]{1,0,3,2:T(8,128)(2,1)S(1)} %copy-done.19), kind=kOutput, calls=%fused_computation.9 | convolution fusion | flops 386311680 | bytes 29675520 | tf_op jit(solution)/shard_map/rqhe,rkhe->rhqk/dot_general | solution.py:246
  546.5 9.5 %multiply_convert_fusion.1 = bf16[15,12,128,128]{2,3,1,0:T(8,128)(2,1)S(1)} fusion(f32[15,12,128,128]{2,3,1,0:T(8,128)} %get-tuple-element.86, f32[15,12,128]{2,1,0:T(8,128)S(1)} %get-tuple-element.85, f32[15,12,128,128]{2,3,1,0:T(8,128)} %get-tuple-element.79, f32[15,12,128]{2,1,0:T(8,128)S(1)} %copy-done.36), kind=kLoop, calls=%fused_computation.8 | loop fusion | flops 11796480 | bytes 29675520 | tf_op jit(solution)/shard_map/convert_element_type | solution.py:250
  558.0 5.6 fusion.9
  570.7 5.0 fusion.81
  579.8 5.5 fusion.82
  586.5 8.4 %multiply_reduce_fusion.2 = (f32[768]{0:T(1024)S(1)}, f32[1920]{0:T(1024)S(1)}, f32[768]{0:T(1024)S(1)}, f32[1920,768]{1,0:T(8,128)}) fusion(f32[15,128,768]{2,1,0:T(8,128)S(1)} %bitcast.165, f32[1920]{0:T(1024)S(1)} %copy-done.37, f32[1920]{0:T(1024)S(1)} %copy-done.38, f32[768]{0:T(1024)S(1)} %copy-done.40, bf16[1920,768]{0,1:T(8,128)(2,1)S(1)} %bitcast.179, ...), kind=kOutput, calls=%fused_computation.26 | convolution fusion | flops 2279666432 | bytes 27753984 | tf_op jit(solution)/shard_map/dot_general | solution.py:29
  595.0 5.2 fusion.70
  621.3 10.9 %fusion.79 = f32[1920,768]{1,0:T(8,128)S(1)} fusion(bf16[1920,2304]{1,0:T(8,128)(2,1)} %get-tuple-element.82, bf16[2304,768]{1,0:T(8,128)(2,1)} %bitcast.198), kind=kOutput, calls=%fused_computation.187 | convolution fusion | flops 6794772480 | bytes 18284544 | tf_op jit(solution)/shard_map/dot_general | solution.py:29
  636.9 53.7 %all-reduce.6.cloned.1.call-done = (f32[1030,192]{0,1:T(8,128)}, f32[768,192]{0,1:T(8,128)}, f32[768,192]{0,1:T(8,128)}, f32[768,192]{0,1:T(8,128)}, f32[192,768]{1,0:T(8,128)}) async-done(((f32[1030,192]{0,1:T(8,128)}, f32[768,192]{0,1:T(8,128)}, f32[768,192]{0,1:T(8,128)}, f32[768,192]{0,1:T(8,128)}, f32[192,768]{1,0:T(8,128)}), (f32[1030,192]{0,1:T(8,128)}, f32[768,192]{0,1:T(8,128)}, ...) | async-done | bytes 3150352 | tf_op jit(solution)/shard_map/psum | solution.py:315
  (295 shorter events, 158.7 us)
Async XLA Ops:
  7.2 17.0 %copy-start = (bf16[1000,768]{1,0:T(8,128)(2,1)S(1)}, bf16[1000,768]{1,0:T(8,128)(2,1)}, u32[]{:S(2)}) copy-start(bf16[1000,768]{1,0:T(8,128)(2,1)} %param.25) | copy-start | bytes 4608004
  7.2 24.3 %copy-start.39 = (f32[768]{0:T(1024)S(1)}, f32[768]{0:T(1024)}, u32[]{:S(2)}) copy-start(f32[768]{0:T(1024)} %param.26) | copy-start | bytes 9220
  7.2 23.5 %copy-start.41 = (s32[15,128]{1,0:T(8,128)S(1)}, s32[15,128]{1,0:T(8,128)}, u32[]{:S(2)}) copy-start(s32[15,128]{1,0:T(8,128)} %param.23) | copy-start | bytes 23044
  7.2 24.3 %copy-start.47 = (f32[768]{0:T(1024)S(1)}, f32[768]{0:T(1024)}, u32[]{:S(2)}) copy-start(f32[768]{0:T(1024)} %param.27) | copy-start | bytes 9220
  7.2 103.4 %all-gather.3.cloned.1.call-start = ((), (), s32[]{:S(2)}) async-start(), calls=%async_computation | async-start | bytes 7299072 | tf_op jit(solution)/shard_map/all_gather | solution.py:61
  11.5 299.7 %all-reduce.4.cloned.1.call-start = ((), (), s32[]{:S(2)}) async-start(), calls=%async_computation.2 | async-start | bytes 9437184 | tf_op jit(solution)/shard_map/psum | solution.py:227
  12.4 27.7 %collective-permute-start.2 = (f32[1152]{0:T(1024)S(1)}, f32[1152]{0:T(1024)S(1)}, u32[]{:S(2)}, u32[]{:S(2)}) collective-permute-start(f32[1152]{0:T(1024)S(1)} %concatenate.53), channel_id=1, source_target_pairs={{0,3},{1,0},{2,1},{3,2},{4,7},{5,4},{6,5},{7,6},{8,11},{9,8},{10,9... | collective-permute-start | bytes 13832 | tf_op jit(solution)/shard_map/ppermute | solution.py:105
  17.5 23.0 %collective-permute-start.1 = (f32[1152]{0:T(1024)S(1)}, f32[1152]{0:T(1024)S(1)}, u32[]{:S(2)}, u32[]{:S(2)}) collective-permute-start(f32[1152]{0:T(1024)S(1)} %concatenate.53), channel_id=1, source_target_pairs={{0,2},{1,3},{2,0},{3,1},{4,6},{5,7},{6,4},{7,5},{8,10},{9,11},{10,... | collective-permute-start | bytes 13832 | tf_op jit(solution)/shard_map/ppermute | solution.py:105
  17.5 23.0 %collective-permute-start = (f32[1152]{0:T(1024)S(1)}, f32[1152]{0:T(1024)S(1)}, u32[]{:S(2)}, u32[]{:S(2)}) collective-permute-start(f32[1152]{0:T(1024)S(1)} %concatenate.53), channel_id=1, source_target_pairs={{0,1},{1,2},{2,3},{3,0},{4,5},{5,6},{6,7},{7,4},{8,9},{9,10},{10,1... | collective-permute-start | bytes 13832 | tf_op jit(solution)/shard_map/ppermute | solution.py:105
  19.5 21.9 %collective-permute-start.5 = (f32[192,768]{1,0:T(8,128)S(1)}, f32[192,768]{1,0:T(8,128)}, u32[]{:S(2)}, u32[]{:S(2)}) collective-permute-start(f32[192,768]{1,0:T(8,128)S(1)} %get-tuple-element.73), channel_id=1, source_target_pairs={{0,3},{1,0},{2,1},{3,2},{4,7},{5,4},{6,5},{7,6},{8,11},{9,8},{10,9... | collective-permute-start | bytes 1769480 | tf_op jit(solution)/shard_map/ppermute | solution.py:92
  22.4 66.1 %collective-permute-start.4 = (f32[192,768]{1,0:T(8,128)S(1)}, f32[192,768]{1,0:T(8,128)}, u32[]{:S(2)}, u32[]{:S(2)}) collective-permute-start(f32[192,768]{1,0:T(8,128)S(1)} %get-tuple-element.73), channel_id=1, source_target_pairs={{0,2},{1,3},{2,0},{3,1},{4,6},{5,7},{6,4},{7,5},{8,10},{9,11},{10,... | collective-permute-start | bytes 1769480 | tf_op jit(solution)/shard_map/ppermute | solution.py:92
  30.7 197.7 %copy-start.33 = (f32[15,128]{1,0:T(8,128)}, f32[15,128]{1,0:T(8,128)S(1)}, u32[]{:S(2)}) copy-start(f32[15,128]{1,0:T(8,128)S(1)} %multiply_reduce_fusion.6) | copy-start | bytes 23044
  40.0 48.4 %collective-permute-start.3 = (f32[192,768]{1,0:T(8,128)S(1)}, f32[192,768]{1,0:T(8,128)S(1)}, u32[]{:S(2)}, u32[]{:S(2)}) collective-permute-start(f32[192,768]{1,0:T(8,128)S(1)} %get-tuple-element.73), channel_id=1, source_target_pairs={{0,1},{1,2},{2,3},{3,0},{4,5},{5,6},{6,7},{7,4},{8,9},{9,10},{10,1... | collective-permute-start | bytes 1769480 | tf_op jit(solution)/shard_map/ppermute | solution.py:92
  176.5 15.8 %copy-start.17 = (bf16[15,128,12,64]{1,0,3,2:T(8,128)(2,1)S(1)}, bf16[15,128,12,64]{1,0,3,2:T(8,128)(2,1)}, u32[]{:S(2)}) copy-start(bf16[15,128,12,64]{1,0,3,2:T(8,128)(2,1)} %reshape.522) | copy-start | bytes 8847364
  225.9 212.8 %all-gather.5.cloned.1.call-start = ((), (), s32[]{:S(2)}) async-start(), calls=%async_computation.1 | async-start | bytes 19464192 | tf_op jit(solution)/shard_map/all_gather | solution.py:61
  228.1 462.5 %all-reduce.6.cloned.1.call-start = ((), (), s32[]{:S(2)}) async-start(), calls=%async_computation.3 | async-start | bytes 6488064 | tf_op jit(solution)/shard_map/psum | solution.py:315
  455.9 13.5 %copy-start.16 = (bf16[3,8,96,768]{3,2,1,0:T(8,128)(2,1)}, bf16[3,8,96,768]{3,2,1,0:T(8,128)(2,1)S(1)}, u32[]{:S(2)}) copy-start(bf16[3,8,96,768]{3,2,1,0:T(8,128)(2,1)S(1)} %get-tuple-element.91) | copy-start | bytes 10616836
  456.3 13.1 %copy-start.24 = (bf16[1920,768]{1,0:T(8,128)(2,1)S(1)}, bf16[1920,768]{1,0:T(8,128)(2,1)}, u32[]{:S(2)}) copy-start(bf16[1920,768]{1,0:T(8,128)(2,1)} %get-tuple-element.21) | copy-start | bytes 8847364
  456.3 42.5 %slice-start.4 = ((s8[5898240]{0:T(1024)(128)(4,1)}), s8[4194304]{0:T(1024)(128)(4,1)S(1)}, s32[]{:S(2)}) async-start(s8[5898240]{0:T(1024)(128)(4,1)} %bitcast.166), calls=%async_computation.8 | async-start | bytes 8388608
  469.4 29.4 %slice-start.5 = ((s8[5898240]{0:T(1024)(128)(4,1)}), s8[1703936]{0:T(1024)(128)(4,1)S(1)}, s32[]{:S(2)}) async-start(s8[5898240]{0:T(1024)(128)(4,1)} %bitcast.166), calls=%async_computation.9 | async-start | bytes 3407872
  469.4 38.2 %slice-start.8 = ((s8[5898240]{0:T(1024)(128)(4,1)}), s8[4194304]{0:T(1024)(128)(4,1)S(1)}, s32[]{:S(2)}) async-start(s8[5898240]{0:T(1024)(128)(4,1)} %bitcast.170), calls=%async_computation.12 | async-start | bytes 8388608
  487.6 11.3 %copy-start.43 = (bf16[768,768]{1,0:T(8,128)(2,1)S(1)}, bf16[768,768]{1,0:T(8,128)(2,1)}, u32[]{:S(2)}) copy-start(bf16[768,768]{1,0:T(8,128)(2,1)} %param.37) | copy-start | bytes 3538948
  487.6 11.3 %copy-start.58 = (bf16[1920,768]{1,0:T(8,128)(2,1)S(1)}, bf16[1920,768]{1,0:T(8,128)(2,1)}, u32[]{:S(2)}) copy-start(bf16[1920,768]{1,0:T(8,128)(2,1)} %copy-done.57) | copy-start | bytes 8847364
  487.6 20.0 %slice-start.9 = ((s8[5898240]{0:T(1024)(128)(4,1)}), s8[1703936]{0:T(1024)(128)(4,1)S(1)}, s32[]{:S(2)}) async-start(s8[5898240]{0:T(1024)(128)(4,1)} %bitcast.170), calls=%async_computation.13 | async-start | bytes 3407872
  570.7 14.6 %copy-start.11 = (bf16[96,8,15,128]{3,1,2,0:T(8,128)(2,1)}, bf16[96,8,15,128]{3,1,2,0:T(8,128)(2,1)S(1)}, u32[]{:S(2)}) copy-start(bf16[96,8,15,128]{3,1,2,0:T(8,128)(2,1)S(1)} %copy.148) | copy-start | bytes 8847364
  586.5 21.5 %slice-start.12 = ((s8[5898240]{0:T(1024)(128)(4,1)}), s8[4194304]{0:T(1024)(128)(4,1)S(1)}, s32[]{:S(2)}) async-start(s8[5898240]{0:T(1024)(128)(4,1)} %bitcast.174), calls=%async_computation.16 | async-start | bytes 8388608
  595.0 13.1 %slice-start.13 = ((s8[5898240]{0:T(1024)(128)(4,1)}), s8[1703936]{0:T(1024)(128)(4,1)S(1)}, s32[]{:S(2)}) async-start(s8[5898240]{0:T(1024)(128)(4,1)} %bitcast.174), calls=%async_computation.17 | async-start | bytes 3407872
  616.4 15.8 %slice-start.6 = ((s8[5898240]{0:T(1024)(128)(4,1)}), s8[1703936]{0:T(1024)(128)(4,1)S(1)}, s32[]{:S(2)}) async-start(s8[5898240]{0:T(1024)(128)(4,1)} %bitcast.168), calls=%async_computation.10 | async-start | bytes 3407872
  632.2 79.2 %copy-start.1 = (bf16[1000,768]{1,0:T(8,128)(2,1)S(1)}, bf16[1000,768]{1,0:T(8,128)(2,1)}, u32[]{:S(2)}) copy-start(bf16[1000,768]{1,0:T(8,128)(2,1)} %param.25) | copy-start | bytes 4608004
  690.6 18.4 %copy-start.32 = (f32[768,192]{0,1:T(8,128)S(1)}, f32[768,192]{0,1:T(8,128)}, u32[]{:S(2)}) copy-start(f32[768,192]{0,1:T(8,128)} %get-tuple-element.98) | copy-start | bytes 1769476
  690.6 19.2 %copy-start.31 = (f32[768,192]{0,1:T(8,128)S(1)}, f32[768,192]{0,1:T(8,128)}, u32[]{:S(2)}) copy-start(f32[768,192]{0,1:T(8,128)} %get-tuple-element.99) | copy-start | bytes 1769476
  690.6 20.0 %copy-start.30 = (f32[192,768]{1,0:T(8,128)S(1)}, f32[192,768]{1,0:T(8,128)}, u32[]{:S(2)}) copy-start(f32[192,768]{1,0:T(8,128)} %get-tuple-element.101) | copy-start | bytes 1769476
  (53 other events, 312.0 us)
Sparse Core Ops, SparseCore 0:
  11.7 98.8 all-gather.2
  226.0 85.1 all-reduce.3
  314.7 124.0 all-gather.4
  621.3 69.1 all-reduce.5

commit v14 on v11

--- a/solution.py
+++ b/solution.py
@@ -82,6 +82,17 @@
         for step in range(1, n_mp)
     ]
     return (jnp.stack(blocks) * one).astype(dtype).reshape((n_mp - 1) * n_dp * rows, width)
+
+
+def sum_over_dp(values):
+    n_dp = lax.axis_size("dp")
+    if n_dp & (n_dp - 1):
+        return lax.psum(values, "dp")
+    step = 1
+    while step < n_dp:
+        values = values + lax.ppermute(values, "dp", [(i, i ^ step) for i in range(n_dp)])
+        step *= 2
+    return values
 
 
 def gather_biases(shards):
@@ -258,6 +269,10 @@
     grad_w_key = over_rows(normed_low, own_columns(grad_keys, qkv_width))
     grad_w_value = over_rows(normed_low, own_grad_values)
     grad_b_value = column_sum(own_grad_values)
+    tie = 0.0 * ffn_grads[0, 0]
+    grad_w_query, grad_w_key, grad_w_value, grad_w_out = lax.psum(
+        (grad_w_query + tie, grad_w_key, grad_w_value, grad_w_out), "dp"
+    )
     grad_normed = (
         product(grad_queries, w_query_t)
         + product(grad_keys, w_key_t)
@@ -293,23 +308,7 @@
     )
     small_rows = jnp.concatenate(small).reshape(-1, column_count)
     packed = jnp.concatenate([table_grad, small_rows], axis=0)
-    tie = 0.0 * ffn_grads[0, 0]
-    (
-        grad_w_query,
-        grad_w_key,
-        grad_w_value,
-        grad_w_out,
-        packed,
-    ) = lax.psum(
-        (
-            grad_w_query + tie,
-            grad_w_key,
-            grad_w_value,
-            grad_w_out,
-            packed,
-        ),
-        "dp",
-    )
+    packed = sum_over_dp(packed)
     table_grad = packed[:step_count]
     flat_small = packed[step_count:].reshape(-1)
     unpacked, at = [], 0

time: 705 us -> 716 us (1.016)
  matrix products: 177 us -> 185 us
    psum x1, waiting for transfers between devices: 53.7 us -> 19.5 us  [on_device(): lax.psum((grad_w_query + tie, grad_w_key, grad_w_value, grad_w_out), 'dp')]
    ppermute x0 -> x3, waiting for transfers between devices: none -> 31.6 us  [sum_over_dp(): lax.ppermute(values, 'dp', [(i, i ^ step) for i in range(n_dp)])]
    dot_general x8, matrix products: 51.2 us -> 60 us  [product(): return jnp.dot(left, right, preferred_element_type=jnp.float32)]
    unnamed x161 -> x147, local copies, waits for them, and re-layouts: 17.2 us -> 18.5 us
  transfers between devices with their start and end apart: 7 -> 10, of which waited for: 4 -> 6; matrix products, arithmetic and copies ran while one was open for 6% -> 10% of each run, Pallas kernels for 0% -> 0%
where the time goes in v14:
time: 716 us; the launch traced here: 711 us
  waiting for transfers between devices  311 us (43%)
  matrix products  185 us (26%)
  local copies, waits for them, and re-layouts  108 us (15%)
  other arithmetic  80.4 us (11%)
  between operations  16.4 us (2%)
  starting transfers between devices  9.53 us (1%)
    all_gather x2, waiting for transfers between devices, gather_pieces(): got = lax.all_gather(sent, ('mp', 'dp'), axis=0)  178 us
    psum x1, waiting for transfers between devices, on_device(): lax.psum(jnp.concatenate([grad_w_down, grad_w_up], axis=0), 'dp')  81.7 us
    dot_general x8, matrix products, over_cols(): lax.dot_general(left, right, CONTRACT_COLS, preferred_element_type=jnp.fl...  63.2 us
    dot_general x8, matrix products, product(): return jnp.dot(left, right, preferred_element_type=jnp.float32)  60 us
    ppermute x3, waiting for transfers between devices, sum_over_dp(): lax.ppermute(values, 'dp', [(i, i ^ step) for i in range(n_dp)])  31.6 us
    psum x1, waiting for transfers between devices, on_device(): lax.psum((grad_w_query + tie, grad_w_key, grad_w_value, grad_w_out), 'dp')  19.5 us
    unnamed x147, local copies, waits for them, and re-layouts  18.5 us
    dot_general x6, matrix products, over_rows(): lax.dot_general(left, right, CONTRACT_ROWS, preferred_element_type=jnp.fl...  16.8 us
  transfers between devices with their start and end apart: 10, of which 6 were waited for; matrix products, arithmetic and copies ran while one was open for 10% of the time, Pallas kernels for 0%

profile of v14, /device:TPU:0, one launch (start us, length us, event | category | flops | bytes accessed | tf_op | source)
XLA Modules:
  0.0 711.3 jit_solution(13932926579582704496)
XLA Ops:
  39.1 57.7 %all-gather.3.cloned.1.call-done = f32[32,96,768]{2,1,0:T(8,128)} async-done(((f32[1,96,768]{2,1,0:T(8,128)}), f32[32,96,768]{2,1,0:T(8,128)}) %all-gather.3.cloned.1.call-update) | async-done | bytes 9437200 | tf_op jit(solution)/shard_map/all_gather | solution.py:61
  96.8 6.2 fusion.24
  111.9 6.1 reshape.506
  118.0 5.9 convolution_convert_fusion.1
  128.7 6.0 reshape.510
  134.7 5.9 add_convert_fusion.5
  145.2 6.6 reshape.508
  151.9 10.4 %fusion.20 = f32[15,12,128,128]{2,3,1,0:T(8,128)} fusion(bf16[15,128,12,64]{1,0,3,2:T(8,128)(2,1)} %reshape.510, bf16[15,128,12,64]{1,0,3,2:T(8,128)(2,1)} %reshape.508), kind=kOutput, calls=%fused_computation.71 | convolution fusion | flops 377487360 | bytes 17694720 | tf_op jit(solution)/shard_map/rqhe,rkhe->rhqk/dot_general | solution.py:47
  162.2 15.8 %fusion.76 = (f32[15,12,128]{2,1,0:T(8,128)S(1)}, f32[15,12,128,128]{2,3,1,0:T(8,128)}) fusion(f32[15,12,128,128]{2,3,1,0:T(8,128)} %fusion.20, pred[15,128,128]{1,2,0:T(8,128)(4,1)S(1)} %or_and_fusion), kind=kOutput, calls=%fused_computation.181 | output fusion | flops 17694848 | bytes 23930880 | tf_op jit(solution)/shard_map/sub | solution.py:196
  178.7 6.9 convert_bitcast_fusion.1
  198.6 5.9 convert_reduce_fusion
  216.1 81.7 %all-reduce.4.cloned.1.call-done = f32[1536,768]{1,0:T(8,128)} async-done(((f32[1536,768]{1,0:T(8,128)}), f32[1536,768]{1,0:T(8,128)}) %all-reduce.4.cloned.1.call-update) | async-done | bytes 4718608 | tf_op jit(solution)/shard_map/psum | solution.py:226
  304.5 120.8 %all-gather.5.cloned.1.call-done = f32[32,192,768]{2,1,0:T(8,128)} async-done(((f32[1,192,768]{2,1,0:T(8,128)}), f32[32,192,768]{2,1,0:T(8,128)}) %all-gather.5.cloned.1.call-update) | async-done | bytes 18874384 | tf_op jit(solution)/shard_map/all_gather | solution.py:61
  425.3 11.6 %fusion.72 = (f32[4,8,96,768]{3,2,1,0:T(8,128)S(1)}, f32[4,8,96,768]{3,2,1,0:T(8,128)}) fusion(f32[4,8,192,768]{3,2,1,0:T(8,128)} %bitcast.168), kind=kLoop, calls=%fused_computation.177 | loop fusion | bytes 37748736 | tf_op jit(solution)/shard_map/slice | solution.py:67
  442.9 13.1 %multiply_convert_fusion = (bf16[1920,2304]{1,0:T(8,128)(2,1)}, f32[1920,2304]{1,0:T(8,128)}) fusion(f32[2304]{0:T(1024)S(1)} %add.357, bf16[1920,768]{1,0:T(8,128)(2,1)S(1)} %copy-done.22, bf16[2304,768]{1,0:T(8,128)(2,1)S(1)} %bitcast.188), kind=kOutput, calls=%fused_computation.5 | convolution fusion | flops 6821314560 | bytes 33039360 | tf_op jit(solution)/shard_map/dot_general | solution.py:37
  456.0 18.1 %add_convert_fusion = bf16[1920,2304]{1,0:T(8,128)(2,1)} fusion(f32[1920,2304]{1,0:T(8,128)} %get-tuple-element.81, f32[2304]{0:T(1024)S(1)} %add.357, bf16[1920,768]{1,0:T(8,128)(2,1)S(1)} %copy-done.25, bf16[2304,768]{1,0:T(8,128)(2,1)S(1)} %bitcast.186), kind=kOutput, calls=%fused_computation.4 | convolution fusion | flops 6856704000 | bytes 33039360 | tf_op jit(solution)/shard_map/dot_general | solution.py:37
  474.2 11.2 %fusion.80 = f32[1920,768]{1,0:T(8,128)} fusion(bf16[1920,2304]{1,0:T(8,128)(2,1)} %add_convert_fusion, bf16[2304,768]{1,0:T(8,128)(2,1)S(1)} %bitcast.189), kind=kOutput, calls=%fused_computation.185 | convolution fusion | flops 6794772480 | bytes 18284544 | tf_op jit(solution)/shard_map/dot_general | solution.py:29
  485.4 5.9 multiply_reduce_fusion.1
  506.9 6.0 reshape.514
  512.9 11.2 %convert_bitcast_fusion = bf16[15,128,12,64]{1,3,2,0:T(8,128)(2,1)} fusion(bf16[15,128,12,64]{1,0,3,2:T(8,128)(2,1)} %reshape.514, f32[15,12,128,128]{2,3,1,0:T(8,128)} %get-tuple-element.77, f32[15,12,128]{2,1,0:T(8,128)S(1)} %copy-done.36), kind=kOutput, calls=%fused_computation.59 | convolution fusion | flops 384860160 | bytes 17786880 | tf_op jit(solution)/shard_map/rhqk,rqhe->rkhe/dot_general | solution.py:258
  524.2 8.8 %multiply_reduce_fusion = (f32[15,12,128]{2,1,0:T(8,128)S(1)}, f32[15,12,128,128]{2,3,1,0:T(8,128)}) fusion(f32[15,12,128,128]{2,3,1,0:T(8,128)} %get-tuple-element.77, f32[15,12,128]{2,1,0:T(8,128)S(1)} %copy-done.36, bf16[15,128,12,64]{1,0,3,2:T(8,128)(2,1)S(1)} %copy-done.19, bf16[15,128,12,64]{1,0,3,2:T(8,128)(2,1)S(1)} %copy-done.20), kind=kOutput, calls=%fused_computation.8 | convolution fusion | flops 386311680 | bytes 29675520 | tf_op jit(solution)/shard_map/rqhe,rkhe->rhqk/dot_general | solution.py:245
  533.0 9.5 %multiply_convert_fusion.1 = bf16[15,12,128,128]{2,3,1,0:T(8,128)(2,1)S(1)} fusion(f32[15,12,128,128]{2,3,1,0:T(8,128)} %get-tuple-element.84, f32[15,12,128]{2,1,0:T(8,128)S(1)} %get-tuple-element.83, f32[15,12,128,128]{2,3,1,0:T(8,128)} %get-tuple-element.77, f32[15,12,128]{2,1,0:T(8,128)S(1)} %copy-done.36), kind=kLoop, calls=%fused_computation.7 | loop fusion | flops 11796480 | bytes 29675520 | tf_op jit(solution)/shard_map/convert_element_type | solution.py:249
  544.5 5.6 fusion.9
  566.3 5.6 fusion.82
  572.3 10.3 %multiply_reduce_fusion.2 = (f32[768]{0:T(1024)S(1)}, f32[1920]{0:T(1024)S(1)}, f32[768]{0:T(1024)S(1)}, f32[1920,768]{1,0:T(8,128)}) fusion(f32[15,128,768]{2,1,0:T(8,128)S(1)} %bitcast.160, f32[1920]{0:T(1024)S(1)} %copy-done.37, f32[1920]{0:T(1024)S(1)} %copy-done.38, f32[768]{0:T(1024)S(1)} %copy-done.40, bf16[1920,768]{0,1:T(8,128)(2,1)S(1)} %bitcast.170, ...), kind=kOutput, calls=%fused_computation.25 | convolution fusion | flops 2279666432 | bytes 27753984 | tf_op jit(solution)/shard_map/dot_general | solution.py:29
  582.7 8.1 %fusion.70 = (f32[1920]{0:T(1024)S(1)}, f32[1920,768]{1,0:T(8,128)}, bf16[1920,768]{1,0:T(8,128)(2,1)}) fusion(f32[1920]{0:T(1024)S(1)} %fusion.49, f32[1920]{0:T(1024)S(1)} %copy-done.37, f32[15,128,768]{2,1,0:T(8,128)S(1)} %bitcast.160, f32[1920]{0:T(1024)S(1)} %copy-done.38, f32[1920,768]{1,0:T(8,128)} %get-tuple-element.85, f32[768]{0:T(1024)S(1)} %copy-done.40, ...), kind=kLoop, calls=%fused_computation.175 | loop fusion | flops 16218240 | bytes 20680704 | tf_op jit(solution)/shard_map/transpose(jvp())/reduce_sum | solution.py:19
  590.8 6.1 fusion.69
  601.3 12.4 %fusion.79 = f32[1920,768]{1,0:T(8,128)} fusion(bf16[1920,2304]{1,0:T(8,128)(2,1)} %get-tuple-element.80, bf16[2304,768]{1,0:T(8,128)(2,1)} %bitcast.187), kind=kOutput, calls=%fused_computation.184 | convolution fusion | flops 6794772480 | bytes 18284544 | tf_op jit(solution)/shard_map/dot_general | solution.py:29
  626.7 19.0 %collective-permute-done.4 = f32[1030,192]{0,1:T(8,128)S(1)} collective-permute-done((f32[1030,192]{0,1:T(8,128)S(1)}, f32[1030,192]{0,1:T(8,128)S(1)}, u32[]{:S(2)}, u32[]{:S(2)}) %collective-permute-start.4) | collective-permute-done | bytes 791072 | tf_op jit(solution)/shard_map/ppermute | solution.py:93
  647.3 10.1 %add_convert_fusion.3 = bf16[1920,768]{1,0:T(8,128)(2,1)} fusion(f32[1920,768]{1,0:T(8,128)} %copy-done.2, f32[1920,768]{1,0:T(8,128)} %fusion.79, bf16[1920,768]{1,0:T(8,128)(2,1)} %copy-done.54, bf16[768,768]{1,0:T(8,128)(2,1)} %param.39, f32[768]{0:T(1024)S(1)} %copy-done.53), kind=kOutput, calls=%fused_computation.34 | convolution fusion | flops 2270822400 | bytes 18877440 | tf_op jit(solution)/shard_map/dot_general | solution.py:29
  657.4 12.6 %collective-permute-done.5 = f32[1030,192]{0,1:T(8,128)S(1)} collective-permute-done((f32[1030,192]{0,1:T(8,128)S(1)}, f32[1030,192]{0,1:T(8,128)S(1)}, u32[]{:S(2)}, u32[]{:S(2)}) %collective-permute-start.5) | collective-permute-done | bytes 791072 | tf_op jit(solution)/shard_map/ppermute | solution.py:93
  677.4 19.5 %all-reduce.6.cloned.1.call-done = (f32[768,192]{0,1:T(8,128)}, f32[768,192]{0,1:T(8,128)}, f32[768,192]{0,1:T(8,128)}, f32[192,768]{1,0:T(8,128)}) async-done(((f32[768,192]{0,1:T(8,128)}, f32[768,192]{0,1:T(8,128)}, f32[768,192]{0,1:T(8,128)}, f32[192,768]{1,0:T(8,128)}), (f32[768,192]{0,1:T(8,128)}, f32[768,192]{0,1:T(8,128)}, f32[768,192]{0,1:T(8,128)}, ...) | async-done | bytes 2359312 | tf_op jit(solution)/shard_map/psum | solution.py:273
  (278 shorter events, 154.1 us)
Async XLA Ops:
  7.2 12.8 %copy-start = (bf16[1000,768]{1,0:T(8,128)(2,1)S(1)}, bf16[1000,768]{1,0:T(8,128)(2,1)}, u32[]{:S(2)}) copy-start(bf16[1000,768]{1,0:T(8,128)(2,1)} %param.25) | copy-start | bytes 4608004
  7.2 22.3 %copy-start.39 = (f32[768]{0:T(1024)S(1)}, f32[768]{0:T(1024)}, u32[]{:S(2)}) copy-start(f32[768]{0:T(1024)} %param.26) | copy-start | bytes 9220
  7.2 21.2 %copy-start.41 = (s32[15,128]{1,0:T(8,128)S(1)}, s32[15,128]{1,0:T(8,128)}, u32[]{:S(2)}) copy-start(s32[15,128]{1,0:T(8,128)} %param.23) | copy-start | bytes 23044
  7.2 22.3 %copy-start.46 = (f32[768]{0:T(1024)S(1)}, f32[768]{0:T(1024)}, u32[]{:S(2)}) copy-start(f32[768]{0:T(1024)} %param.27) | copy-start | bytes 9220
  7.2 89.5 %all-gather.3.cloned.1.call-start = ((), (), s32[]{:S(2)}) async-start(), calls=%async_computation | async-start | bytes 9732096 | tf_op jit(solution)/shard_map/all_gather | solution.py:61
  12.3 285.5 %all-reduce.4.cloned.1.call-start = ((), (), s32[]{:S(2)}) async-start(), calls=%async_computation.2 | async-start | bytes 9437184 | tf_op jit(solution)/shard_map/psum | solution.py:226
  13.2 25.0 %collective-permute-start.2 = (f32[1152]{0:T(1024)S(1)}, f32[1152]{0:T(1024)S(1)}, u32[]{:S(2)}, u32[]{:S(2)}) collective-permute-start(f32[1152]{0:T(1024)S(1)} %concatenate.56), channel_id=1, source_target_pairs={{0,3},{1,0},{2,1},{3,2},{4,7},{5,4},{6,5},{7,6},{8,11},{9,8},{10,9... | collective-permute-start | bytes 13832 | tf_op jit(solution)/shard_map/ppermute | solution.py:103
  18.3 19.9 %collective-permute-start.1 = (f32[1152]{0:T(1024)S(1)}, f32[1152]{0:T(1024)S(1)}, u32[]{:S(2)}, u32[]{:S(2)}) collective-permute-start(f32[1152]{0:T(1024)S(1)} %concatenate.56), channel_id=1, source_target_pairs={{0,2},{1,3},{2,0},{3,1},{4,6},{5,7},{6,4},{7,5},{8,10},{9,11},{10,... | collective-permute-start | bytes 13832 | tf_op jit(solution)/shard_map/ppermute | solution.py:103
  18.3 19.9 %collective-permute-start = (f32[1152]{0:T(1024)S(1)}, f32[1152]{0:T(1024)S(1)}, u32[]{:S(2)}, u32[]{:S(2)}) collective-permute-start(f32[1152]{0:T(1024)S(1)} %concatenate.56), channel_id=1, source_target_pairs={{0,1},{1,2},{2,3},{3,0},{4,5},{5,6},{6,7},{7,4},{8,9},{9,10},{10,1... | collective-permute-start | bytes 13832 | tf_op jit(solution)/shard_map/ppermute | solution.py:103
  28.4 186.4 %copy-start.33 = (f32[15,128]{1,0:T(8,128)}, f32[15,128]{1,0:T(8,128)S(1)}, u32[]{:S(2)}) copy-start(f32[15,128]{1,0:T(8,128)S(1)} %multiply_reduce_fusion.6) | copy-start | bytes 23044
  103.0 14.9 %copy-start.28 = (bf16[4,8,24,768]{3,2,1,0:T(8,128)(2,1)}, bf16[4,8,24,768]{3,2,1,0:T(8,128)(2,1)S(1)}, u32[]{:S(2)}) copy-start(bf16[4,8,24,768]{3,2,1,0:T(8,128)(2,1)S(1)} %get-tuple-element.53) | copy-start | bytes 3538948
  162.2 16.5 %copy-start.18 = (bf16[15,128,12,64]{1,0,3,2:T(8,128)(2,1)S(1)}, bf16[15,128,12,64]{1,0,3,2:T(8,128)(2,1)}, u32[]{:S(2)}) copy-start(bf16[15,128,12,64]{1,0,3,2:T(8,128)(2,1)} %reshape.506) | copy-start | bytes 8847364
  212.5 212.8 %all-gather.5.cloned.1.call-start = ((), (), s32[]{:S(2)}) async-start(), calls=%async_computation.1 | async-start | bytes 19464192 | tf_op jit(solution)/shard_map/all_gather | solution.py:61
  214.7 482.2 %all-reduce.6.cloned.1.call-start = ((), (), s32[]{:S(2)}) async-start(), calls=%async_computation.3 | async-start | bytes 4718592 | tf_op jit(solution)/shard_map/psum | solution.py:273
  442.6 13.5 %copy-start.17 = (bf16[3,8,96,768]{3,2,1,0:T(8,128)(2,1)}, bf16[3,8,96,768]{3,2,1,0:T(8,128)(2,1)S(1)}, u32[]{:S(2)}) copy-start(bf16[3,8,96,768]{3,2,1,0:T(8,128)(2,1)S(1)} %get-tuple-element.89) | copy-start | bytes 10616836
  442.9 13.1 %copy-start.25 = (bf16[1920,768]{1,0:T(8,128)(2,1)S(1)}, bf16[1920,768]{1,0:T(8,128)(2,1)}, u32[]{:S(2)}) copy-start(bf16[1920,768]{1,0:T(8,128)(2,1)} %get-tuple-element.21) | copy-start | bytes 8847364
  442.9 42.4 %slice-start = ((s8[5898240]{0:T(1024)(128)(4,1)}), s8[4194304]{0:T(1024)(128)(4,1)S(1)}, s32[]{:S(2)}) async-start(s8[5898240]{0:T(1024)(128)(4,1)} %bitcast.155), calls=%async_computation.4 | async-start | bytes 8388608
  456.0 29.4 %slice-start.1 = ((s8[5898240]{0:T(1024)(128)(4,1)}), s8[1703936]{0:T(1024)(128)(4,1)S(1)}, s32[]{:S(2)}) async-start(s8[5898240]{0:T(1024)(128)(4,1)} %bitcast.155), calls=%async_computation.5 | async-start | bytes 3407872
  456.0 38.1 %slice-start.6 = ((s8[5898240]{0:T(1024)(128)(4,1)}), s8[4194304]{0:T(1024)(128)(4,1)S(1)}, s32[]{:S(2)}) async-start(s8[5898240]{0:T(1024)(128)(4,1)} %bitcast.161), calls=%async_computation.10 | async-start | bytes 8388608
  474.2 20.0 %slice-start.7 = ((s8[5898240]{0:T(1024)(128)(4,1)}), s8[1703936]{0:T(1024)(128)(4,1)S(1)}, s32[]{:S(2)}) async-start(s8[5898240]{0:T(1024)(128)(4,1)} %bitcast.161), calls=%async_computation.11 | async-start | bytes 3407872
  553.6 18.6 %copy-start.8 = (bf16[96,8,15,128]{3,1,2,0:T(8,128)(2,1)}, bf16[96,8,15,128]{3,1,2,0:T(8,128)(2,1)S(1)}, u32[]{:S(2)}) copy-start(bf16[96,8,15,128]{3,1,2,0:T(8,128)(2,1)S(1)} %copy.146) | copy-start | bytes 8847364
  557.2 14.7 %copy-start.12 = (bf16[96,8,15,128]{3,1,2,0:T(8,128)(2,1)}, bf16[96,8,15,128]{3,1,2,0:T(8,128)(2,1)S(1)}, u32[]{:S(2)}) copy-start(bf16[96,8,15,128]{3,1,2,0:T(8,128)(2,1)S(1)} %copy.148) | copy-start | bytes 8847364
  566.2 24.5 %slice-start.8 = ((s8[5898240]{0:T(1024)(128)(4,1)}), s8[4194304]{0:T(1024)(128)(4,1)S(1)}, s32[]{:S(2)}) async-start(s8[5898240]{0:T(1024)(128)(4,1)} %bitcast.163), calls=%async_computation.12 | async-start | bytes 8388608
  566.2 24.5 %slice-start.10 = ((s8[5898240]{0:T(1024)(128)(4,1)}), s8[4194304]{0:T(1024)(128)(4,1)S(1)}, s32[]{:S(2)}) async-start(s8[5898240]{0:T(1024)(128)(4,1)} %bitcast.165), calls=%async_computation.14 | async-start | bytes 8388608
  572.3 18.5 %slice-start.9 = ((s8[5898240]{0:T(1024)(128)(4,1)}), s8[1703936]{0:T(1024)(128)(4,1)S(1)}, s32[]{:S(2)}) async-start(s8[5898240]{0:T(1024)(128)(4,1)} %bitcast.163), calls=%async_computation.13 | async-start | bytes 3407872
  572.3 18.5 %slice-start.11 = ((s8[5898240]{0:T(1024)(128)(4,1)}), s8[1703936]{0:T(1024)(128)(4,1)S(1)}, s32[]{:S(2)}) async-start(s8[5898240]{0:T(1024)(128)(4,1)} %bitcast.165), calls=%async_computation.15 | async-start | bytes 3407872
  601.0 12.7 %copy-start.4 = (bf16[1920,768]{1,0:T(8,128)(2,1)S(1)}, bf16[1920,768]{1,0:T(8,128)(2,1)}, u32[]{:S(2)}) copy-start(bf16[1920,768]{1,0:T(8,128)(2,1)} %get-tuple-element.56) | copy-start | bytes 8847364
  601.0 15.7 %collective-permute-start.3 = (f32[1030,192]{0,1:T(8,128)S(1)}, f32[1030,192]{0,1:T(8,128)S(1)}, u32[]{:S(2)}, u32[]{:S(2)}) collective-permute-start(f32[1030,192]{0,1:T(8,128)S(1)} %pad_maximum_fusion.1), channel_id=1, source_target_pairs={{0,4},{4,0},{8,12},{12,8},{16,20},{20,16},{24,28},{28,24},{1,5},{5... | collective-permute-start | bytes 2373128 | tf_op jit(solution)/shard_map/ppermute | solution.py:93
  616.8 28.9 %collective-permute-start.4 = (f32[1030,192]{0,1:T(8,128)S(1)}, f32[1030,192]{0,1:T(8,128)S(1)}, u32[]{:S(2)}, u32[]{:S(2)}) collective-permute-start(f32[1030,192]{0,1:T(8,128)S(1)} %fusion.66), channel_id=1, source_target_pairs={{0,8},{4,12},{8,0},{12,4},{16,24},{20,28},{24,16},{28,20},{1,9},{5... | collective-permute-start | bytes 2373128 | tf_op jit(solution)/shard_map/ppermute | solution.py:93
  621.1 26.2 %copy-start.53 = (f32[768]{0:T(1024)S(1)}, f32[768]{0:T(1024)}, u32[]{:S(2)}) copy-start(f32[768]{0:T(1024)} %param.40) | copy-start | bytes 9220
  645.8 24.1 %collective-permute-start.5 = (f32[1030,192]{0,1:T(8,128)S(1)}, f32[1030,192]{0,1:T(8,128)S(1)}, u32[]{:S(2)}, u32[]{:S(2)}) collective-permute-start(f32[1030,192]{0,1:T(8,128)S(1)} %add.374), channel_id=1, source_target_pairs={{0,16},{4,20},{8,24},{12,28},{16,0},{20,4},{24,8},{28,12},{1,17},{... | collective-permute-start | bytes 2373128 | tf_op jit(solution)/shard_map/ppermute | solution.py:93
  647.3 57.3 %copy-start.1 = (bf16[1000,768]{1,0:T(8,128)(2,1)S(1)}, bf16[1000,768]{1,0:T(8,128)(2,1)}, u32[]{:S(2)}) copy-start(bf16[1000,768]{1,0:T(8,128)(2,1)} %param.25) | copy-start | bytes 4608004
  (47 other events, 275.3 us)
Sparse Core Ops, SparseCore 0:
  12.5 84.2 all-gather.2
  212.7 85.0 all-reduce.3
  301.3 124.0 all-gather.4
  626.8 70.0 all-reduce.5

commit v15 on v14

--- a/solution.py
+++ b/solution.py
@@ -84,15 +84,22 @@
     return (jnp.stack(blocks) * one).astype(dtype).reshape((n_mp - 1) * n_dp * rows, width)
 
 
-def sum_over_dp(values):
+def gather_over_dp(block):
     n_dp = lax.axis_size("dp")
     if n_dp & (n_dp - 1):
-        return lax.psum(values, "dp")
+        return lax.all_gather(block, "dp", axis=0, tiled=True)
+    me = lax.axis_index("dp")
     step = 1
     while step < n_dp:
-        values = values + lax.ppermute(values, "dp", [(i, i ^ step) for i in range(n_dp)])
+        other = lax.ppermute(block, "dp", [(i, i ^ step) for i in range(n_dp)])
+        upper = (me & step) != 0
+        block = jnp.where(
+            upper,
+            jnp.concatenate([other, block], axis=0),
+            jnp.concatenate([block, other], axis=0),
+        )
         step *= 2
-    return values
+    return block
 
 
 def gather_biases(shards):
@@ -284,17 +291,6 @@
     row_sums = jnp.sum(grad_start.reshape(row_count, seq_len, model_width), axis=1)
     column_count = model_width // lax.axis_size("mp")
     table_columns = own_columns(row_sums, column_count)
-    step_count = step_table.shape[0]
-    one_hot = (timesteps[:, None] == jnp.arange(step_count, dtype=jnp.int32)[None, :]).astype(
-        jnp.float32
-    )
-    table_grad = lax.dot_general(
-        one_hot,
-        table_columns,
-        CONTRACT_ROWS,
-        precision=lax.Precision.HIGHEST,
-        preferred_element_type=jnp.float32,
-    )
     small = (
         grad_ln1_gain,
         grad_ln1_shift,
@@ -307,10 +303,30 @@
         grad_ln2_shift,
     )
     small_rows = jnp.concatenate(small).reshape(-1, column_count)
-    packed = jnp.concatenate([table_grad, small_rows], axis=0)
-    packed = sum_over_dp(packed)
-    table_grad = packed[:step_count]
-    flat_small = packed[step_count:].reshape(-1)
+    step_row = jnp.pad(
+        timesteps.astype(jnp.float32), (0, column_count - row_count)
+    ).reshape(1, column_count)
+    block = jnp.concatenate([table_columns, small_rows, step_row], axis=0)
+    blocks = gather_over_dp(block)
+    n_blocks = blocks.shape[0] // block.shape[0]
+    blocks = blocks.reshape(n_blocks, block.shape[0], column_count)
+    all_rows = blocks[:, :row_count].reshape(n_blocks * row_count, column_count)
+    all_steps = blocks[:, -1, :row_count].reshape(-1).astype(jnp.int32)
+    step_count = step_table.shape[0]
+    one_hot = (all_steps[:, None] == jnp.arange(step_count, dtype=jnp.int32)[None, :]).astype(
+        jnp.float32
+    )
+    table_grad = lax.dot_general(
+        one_hot,
+        all_rows,
+        CONTRACT_ROWS,
+        precision=lax.Precision.HIGHEST,
+        preferred_element_type=jnp.float32,
+    )
+    small_sum = blocks[0, row_count:-1]
+    for i in range(1, n_blocks):
+        small_sum = small_sum + blocks[i, row_count:-1]
+    flat_small = small_sum.reshape(-1)
     unpacked, at = [], 0
     for item in small:
         unpacked.append(flat_small[at : at + item.shape[0]])

time: 716 us -> 693 us (0.968)
  waiting for transfers between devices: 311 us -> 303 us
  other arithmetic: 80.4 us -> 73.2 us
    ppermute x3, waiting for transfers between devices: 31.6 us -> 0.01 us  [gather_over_dp(): other = lax.ppermute(block, 'dp', [(i, i ^ step) for i in range(n_dp)])]
    psum x1, waiting for transfers between devices: 19.5 us -> 43.2 us  [on_device(): lax.psum((grad_w_query + tie, grad_w_key, grad_w_value, grad_w_out), 'dp')]
    dot_general x8, matrix products: 60 us -> 51.9 us  [product(): return jnp.dot(left, right, preferred_element_type=jnp.float32)]
  transfers between devices with their start and end apart: 10 -> 10, of which waited for: 6 -> 4; matrix products, arithmetic and copies ran while one was open for 10% -> 8% of each run, Pallas kernels for 0% -> 0%
where the time goes in v15:
time: 693 us; the launch traced here: 688 us
  waiting for transfers between devices  303 us (44%)
  matrix products  179 us (26%)
  local copies, waits for them, and re-layouts  107 us (15%)
  other arithmetic  73.2 us (11%)
  between operations  16.5 us (2%)
  starting transfers between devices  9.45 us (1%)
    all_gather x2, waiting for transfers between devices, gather_pieces(): got = lax.all_gather(sent, ('mp', 'dp'), axis=0)  179 us
    psum x1, waiting for transfers between devices, on_device(): lax.psum(jnp.concatenate([grad_w_down, grad_w_up], axis=0), 'dp')  81.1 us
    dot_general x8, matrix products, over_cols(): lax.dot_general(left, right, CONTRACT_COLS, preferred_element_type=jnp.fl...  63.1 us
    dot_general x8, matrix products, product(): return jnp.dot(left, right, preferred_element_type=jnp.float32)  51.9 us
    psum x1, waiting for transfers between devices, on_device(): lax.psum((grad_w_query + tie, grad_w_key, grad_w_value, grad_w_out), 'dp')  43.2 us
    unnamed x147, local copies, waits for them, and re-layouts  18.8 us
    dot_general x6, matrix products, over_rows(): lax.dot_general(left, right, CONTRACT_ROWS, preferred_element_type=jnp.fl...  17.9 us
    sub x1, other arithmetic, on_device(): powers = jnp.exp(scores - row_max)  15.8 us
  transfers between devices with their start and end apart: 10, of which 4 were waited for; matrix products, arithmetic and copies ran while one was open for 8% of the time, Pallas kernels for 0%

profile of v15, /device:TPU:0, one launch (start us, length us, event | category | flops | bytes accessed | tf_op | source)
XLA Modules:
  0.0 688.1 jit_solution(2160137981840596504)
XLA Ops:
  13.2 5.1 collective-permute-start.2
  39.1 57.7 %all-gather.3.cloned.1.call-done = f32[32,96,768]{2,1,0:T(8,128)} async-done(((f32[1,96,768]{2,1,0:T(8,128)}), f32[32,96,768]{2,1,0:T(8,128)}) %all-gather.3.cloned.1.call-update) | async-done | bytes 9437200 | tf_op jit(solution)/shard_map/all_gather | solution.py:61
  96.8 6.2 fusion.24
  107.1 4.6 copy.72
  111.8 6.0 reshape.526
  117.8 5.9 convolution_convert_fusion.1
  123.7 4.8 copy.74
  128.5 6.0 reshape.530
  134.5 5.9 add_convert_fusion.5
  145.0 6.6 reshape.528
  151.7 10.3 %fusion.20 = f32[15,12,128,128]{2,3,1,0:T(8,128)} fusion(bf16[15,128,12,64]{1,0,3,2:T(8,128)(2,1)} %reshape.530, bf16[15,128,12,64]{1,0,3,2:T(8,128)(2,1)} %reshape.528), kind=kOutput, calls=%fused_computation.71 | convolution fusion | flops 377487360 | bytes 17694720 | tf_op jit(solution)/shard_map/rqhe,rkhe->rhqk/dot_general | solution.py:47
  162.0 15.8 %fusion.76 = (f32[15,12,128]{2,1,0:T(8,128)S(1)}, f32[15,12,128,128]{2,3,1,0:T(8,128)}) fusion(f32[15,12,128,128]{2,3,1,0:T(8,128)} %fusion.20, pred[15,128,128]{1,2,0:T(8,128)(4,1)S(1)} %or_and_fusion), kind=kOutput, calls=%fused_computation.191 | output fusion | flops 17694848 | bytes 23930880 | tf_op jit(solution)/shard_map/sub | solution.py:203
  178.5 6.9 convert_bitcast_fusion.1
  198.4 5.9 convert_reduce_fusion
  216.4 81.1 %all-reduce.5.cloned.1.call-done = f32[1536,768]{1,0:T(8,128)} async-done(((f32[1536,768]{1,0:T(8,128)}), f32[1536,768]{1,0:T(8,128)}) %all-reduce.5.cloned.1.call-update) | async-done | bytes 4718608 | tf_op jit(solution)/shard_map/psum | solution.py:233
  299.4 4.9 fusion.71
  304.3 120.8 %all-gather.5.cloned.1.call-done = f32[32,192,768]{2,1,0:T(8,128)} async-done(((f32[1,192,768]{2,1,0:T(8,128)}), f32[32,192,768]{2,1,0:T(8,128)}) %all-gather.5.cloned.1.call-update) | async-done | bytes 18874384 | tf_op jit(solution)/shard_map/all_gather | solution.py:61
  425.1 11.6 %fusion.70 = (f32[4,8,96,768]{3,2,1,0:T(8,128)S(1)}, f32[4,8,96,768]{3,2,1,0:T(8,128)}) fusion(f32[4,8,192,768]{3,2,1,0:T(8,128)} %bitcast.172), kind=kLoop, calls=%fused_computation.185 | loop fusion | bytes 37748736 | tf_op jit(solution)/shard_map/slice | solution.py:67
  442.7 13.1 %multiply_convert_fusion = (bf16[1920,2304]{1,0:T(8,128)(2,1)}, f32[1920,2304]{1,0:T(8,128)}) fusion(f32[2304]{0:T(1024)S(1)} %add.377, bf16[1920,768]{1,0:T(8,128)(2,1)S(1)} %copy-done.21, bf16[2304,768]{1,0:T(8,128)(2,1)S(1)} %bitcast.192), kind=kOutput, calls=%fused_computation.5 | convolution fusion | flops 6821314560 | bytes 33039360 | tf_op jit(solution)/shard_map/dot_general | solution.py:37
  455.8 18.0 %add_convert_fusion = bf16[1920,2304]{1,0:T(8,128)(2,1)} fusion(f32[1920,2304]{1,0:T(8,128)} %get-tuple-element.83, f32[2304]{0:T(1024)S(1)} %add.377, bf16[1920,768]{1,0:T(8,128)(2,1)S(1)} %copy-done.24, bf16[2304,768]{1,0:T(8,128)(2,1)S(1)} %bitcast.190), kind=kOutput, calls=%fused_computation.4 | convolution fusion | flops 6856704000 | bytes 33039360 | tf_op jit(solution)/shard_map/dot_general | solution.py:37
  473.8 11.2 %fusion.80 = f32[1920,768]{1,0:T(8,128)} fusion(bf16[1920,2304]{1,0:T(8,128)(2,1)} %add_convert_fusion, bf16[2304,768]{1,0:T(8,128)(2,1)S(1)} %bitcast.193), kind=kOutput, calls=%fused_computation.195 | convolution fusion | flops 6794772480 | bytes 18284544 | tf_op jit(solution)/shard_map/dot_general | solution.py:29
  485.1 5.9 multiply_reduce_fusion.1
  506.6 6.0 reshape.534
  512.6 11.2 %convert_bitcast_fusion = bf16[15,128,12,64]{1,3,2,0:T(8,128)(2,1)} fusion(bf16[15,128,12,64]{1,0,3,2:T(8,128)(2,1)} %reshape.534, f32[15,12,128,128]{2,3,1,0:T(8,128)} %get-tuple-element.79, f32[15,12,128]{2,1,0:T(8,128)S(1)} %copy-done.35), kind=kOutput, calls=%fused_computation.59 | convolution fusion | flops 384860160 | bytes 17786880 | tf_op jit(solution)/shard_map/rhqk,rqhe->rkhe/dot_general | solution.py:265
  523.8 8.7 %multiply_reduce_fusion = (f32[15,12,128]{2,1,0:T(8,128)S(1)}, f32[15,12,128,128]{2,3,1,0:T(8,128)}) fusion(f32[15,12,128,128]{2,3,1,0:T(8,128)} %get-tuple-element.79, f32[15,12,128]{2,1,0:T(8,128)S(1)} %copy-done.35, bf16[15,128,12,64]{1,0,3,2:T(8,128)(2,1)S(1)} %copy-done.18, bf16[15,128,12,64]{1,0,3,2:T(8,128)(2,1)S(1)} %copy-done.19), kind=kOutput, calls=%fused_computation.8 | convolution fusion | flops 386311680 | bytes 29675520 | tf_op jit(solution)/shard_map/rqhe,rkhe->rhqk/dot_general | solution.py:252
  532.6 9.5 %multiply_convert_fusion.1 = bf16[15,12,128,128]{2,3,1,0:T(8,128)(2,1)S(1)} fusion(f32[15,12,128,128]{2,3,1,0:T(8,128)} %get-tuple-element.86, f32[15,12,128]{2,1,0:T(8,128)S(1)} %get-tuple-element.85, f32[15,12,128,128]{2,3,1,0:T(8,128)} %get-tuple-element.79, f32[15,12,128]{2,1,0:T(8,128)S(1)} %copy-done.35), kind=kLoop, calls=%fused_computation.7 | loop fusion | flops 11796480 | bytes 29675520 | tf_op jit(solution)/shard_map/convert_element_type | solution.py:256
  544.1 5.6 fusion.9
  563.7 5.0 fusion.82
  569.1 6.4 multiply_reduce_fusion.2
  583.8 11.2 %fusion.79 = f32[1920,768]{1,0:T(8,128)} fusion(bf16[1920,2304]{1,0:T(8,128)(2,1)} %get-tuple-element.82, bf16[2304,768]{1,0:T(8,128)(2,1)S(1)} %bitcast.191), kind=kOutput, calls=%fused_computation.194 | convolution fusion | flops 6794772480 | bytes 18284544 | tf_op jit(solution)/shard_map/dot_general | solution.py:29
  613.5 10.0 %add_convert_fusion.3 = bf16[1920,768]{1,0:T(8,128)(2,1)} fusion(f32[1920,768]{1,0:T(8,128)} %copy-done.2, f32[1920,768]{1,0:T(8,128)} %fusion.79, bf16[1920,768]{1,0:T(8,128)(2,1)} %copy-done.54, bf16[768,768]{1,0:T(8,128)(2,1)S(1)} %copy-done.44, f32[768]{0:T(1024)S(1)} %copy-done.53), kind=kOutput, calls=%fused_computation.34 | convolution fusion | flops 2270822400 | bytes 18877440 | tf_op jit(solution)/shard_map/dot_general | solution.py:29
  630.5 43.2 %all-reduce.7.cloned.1.call-done = (f32[768,192]{0,1:T(8,128)}, f32[768,192]{0,1:T(8,128)}, f32[768,192]{0,1:T(8,128)}, f32[192,768]{1,0:T(8,128)}) async-done(((f32[768,192]{0,1:T(8,128)}, f32[768,192]{0,1:T(8,128)}, f32[768,192]{0,1:T(8,128)}, f32[192,768]{1,0:T(8,128)}), (f32[768,192]{0,1:T(8,128)}, f32[768,192]{0,1:T(8,128)}, f32[768,192]{0,1:T(8,128)}, ...) | async-done | bytes 2359312 | tf_op jit(solution)/shard_map/psum | solution.py:280
  (277 shorter events, 140.1 us)
Async XLA Ops:
  7.2 12.8 %copy-start = (bf16[1000,768]{1,0:T(8,128)(2,1)S(1)}, bf16[1000,768]{1,0:T(8,128)(2,1)}, u32[]{:S(2)}) copy-start(bf16[1000,768]{1,0:T(8,128)(2,1)} %param.25) | copy-start | bytes 4608004
  7.2 22.4 %copy-start.38 = (f32[768]{0:T(1024)S(1)}, f32[768]{0:T(1024)}, u32[]{:S(2)}) copy-start(f32[768]{0:T(1024)} %param.26) | copy-start | bytes 9220
  7.2 21.3 %copy-start.40 = (s32[15,128]{1,0:T(8,128)S(1)}, s32[15,128]{1,0:T(8,128)}, u32[]{:S(2)}) copy-start(s32[15,128]{1,0:T(8,128)} %param.23) | copy-start | bytes 23044
  7.2 22.4 %copy-start.46 = (f32[768]{0:T(1024)S(1)}, f32[768]{0:T(1024)}, u32[]{:S(2)}) copy-start(f32[768]{0:T(1024)} %param.27) | copy-start | bytes 9220
  7.2 89.5 %all-gather.3.cloned.1.call-start = ((), (), s32[]{:S(2)}) async-start(), calls=%async_computation | async-start | bytes 9732096 | tf_op jit(solution)/shard_map/all_gather | solution.py:61
  12.3 285.2 %all-reduce.5.cloned.1.call-start = ((), (), s32[]{:S(2)}) async-start(), calls=%async_computation.2 | async-start | bytes 9437184 | tf_op jit(solution)/shard_map/psum | solution.py:233
  13.2 24.9 %collective-permute-start.2 = (f32[1152]{0:T(1024)S(1)}, f32[1152]{0:T(1024)S(1)}, u32[]{:S(2)}, u32[]{:S(2)}) collective-permute-start(f32[1152]{0:T(1024)S(1)} %concatenate.76), channel_id=1, source_target_pairs={{0,3},{1,0},{2,1},{3,2},{4,7},{5,4},{6,5},{7,6},{8,11},{9,8},{10,9... | collective-permute-start | bytes 13832 | tf_op jit(solution)/shard_map/ppermute | solution.py:110
  18.3 19.8 %collective-permute-start.1 = (f32[1152]{0:T(1024)S(1)}, f32[1152]{0:T(1024)S(1)}, u32[]{:S(2)}, u32[]{:S(2)}) collective-permute-start(f32[1152]{0:T(1024)S(1)} %concatenate.76), channel_id=1, source_target_pairs={{0,2},{1,3},{2,0},{3,1},{4,6},{5,7},{6,4},{7,5},{8,10},{9,11},{10,... | collective-permute-start | bytes 13832 | tf_op jit(solution)/shard_map/ppermute | solution.py:110
  18.3 19.9 %collective-permute-start = (f32[1152]{0:T(1024)S(1)}, f32[1152]{0:T(1024)S(1)}, u32[]{:S(2)}, u32[]{:S(2)}) collective-permute-start(f32[1152]{0:T(1024)S(1)} %concatenate.76), channel_id=1, source_target_pairs={{0,1},{1,2},{2,3},{3,0},{4,5},{5,6},{6,7},{7,4},{8,9},{9,10},{10,1... | collective-permute-start | bytes 13832 | tf_op jit(solution)/shard_map/ppermute | solution.py:110
  28.5 186.7 %copy-start.32 = (f32[15,128]{1,0:T(8,128)}, f32[15,128]{1,0:T(8,128)S(1)}, u32[]{:S(2)}) copy-start(f32[15,128]{1,0:T(8,128)S(1)} %multiply_reduce_fusion.6) | copy-start | bytes 23044
  103.0 14.8 %copy-start.27 = (bf16[4,8,24,768]{3,2,1,0:T(8,128)(2,1)}, bf16[4,8,24,768]{3,2,1,0:T(8,128)(2,1)S(1)}, u32[]{:S(2)}) copy-start(bf16[4,8,24,768]{3,2,1,0:T(8,128)(2,1)S(1)} %get-tuple-element.51) | copy-start | bytes 3538948
  162.0 16.5 %copy-start.17 = (bf16[15,128,12,64]{1,0,3,2:T(8,128)(2,1)S(1)}, bf16[15,128,12,64]{1,0,3,2:T(8,128)(2,1)}, u32[]{:S(2)}) copy-start(bf16[15,128,12,64]{1,0,3,2:T(8,128)(2,1)} %reshape.526) | copy-start | bytes 8847364
  177.9 11.2 %slice-start.2 = ((s8[5898240]{0:T(1024)(128)(4,1)}), s8[4194304]{0:T(1024)(128)(4,1)S(1)}, s32[]{:S(2)}) async-start(s8[5898240]{0:T(1024)(128)(4,1)} %bitcast.161), calls=%async_computation.6 | async-start | bytes 8388608
  212.3 212.8 %all-gather.5.cloned.1.call-start = ((), (), s32[]{:S(2)}) async-start(), calls=%async_computation.1 | async-start | bytes 19464192 | tf_op jit(solution)/shard_map/all_gather | solution.py:61
  214.4 459.3 %all-reduce.7.cloned.1.call-start = ((), (), s32[]{:S(2)}) async-start(), calls=%async_computation.3 | async-start | bytes 4718592 | tf_op jit(solution)/shard_map/psum | solution.py:280
  442.3 13.5 %copy-start.15 = (bf16[3,8,96,768]{3,2,1,0:T(8,128)(2,1)}, bf16[3,8,96,768]{3,2,1,0:T(8,128)(2,1)S(1)}, u32[]{:S(2)}) copy-start(bf16[3,8,96,768]{3,2,1,0:T(8,128)(2,1)S(1)} %get-tuple-element.91) | copy-start | bytes 10616836
  442.7 13.1 %copy-start.24 = (bf16[1920,768]{1,0:T(8,128)(2,1)S(1)}, bf16[1920,768]{1,0:T(8,128)(2,1)}, u32[]{:S(2)}) copy-start(bf16[1920,768]{1,0:T(8,128)(2,1)} %get-tuple-element.21) | copy-start | bytes 8847364
  442.7 42.4 %slice-start = ((s8[5898240]{0:T(1024)(128)(4,1)}), s8[4194304]{0:T(1024)(128)(4,1)S(1)}, s32[]{:S(2)}) async-start(s8[5898240]{0:T(1024)(128)(4,1)} %bitcast.159), calls=%async_computation.4 | async-start | bytes 8388608
  455.8 29.3 %slice-start.1 = ((s8[5898240]{0:T(1024)(128)(4,1)}), s8[1703936]{0:T(1024)(128)(4,1)S(1)}, s32[]{:S(2)}) async-start(s8[5898240]{0:T(1024)(128)(4,1)} %bitcast.159), calls=%async_computation.5 | async-start | bytes 3407872
  455.8 38.0 %slice-start.6 = ((s8[5898240]{0:T(1024)(128)(4,1)}), s8[4194304]{0:T(1024)(128)(4,1)S(1)}, s32[]{:S(2)}) async-start(s8[5898240]{0:T(1024)(128)(4,1)} %bitcast.165), calls=%async_computation.10 | async-start | bytes 8388608
  473.8 11.2 %copy-start.42 = (bf16[768,768]{1,0:T(8,128)(2,1)S(1)}, bf16[768,768]{1,0:T(8,128)(2,1)}, u32[]{:S(2)}) copy-start(bf16[768,768]{1,0:T(8,128)(2,1)} %param.37) | copy-start | bytes 3538948
  473.8 11.2 %copy-start.56 = (bf16[1920,768]{1,0:T(8,128)(2,1)S(1)}, bf16[1920,768]{1,0:T(8,128)(2,1)}, u32[]{:S(2)}) copy-start(bf16[1920,768]{1,0:T(8,128)(2,1)} %copy-done.55) | copy-start | bytes 8847364
  473.8 20.0 %slice-start.7 = ((s8[5898240]{0:T(1024)(128)(4,1)}), s8[1703936]{0:T(1024)(128)(4,1)S(1)}, s32[]{:S(2)}) async-start(s8[5898240]{0:T(1024)(128)(4,1)} %bitcast.165), calls=%async_computation.11 | async-start | bytes 3407872
  556.7 11.9 %copy-start.10 = (bf16[96,8,15,128]{3,1,2,0:T(8,128)(2,1)}, bf16[96,8,15,128]{3,1,2,0:T(8,128)(2,1)S(1)}, u32[]{:S(2)}) copy-start(bf16[96,8,15,128]{3,1,2,0:T(8,128)(2,1)S(1)} %copy.132) | copy-start | bytes 8847364
  578.7 16.3 %slice-start.8 = ((s8[5898240]{0:T(1024)(128)(4,1)}), s8[4194304]{0:T(1024)(128)(4,1)S(1)}, s32[]{:S(2)}) async-start(s8[5898240]{0:T(1024)(128)(4,1)} %bitcast.167), calls=%async_computation.12 | async-start | bytes 8388608
  582.2 12.8 %slice-start.10 = ((s8[5898240]{0:T(1024)(128)(4,1)}), s8[4194304]{0:T(1024)(128)(4,1)S(1)}, s32[]{:S(2)}) async-start(s8[5898240]{0:T(1024)(128)(4,1)} %bitcast.169), calls=%async_computation.14 | async-start | bytes 8388608
  583.8 11.2 %slice-start.9 = ((s8[5898240]{0:T(1024)(128)(4,1)}), s8[1703936]{0:T(1024)(128)(4,1)S(1)}, s32[]{:S(2)}) async-start(s8[5898240]{0:T(1024)(128)(4,1)} %bitcast.167), calls=%async_computation.13 | async-start | bytes 3407872
  583.8 11.3 %slice-start.11 = ((s8[5898240]{0:T(1024)(128)(4,1)}), s8[1703936]{0:T(1024)(128)(4,1)S(1)}, s32[]{:S(2)}) async-start(s8[5898240]{0:T(1024)(128)(4,1)} %bitcast.169), calls=%async_computation.15 | async-start | bytes 3407872
  602.9 4.0 collective-permute-start.3
  606.9 5.2 collective-permute-start.4
  612.1 11.4 %collective-permute-start.5 = (f32[184,192]{1,0:T(8,128)S(1)}, f32[184,192]{1,0:T(8,128)S(1)}, u32[]{:S(2)}, u32[]{:S(2)}) collective-permute-start(f32[184,192]{1,0:T(8,128)S(1)} %maximum_select_fusion.1), channel_id=1, source_target_pairs={{0,16},{4,20},{8,24},{12,28},{16,0},{20,4},{24,8},{28,12},{1,17},{... | collective-permute-start | bytes 423944 | tf_op jit(solution)/shard_map/ppermute | solution.py:94
  613.5 67.9 %copy-start.1 = (bf16[1000,768]{1,0:T(8,128)(2,1)S(1)}, bf16[1000,768]{1,0:T(8,128)(2,1)}, u32[]{:S(2)}) copy-start(bf16[1000,768]{1,0:T(8,128)(2,1)} %param.25) | copy-start | bytes 4608004
  (47 other events, 248.2 us)
Sparse Core Ops, SparseCore 0:
  12.5 84.2 all-gather.2
  212.4 85.1 all-reduce.4
  301.0 124.0 all-gather.4
  612.2 61.4 all-reduce.6
